TPU v7x, 32 devices: a whole 2x2x4 slice. The times are simulated.
32 devices in a mesh: groups: 2 (over x), row: 16 (over z, y, core).
Axes of the slice: x: 2, y: 2, z: 4, core: 2. Of those that a mesh axis runs over, the one named last changes fastest.
Arguments:
- left_proj: bfloat16 [128, 8192], P('groups', 'row'), parts along dimension 0, may hold values from -6 to 6
- right_proj: bfloat16 [128, 8192], P('groups', 'row'), parts along dimension 0, may hold values from -6 to 6
- pair_cot: bfloat16 [512, 256, 128], P(('groups', 'row')), parts along dimension 0, may hold values from -6 to 6
- out_weight: bfloat16 [1024, 128], replicated, may hold values from -0.1875 to 0.1875
Outputs:
- grad_left: bfloat16 [128, 8192], P('groups', 'row'), parts along dimension 0
- grad_right: bfloat16 [128, 8192], P('groups', 'row'), parts along dimension 0
There are 2 independent parts, one for each index of `groups`. A program takes and returns all parts, laid end to end along the dimension named above; an argument that names none is the same for every part. Nothing has to cross between parts.
All inputs are finite; a program needn't handle non-finite values.
Results may differ from a plain program's by a relative error of at most 0.005.
Values may be sent and summed in bfloat16 or wider, within the bound.
No kernel may reach another device: no remote copies, remote signals or barrier semaphores. Data moves between devices by JAX's collectives and lax.ppermute only.
A program may use at most 128 MiB of HBM per device.

v0:
```python
import math

import jax
import jax.numpy as jnp
from jax import lax
from jax.sharding import PartitionSpec as P

C = 32


def project_tile(slab, out_weight, n_seq):
    rows = slab.shape[0] * slab.shape[1]
    flat = slab.reshape(rows, slab.shape[2])
    prod = lax.dot_general(
        flat, out_weight, (((1,), (1,)), ((), ())), preferred_element_type=jnp.float32
    )
    return (prod / n_seq).astype(jnp.bfloat16).reshape(slab.shape[0], slab.shape[1], C, C)


def column_blocks(pair_cot, right_full, left_own, out_weight):
    n_seq = right_full.shape[0]
    own_rows = pair_cot.shape[0]
    total = pair_cot.shape[1]
    width = math.gcd(total, 256)
    n_blocks = total // width

    def block_step(carry, index):
        row_acc, partial_value = carry
        begin = index * width
        slab = lax.dynamic_slice_in_dim(pair_cot, begin, width, 1)
        right_blk = lax.dynamic_slice_in_dim(right_full, begin, width, 1)
        grad = project_tile(slab, out_weight, n_seq)
        row_acc = row_acc + jnp.einsum(
            "ijce,sje->sic", grad, right_blk, preferred_element_type=jnp.float32
        )
        piece = jnp.einsum("ijce,sic->sje", grad, left_own, preferred_element_type=jnp.float32)
        partial_value = lax.dynamic_update_slice_in_dim(partial_value, piece, begin, 1)
        return ((row_acc, partial_value), None)

    row_start = jnp.zeros((n_seq, own_rows, C), jnp.float32)
    part_start = jnp.zeros((n_seq, total, C), jnp.float32)
    (row_acc, partial_value), unused = lax.scan(
        block_step, (row_start, part_start), jnp.arange(n_blocks, dtype=jnp.int32)
    )
    return (row_acc, partial_value)


def per_device(left_proj, right_proj, pair_cot, out_weight):
    n_seq = left_proj.shape[0]
    own_rows = pair_cot.shape[0]
    total = pair_cot.shape[1]
    right_full = lax.all_gather(right_proj, "row", axis=1, tiled=True).reshape(n_seq, total, C)
    left_own = left_proj.reshape(n_seq, own_rows, C)
    row_acc, partial_sum = column_blocks(pair_cot, right_full, left_own, out_weight)
    summed = lax.psum_scatter(
        partial_sum.reshape(n_seq, total * C), "row", scatter_dimension=1, tiled=True
    )
    grad_right = summed.astype(jnp.bfloat16)
    grad_left = row_acc.reshape(n_seq, own_rows * C).astype(jnp.bfloat16)
    return (grad_left, grad_right)


def solution(mesh):
    return jax.shard_map(
        per_device,
        mesh=mesh,
        in_specs=(P("groups", "row"), P("groups", "row"), P(("groups", "row"), None, None), P()),
        out_specs=(P("groups", "row"), P("groups", "row")),
        check_vma=False,
    )
```

profile of v0, /device:TPU:0, one launch (start us, length us, event | category | flops | bytes accessed | tf_op | source)
XLA Modules:
  0.0 134.1 jit_solution(7083638522827316975)
XLA Ops:
  7.2 0.0 copy-start
  7.2 0.0 all-gather.2.cloned.1.call-start
  7.2 0.7 all-gather.2.cloned.1.call-update
  7.9 0.0 reduce-scatter.2.cloned.1.call-start
  8.0 0.4 copy-done
  8.4 6.5 %multiply_convert_fusion = bf16[4096,1024]{1,0:T(8,128)(2,1)} fusion(bf16[4096,128]{1,0:T(8,128)(2,1)S(1)} %bitcast.28, bf16[1024,128]{1,0:T(8,128)(2,1)} %param.7), kind=kOutput, calls=%fused_computation | convolution fusion | flops 1082130432 | bytes 9699328 | tf_op jit(solution)/shard_map/while/body/eval_jaxpr/dot_general | solution.py:14
  14.9 11.7 %copy.10 = bf16[4096,1024]{0,1:T(8,128)(2,1)} copy(bf16[4096,1024]{1,0:T(8,128)(2,1)} %multiply_convert_fusion) | data formatting | bytes 16777216 | tf_op jit(solution)/shard_map/while/body/eval_jaxpr/convert_element_type | solution.py:17
  26.6 0.0 copy-start.1
  26.6 9.8 %copy.23 = bf16[128,8,16,256]{3,2,1,0:T(8,128)(2,1)} copy(bf16[128,8,16,256]{3,1,2,0:T(8,128)(2,1)} %bitcast.31) | data formatting | bytes 16777216
  36.3 0.0 copy-done.1
  36.3 0.1 copy.14
  36.5 5.0 %convolution_bitcast_fusion = f32[64,256,32]{1,0,2:T(8,128)S(1)} fusion(bf16[16,256,32,32]{1,0,3,2:T(8,128)(2,1)} %bitcast.29, bf16[64,16,32,1]{0,2,1,3:T(8,128)(2,1)S(1)} %bitcast.35), kind=kOutput, calls=%fused_computation.1 | convolution fusion | flops 536870912 | bytes 10551296 | tf_op jit(solution)/shard_map/while/body/eval_jaxpr/ijce,sic->sje/dot_general | solution.py:36
  41.5 4.5 %copy.16 = f32[64,256,32]{0,2,1:T(8,128)} copy(f32[64,256,32]{1,0,2:T(8,128)S(1)} %convolution_bitcast_fusion) | data formatting | bytes 4194304 | tf_op jit(solution)/shard_map/while/body/eval_jaxpr/ijce,sic->sje/dot_general | solution.py:36
  46.0 0.0 reduce-scatter.2.cloned.1.call-update
  46.0 3.7 %all-gather.2.cloned.1.call-done = bf16[64,8192]{1,0:T(8,128)(2,1)} async-done(((bf16[64,512]{1,0:T(8,128)(2,1)}), bf16[64,8192]{1,0:T(8,128)(2,1)}) %all-gather.2.cloned.1.call-update) | async-done | bytes 1048592 | tf_op jit(solution)/shard_map/all_gather | solution.py:52
  49.7 2.0 %copy.11 = bf16[64,8192]{0,1:T(8,128)(2,1)S(1)} copy(bf16[64,8192]{1,0:T(8,128)(2,1)} %all-gather.2.cloned.1.call-done) | data formatting | bytes 2097152 | tf_op jit(solution)/shard_map/all_gather | solution.py:52
  51.7 2.5 %copy.13 = bf16[64,256,32]{1,0,2:T(8,128)(2,1)} copy(bf16[64,256,32]{0,2,1:T(8,128)(2,1)S(1)} %bitcast.33) | data formatting | bytes 2097152 | tf_op jit(solution)/shard_map/reshape | solution.py:52
  54.3 5.9 %fusion = bf16[16,32,64,1]{2,0,3,1:T(8,128)(2,1)S(1)} fusion(bf16[16,256,32,32]{1,0,3,2:T(8,128)(2,1)} %bitcast.30, bf16[64,256,32]{1,0,2:T(8,128)(2,1)} %copy.13), kind=kOutput, calls=%fused_computation.2 | convolution fusion | flops 536870912 | bytes 9502720 | tf_op jit(solution)/shard_map/while/body/eval_jaxpr/ijce,sje->sic/dot_general | solution.py:33
  60.2 0.7 copy.17
  60.9 64.6 %reduce-scatter.2.cloned.1.call-done = f32[64,512]{0,1:T(8,128)} async-done(((f32[64,8192]{0,1:T(8,128)}), f32[64,512]{0,1:T(8,128)}) %reduce-scatter.2.cloned.1.call-update) | async-done | bytes 131088 | tf_op jit(solution)/shard_map/reduce_scatter | solution.py:55
  125.6 1.0 convert_element_type.20
  126.5 0.7 copy.18
  (1 shorter events, 0.0 us)
Async XLA Ops:
  7.2 1.2 copy-start
  7.2 42.5 %all-gather.2.cloned.1.call-start = ((), (), s32[]{:S(2)}) async-start(), calls=%async_computation.1 | async-start | bytes 1114112 | tf_op jit(solution)/shard_map/all_gather | solution.py:52
  7.9 117.6 %reduce-scatter.2.cloned.1.call-start = ((), (), s32[]{:S(2)}) async-start(), calls=%async_computation.2 | async-start | bytes 4456448 | tf_op jit(solution)/shard_map/reduce_scatter | solution.py:55
  26.6 9.8 %copy-start.1 = (bf16[64,512]{1,0:T(8,128)(2,1)S(1)}, bf16[64,512]{1,0:T(8,128)(2,1)}, u32[]{:S(2)}) copy-start(bf16[64,512]{1,0:T(8,128)(2,1)} %param.4) | copy-start | bytes 196612
Sparse Core Ops, SparseCore 0:
  10.2 39.4 all-gather.1
  53.6 71.9 reduce-scatter.1
where the time goes:
time: 135 us; the launch traced here: 134 us
  waiting for transfers between devices  69 us (51%)
  local copies, waits for them, and re-layouts  32.5 us (24%)
  matrix products  17.5 us (13%)
  between operations  14.1 us (10%)
    reduce_scatter x1, waiting for transfers between devices, per_device(): lax.psum_scatter(partial_sum.reshape(n_seq, total * C), 'row', scatter_di...  64.6 us
    unnamed x8, local copies, waits for them, and re-layouts  11.8 us
    convert_element_type x1, local copies, waits for them, and re-layouts, project_tile(): (prod / n_seq).astype(jnp.bfloat16)  11.7 us
    dot_general x1, matrix products, project_tile(): lax.dot_general(flat, out_weight, (((1,), (1,)), ((), ())), preferred_ele...  6.52 us
    dot_general x1, matrix products, block_step(): jnp.einsum('ijce,sje->sic', grad, right_blk, preferred_element_type=jnp.f...  5.91 us
    dot_general x1, matrix products, block_step(): jnp.einsum('ijce,sic->sje', grad, left_own, preferred_element_type=jnp.fl...  5.02 us
    dot_general x1, local copies, waits for them, and re-layouts, block_step(): jnp.einsum('ijce,sic->sje', grad, left_own, preferred_element_type=jnp.fl...  4.48 us
    all_gather x1, waiting for transfers between devices, per_device(): lax.all_gather(right_proj, 'row', axis=1, tiled=True)  3.71 us
  transfers between devices with their start and end apart: 2, of which 2 were waited for; matrix products, arithmetic and copies ran while one was open for 36% of the time, Pallas kernels for 0%

commit v1 on v0

v1 whole, which is shorter than its diff:
```python
import math

import jax
import jax.numpy as jnp
from jax import lax
from jax.sharding import PartitionSpec as P

C = 32


def xor_pairs(n, bit):
    return [(i, i ^ (1 << bit)) for i in range(n)]


def gather_blocks(x, axis, n, bits):
    me = lax.axis_index(axis)
    buf = x[None]
    done = []
    for bit in bits:
        other = lax.ppermute(buf, axis, xor_pairs(n, bit))
        mine = (me >> bit) & 1
        low = jnp.where(mine == 0, buf, other)
        high = jnp.where(mine == 0, other, buf)
        buf = jnp.concatenate([low, high], 0)
        done = [bit] + done
    k = len(done)
    buf = buf.reshape((2,) * k + x.shape)
    order = sorted(range(k), key=lambda t: -done[t])
    buf = buf.transpose(order + list(range(k, k + x.ndim)))
    return buf.reshape((n,) + x.shape)


def scatter_sum(x, axis, n, bits):
    me = lax.axis_index(axis)
    k = n.bit_length() - 1
    buf = x.reshape((2,) * k + x.shape[1:])
    left = list(range(k - 1, -1, -1))
    for bit in bits:
        t = left.index(bit)
        mine = (me >> bit) & 1
        moved = jnp.moveaxis(buf, t, 0)
        keep = lax.dynamic_index_in_dim(moved, mine, 0, keepdims=False)
        send = lax.dynamic_index_in_dim(moved, 1 - mine, 0, keepdims=False)
        buf = keep + lax.ppermute(send, axis, xor_pairs(n, bit))
        left.pop(t)
    return buf


def index_bits(n):
    return list(range(n.bit_length() - 1))


def per_device(left_proj, right_proj, pair_cot, out_weight):
    n_seq = left_proj.shape[0]
    own_rows = pair_cot.shape[0]
    total = pair_cot.shape[1]
    p_size = pair_cot.shape[2]
    n = lax.axis_size("row")
    width = right_proj.shape[1]
    bits = index_bits(n)
    block = math.gcd(total, 256)

    right_blocks = gather_blocks(right_proj, "row", n, bits[::-1])
    right_full = right_blocks.transpose(1, 0, 2).reshape(n_seq, total, C)

    weight_ec = out_weight.reshape(C, C, p_size).transpose(1, 0, 2).reshape(C * C, p_size)

    pieces = []
    grads = []
    for begin in range(0, total, block):
        slab = pair_cot[:, begin:begin + block, :]
        prod = jnp.einsum("xk,ijk->ixj", weight_ec, slab, preferred_element_type=jnp.float32)
        grad = (prod / n_seq).astype(jnp.bfloat16)
        grad_m = grad.reshape(own_rows, C, C, block).transpose(0, 2, 1, 3).reshape(own_rows * C, C * block)
        grads.append(grad_m)
        piece = jnp.dot(left_proj, grad_m, preferred_element_type=jnp.float32)
        pieces.append(piece.reshape(n_seq, C, block).transpose(0, 2, 1))
    partial = jnp.concatenate(pieces, 1)
    partial_blocks = partial.reshape(n_seq, n, width).transpose(1, 0, 2)
    grad_right = scatter_sum(partial_blocks, "row", n, bits).astype(jnp.bfloat16)

    grad_left = jnp.zeros((n_seq, own_rows * C), jnp.float32)
    for index, begin in enumerate(range(0, total, block)):
        right_t = right_full[:, begin:begin + block, :].transpose(0, 2, 1).reshape(n_seq, C * block)
        grad_left = grad_left + lax.dot_general(
            right_t, grads[index], (((1,), (1,)), ((), ())), preferred_element_type=jnp.float32
        )
    return (grad_left.astype(jnp.bfloat16), grad_right)


def solution(mesh):
    return jax.shard_map(
        per_device,
        mesh=mesh,
        in_specs=(P("groups", "row"), P("groups", "row"), P(("groups", "row"), None, None), P()),
        out_specs=(P("groups", "row"), P("groups", "row")),
        check_vma=False,
    )
```

time: 135 us -> 120 us (0.89)
  waiting for transfers between devices: 69 us -> 21.7 us
  local copies, waits for them, and re-layouts: 32.5 us -> 63.1 us
  between operations: 14.1 us -> 0.8 us
  starting transfers between devices: 0.08 us -> 11.6 us
  other arithmetic: 0.96 us -> 4.61 us
    reduce_scatter x1 -> x0, waiting for transfers between devices: 64.6 us -> none  [per_device(): lax.psum_scatter(partial_sum.reshape(n_seq, total * C), 'row', scatter_di...]
    transpose x0 -> x6, local copies, waits for them, and re-layouts: none -> 23 us  [the longest x1 12.3 us: per_device(): grad.reshape(own_rows, C, C, block).transpose(0, 2, 1, 3)]
    ppermute x0 -> x8, waiting for transfers between devices: none -> 21.7 us  [the longest x4 12.6 us: gather_blocks(): other = lax.ppermute(buf, axis, xor_pairs(n, bit))]
    ppermute x0 -> x8, starting transfers between devices: none -> 11.6 us  [the longest x4 5.81 us: scatter_sum(): buf = keep + lax.ppermute(send, axis, xor_pairs(n, bit))]
    unnamed x8 -> x13, local copies, waits for them, and re-layouts: 11.8 us -> 21.2 us
    dot_general x2 -> x0, local copies, waits for them, and re-layouts: 4.51 us -> none  [the longest x1 4.48 us: block_step(): jnp.einsum('ijce,sic->sje', grad, left_own, preferred_element_type=jnp.fl...]
    all_gather x1 -> x0, waiting for transfers between devices: 3.71 us -> none  [per_device(): lax.all_gather(right_proj, 'row', axis=1, tiled=True)]
    add x0 -> x3, other arithmetic: none -> 3.63 us  [scatter_sum(): buf = keep + lax.ppermute(send, axis, xor_pairs(n, bit))]
  transfers between devices with their start and end apart: 2 -> 8, of which waited for: 2 -> 4; matrix products, arithmetic and copies ran while one was open for 36% -> 16% of each run, Pallas kernels for 0% -> 0%
where the time goes in v1:
time: 120 us; the launch traced here: 119 us
  local copies, waits for them, and re-layouts  63.1 us (53%)
  waiting for transfers between devices  21.7 us (18%)
  matrix products  17.2 us (14%)
  starting transfers between devices  11.6 us (10%)
  other arithmetic  4.61 us (4%)
    unnamed x13, local copies, waits for them, and re-layouts  21.2 us
    ppermute x4, waiting for transfers between devices, gather_blocks(): other = lax.ppermute(buf, axis, xor_pairs(n, bit))  12.6 us
    transpose x1, local copies, waits for them, and re-layouts, per_device(): grad.reshape(own_rows, C, C, block).transpose(0, 2, 1, 3)  12.3 us
    convert_element_type x1, local copies, waits for them, and re-layouts, per_device(): grad = (prod / n_seq).astype(jnp.bfloat16)  12.3 us
    ppermute x4, waiting for transfers between devices, scatter_sum(): buf = keep + lax.ppermute(send, axis, xor_pairs(n, bit))  9.09 us
    dot_general x1, matrix products, per_device(): lax.dot_general(right_t, grads[index], (((1,), (1,)), ((), ())), preferre...  6.71 us
    ppermute x4, starting transfers between devices, scatter_sum(): buf = keep + lax.ppermute(send, axis, xor_pairs(n, bit))  5.81 us
    ppermute x4, starting transfers between devices, gather_blocks(): other = lax.ppermute(buf, axis, xor_pairs(n, bit))  5.75 us
  transfers between devices with their start and end apart: 8, of which 4 were waited for; matrix products, arithmetic and copies ran while one was open for 16% of the time, Pallas kernels for 0%

profile of v1, /device:TPU:0, one launch (start us, length us, event | category | flops | bytes accessed | tf_op | source)
XLA Modules:
  0.0 119.1 jit_solution(10962115047006216743)
XLA Ops:
  0.6 0.0 copy-start
  0.7 1.1 copy.25
  1.8 0.1 copy-done
  1.9 5.6 %fusion = bf16[16,1024,256]{1,2,0:T(8,128)(2,1)} fusion(bf16[16,256,128]{2,1,0:T(8,128)(2,1)S(1)} %copy-done, bf16[1024,128,1]{1,0,2:T(8,128)(2,1)S(1)} %bitcast.75), kind=kOutput, calls=%fused_computation.1 | convolution fusion | flops 1082130432 | bytes 9699328 | tf_op jit(solution)/shard_map/xk,ijk->ixj/dot_general | solution.py:72
  7.5 12.3 %copy.26 = bf16[16,1024,256]{2,1,0:T(8,128)(2,1)} copy(bf16[16,1024,256]{1,2,0:T(8,128)(2,1)} %fusion) | data formatting | bytes 16777216 | tf_op jit(solution)/shard_map/convert_element_type | solution.py:73
  19.8 12.3 %copy.27 = bf16[16,32,32,256]{3,2,1,0:T(8,128)(2,1)} copy(bf16[16,32,32,256]{3,1,2,0:T(8,128)(2,1)} %bitcast.63) | data formatting | bytes 16777216 | tf_op jit(solution)/shard_map/transpose | solution.py:74
  32.2 0.0 copy-start.3
  32.2 16.7 %copy.31 = bf16[64,8,32,256]{3,1,2,0:T(8,128)(2,1)} copy(bf16[64,8,32,256]{3,2,1,0:T(8,128)(2,1)} %bitcast.64) | data formatting | bytes 16777216
  48.9 0.0 copy-done.3
  48.9 4.9 %fusion.2 = f32[8192,64]{0,1:T(8,128)S(1)} fusion(bf16[64,512]{1,0:T(8,128)(2,1)S(1)} %copy-done.3, bf16[512,8192]{1,0:T(8,128)(2,1)} %bitcast.61), kind=kOutput, calls=%fused_computation.24 | convolution fusion | flops 536870912 | bytes 10551296 | tf_op jit(solution)/shard_map/dot_general | solution.py:76
  53.8 0.6 copy.32
  54.5 0.0 copy-start.4
  54.5 4.5 %copy.28 = f32[64,32,256]{0,1,2:T(8,128)} copy(f32[64,32,256]{2,1,0:T(8,128)S(1)} %bitcast.68) | data formatting | bytes 4194304 | tf_op jit(solution)/shard_map/reshape | solution.py:77
  59.0 2.8 %copy.29 = f32[16,64,512]{2,1,0:T(8,128)S(1)} copy(f32[16,64,512]{1,2,0:T(8,128)} %bitcast.65) | data formatting | bytes 4194304 | tf_op jit(solution)/shard_map/transpose | solution.py:79
  61.8 1.2 dynamic-slice_bitcast_fusion
  63.0 0.5 collective-permute-start.4
  63.5 0.0 copy-done.4
  63.5 3.6 %collective-permute-start = (bf16[1,64,512]{2,1,0:T(8,128)(2,1)S(1)}, bf16[1,64,512]{2,1,0:T(8,128)(2,1)S(1)}, u32[]{:S(2)}, u32[]{:S(2)}) collective-permute-start(bf16[1,64,512]{2,1,0:T(8,128)(2,1)S(1)} %bitcast.77), channel_id=1, source_target_pairs={{0,8},{1,9},{2,10},{3,11},{4,12},{5,13},{6,14},{7,15},{8,0},{9,1},... | collective-permute-start | bytes 196616 | tf_op jit(solution)/shard_map/ppermute | solution.py:20
  67.0 4.2 %collective-permute-done = bf16[1,64,512]{2,1,0:T(8,128)(2,1)S(1)} collective-permute-done((bf16[1,64,512]{2,1,0:T(8,128)(2,1)S(1)}, bf16[1,64,512]{2,1,0:T(8,128)(2,1)S(1)}, u32[]{:S(2)}, u32[]{:S(2)}) %collective-permute-start) | collective-permute-done | bytes 65568 | tf_op jit(solution)/shard_map/ppermute | solution.py:20
  71.2 0.8 collective-permute-start.1
  72.1 4.6 %collective-permute-done.1 = bf16[2,64,512]{2,1,0:T(8,128)(2,1)S(1)} collective-permute-done((bf16[2,64,512]{2,1,0:T(8,128)(2,1)S(1)}, bf16[2,64,512]{2,1,0:T(8,128)(2,1)S(1)}, u32[]{:S(2)}, u32[]{:S(2)}) %collective-permute-start.1) | collective-permute-done | bytes 131104 | tf_op jit(solution)/shard_map/ppermute | solution.py:20
  76.7 1.3 %collective-permute-start.2 = (bf16[4,64,512]{2,1,0:T(8,128)(2,1)S(1)}, bf16[4,64,512]{2,1,0:T(8,128)(2,1)S(1)}, u32[]{:S(2)}, u32[]{:S(2)}) collective-permute-start(bf16[4,64,512]{2,1,0:T(8,128)(2,1)S(1)} %pad_maximum_fusion.2), channel_id=1, source_target_pairs={{0,2},{1,3},{2,0},{3,1},{4,6},{5,7},{6,4},{7,5},{8,10},{9,11},{10,... | collective-permute-start | bytes 786440 | tf_op jit(solution)/shard_map/ppermute | solution.py:20
  78.0 0.0 collective-permute-done.4
  78.0 1.4 %bitcast_add_fusion = f32[2,2,2,64,512]{4,3,2,1,0:T(8,128)S(1)} fusion(f32[2,2,2,64,512]{4,3,2,1,0:T(8,128)} %collective-permute-done.4, f32[2,2,2,2,64,512]{5,4,3,2,1,0:T(8,128)S(1)} %bitcast.67, s32[]{:T(128)S(6)} %select_n.88), kind=kLoop, calls=%fused_computation.4 | loop fusion | flops 262144 | bytes 3145732 | tf_op jit(solution)/shard_map/add | solution.py:44
  79.4 0.0 copy-start.1
  79.4 1.1 copy-done.1
  80.5 0.8 dynamic-slice_bitcast_fusion.1
  81.3 0.8 collective-permute-start.5
  82.1 3.9 %collective-permute-done.2 = bf16[4,64,512]{2,1,0:T(8,128)(2,1)S(1)} collective-permute-done((bf16[4,64,512]{2,1,0:T(8,128)(2,1)S(1)}, bf16[4,64,512]{2,1,0:T(8,128)(2,1)S(1)}, u32[]{:S(2)}, u32[]{:S(2)}) %collective-permute-start.2) | collective-permute-done | bytes 262176 | tf_op jit(solution)/shard_map/ppermute | solution.py:20
  86.1 0.1 collective-permute-start.3
  86.2 9.1 %collective-permute-done.5 = f32[2,2,64,512]{3,2,1,0:T(8,128)S(1)} collective-permute-done((f32[2,2,64,512]{3,2,1,0:T(8,128)}, f32[2,2,64,512]{3,2,1,0:T(8,128)S(1)}, u32[]{:S(2)}, u32[]{:S(2)}) %collective-permute-start.5) | collective-permute-done | bytes 524320 | tf_op jit(solution)/shard_map/ppermute | solution.py:44
  95.3 1.1 bitcast_add_fusion.1
  96.4 0.0 copy-start.2
  96.4 0.8 copy-done.2
  97.2 1.1 collective-permute-start.6
  98.3 0.0 collective-permute-done.3
  98.3 0.1 broadcast_select_fusion.1
  98.4 0.1 pad_maximum_fusion
  98.5 1.1 copy.22
  99.6 2.0 %copy.23 = bf16[64,16,512]{0,2,1:T(8,128)(2,1)S(1)} copy(bf16[64,16,512]{2,0,1:T(8,128)(2,1)} %bitcast.72) | data formatting | bytes 2097152 | tf_op jit(solution)/shard_map/transpose | solution.py:64
  101.6 3.6 %copy.24 = bf16[64,32,256]{2,1,0:T(8,128)(2,1)} copy(bf16[64,32,256]{0,1,2:T(8,128)(2,1)S(1)} %bitcast.70) | data formatting | bytes 2097152 | tf_op jit(solution)/shard_map/transpose | solution.py:84
  105.3 1.9 %copy.30 = bf16[8,8,32,256]{3,1,2,0:T(8,128)(2,1)S(1)} copy(bf16[8,8,32,256]{3,2,1,0:T(8,128)(2,1)} %bitcast.73) | data formatting | bytes 2097152
  107.1 0.0 collective-permute-done.6
  107.1 1.1 bitcast_add_fusion.2
  108.2 3.5 %collective-permute-start.7 = (f32[64,512]{1,0:T(8,128)S(1)}, f32[64,512]{1,0:T(8,128)S(1)}, u32[]{:S(2)}, u32[]{:S(2)}) collective-permute-start(f32[64,512]{1,0:T(8,128)S(1)} %dynamic-slice_bitcast_fusion.3), channel_id=1, source_target_pairs={{0,8},{1,9},{2,10},{3,11},{4,12},{5,13},{6,14},{7,15},{8,0},{9,1},... | collective-permute-start | bytes 393224 | tf_op jit(solution)/shard_map/ppermute | solution.py:44
  111.7 6.7 %convolution_convert_fusion = bf16[64,512]{1,0:T(8,128)(2,1)} fusion(bf16[64,8192]{1,0:T(8,128)(2,1)S(1)} %bitcast.71, bf16[512,8192]{1,0:T(8,128)(2,1)} %bitcast.62), kind=kOutput, calls=%fused_computation.2 | convolution fusion | flops 536903680 | bytes 9502720 | tf_op jit(solution)/shard_map/dot_general | solution.py:85
  118.4 0.0 collective-permute-done.7
  118.4 0.6 fusion.1
  (8 shorter events, 0.2 us)
Async XLA Ops:
  0.6 1.3 %copy-start = (bf16[16,256,128]{2,1,0:T(8,128)(2,1)S(1)}, bf16[16,256,128]{2,1,0:T(8,128)(2,1)}, u32[]{:S(2)}) copy-start(bf16[16,256,128]{2,1,0:T(8,128)(2,1)} %param.6) | copy-start | bytes 3145732
  32.2 16.7 %copy-start.3 = (bf16[64,512]{1,0:T(8,128)(2,1)S(1)}, bf16[64,512]{1,0:T(8,128)(2,1)}, u32[]{:S(2)}) copy-start(bf16[64,512]{1,0:T(8,128)(2,1)} %param.4) | copy-start | bytes 196612
  54.5 9.0 %copy-start.4 = (bf16[64,512]{1,0:T(8,128)(2,1)S(1)}, bf16[64,512]{1,0:T(8,128)(2,1)}, u32[]{:S(2)}) copy-start(bf16[64,512]{1,0:T(8,128)(2,1)} %param.5) | copy-start | bytes 196612
  63.0 15.0 %collective-permute-start.4 = (f32[2,2,2,64,512]{4,3,2,1,0:T(8,128)}, f32[2,2,2,64,512]{4,3,2,1,0:T(8,128)}, u32[]{:S(2)}, u32[]{:S(2)}) collective-permute-start(f32[2,2,2,64,512]{4,3,2,1,0:T(8,128)} %dynamic-slice_bitcast_fusion), channel_id=1, source_target_pairs={{0,1},{1,0},{2,3},{3,2},{4,5},{5,4},{6,7},{7,6},{8,9},{9,8},{10,11... | collective-permute-start | bytes 3145736 | tf_op jit(solution)/shard_map/ppermute | solution.py:44
  63.5 7.8 %collective-permute-start = (bf16[1,64,512]{2,1,0:T(8,128)(2,1)S(1)}, bf16[1,64,512]{2,1,0:T(8,128)(2,1)S(1)}, u32[]{:S(2)}, u32[]{:S(2)}) collective-permute-start(bf16[1,64,512]{2,1,0:T(8,128)(2,1)S(1)} %bitcast.77), channel_id=1, source_target_pairs={{0,8},{1,9},{2,10},{3,11},{4,12},{5,13},{6,14},{7,15},{8,0},{9,1},... | collective-permute-start | bytes 196616 | tf_op jit(solution)/shard_map/ppermute | solution.py:20
  71.2 5.4 %collective-permute-start.1 = (bf16[2,64,512]{2,1,0:T(8,128)(2,1)S(1)}, bf16[2,64,512]{2,1,0:T(8,128)(2,1)S(1)}, u32[]{:S(2)}, u32[]{:S(2)}) collective-permute-start(bf16[2,64,512]{2,1,0:T(8,128)(2,1)S(1)} %pad_maximum_fusion.3), channel_id=1, source_target_pairs={{0,4},{1,5},{2,6},{3,7},{4,0},{5,1},{6,2},{7,3},{8,12},{9,13},{10,... | collective-permute-start | bytes 393224 | tf_op jit(solution)/shard_map/ppermute | solution.py:20
  76.7 9.3 %collective-permute-start.2 = (bf16[4,64,512]{2,1,0:T(8,128)(2,1)S(1)}, bf16[4,64,512]{2,1,0:T(8,128)(2,1)S(1)}, u32[]{:S(2)}, u32[]{:S(2)}) collective-permute-start(bf16[4,64,512]{2,1,0:T(8,128)(2,1)S(1)} %pad_maximum_fusion.2), channel_id=1, source_target_pairs={{0,2},{1,3},{2,0},{3,1},{4,6},{5,7},{6,4},{7,5},{8,10},{9,11},{10,... | collective-permute-start | bytes 786440 | tf_op jit(solution)/shard_map/ppermute | solution.py:20
  79.4 1.1 copy-start.1
  81.3 14.0 %collective-permute-start.5 = (f32[2,2,64,512]{3,2,1,0:T(8,128)}, f32[2,2,64,512]{3,2,1,0:T(8,128)S(1)}, u32[]{:S(2)}, u32[]{:S(2)}) collective-permute-start(f32[2,2,64,512]{3,2,1,0:T(8,128)} %dynamic-slice_bitcast_fusion.1), channel_id=1, source_target_pairs={{0,2},{1,3},{2,0},{3,1},{4,6},{5,7},{6,4},{7,5},{8,10},{9,11},{10,... | collective-permute-start | bytes 1572872 | tf_op jit(solution)/shard_map/ppermute | solution.py:44
  86.1 12.2 %collective-permute-start.3 = (bf16[8,64,512]{2,1,0:T(8,128)(2,1)S(1)}, bf16[8,64,512]{2,1,0:T(8,128)(2,1)S(1)}, u32[]{:S(2)}, u32[]{:S(2)}) collective-permute-start(bf16[8,64,512]{2,1,0:T(8,128)(2,1)S(1)} %pad_maximum_fusion.1), channel_id=1, source_target_pairs={{0,1},{1,0},{2,3},{3,2},{4,5},{5,4},{6,7},{7,6},{8,9},{9,8},{10,11... | collective-permute-start | bytes 1572872 | tf_op jit(solution)/shard_map/ppermute | solution.py:20
  96.4 0.8 copy-start.2
  97.2 9.9 %collective-permute-start.6 = (f32[2,64,512]{2,1,0:T(8,128)S(1)}, f32[2,64,512]{2,1,0:T(8,128)}, u32[]{:S(2)}, u32[]{:S(2)}) collective-permute-start(f32[2,64,512]{2,1,0:T(8,128)S(1)} %dynamic-slice_bitcast_fusion.2), channel_id=1, source_target_pairs={{0,4},{1,5},{2,6},{3,7},{4,0},{5,1},{6,2},{7,3},{8,12},{9,13},{10,... | collective-permute-start | bytes 786440 | tf_op jit(solution)/shard_map/ppermute | solution.py:44
  108.2 10.2 %collective-permute-start.7 = (f32[64,512]{1,0:T(8,128)S(1)}, f32[64,512]{1,0:T(8,128)S(1)}, u32[]{:S(2)}, u32[]{:S(2)}) collective-permute-start(f32[64,512]{1,0:T(8,128)S(1)} %dynamic-slice_bitcast_fusion.3), channel_id=1, source_target_pairs={{0,8},{1,9},{2,10},{3,11},{4,12},{5,13},{6,14},{7,15},{8,0},{9,1},... | collective-permute-start | bytes 393224 | tf_op jit(solution)/shard_map/ppermute | solution.py:44

commit v2 on v1

v2 whole, which is shorter than its diff:
```python
import functools
import math

import jax
import jax.numpy as jnp
from jax import lax
from jax.experimental import pallas as pl
from jax.experimental.pallas import tpu as pltpu
from jax.sharding import PartitionSpec as P

C = 32


def xor_pairs(n, bit):
    return [(i, i ^ (1 << bit)) for i in range(n)]


def gather_blocks(x, axis, n, bits):
    me = lax.axis_index(axis)
    buf = x[None]
    done = []
    for bit in bits:
        other = lax.ppermute(buf, axis, xor_pairs(n, bit))
        mine = (me >> bit) & 1
        low = jnp.where(mine == 0, buf, other)
        high = jnp.where(mine == 0, other, buf)
        buf = jnp.concatenate([low, high], 0)
        done = [bit] + done
    k = len(done)
    buf = buf.reshape((2,) * k + x.shape)
    order = sorted(range(k), key=lambda t: -done[t])
    buf = buf.transpose(order + list(range(k, k + x.ndim)))
    return buf.reshape((n,) + x.shape)


def scatter_sum(x, axis, n, bits):
    me = lax.axis_index(axis)
    k = n.bit_length() - 1
    buf = x.reshape((2,) * k + x.shape[1:])
    left = list(range(k - 1, -1, -1))
    for bit in bits:
        t = left.index(bit)
        mine = (me >> bit) & 1
        moved = jnp.moveaxis(buf, t, 0)
        keep = lax.dynamic_index_in_dim(moved, mine, 0, keepdims=False)
        send = lax.dynamic_index_in_dim(moved, 1 - mine, 0, keepdims=False)
        buf = keep + lax.ppermute(send, axis, xor_pairs(n, bit))
        left.pop(t)
    return buf


def index_bits(n):
    return list(range(n.bit_length() - 1))


def project_kernel(p_ref, w_ref, l_ref, gm_ref, pt_ref, *, n_seq):
    rows = p_ref.shape[0]
    width = p_ref.shape[1]
    for i in range(rows):
        prod = lax.dot_general(
            w_ref[...], p_ref[i], (((1,), (1,)), ((), ())), preferred_element_type=jnp.float32
        )
        grad = (prod / n_seq).astype(jnp.bfloat16)
        for e in range(C):
            gm_ref[e, i * C:(i + 1) * C, :] = grad[e * C:(e + 1) * C, :]
    for e in range(C):
        part = lax.dot_general(
            gm_ref[e], l_ref[...], (((0,), (1,)), ((), ())), preferred_element_type=jnp.float32
        )
        pt_ref[:, e, :, :] = part.reshape(width // 16, 16, part.shape[1])


def left_kernel(gm_ref, rt_ref, out_ref):
    @pl.when(pl.program_id(0) == 0)
    def _():
        out_ref[...] = jnp.zeros_like(out_ref)

    width = gm_ref.shape[2]
    acc = out_ref[...]
    for e in range(C):
        right_e = rt_ref[:, e, :, :].reshape(width, rt_ref.shape[3]).astype(jnp.bfloat16)
        acc = acc + jnp.dot(gm_ref[e], right_e, preferred_element_type=jnp.float32)
    out_ref[...] = acc


def per_device(left_proj, right_proj, pair_cot, out_weight):
    n_seq = left_proj.shape[0]
    own_rows = pair_cot.shape[0]
    total = pair_cot.shape[1]
    p_size = pair_cot.shape[2]
    n = lax.axis_size("row")
    bits = index_bits(n)
    block = math.gcd(total, 256)
    steps = total // block
    per_dev = right_proj.shape[1] // C

    right_t = right_proj.reshape(n_seq, per_dev, C).transpose(2, 1, 0)
    right_blocks = gather_blocks(right_t, "row", n, bits[::-1]).astype(jnp.float32)

    weight_ec = out_weight.reshape(C, C, p_size).transpose(1, 0, 2).reshape(C * C, p_size)

    grad_m, part_t = pl.pallas_call(
        functools.partial(project_kernel, n_seq=n_seq),
        grid=(steps,),
        in_specs=[
            pl.BlockSpec((own_rows, block, p_size), lambda b: (0, b, 0)),
            pl.BlockSpec((C * C, p_size), lambda b: (0, 0)),
            pl.BlockSpec((n_seq, own_rows * C), lambda b: (0, 0)),
        ],
        out_specs=[
            pl.BlockSpec((C, own_rows * C, block), lambda b: (0, 0, b)),
            pl.BlockSpec((block // 16, C, 16, n_seq), lambda b: (b, 0, 0, 0)),
        ],
        out_shape=[
            jax.ShapeDtypeStruct((C, own_rows * C, total), jnp.bfloat16),
            jax.ShapeDtypeStruct((total // 16, C, 16, n_seq), jnp.float32),
        ],
        compiler_params=pltpu.CompilerParams(vmem_limit_bytes=56 * 1024 * 1024),
    )(pair_cot, weight_ec, left_proj)

    summed = scatter_sum(part_t, "row", n, bits)
    grad_right = summed.transpose(2, 1, 0).reshape(n_seq, per_dev * C).astype(jnp.bfloat16)

    left_t = pl.pallas_call(
        left_kernel,
        grid=(steps,),
        in_specs=[
            pl.BlockSpec((C, own_rows * C, block), lambda b: (0, 0, b)),
            pl.BlockSpec((block // 16, C, 16, n_seq), lambda b: (b, 0, 0, 0)),
        ],
        out_specs=pl.BlockSpec((own_rows * C, n_seq), lambda b: (0, 0)),
        out_shape=jax.ShapeDtypeStruct((own_rows * C, n_seq), jnp.float32),
        compiler_params=pltpu.CompilerParams(vmem_limit_bytes=56 * 1024 * 1024),
    )(grad_m, right_blocks)
    grad_left = left_t.T.astype(jnp.bfloat16)
    return (grad_left, grad_right)


def solution(mesh):
    return jax.shard_map(
        per_device,
        mesh=mesh,
        in_specs=(P("groups", "row"), P("groups", "row"), P(("groups", "row"), None, None), P()),
        out_specs=(P("groups", "row"), P("groups", "row")),
        check_vma=False,
    )
```

time: 120 us -> 102 us (0.85)
  local copies, waits for them, and re-layouts: 63.1 us -> 14.2 us
  waiting for transfers between devices: 21.7 us -> 52.8 us
  matrix products: 17.2 us -> 0 us
  Pallas kernels: 0 us -> 15.8 us
  other arithmetic: 4.61 us -> 7.03 us
    transpose x6 -> x0, local copies, waits for them, and re-layouts: 23 us -> none  [the longest x1 12.3 us: per_device(): grad.reshape(own_rows, C, C, block).transpose(0, 2, 1, 3)]
    unnamed x13 -> x11, local copies, waits for them, and re-layouts: 21.2 us -> 1.59 us
    ppermute x4, waiting for transfers between devices: 9.09 us -> 28.6 us  [scatter_sum(): buf = keep + lax.ppermute(send, axis, xor_pairs(n, bit))]
    dot_general x3 -> x0, matrix products: 17.2 us -> none  [the longest x1 6.71 us: per_device(): lax.dot_general(right_t, grads[index], (((1,), (1,)), ((), ())), preferre...]
    pallas_call x0 -> x2, Pallas kernels: none -> 15.8 us  [the longest x1 8.2 us: per_device(): pl.pallas_call(functools.partial(project_kernel, n_seq=n_seq), grid=(step...]
    ppermute x4, waiting for transfers between devices: 12.6 us -> 24.1 us  [gather_blocks(): other = lax.ppermute(buf, axis, xor_pairs(n, bit))]
    convert_element_type x1, local copies, waits for them, and re-layouts: 12.3 us -> 5.23 us  [per_device(): gather_blocks(right_t, 'row', n, bits[::-1]).astype(jnp.float32)]
    another operation x0 -> x2, local copies, waits for them, and re-layouts: none -> 4.29 us
  transfers between devices with their start and end apart: 8 -> 8, of which waited for: 4 -> 5; matrix products, arithmetic and copies ran while one was open for 16% -> 14% of each run, Pallas kernels for 0% -> 7%
where the time goes in v2:
time: 102 us
  waiting for transfers between devices  52.8 us (52%)
  Pallas kernels  15.8 us (15%)
  local copies, waits for them, and re-layouts  14.2 us (14%)
  starting transfers between devices  11.6 us (11%)
  other arithmetic  7.03 us (7%)
    ppermute x4, waiting for transfers between devices, scatter_sum(): buf = keep + lax.ppermute(send, axis, xor_pairs(n, bit))  28.6 us
    ppermute x4, waiting for transfers between devices, gather_blocks(): other = lax.ppermute(buf, axis, xor_pairs(n, bit))  24.1 us
    pallas_call x1, Pallas kernels, per_device(): pl.pallas_call(functools.partial(project_kernel, n_seq=n_seq), grid=(step...  8.2 us
    pallas_call x1, Pallas kernels, per_device(): pl.pallas_call(left_kernel, grid=(steps,), in_specs=[pl.BlockSpec((C, own...  7.61 us
    ppermute x4, starting transfers between devices, gather_blocks(): other = lax.ppermute(buf, axis, xor_pairs(n, bit))  5.9 us
    ppermute x4, starting transfers between devices, scatter_sum(): buf = keep + lax.ppermute(send, axis, xor_pairs(n, bit))  5.65 us
    convert_element_type x1, local copies, waits for them, and re-layouts, per_device(): gather_blocks(right_t, 'row', n, bits[::-1]).astype(jnp.float32)  5.23 us
    another operation x2, local copies, waits for them, and re-layouts  4.29 us
  transfers between devices with their start and end apart: 8, of which 5 were waited for; matrix products, arithmetic and copies ran while one was open for 14% of the time, Pallas kernels for 7%

profile of v2, /device:TPU:0, one launch (start us, length us, event | category | flops | bytes accessed | tf_op | source)
XLA Modules:
  0.0 102.2 jit_solution(9891661316091286591)
XLA Ops:
  0.6 1.8 %copy.8 = bf16[32,32,128]{2,0,1:T(8,128)(2,1)} copy(bf16[32,32,128]{2,1,0:T(8,128)(2,1)} %bitcast.46) | data formatting | bytes 524288 | tf_op jit(solution)/shard_map/reshape | solution.py:100
  2.4 8.2 %shard_map.59 = (bf16[32,512,256]{2,1,0:T(8,128)(2,1)}, f32[16,32,16,64]{3,2,1,0:T(8,128)}) custom-call(bf16[16,256,128]{2,1,0:T(8,128)(2,1)} %p_ref.1, bf16[1024,128]{1,0:T(8,128)(2,1)} %bitcast.42, bf16[64,512]{1,0:T(8,128)(2,1)} %l_ref.1), custom_call_target="tpu_custom_call" | custom-call | tf_op jit(solution)/shard_map/pallas_call | solution.py:102
  10.6 2.7 %constant_dynamic-slice_fusion.3 = (f32[2,2,2,1,32,16,64]{6,5,4,3,2,1,0:T(8,128)S(1)}, f32[2,2,2,1,32,16,64]{6,5,4,3,2,1,0:T(8,128)S(1)}) fusion(f32[2,2,2,2,32,16,64]{6,5,4,3,2,1,0:T(8,128)} %bitcast.41, s32[]{:T(128)S(6)} %select_n.88, s32[]{:T(128)S(6)} %select_n.89), kind=kLoop, calls=%fused_computation.25 | loop fusion | bytes 4194312 | tf_op jit(solution)/shard_map/dynamic-slice
  13.3 0.0 copy-start.3
  13.3 1.6 %copy.23 = f32[2,2,2,1,32,16,64]{6,5,4,1,0,2,3:T(8,128)} copy(f32[2,2,2,1,32,16,64]{6,5,4,3,2,1,0:T(8,128)S(1)} %get-tuple-element.11) | data formatting | bytes 2097152 | tf_op jit(solution)/shard_map/dynamic-slice.1
  14.9 0.5 collective-permute-start.4
  15.4 0.0 copy-done.3
  15.4 0.1 copy.9
  15.5 3.7 %collective-permute-start = (bf16[1,32,16,64]{3,1,2,0:T(8,128)(2,1)S(1)}, bf16[1,32,16,64]{3,1,2,0:T(8,128)(2,1)S(1)}, u32[]{:S(2)}, u32[]{:S(2)}) collective-permute-start(bf16[1,32,16,64]{3,1,2,0:T(8,128)(2,1)S(1)} %bitcast.43), channel_id=1, source_target_pairs={{0,8},{1,9},{2,10},{3,11},{4,12},{5,13},{6,14},{7,15},{8,0},{9,1},... | collective-permute-start | bytes 196616 | tf_op jit(solution)/shard_map/ppermute | solution.py:23
  19.1 7.0 %collective-permute-done = bf16[1,32,16,64]{3,1,2,0:T(8,128)(2,1)S(1)} collective-permute-done((bf16[1,32,16,64]{3,1,2,0:T(8,128)(2,1)S(1)}, bf16[1,32,16,64]{3,1,2,0:T(8,128)(2,1)S(1)}, u32[]{:S(2)}, u32[]{:S(2)}) %collective-permute-start) | collective-permute-done | bytes 65568 | tf_op jit(solution)/shard_map/ppermute | solution.py:23
  26.1 0.1 pad_maximum_fusion.2
  26.2 0.8 collective-permute-start.1
  27.0 7.4 %collective-permute-done.1 = bf16[2,32,16,64]{3,1,2,0:T(8,128)(2,1)S(1)} collective-permute-done((bf16[2,32,16,64]{3,1,2,0:T(8,128)(2,1)S(1)}, bf16[2,32,16,64]{3,1,2,0:T(8,128)(2,1)S(1)}, u32[]{:S(2)}, u32[]{:S(2)}) %collective-permute-start.1) | collective-permute-done | bytes 131104 | tf_op jit(solution)/shard_map/ppermute | solution.py:23
  34.4 0.1 broadcast_select_fusion.5
  34.5 0.1 pad_maximum_fusion.1
  34.6 1.4 %collective-permute-start.2 = (bf16[4,32,16,64]{3,1,2,0:T(8,128)(2,1)S(1)}, bf16[4,32,16,64]{3,1,2,0:T(8,128)(2,1)S(1)}, u32[]{:S(2)}, u32[]{:S(2)}) collective-permute-start(bf16[4,32,16,64]{3,1,2,0:T(8,128)(2,1)S(1)} %pad_maximum_fusion.1), channel_id=1, source_target_pairs={{0,2},{1,3},{2,0},{3,1},{4,6},{5,7},{6,4},{7,5},{8,10},{9,11},{10,... | collective-permute-start | bytes 786440 | tf_op jit(solution)/shard_map/ppermute | solution.py:23
  36.0 0.0 collective-permute-done.4
  36.0 1.9 %bitcast_add_fusion = f32[2,2,2,32,16,64]{5,4,3,1,0,2:T(8,128)S(1)} fusion(f32[2,2,2,32,16,64]{5,4,3,1,0,2:T(8,128)} %collective-permute-done.4, f32[2,2,2,1,32,16,64]{6,5,4,3,2,1,0:T(8,128)S(1)} %get-tuple-element.10), kind=kLoop, calls=%fused_computation.1 | loop fusion | flops 262144 | bytes 3145728 | tf_op jit(solution)/shard_map/add | solution.py:47
  37.9 0.0 copy-start
  37.9 1.2 %dynamic-slice_bitcast_fusion = f32[2,2,32,16,64]{4,3,2,1,0:T(8,128)} fusion(f32[2,2,2,32,16,64]{5,4,3,1,0,2:T(8,128)S(1)} %bitcast_add_fusion, s32[]{:T(128)S(6)} %select_n.91), kind=kLoop, calls=%fused_computation.5 | loop fusion | bytes 1048580 | tf_op jit(solution)/shard_map/jit(dynamic_index_in_dim)/squeeze | solution.py:46
  39.1 0.7 collective-permute-start.5
  39.8 9.8 %collective-permute-done.2 = bf16[4,32,16,64]{3,1,2,0:T(8,128)(2,1)S(1)} collective-permute-done((bf16[4,32,16,64]{3,1,2,0:T(8,128)(2,1)S(1)}, bf16[4,32,16,64]{3,1,2,0:T(8,128)(2,1)S(1)}, u32[]{:S(2)}, u32[]{:S(2)}) %collective-permute-start.2) | collective-permute-done | bytes 262176 | tf_op jit(solution)/shard_map/ppermute | solution.py:23
  49.5 0.1 broadcast_select_fusion.3
  49.7 0.0 copy-done
  49.7 0.0 copy-start.1
  49.7 1.2 %pad_maximum_fusion = bf16[8,32,16,64]{3,1,2,0:T(8,128)(2,1)} fusion(bf16[4,32,16,64]{3,1,2,0:T(8,128)(2,1)S(1)} %get-tuple-element.15, bf16[4,32,16,64]{3,1,2,0:T(8,128)(2,1)S(1)} %get-tuple-element.14), kind=kLoop, calls=%fused_computation.3 | loop fusion | flops 262144 | bytes 1048576 | tf_op jit(solution)/shard_map/concatenate | solution.py:27
  50.9 0.0 collective-permute-start.3
  50.9 19.3 %collective-permute-done.5 = f32[2,2,32,16,64]{4,3,2,1,0:T(8,128)} collective-permute-done((f32[2,2,32,16,64]{4,3,2,1,0:T(8,128)}, f32[2,2,32,16,64]{4,3,2,1,0:T(8,128)}, u32[]{:S(2)}, u32[]{:S(2)}) %collective-permute-start.5) | collective-permute-done | bytes 524320 | tf_op jit(solution)/shard_map/ppermute | solution.py:47
  70.1 0.0 copy-done.1
  70.1 1.4 %bitcast_add_fusion.1 = f32[2,2,32,16,64]{4,3,2,1,0:T(8,128)S(1)} fusion(f32[2,2,32,16,64]{4,3,2,1,0:T(8,128)} %collective-permute-done.5, f32[2,2,2,32,16,64]{5,4,3,1,0,2:T(8,128)S(1)} %copy-done.1, s32[]{:T(128)S(6)} %select_n.90), kind=kLoop, calls=%fused_computation.4 | loop fusion | flops 131072 | bytes 1572868 | tf_op jit(solution)/shard_map/add | solution.py:47
  71.6 1.1 %collective-permute-start.6 = (f32[2,32,16,64]{3,2,1,0:T(8,128)S(1)}, f32[2,32,16,64]{3,2,1,0:T(8,128)S(1)}, u32[]{:S(2)}, u32[]{:S(2)}) collective-permute-start(f32[2,32,16,64]{3,2,1,0:T(8,128)S(1)} %dynamic-slice_bitcast_fusion.1), channel_id=1, source_target_pairs={{0,4},{1,5},{2,6},{3,7},{4,0},{5,1},{6,2},{7,3},{8,12},{9,13},{10,... | collective-permute-start | bytes 786440 | tf_op jit(solution)/shard_map/ppermute | solution.py:47
  72.6 0.0 collective-permute-done.3
  72.6 1.5 %broadcast_select_fusion.1 = (bf16[8,32,16,64]{3,1,2,0:T(8,128)(2,1)S(1)}, bf16[8,32,16,64]{3,1,2,0:T(8,128)(2,1)S(1)}) fusion(bf16[8,32,16,64]{3,1,2,0:T(8,128)(2,1)} %collective-permute-done.3, pred[]{:T(512)S(6)} %eq.16, bf16[4,32,16,64]{3,1,2,0:T(8,128)(2,1)S(1)} %get-tuple-element.15, bf16[4,32,16,64]{3,1,2,0:T(8,128)(2,1)S(1)} %get-tuple-element.14), kind=kLoop, calls=%fused_computation.7 | loop fusion | flops 786432 | bytes 2097153 | tf_op jit(solution)/shard_map/jit(_where)/select_n | solution.py:25
  74.1 0.5 maximum_convert_fusion
  74.7 5.2 %copy.11 = f32[2,2,2,2,32,16,64]{6,5,4,3,2,1,0:T(8,128)} copy(f32[2,2,2,2,32,16,64]{6,4,5,0,1,2,3:T(8,128)S(1)} %bitcast.40) | data formatting | bytes 4194304 | tf_op jit(solution)/shard_map/convert_element_type | solution.py:98
  79.9 7.6 %shard_map.60 = f32[512,64]{1,0:T(8,128)} custom-call(bf16[32,512,256]{2,1,0:T(8,128)(2,1)} %get-tuple-element.4.gm_ref, f32[16,32,16,64]{3,2,1,0:T(8,128)} %bitcast.39), custom_call_target="tpu_custom_call" | custom-call | tf_op jit(solution)/shard_map/pallas_call | solution.py:124
  87.5 0.0 copy-start.2
  87.5 0.0 collective-permute-done.6
  87.5 0.1 bitcast_add_fusion.2
  87.6 0.1 copy.24
  87.7 3.5 %collective-permute-start.7 = (f32[32,16,64]{2,0,1:T(8,128)S(1)}, f32[32,16,64]{2,0,1:T(8,128)S(1)}, u32[]{:S(2)}, u32[]{:S(2)}) collective-permute-start(f32[32,16,64]{2,0,1:T(8,128)S(1)} %bitcast.47), channel_id=1, source_target_pairs={{0,8},{1,9},{2,10},{3,11},{4,12},{5,13},{6,14},{7,15},{8,0},{9,1},... | collective-permute-start | bytes 393224 | tf_op jit(solution)/shard_map/ppermute | solution.py:47
  91.2 0.0 copy-done.2
  91.2 0.7 copy.16
  92.0 9.4 %collective-permute-done.7 = f32[32,16,64]{2,0,1:T(8,128)S(1)} collective-permute-done((f32[32,16,64]{2,0,1:T(8,128)S(1)}, f32[32,16,64]{2,0,1:T(8,128)S(1)}, u32[]{:S(2)}, u32[]{:S(2)}) %collective-permute-start.7) | collective-permute-done | bytes 131104 | tf_op jit(solution)/shard_map/ppermute | solution.py:47
  101.3 0.1 fusion
  101.4 0.7 copy.17
  (4 shorter events, 0.1 us)
Async XLA Ops:
  13.3 2.1 %copy-start.3 = (bf16[64,512]{1,0:T(8,128)(2,1)S(1)}, bf16[64,512]{1,0:T(8,128)(2,1)}, u32[]{:S(2)}) copy-start(bf16[64,512]{1,0:T(8,128)(2,1)} %param.5) | copy-start | bytes 196612
  14.9 21.1 %collective-permute-start.4 = (f32[2,2,2,32,16,64]{5,4,3,1,0,2:T(8,128)}, f32[2,2,2,32,16,64]{5,4,3,1,0,2:T(8,128)}, u32[]{:S(2)}, u32[]{:S(2)}) collective-permute-start(f32[2,2,2,32,16,64]{5,4,3,1,0,2:T(8,128)} %bitcast.37), channel_id=1, source_target_pairs={{0,1},{1,0},{2,3},{3,2},{4,5},{5,4},{6,7},{7,6},{8,9},{9,8},{10,11... | collective-permute-start | bytes 3145736 | tf_op jit(solution)/shard_map/ppermute | solution.py:47
  15.5 10.6 %collective-permute-start = (bf16[1,32,16,64]{3,1,2,0:T(8,128)(2,1)S(1)}, bf16[1,32,16,64]{3,1,2,0:T(8,128)(2,1)S(1)}, u32[]{:S(2)}, u32[]{:S(2)}) collective-permute-start(bf16[1,32,16,64]{3,1,2,0:T(8,128)(2,1)S(1)} %bitcast.43), channel_id=1, source_target_pairs={{0,8},{1,9},{2,10},{3,11},{4,12},{5,13},{6,14},{7,15},{8,0},{9,1},... | collective-permute-start | bytes 196616 | tf_op jit(solution)/shard_map/ppermute | solution.py:23
  26.2 8.2 %collective-permute-start.1 = (bf16[2,32,16,64]{3,1,2,0:T(8,128)(2,1)S(1)}, bf16[2,32,16,64]{3,1,2,0:T(8,128)(2,1)S(1)}, u32[]{:S(2)}, u32[]{:S(2)}) collective-permute-start(bf16[2,32,16,64]{3,1,2,0:T(8,128)(2,1)S(1)} %pad_maximum_fusion.2), channel_id=1, source_target_pairs={{0,4},{1,5},{2,6},{3,7},{4,0},{5,1},{6,2},{7,3},{8,12},{9,13},{10,... | collective-permute-start | bytes 393224 | tf_op jit(solution)/shard_map/ppermute | solution.py:23
  34.6 14.9 %collective-permute-start.2 = (bf16[4,32,16,64]{3,1,2,0:T(8,128)(2,1)S(1)}, bf16[4,32,16,64]{3,1,2,0:T(8,128)(2,1)S(1)}, u32[]{:S(2)}, u32[]{:S(2)}) collective-permute-start(bf16[4,32,16,64]{3,1,2,0:T(8,128)(2,1)S(1)} %pad_maximum_fusion.1), channel_id=1, source_target_pairs={{0,2},{1,3},{2,0},{3,1},{4,6},{5,7},{6,4},{7,5},{8,10},{9,11},{10,... | collective-permute-start | bytes 786440 | tf_op jit(solution)/shard_map/ppermute | solution.py:23
  37.9 11.8 %copy-start = (f32[2,2,2,32,16,64]{5,4,3,1,0,2:T(8,128)}, f32[2,2,2,32,16,64]{5,4,3,1,0,2:T(8,128)S(1)}, u32[]{:S(2)}) copy-start(f32[2,2,2,32,16,64]{5,4,3,1,0,2:T(8,128)S(1)} %bitcast_add_fusion) | copy-start | bytes 3145732
  39.1 31.0 %collective-permute-start.5 = (f32[2,2,32,16,64]{4,3,2,1,0:T(8,128)}, f32[2,2,32,16,64]{4,3,2,1,0:T(8,128)}, u32[]{:S(2)}, u32[]{:S(2)}) collective-permute-start(f32[2,2,32,16,64]{4,3,2,1,0:T(8,128)} %dynamic-slice_bitcast_fusion), channel_id=1, source_target_pairs={{0,2},{1,3},{2,0},{3,1},{4,6},{5,7},{6,4},{7,5},{8,10},{9,11},{10,... | collective-permute-start | bytes 1572872 | tf_op jit(solution)/shard_map/ppermute | solution.py:47
  49.7 20.5 %copy-start.1 = (f32[2,2,2,32,16,64]{5,4,3,1,0,2:T(8,128)S(1)}, f32[2,2,2,32,16,64]{5,4,3,1,0,2:T(8,128)}, u32[]{:S(2)}) copy-start(f32[2,2,2,32,16,64]{5,4,3,1,0,2:T(8,128)} %copy-done) | copy-start | bytes 3145732
  50.9 21.7 %collective-permute-start.3 = (bf16[8,32,16,64]{3,1,2,0:T(8,128)(2,1)}, bf16[8,32,16,64]{3,1,2,0:T(8,128)(2,1)}, u32[]{:S(2)}, u32[]{:S(2)}) collective-permute-start(bf16[8,32,16,64]{3,1,2,0:T(8,128)(2,1)} %pad_maximum_fusion), channel_id=1, source_target_pairs={{0,1},{1,0},{2,3},{3,2},{4,5},{5,4},{6,7},{7,6},{8,9},{9,8},{10,11... | collective-permute-start | bytes 1572872 | tf_op jit(solution)/shard_map/ppermute | solution.py:23
  71.6 16.0 %collective-permute-start.6 = (f32[2,32,16,64]{3,2,1,0:T(8,128)S(1)}, f32[2,32,16,64]{3,2,1,0:T(8,128)S(1)}, u32[]{:S(2)}, u32[]{:S(2)}) collective-permute-start(f32[2,32,16,64]{3,2,1,0:T(8,128)S(1)} %dynamic-slice_bitcast_fusion.1), channel_id=1, source_target_pairs={{0,4},{1,5},{2,6},{3,7},{4,0},{5,1},{6,2},{7,3},{8,12},{9,13},{10,... | collective-permute-start | bytes 786440 | tf_op jit(solution)/shard_map/ppermute | solution.py:47
  87.5 3.7 %copy-start.2 = (f32[512,64]{1,0:T(8,128)S(1)}, f32[512,64]{1,0:T(8,128)}, u32[]{:S(2)}) copy-start(f32[512,64]{1,0:T(8,128)} %shard_map.60) | copy-start | bytes 393220
  87.7 13.6 %collective-permute-start.7 = (f32[32,16,64]{2,0,1:T(8,128)S(1)}, f32[32,16,64]{2,0,1:T(8,128)S(1)}, u32[]{:S(2)}, u32[]{:S(2)}) collective-permute-start(f32[32,16,64]{2,0,1:T(8,128)S(1)} %bitcast.47), channel_id=1, source_target_pairs={{0,8},{1,9},{2,10},{3,11},{4,12},{5,13},{6,14},{7,15},{8,0},{9,1},... | collective-permute-start | bytes 393224 | tf_op jit(solution)/shard_map/ppermute | solution.py:47

commit v3 on v2

--- a/solution.py
+++ b/solution.py
@@ -78,7 +78,7 @@
     width = gm_ref.shape[2]
     acc = out_ref[...]
     for e in range(C):
-        right_e = rt_ref[:, e, :, :].reshape(width, rt_ref.shape[3]).astype(jnp.bfloat16)
+        right_e = rt_ref[:, e, :, :].reshape(width, rt_ref.shape[3])
         acc = acc + jnp.dot(gm_ref[e], right_e, preferred_element_type=jnp.float32)
     out_ref[...] = acc
 
@@ -95,7 +95,8 @@
     per_dev = right_proj.shape[1] // C
 
     right_t = right_proj.reshape(n_seq, per_dev, C).transpose(2, 1, 0)
-    right_blocks = gather_blocks(right_t, "row", n, bits[::-1]).astype(jnp.float32)
+    right_blocks = gather_blocks(right_t, "row", n, bits[::-1])
+    pair_cot, right_blocks = lax.optimization_barrier((pair_cot, right_blocks))
 
     weight_ec = out_weight.reshape(C, C, p_size).transpose(1, 0, 2).reshape(C * C, p_size)
 

time: 102 us -> 114 us (1.12)
  waiting for transfers between devices: 52.8 us -> 68.2 us
  local copies, waits for them, and re-layouts: 14.2 us -> 11.4 us
  other arithmetic: 7.03 us -> 4.69 us
  starting transfers between devices: 11.6 us -> 13.9 us
    ppermute x4, waiting for transfers between devices: 28.6 us -> 42.4 us  [scatter_sum(): buf = keep + lax.ppermute(send, axis, xor_pairs(n, bit))]
    convert_element_type x1 -> x0, local copies, waits for them, and re-layouts: 5.23 us -> none  [per_device(): gather_blocks(right_t, 'row', n, bits[::-1]).astype(jnp.float32)]
    transpose x0 -> x1, local copies, waits for them, and re-layouts: none -> 2.22 us  [gather_blocks(): buf = buf.transpose(order + list(range(k, k + x.ndim)))]
    unnamed x11 -> x9, local copies, waits for them, and re-layouts: 1.59 us -> 3.79 us
    ppermute x4, starting transfers between devices: 5.65 us -> 7.61 us  [scatter_sum(): buf = keep + lax.ppermute(send, axis, xor_pairs(n, bit))]
    ppermute x4, waiting for transfers between devices: 24.1 us -> 25.8 us  [gather_blocks(): other = lax.ppermute(buf, axis, xor_pairs(n, bit))]
    select_n x4, other arithmetic: 1.73 us -> 0.51 us  [gather_blocks(): low = jnp.where(mine == 0, buf, other)]
  transfers between devices with their start and end apart: 8 -> 8, of which waited for: 5 -> 8; matrix products, arithmetic and copies ran while one was open for 14% -> 1% of each run, Pallas kernels for 7% -> 6%
where the time goes in v3:
time: 114 us
  waiting for transfers between devices  68.2 us (60%)
  Pallas kernels  15.2 us (13%)
  starting transfers between devices  13.9 us (12%)
  local copies, waits for them, and re-layouts  11.4 us (10%)
  other arithmetic  4.69 us (4%)
    ppermute x4, waiting for transfers between devices, scatter_sum(): buf = keep + lax.ppermute(send, axis, xor_pairs(n, bit))  42.4 us
    ppermute x4, waiting for transfers between devices, gather_blocks(): other = lax.ppermute(buf, axis, xor_pairs(n, bit))  25.8 us
    pallas_call x1, Pallas kernels, per_device(): pl.pallas_call(functools.partial(project_kernel, n_seq=n_seq), grid=(step...  8.18 us
    ppermute x4, starting transfers between devices, scatter_sum(): buf = keep + lax.ppermute(send, axis, xor_pairs(n, bit))  7.61 us
    pallas_call x1, Pallas kernels, per_device(): pl.pallas_call(left_kernel, grid=(steps,), in_specs=[pl.BlockSpec((C, own...  7 us
    ppermute x4, starting transfers between devices, gather_blocks(): other = lax.ppermute(buf, axis, xor_pairs(n, bit))  6.3 us
    another operation x2, local copies, waits for them, and re-layouts  4.28 us
    unnamed x9, local copies, waits for them, and re-layouts  3.79 us
  transfers between devices with their start and end apart: 8, of which 8 were waited for; matrix products, arithmetic and copies ran while one was open for 1% of the time, Pallas kernels for 6%

profile of v3, /device:TPU:0, one launch (start us, length us, event | category | flops | bytes accessed | tf_op | source)
XLA Modules:
  0.0 114.1 jit_solution(4605404577540245216)
XLA Ops:
  0.6 1.0 copy.8
  1.6 4.1 %collective-permute-start = (bf16[1,32,16,64]{3,1,2,0:T(8,128)(2,1)S(1)}, bf16[1,32,16,64]{3,1,2,0:T(8,128)(2,1)S(1)}, u32[]{:S(2)}, u32[]{:S(2)}) collective-permute-start(bf16[1,32,16,64]{3,1,2,0:T(8,128)(2,1)S(1)} %bitcast.43), channel_id=1, source_target_pairs={{0,8},{1,9},{2,10},{3,11},{4,12},{5,13},{6,14},{7,15},{8,0},{9,1},... | collective-permute-start | bytes 196616 | tf_op jit(solution)/shard_map/ppermute | solution.py:23
  5.7 6.3 %collective-permute-done = bf16[1,32,16,64]{3,1,2,0:T(8,128)(2,1)S(1)} collective-permute-done((bf16[1,32,16,64]{3,1,2,0:T(8,128)(2,1)S(1)}, bf16[1,32,16,64]{3,1,2,0:T(8,128)(2,1)S(1)}, u32[]{:S(2)}, u32[]{:S(2)}) %collective-permute-start) | collective-permute-done | bytes 65568 | tf_op jit(solution)/shard_map/ppermute | solution.py:23
  12.0 0.1 pad_maximum_fusion.3
  12.1 0.8 collective-permute-start.1
  12.9 6.8 %collective-permute-done.1 = bf16[2,32,16,64]{3,1,2,0:T(8,128)(2,1)S(1)} collective-permute-done((bf16[2,32,16,64]{3,1,2,0:T(8,128)(2,1)S(1)}, bf16[2,32,16,64]{3,1,2,0:T(8,128)(2,1)S(1)}, u32[]{:S(2)}, u32[]{:S(2)}) %collective-permute-start.1) | collective-permute-done | bytes 131104 | tf_op jit(solution)/shard_map/ppermute | solution.py:23
  19.6 0.1 broadcast_select_fusion.5
  19.7 0.1 pad_maximum_fusion.2
  19.8 1.3 %collective-permute-start.2 = (bf16[4,32,16,64]{3,1,2,0:T(8,128)(2,1)S(1)}, bf16[4,32,16,64]{3,1,2,0:T(8,128)(2,1)S(1)}, u32[]{:S(2)}, u32[]{:S(2)}) collective-permute-start(bf16[4,32,16,64]{3,1,2,0:T(8,128)(2,1)S(1)} %pad_maximum_fusion.2), channel_id=1, source_target_pairs={{0,2},{1,3},{2,0},{3,1},{4,6},{5,7},{6,4},{7,5},{8,10},{9,11},{10,... | collective-permute-start | bytes 786440 | tf_op jit(solution)/shard_map/ppermute | solution.py:23
  21.2 0.0 copy-start.2
  21.2 10.9 %collective-permute-done.2 = bf16[4,32,16,64]{3,1,2,0:T(8,128)(2,1)S(1)} collective-permute-done((bf16[4,32,16,64]{3,1,2,0:T(8,128)(2,1)S(1)}, bf16[4,32,16,64]{3,1,2,0:T(8,128)(2,1)S(1)}, u32[]{:S(2)}, u32[]{:S(2)}) %collective-permute-start.2) | collective-permute-done | bytes 262176 | tf_op jit(solution)/shard_map/ppermute | solution.py:23
  32.1 0.1 broadcast_select_fusion.3
  32.2 0.2 pad_maximum_fusion.1
  32.5 0.1 collective-permute-start.3
  32.5 0.0 copy-done.2
  32.5 0.8 copy.11
  33.4 1.8 %collective-permute-done.3 = bf16[8,32,16,64]{3,1,2,0:T(8,128)(2,1)S(1)} collective-permute-done((bf16[8,32,16,64]{3,1,2,0:T(8,128)(2,1)S(1)}, bf16[8,32,16,64]{3,1,2,0:T(8,128)(2,1)S(1)}, u32[]{:S(2)}, u32[]{:S(2)}) %collective-permute-start.3) | collective-permute-done | bytes 524320 | tf_op jit(solution)/shard_map/ppermute | solution.py:23
  35.2 0.3 broadcast_select_fusion.1
  35.5 0.4 pad_maximum_fusion
  35.9 2.2 %copy.10 = bf16[2,2,2,2,32,16,64]{6,5,4,3,2,1,0:T(8,128)(2,1)} copy(bf16[2,2,2,2,32,16,64]{6,4,5,0,1,2,3:T(8,128)(2,1)S(1)} %bitcast.39) | data formatting | bytes 2097152 | tf_op jit(solution)/shard_map/transpose | solution.py:32
  38.1 8.2 %shard_map.59 = (bf16[32,512,256]{2,1,0:T(8,128)(2,1)}, f32[16,32,16,64]{3,2,1,0:T(8,128)}) custom-call(bf16[16,256,128]{2,1,0:T(8,128)(2,1)} %p_ref, bf16[1024,128]{1,0:T(8,128)(2,1)} %bitcast.42, bf16[64,512]{1,0:T(8,128)(2,1)} %l_ref.1), custom_call_target="tpu_custom_call" | custom-call | tf_op jit(solution)/shard_map/pallas_call | solution.py:103
  46.3 2.7 %constant_dynamic-slice_fusion.3 = (f32[2,2,2,1,32,16,64]{6,5,4,3,2,1,0:T(8,128)S(1)}, f32[2,2,2,1,32,16,64]{6,5,4,3,2,1,0:T(8,128)S(1)}) fusion(f32[2,2,2,2,32,16,64]{6,5,4,3,2,1,0:T(8,128)} %bitcast.41, s32[]{:T(128)S(6)} %select_n.88, s32[]{:T(128)S(6)} %select_n.89), kind=kLoop, calls=%fused_computation.25 | loop fusion | bytes 4194312 | tf_op jit(solution)/shard_map/dynamic-slice
  48.9 1.6 %copy.23 = f32[2,2,2,1,32,16,64]{6,5,4,1,0,2,3:T(8,128)} copy(f32[2,2,2,1,32,16,64]{6,5,4,3,2,1,0:T(8,128)S(1)} %get-tuple-element.15) | data formatting | bytes 2097152 | tf_op jit(solution)/shard_map/dynamic-slice.1
  50.6 0.1 collective-permute-start.4
  50.7 4.4 %collective-permute-done.4 = f32[2,2,2,32,16,64]{5,4,3,1,0,2:T(8,128)} collective-permute-done((f32[2,2,2,32,16,64]{5,4,3,1,0,2:T(8,128)}, f32[2,2,2,32,16,64]{5,4,3,1,0,2:T(8,128)}, u32[]{:S(2)}, u32[]{:S(2)}) %collective-permute-start.4) | collective-permute-done | bytes 1048608 | tf_op jit(solution)/shard_map/ppermute | solution.py:47
  55.1 1.9 %bitcast_add_fusion = f32[2,2,2,32,16,64]{5,4,3,1,0,2:T(8,128)S(1)} fusion(f32[2,2,2,32,16,64]{5,4,3,1,0,2:T(8,128)} %collective-permute-done.4, f32[2,2,2,1,32,16,64]{6,5,4,3,2,1,0:T(8,128)S(1)} %get-tuple-element.14), kind=kLoop, calls=%fused_computation.1 | loop fusion | flops 262144 | bytes 3145728 | tf_op jit(solution)/shard_map/add | solution.py:47
  56.9 0.0 copy-start
  56.9 1.4 %copy-done = f32[2,2,2,32,16,64]{5,4,3,1,0,2:T(8,128)} copy-done((f32[2,2,2,32,16,64]{5,4,3,1,0,2:T(8,128)}, f32[2,2,2,32,16,64]{5,4,3,1,0,2:T(8,128)S(1)}, u32[]{:S(2)}) %copy-start) | copy-done | bytes 1048600
  58.3 0.1 dynamic-slice_bitcast_fusion
  58.4 1.4 %collective-permute-start.5 = (f32[2,2,32,16,64]{4,3,2,1,0:T(8,128)S(1)}, f32[2,2,32,16,64]{4,3,2,1,0:T(8,128)S(1)}, u32[]{:S(2)}, u32[]{:S(2)}) collective-permute-start(f32[2,2,32,16,64]{4,3,2,1,0:T(8,128)S(1)} %dynamic-slice_bitcast_fusion), channel_id=1, source_target_pairs={{0,2},{1,3},{2,0},{3,1},{4,6},{5,7},{6,4},{7,5},{8,10},{9,11},{10,... | collective-permute-start | bytes 1572872 | tf_op jit(solution)/shard_map/ppermute | solution.py:47
  59.8 23.9 %collective-permute-done.5 = f32[2,2,32,16,64]{4,3,2,1,0:T(8,128)S(1)} collective-permute-done((f32[2,2,32,16,64]{4,3,2,1,0:T(8,128)S(1)}, f32[2,2,32,16,64]{4,3,2,1,0:T(8,128)S(1)}, u32[]{:S(2)}, u32[]{:S(2)}) %collective-permute-start.5) | collective-permute-done | bytes 524320 | tf_op jit(solution)/shard_map/ppermute | solution.py:47
  83.7 1.4 %bitcast_add_fusion.1 = f32[2,2,32,16,64]{4,3,2,1,0:T(8,128)S(1)} fusion(f32[2,2,32,16,64]{4,3,2,1,0:T(8,128)S(1)} %collective-permute-done.5, f32[2,2,2,32,16,64]{5,4,3,1,0,2:T(8,128)} %copy-done, s32[]{:T(128)S(6)} %select_n.90), kind=kLoop, calls=%fused_computation.4 | loop fusion | flops 131072 | bytes 1572868 | tf_op jit(solution)/shard_map/add | solution.py:47
  85.1 2.3 %collective-permute-start.6 = (f32[2,32,16,64]{3,2,1,0:T(8,128)S(1)}, f32[2,32,16,64]{3,2,1,0:T(8,128)S(1)}, u32[]{:S(2)}, u32[]{:S(2)}) collective-permute-start(f32[2,32,16,64]{3,2,1,0:T(8,128)S(1)} %dynamic-slice_bitcast_fusion.1), channel_id=1, source_target_pairs={{0,4},{1,5},{2,6},{3,7},{4,0},{5,1},{6,2},{7,3},{8,12},{9,13},{10,... | collective-permute-start | bytes 786440 | tf_op jit(solution)/shard_map/ppermute | solution.py:47
  87.4 7.0 %shard_map.60 = f32[512,64]{1,0:T(8,128)} custom-call(bf16[32,512,256]{2,1,0:T(8,128)(2,1)} %get-tuple-element.7.gm_ref, bf16[16,32,16,64]{3,2,1,0:T(8,128)(2,1)} %bitcast.40), custom_call_target="tpu_custom_call" | custom-call | tf_op jit(solution)/shard_map/pallas_call | solution.py:125
  94.4 0.0 copy-start.1
  94.4 4.4 %collective-permute-done.6 = f32[2,32,16,64]{3,2,1,0:T(8,128)S(1)} collective-permute-done((f32[2,32,16,64]{3,2,1,0:T(8,128)S(1)}, f32[2,32,16,64]{3,2,1,0:T(8,128)S(1)}, u32[]{:S(2)}, u32[]{:S(2)}) %collective-permute-start.6) | collective-permute-done | bytes 262176 | tf_op jit(solution)/shard_map/ppermute | solution.py:47
  98.8 0.1 bitcast_add_fusion.2
  98.9 0.1 copy.24
  99.0 3.8 %collective-permute-start.7 = (f32[32,16,64]{2,0,1:T(8,128)S(1)}, f32[32,16,64]{2,0,1:T(8,128)S(1)}, u32[]{:S(2)}, u32[]{:S(2)}) collective-permute-start(f32[32,16,64]{2,0,1:T(8,128)S(1)} %bitcast.47), channel_id=1, source_target_pairs={{0,8},{1,9},{2,10},{3,11},{4,12},{5,13},{6,14},{7,15},{8,0},{9,1},... | collective-permute-start | bytes 393224 | tf_op jit(solution)/shard_map/ppermute | solution.py:47
  102.8 0.0 copy-done.1
  102.8 0.7 copy.16
  103.5 9.7 %collective-permute-done.7 = f32[32,16,64]{2,0,1:T(8,128)S(1)} collective-permute-done((f32[32,16,64]{2,0,1:T(8,128)S(1)}, f32[32,16,64]{2,0,1:T(8,128)S(1)}, u32[]{:S(2)}, u32[]{:S(2)}) %collective-permute-start.7) | collective-permute-done | bytes 131104 | tf_op jit(solution)/shard_map/ppermute | solution.py:47
  113.3 0.1 fusion
  113.4 0.7 copy.17
  (4 shorter events, 0.1 us)
Async XLA Ops:
  1.6 10.4 %collective-permute-start = (bf16[1,32,16,64]{3,1,2,0:T(8,128)(2,1)S(1)}, bf16[1,32,16,64]{3,1,2,0:T(8,128)(2,1)S(1)}, u32[]{:S(2)}, u32[]{:S(2)}) collective-permute-start(bf16[1,32,16,64]{3,1,2,0:T(8,128)(2,1)S(1)} %bitcast.43), channel_id=1, source_target_pairs={{0,8},{1,9},{2,10},{3,11},{4,12},{5,13},{6,14},{7,15},{8,0},{9,1},... | collective-permute-start | bytes 196616 | tf_op jit(solution)/shard_map/ppermute | solution.py:23
  12.1 7.6 %collective-permute-start.1 = (bf16[2,32,16,64]{3,1,2,0:T(8,128)(2,1)S(1)}, bf16[2,32,16,64]{3,1,2,0:T(8,128)(2,1)S(1)}, u32[]{:S(2)}, u32[]{:S(2)}) collective-permute-start(bf16[2,32,16,64]{3,1,2,0:T(8,128)(2,1)S(1)} %pad_maximum_fusion.3), channel_id=1, source_target_pairs={{0,4},{1,5},{2,6},{3,7},{4,0},{5,1},{6,2},{7,3},{8,12},{9,13},{10,... | collective-permute-start | bytes 393224 | tf_op jit(solution)/shard_map/ppermute | solution.py:23
  19.8 12.3 %collective-permute-start.2 = (bf16[4,32,16,64]{3,1,2,0:T(8,128)(2,1)S(1)}, bf16[4,32,16,64]{3,1,2,0:T(8,128)(2,1)S(1)}, u32[]{:S(2)}, u32[]{:S(2)}) collective-permute-start(bf16[4,32,16,64]{3,1,2,0:T(8,128)(2,1)S(1)} %pad_maximum_fusion.2), channel_id=1, source_target_pairs={{0,2},{1,3},{2,0},{3,1},{4,6},{5,7},{6,4},{7,5},{8,10},{9,11},{10,... | collective-permute-start | bytes 786440 | tf_op jit(solution)/shard_map/ppermute | solution.py:23
  21.2 11.4 %copy-start.2 = (bf16[1024,128]{1,0:T(8,128)(2,1)S(1)}, bf16[1024,128]{1,0:T(8,128)(2,1)}, u32[]{:S(2)}) copy-start(bf16[1024,128]{1,0:T(8,128)(2,1)} %param.7) | copy-start | bytes 786436
  32.5 2.7 %collective-permute-start.3 = (bf16[8,32,16,64]{3,1,2,0:T(8,128)(2,1)S(1)}, bf16[8,32,16,64]{3,1,2,0:T(8,128)(2,1)S(1)}, u32[]{:S(2)}, u32[]{:S(2)}) collective-permute-start(bf16[8,32,16,64]{3,1,2,0:T(8,128)(2,1)S(1)} %pad_maximum_fusion.1), channel_id=1, source_target_pairs={{0,1},{1,0},{2,3},{3,2},{4,5},{5,4},{6,7},{7,6},{8,9},{9,8},{10,11... | collective-permute-start | bytes 1572872 | tf_op jit(solution)/shard_map/ppermute | solution.py:23
  50.6 4.5 %collective-permute-start.4 = (f32[2,2,2,32,16,64]{5,4,3,1,0,2:T(8,128)}, f32[2,2,2,32,16,64]{5,4,3,1,0,2:T(8,128)}, u32[]{:S(2)}, u32[]{:S(2)}) collective-permute-start(f32[2,2,2,32,16,64]{5,4,3,1,0,2:T(8,128)} %bitcast.37), channel_id=1, source_target_pairs={{0,1},{1,0},{2,3},{3,2},{4,5},{5,4},{6,7},{7,6},{8,9},{9,8},{10,11... | collective-permute-start | bytes 3145736 | tf_op jit(solution)/shard_map/ppermute | solution.py:47
  56.9 1.4 %copy-start = (f32[2,2,2,32,16,64]{5,4,3,1,0,2:T(8,128)}, f32[2,2,2,32,16,64]{5,4,3,1,0,2:T(8,128)S(1)}, u32[]{:S(2)}) copy-start(f32[2,2,2,32,16,64]{5,4,3,1,0,2:T(8,128)S(1)} %bitcast_add_fusion) | copy-start | bytes 3145732
  58.4 25.3 %collective-permute-start.5 = (f32[2,2,32,16,64]{4,3,2,1,0:T(8,128)S(1)}, f32[2,2,32,16,64]{4,3,2,1,0:T(8,128)S(1)}, u32[]{:S(2)}, u32[]{:S(2)}) collective-permute-start(f32[2,2,32,16,64]{4,3,2,1,0:T(8,128)S(1)} %dynamic-slice_bitcast_fusion), channel_id=1, source_target_pairs={{0,2},{1,3},{2,0},{3,1},{4,6},{5,7},{6,4},{7,5},{8,10},{9,11},{10,... | collective-permute-start | bytes 1572872 | tf_op jit(solution)/shard_map/ppermute | solution.py:47
  85.1 13.7 %collective-permute-start.6 = (f32[2,32,16,64]{3,2,1,0:T(8,128)S(1)}, f32[2,32,16,64]{3,2,1,0:T(8,128)S(1)}, u32[]{:S(2)}, u32[]{:S(2)}) collective-permute-start(f32[2,32,16,64]{3,2,1,0:T(8,128)S(1)} %dynamic-slice_bitcast_fusion.1), channel_id=1, source_target_pairs={{0,4},{1,5},{2,6},{3,7},{4,0},{5,1},{6,2},{7,3},{8,12},{9,13},{10,... | collective-permute-start | bytes 786440 | tf_op jit(solution)/shard_map/ppermute | solution.py:47
  94.4 8.4 %copy-start.1 = (f32[512,64]{1,0:T(8,128)S(1)}, f32[512,64]{1,0:T(8,128)}, u32[]{:S(2)}) copy-start(f32[512,64]{1,0:T(8,128)} %shard_map.60) | copy-start | bytes 393220
  99.0 14.2 %collective-permute-start.7 = (f32[32,16,64]{2,0,1:T(8,128)S(1)}, f32[32,16,64]{2,0,1:T(8,128)S(1)}, u32[]{:S(2)}, u32[]{:S(2)}) collective-permute-start(f32[32,16,64]{2,0,1:T(8,128)S(1)} %bitcast.47), channel_id=1, source_target_pairs={{0,8},{1,9},{2,10},{3,11},{4,12},{5,13},{6,14},{7,15},{8,0},{9,1},... | collective-permute-start | bytes 393224 | tf_op jit(solution)/shard_map/ppermute | solution.py:47

commit v4 on v3

--- a/solution.py
+++ b/solution.py
@@ -95,8 +95,7 @@
     per_dev = right_proj.shape[1] // C
 
     right_t = right_proj.reshape(n_seq, per_dev, C).transpose(2, 1, 0)
-    right_blocks = gather_blocks(right_t, "row", n, bits[::-1])
-    pair_cot, right_blocks = lax.optimization_barrier((pair_cot, right_blocks))
+    right_blocks = lax.all_gather(right_t, "row", axis=0)
 
     weight_ec = out_weight.reshape(C, C, p_size).transpose(1, 0, 2).reshape(C * C, p_size)
 

time: 114 us -> 112 us (0.982)
  between operations: 0.78 us -> 14.1 us
  waiting for transfers between devices: 68.2 us -> 55.8 us
  starting transfers between devices: 13.9 us -> 7.58 us
  local copies, waits for them, and re-layouts: 11.4 us -> 14 us
    ppermute x4 -> x0, waiting for transfers between devices: 25.8 us -> none  [gather_blocks(): other = lax.ppermute(buf, axis, xor_pairs(n, bit))]
    ppermute x4, waiting for transfers between devices: 42.4 us -> 55.8 us  [scatter_sum(): buf = keep + lax.ppermute(send, axis, xor_pairs(n, bit))]
    ppermute x4 -> x0, starting transfers between devices: 6.3 us -> none  [gather_blocks(): other = lax.ppermute(buf, axis, xor_pairs(n, bit))]
    all_gather x0 -> x1, local copies, waits for them, and re-layouts: none -> 4.27 us  [per_device(): right_blocks = lax.all_gather(right_t, 'row', axis=0)]
    transpose x1 -> x0, local copies, waits for them, and re-layouts: 2.22 us -> none  [gather_blocks(): buf = buf.transpose(order + list(range(k, k + x.ndim)))]
    unnamed x9 -> x7, local copies, waits for them, and re-layouts: 3.79 us -> 3.54 us
  transfers between devices with their start and end apart: 8 -> 5, of which waited for: 8 -> 4; matrix products, arithmetic and copies ran while one was open for 1% -> 5% of each run, Pallas kernels for 6% -> 0%
where the time goes in v4:
time: 112 us; the launch traced here: 111 us
  waiting for transfers between devices  55.8 us (50%)
  Pallas kernels  15.2 us (14%)
  between operations  14.1 us (13%)
  local copies, waits for them, and re-layouts  14 us (12%)
  starting transfers between devices  7.58 us (7%)
  other arithmetic  4.35 us (4%)
    ppermute x4, waiting for transfers between devices, scatter_sum(): buf = keep + lax.ppermute(send, axis, xor_pairs(n, bit))  55.8 us
    pallas_call x1, Pallas kernels, per_device(): pl.pallas_call(functools.partial(project_kernel, n_seq=n_seq), grid=(step...  8.19 us
    ppermute x4, starting transfers between devices, scatter_sum(): buf = keep + lax.ppermute(send, axis, xor_pairs(n, bit))  7.54 us
    pallas_call x1, Pallas kernels, per_device(): pl.pallas_call(left_kernel, grid=(steps,), in_specs=[pl.BlockSpec((C, own...  7.03 us
    all_gather x1, local copies, waits for them, and re-layouts, per_device(): right_blocks = lax.all_gather(right_t, 'row', axis=0)  4.27 us
    another operation x2, local copies, waits for them, and re-layouts  4.22 us
    unnamed x7, local copies, waits for them, and re-layouts  3.54 us
    add x3, other arithmetic, scatter_sum(): buf = keep + lax.ppermute(send, axis, xor_pairs(n, bit))  3.29 us
  transfers between devices with their start and end apart: 5, of which 4 were waited for; matrix products, arithmetic and copies ran while one was open for 5% of the time, Pallas kernels for 0%

profile of v4, /device:TPU:0, one launch (start us, length us, event | category | flops | bytes accessed | tf_op | source)
XLA Modules:
  0.0 111.1 jit_solution(14763550313824851231)
XLA Ops:
  7.2 0.0 all-gather.3.cloned.1.call-start
  7.2 1.8 %copy.9 = bf16[32,32,128]{2,0,1:T(8,128)(2,1)} copy(bf16[32,32,128]{2,1,0:T(8,128)(2,1)} %bitcast.39) | data formatting | bytes 524288 | tf_op jit(solution)/shard_map/reshape | solution.py:100
  9.0 8.2 %shard_map.59 = (bf16[32,512,256]{2,1,0:T(8,128)(2,1)}, f32[16,32,16,64]{3,2,1,0:T(8,128)}) custom-call(bf16[16,256,128]{2,1,0:T(8,128)(2,1)} %p_ref.1, bf16[1024,128]{1,0:T(8,128)(2,1)} %bitcast.36, bf16[64,512]{1,0:T(8,128)(2,1)} %l_ref.1), custom_call_target="tpu_custom_call" | custom-call | tf_op jit(solution)/shard_map/pallas_call | solution.py:102
  17.2 2.7 %constant_dynamic-slice_fusion.3 = (f32[2,2,2,1,32,16,64]{6,5,4,3,2,1,0:T(8,128)S(1)}, f32[2,2,2,1,32,16,64]{6,5,4,3,2,1,0:T(8,128)S(1)}) fusion(f32[2,2,2,2,32,16,64]{6,5,4,3,2,1,0:T(8,128)} %bitcast.35, s32[]{:T(128)S(6)} %select_n.28, s32[]{:T(128)S(6)} %select_n.29), kind=kLoop, calls=%fused_computation.13 | loop fusion | bytes 4194312 | tf_op jit(solution)/shard_map/dynamic-slice
  19.8 0.0 copy-start.1
  19.9 1.6 %copy.22 = f32[2,2,2,1,32,16,64]{6,5,4,1,0,2,3:T(8,128)} copy(f32[2,2,2,1,32,16,64]{6,5,4,3,2,1,0:T(8,128)S(1)} %get-tuple-element.11) | data formatting | bytes 2097152 | tf_op jit(solution)/shard_map/dynamic-slice.1
  21.4 0.5 collective-permute-start
  21.9 0.0 copy-done.1
  21.9 0.8 copy.10
  22.6 0.0 all-gather.3.cloned.1.call-update
  22.7 3.3 %collective-permute-done = f32[2,2,2,32,16,64]{5,4,3,1,0,2:T(8,128)} collective-permute-done((f32[2,2,2,32,16,64]{5,4,3,1,0,2:T(8,128)}, f32[2,2,2,32,16,64]{5,4,3,1,0,2:T(8,128)}, u32[]{:S(2)}, u32[]{:S(2)}) %collective-permute-start) | collective-permute-done | bytes 1048608 | tf_op jit(solution)/shard_map/ppermute | solution.py:47
  26.0 1.9 %bitcast_add_fusion = f32[2,2,2,32,16,64]{5,4,3,1,0,2:T(8,128)S(1)} fusion(f32[2,2,2,32,16,64]{5,4,3,1,0,2:T(8,128)} %collective-permute-done, f32[2,2,2,1,32,16,64]{6,5,4,3,2,1,0:T(8,128)S(1)} %get-tuple-element.10), kind=kLoop, calls=%fused_computation | loop fusion | flops 262144 | bytes 3145728 | tf_op jit(solution)/shard_map/add | solution.py:47
  27.9 0.0 copy-start
  27.9 1.3 %copy-done = f32[2,2,2,32,16,64]{5,4,3,1,0,2:T(8,128)} copy-done((f32[2,2,2,32,16,64]{5,4,3,1,0,2:T(8,128)}, f32[2,2,2,32,16,64]{5,4,3,1,0,2:T(8,128)S(1)}, u32[]{:S(2)}) %copy-start) | copy-done | bytes 1048600
  29.2 0.1 dynamic-slice_bitcast_fusion
  29.3 3.0 %collective-permute-start.1 = (f32[2,2,32,16,64]{4,3,2,1,0:T(8,128)S(1)}, f32[2,2,32,16,64]{4,3,2,1,0:T(8,128)S(1)}, u32[]{:S(2)}, u32[]{:S(2)}) collective-permute-start(f32[2,2,32,16,64]{4,3,2,1,0:T(8,128)S(1)} %dynamic-slice_bitcast_fusion), channel_id=1, source_target_pairs={{0,2},{1,3},{2,0},{3,1},{4,6},{5,7},{6,4},{7,5},{8,10},{9,11},{10,... | collective-permute-start | bytes 1572872 | tf_op jit(solution)/shard_map/ppermute | solution.py:47
  32.2 29.5 %collective-permute-done.1 = f32[2,2,32,16,64]{4,3,2,1,0:T(8,128)S(1)} collective-permute-done((f32[2,2,32,16,64]{4,3,2,1,0:T(8,128)S(1)}, f32[2,2,32,16,64]{4,3,2,1,0:T(8,128)S(1)}, u32[]{:S(2)}, u32[]{:S(2)}) %collective-permute-start.1) | collective-permute-done | bytes 524320 | tf_op jit(solution)/shard_map/ppermute | solution.py:47
  61.8 1.4 %bitcast_add_fusion.1 = f32[2,2,32,16,64]{4,3,2,1,0:T(8,128)S(1)} fusion(f32[2,2,32,16,64]{4,3,2,1,0:T(8,128)S(1)} %collective-permute-done.1, f32[2,2,2,32,16,64]{5,4,3,1,0,2:T(8,128)} %copy-done, s32[]{:T(128)S(6)} %select_n.30), kind=kLoop, calls=%fused_computation.2 | loop fusion | flops 131072 | bytes 1572868 | tf_op jit(solution)/shard_map/add | solution.py:47
  63.2 1.5 %collective-permute-start.2 = (f32[2,32,16,64]{3,2,1,0:T(8,128)S(1)}, f32[2,32,16,64]{3,2,1,0:T(8,128)S(1)}, u32[]{:S(2)}, u32[]{:S(2)}) collective-permute-start(f32[2,32,16,64]{3,2,1,0:T(8,128)S(1)} %dynamic-slice_bitcast_fusion.1), channel_id=1, source_target_pairs={{0,4},{1,5},{2,6},{3,7},{4,0},{5,1},{6,2},{7,3},{8,12},{9,13},{10,... | collective-permute-start | bytes 786440 | tf_op jit(solution)/shard_map/ppermute | solution.py:47
  64.7 13.0 %collective-permute-done.2 = f32[2,32,16,64]{3,2,1,0:T(8,128)S(1)} collective-permute-done((f32[2,32,16,64]{3,2,1,0:T(8,128)S(1)}, f32[2,32,16,64]{3,2,1,0:T(8,128)S(1)}, u32[]{:S(2)}, u32[]{:S(2)}) %collective-permute-start.2) | collective-permute-done | bytes 262176 | tf_op jit(solution)/shard_map/ppermute | solution.py:47
  77.6 0.1 bitcast_add_fusion.2
  77.8 0.1 copy.23
  77.8 2.6 %collective-permute-start.3 = (f32[32,16,64]{2,0,1:T(8,128)S(1)}, f32[32,16,64]{2,0,1:T(8,128)S(1)}, u32[]{:S(2)}, u32[]{:S(2)}) collective-permute-start(f32[32,16,64]{2,0,1:T(8,128)S(1)} %bitcast.40), channel_id=1, source_target_pairs={{0,8},{1,9},{2,10},{3,11},{4,12},{5,13},{6,14},{7,15},{8,0},{9,1},... | collective-permute-start | bytes 393224 | tf_op jit(solution)/shard_map/ppermute | solution.py:47
  80.5 10.0 %collective-permute-done.3 = f32[32,16,64]{2,0,1:T(8,128)S(1)} collective-permute-done((f32[32,16,64]{2,0,1:T(8,128)S(1)}, f32[32,16,64]{2,0,1:T(8,128)S(1)}, u32[]{:S(2)}, u32[]{:S(2)}) %collective-permute-start.3) | collective-permute-done | bytes 131104 | tf_op jit(solution)/shard_map/ppermute | solution.py:47
  90.5 0.1 fusion
  90.5 0.7 copy.17
  91.3 0.0 all-gather.3.cloned.1.call-done
  91.3 4.3 %copy.11 = bf16[512,16,64]{2,1,0:T(8,128)(2,1)} copy(bf16[512,16,64]{2,0,1:T(8,128)(2,1)} %all-gather.3.cloned.1.call-done) | data formatting | bytes 2097152 | tf_op jit(solution)/shard_map/all_gather | solution.py:98
  95.5 7.0 %shard_map.60 = f32[512,64]{1,0:T(8,128)} custom-call(bf16[32,512,256]{2,1,0:T(8,128)(2,1)} %get-tuple-element.4.gm_ref, bf16[16,32,16,64]{3,2,1,0:T(8,128)(2,1)} %bitcast.34), custom_call_target="tpu_custom_call" | custom-call | tf_op jit(solution)/shard_map/pallas_call | solution.py:124
  102.6 1.0 convert_bitcast_fusion
  103.5 0.7 copy.16
  (2 shorter events, 0.1 us)
Async XLA Ops:
  7.2 84.1 %all-gather.3.cloned.1.call-start = ((), (), s32[]{:S(2)}) async-start(), calls=%async_computation | async-start | bytes 2228224 | tf_op jit(solution)/shard_map/all_gather | solution.py:98
  19.8 2.0 %copy-start.1 = (bf16[64,512]{1,0:T(8,128)(2,1)S(1)}, bf16[64,512]{1,0:T(8,128)(2,1)}, u32[]{:S(2)}) copy-start(bf16[64,512]{1,0:T(8,128)(2,1)} %param.5) | copy-start | bytes 196612
  21.4 4.6 %collective-permute-start = (f32[2,2,2,32,16,64]{5,4,3,1,0,2:T(8,128)}, f32[2,2,2,32,16,64]{5,4,3,1,0,2:T(8,128)}, u32[]{:S(2)}, u32[]{:S(2)}) collective-permute-start(f32[2,2,2,32,16,64]{5,4,3,1,0,2:T(8,128)} %bitcast.32), channel_id=1, source_target_pairs={{0,1},{1,0},{2,3},{3,2},{4,5},{5,4},{6,7},{7,6},{8,9},{9,8},{10,11... | collective-permute-start | bytes 3145736 | tf_op jit(solution)/shard_map/ppermute | solution.py:47
  27.9 1.3 %copy-start = (f32[2,2,2,32,16,64]{5,4,3,1,0,2:T(8,128)}, f32[2,2,2,32,16,64]{5,4,3,1,0,2:T(8,128)S(1)}, u32[]{:S(2)}) copy-start(f32[2,2,2,32,16,64]{5,4,3,1,0,2:T(8,128)S(1)} %bitcast_add_fusion) | copy-start | bytes 3145732
  29.3 32.5 %collective-permute-start.1 = (f32[2,2,32,16,64]{4,3,2,1,0:T(8,128)S(1)}, f32[2,2,32,16,64]{4,3,2,1,0:T(8,128)S(1)}, u32[]{:S(2)}, u32[]{:S(2)}) collective-permute-start(f32[2,2,32,16,64]{4,3,2,1,0:T(8,128)S(1)} %dynamic-slice_bitcast_fusion), channel_id=1, source_target_pairs={{0,2},{1,3},{2,0},{3,1},{4,6},{5,7},{6,4},{7,5},{8,10},{9,11},{10,... | collective-permute-start | bytes 1572872 | tf_op jit(solution)/shard_map/ppermute | solution.py:47
  63.2 14.5 %collective-permute-start.2 = (f32[2,32,16,64]{3,2,1,0:T(8,128)S(1)}, f32[2,32,16,64]{3,2,1,0:T(8,128)S(1)}, u32[]{:S(2)}, u32[]{:S(2)}) collective-permute-start(f32[2,32,16,64]{3,2,1,0:T(8,128)S(1)} %dynamic-slice_bitcast_fusion.1), channel_id=1, source_target_pairs={{0,4},{1,5},{2,6},{3,7},{4,0},{5,1},{6,2},{7,3},{8,12},{9,13},{10,... | collective-permute-start | bytes 786440 | tf_op jit(solution)/shard_map/ppermute | solution.py:47
  77.8 12.6 %collective-permute-start.3 = (f32[32,16,64]{2,0,1:T(8,128)S(1)}, f32[32,16,64]{2,0,1:T(8,128)S(1)}, u32[]{:S(2)}, u32[]{:S(2)}) collective-permute-start(f32[32,16,64]{2,0,1:T(8,128)S(1)} %bitcast.40), channel_id=1, source_target_pairs={{0,8},{1,9},{2,10},{3,11},{4,12},{5,13},{6,14},{7,15},{8,0},{9,1},... | collective-permute-start | bytes 393224 | tf_op jit(solution)/shard_map/ppermute | solution.py:47
Sparse Core Ops, SparseCore 0:
  22.8 49.3 all-gather.2

commit v5 on v3

--- a/solution.py
+++ b/solution.py
@@ -96,7 +96,6 @@
 
     right_t = right_proj.reshape(n_seq, per_dev, C).transpose(2, 1, 0)
     right_blocks = gather_blocks(right_t, "row", n, bits[::-1])
-    pair_cot, right_blocks = lax.optimization_barrier((pair_cot, right_blocks))
 
     weight_ec = out_weight.reshape(C, C, p_size).transpose(1, 0, 2).reshape(C * C, p_size)
 
@@ -117,6 +116,11 @@
             jax.ShapeDtypeStruct((total // 16, C, 16, n_seq), jnp.float32),
         ],
         compiler_params=pltpu.CompilerParams(vmem_limit_bytes=56 * 1024 * 1024),
+        cost_estimate=pl.CostEstimate(
+            flops=2 * own_rows * total * C * C * (p_size + n_seq),
+            transcendentals=0,
+            bytes_accessed=2 * own_rows * total * (p_size + C * C) + 4 * total * C * n_seq,
+        ),
     )(pair_cot, weight_ec, left_proj)
 
     summed = scatter_sum(part_t, "row", n, bits)
@@ -132,6 +136,11 @@
         out_specs=pl.BlockSpec((own_rows * C, n_seq), lambda b: (0, 0)),
         out_shape=jax.ShapeDtypeStruct((own_rows * C, n_seq), jnp.float32),
         compiler_params=pltpu.CompilerParams(vmem_limit_bytes=56 * 1024 * 1024),
+        cost_estimate=pl.CostEstimate(
+            flops=2 * own_rows * total * C * C * n_seq,
+            transcendentals=0,
+            bytes_accessed=2 * own_rows * total * C * C + 2 * total * C * n_seq,
+        ),
     )(grad_m, right_blocks)
     grad_left = left_t.T.astype(jnp.bfloat16)
     return (grad_left, grad_right)

time: 114 us -> 98.8 us (0.87)
  waiting for transfers between devices: 68.2 us -> 52.8 us
  starting transfers between devices: 13.9 us -> 11.6 us
  other arithmetic: 4.69 us -> 6.89 us
    ppermute x4, waiting for transfers between devices: 42.4 us -> 28.6 us  [scatter_sum(): buf = keep + lax.ppermute(send, axis, xor_pairs(n, bit))]
    unnamed x9 -> x11, local copies, waits for them, and re-layouts: 3.79 us -> 1.59 us
    ppermute x4, starting transfers between devices: 7.61 us -> 5.65 us  [scatter_sum(): buf = keep + lax.ppermute(send, axis, xor_pairs(n, bit))]
    ppermute x4, waiting for transfers between devices: 25.8 us -> 24.1 us  [gather_blocks(): other = lax.ppermute(buf, axis, xor_pairs(n, bit))]
    select_n x4, other arithmetic: 0.51 us -> 1.73 us  [gather_blocks(): low = jnp.where(mine == 0, buf, other)]
  transfers between devices with their start and end apart: 8 -> 8, of which waited for: 8 -> 5; matrix products, arithmetic and copies ran while one was open for 1% -> 11% of each run, Pallas kernels for 6% -> 7%
where the time goes in v5:
time: 98.8 us; the launch traced here: 98.5 us
  waiting for transfers between devices  52.8 us (53%)
  Pallas kernels  15.2 us (15%)
  starting transfers between devices  11.6 us (12%)
  local copies, waits for them, and re-layouts  11.3 us (11%)
  other arithmetic  6.89 us (7%)
    ppermute x4, waiting for transfers between devices, scatter_sum(): buf = keep + lax.ppermute(send, axis, xor_pairs(n, bit))  28.6 us
    ppermute x4, waiting for transfers between devices, gather_blocks(): other = lax.ppermute(buf, axis, xor_pairs(n, bit))  24.1 us
    pallas_call x1, Pallas kernels, per_device(): pl.pallas_call(functools.partial(project_kernel, n_seq=n_seq), grid=(step...  8.2 us
    pallas_call x1, Pallas kernels, per_device(): pl.pallas_call(left_kernel, grid=(steps,), in_specs=[pl.BlockSpec((C, own...  7.02 us
    ppermute x4, starting transfers between devices, gather_blocks(): other = lax.ppermute(buf, axis, xor_pairs(n, bit))  5.9 us
    ppermute x4, starting transfers between devices, scatter_sum(): buf = keep + lax.ppermute(send, axis, xor_pairs(n, bit))  5.65 us
    another operation x2, local copies, waits for them, and re-layouts  4.29 us
    add x3, other arithmetic, scatter_sum(): buf = keep + lax.ppermute(send, axis, xor_pairs(n, bit))  3.29 us
  transfers between devices with their start and end apart: 8, of which 5 were waited for; matrix products, arithmetic and copies ran while one was open for 11% of the time, Pallas kernels for 7%

profile of v5, /device:TPU:0, one launch (start us, length us, event | category | flops | bytes accessed | tf_op | source)
XLA Modules:
  0.0 98.5 jit_solution(2357055900788691882)
XLA Ops:
  0.6 1.8 %copy.8 = bf16[32,32,128]{2,0,1:T(8,128)(2,1)} copy(bf16[32,32,128]{2,1,0:T(8,128)(2,1)} %bitcast.45) | data formatting | bytes 524288 | tf_op jit(solution)/shard_map/reshape | solution.py:100
  2.4 8.2 %shard_map.59 = (bf16[32,512,256]{2,1,0:T(8,128)(2,1)}, f32[16,32,16,64]{3,2,1,0:T(8,128)}) custom-call(bf16[16,256,128]{2,1,0:T(8,128)(2,1)} %p_ref.1, bf16[1024,128]{1,0:T(8,128)(2,1)} %bitcast.46, bf16[64,512]{1,0:T(8,128)(2,1)} %l_ref.1), custom_call_target="tpu_custom_call" | custom-call | flops 1610612736 | bytes 11534336 | tf_op jit(solution)/shard_map/pallas_call | solution.py:102
  10.6 2.7 %constant_dynamic-slice_fusion.3 = (f32[2,2,2,1,32,16,64]{6,5,4,3,2,1,0:T(8,128)S(1)}, f32[2,2,2,1,32,16,64]{6,5,4,3,2,1,0:T(8,128)S(1)}) fusion(f32[2,2,2,2,32,16,64]{6,5,4,3,2,1,0:T(8,128)} %bitcast.41, s32[]{:T(128)S(6)} %select_n.88, s32[]{:T(128)S(6)} %select_n.89), kind=kLoop, calls=%fused_computation.25 | loop fusion | bytes 4194312 | tf_op jit(solution)/shard_map/dynamic-slice
  13.3 0.0 copy-start.3
  13.3 1.6 %copy.23 = f32[2,2,2,1,32,16,64]{6,5,4,1,0,2,3:T(8,128)} copy(f32[2,2,2,1,32,16,64]{6,5,4,3,2,1,0:T(8,128)S(1)} %get-tuple-element.11) | data formatting | bytes 2097152 | tf_op jit(solution)/shard_map/dynamic-slice.1
  14.9 0.5 collective-permute-start.4
  15.4 0.0 copy-done.3
  15.4 0.1 copy.9
  15.5 3.7 %collective-permute-start = (bf16[1,32,16,64]{3,1,2,0:T(8,128)(2,1)S(1)}, bf16[1,32,16,64]{3,1,2,0:T(8,128)(2,1)S(1)}, u32[]{:S(2)}, u32[]{:S(2)}) collective-permute-start(bf16[1,32,16,64]{3,1,2,0:T(8,128)(2,1)S(1)} %bitcast.42), channel_id=1, source_target_pairs={{0,8},{1,9},{2,10},{3,11},{4,12},{5,13},{6,14},{7,15},{8,0},{9,1},... | collective-permute-start | bytes 196616 | tf_op jit(solution)/shard_map/ppermute | solution.py:23
  19.1 7.0 %collective-permute-done = bf16[1,32,16,64]{3,1,2,0:T(8,128)(2,1)S(1)} collective-permute-done((bf16[1,32,16,64]{3,1,2,0:T(8,128)(2,1)S(1)}, bf16[1,32,16,64]{3,1,2,0:T(8,128)(2,1)S(1)}, u32[]{:S(2)}, u32[]{:S(2)}) %collective-permute-start) | collective-permute-done | bytes 65568 | tf_op jit(solution)/shard_map/ppermute | solution.py:23
  26.1 0.1 pad_maximum_fusion.3
  26.2 0.8 collective-permute-start.1
  27.0 7.4 %collective-permute-done.1 = bf16[2,32,16,64]{3,1,2,0:T(8,128)(2,1)S(1)} collective-permute-done((bf16[2,32,16,64]{3,1,2,0:T(8,128)(2,1)S(1)}, bf16[2,32,16,64]{3,1,2,0:T(8,128)(2,1)S(1)}, u32[]{:S(2)}, u32[]{:S(2)}) %collective-permute-start.1) | collective-permute-done | bytes 131104 | tf_op jit(solution)/shard_map/ppermute | solution.py:23
  34.4 0.1 broadcast_select_fusion.5
  34.5 0.1 pad_maximum_fusion.2
  34.6 1.4 %collective-permute-start.2 = (bf16[4,32,16,64]{3,1,2,0:T(8,128)(2,1)S(1)}, bf16[4,32,16,64]{3,1,2,0:T(8,128)(2,1)S(1)}, u32[]{:S(2)}, u32[]{:S(2)}) collective-permute-start(bf16[4,32,16,64]{3,1,2,0:T(8,128)(2,1)S(1)} %pad_maximum_fusion.2), channel_id=1, source_target_pairs={{0,2},{1,3},{2,0},{3,1},{4,6},{5,7},{6,4},{7,5},{8,10},{9,11},{10,... | collective-permute-start | bytes 786440 | tf_op jit(solution)/shard_map/ppermute | solution.py:23
  36.0 0.0 collective-permute-done.4
  36.0 1.9 %bitcast_add_fusion = f32[2,2,2,32,16,64]{5,4,3,1,0,2:T(8,128)S(1)} fusion(f32[2,2,2,32,16,64]{5,4,3,1,0,2:T(8,128)} %collective-permute-done.4, f32[2,2,2,1,32,16,64]{6,5,4,3,2,1,0:T(8,128)S(1)} %get-tuple-element.10), kind=kLoop, calls=%fused_computation.1 | loop fusion | flops 262144 | bytes 3145728 | tf_op jit(solution)/shard_map/add | solution.py:47
  37.9 0.0 copy-start
  37.9 1.2 %dynamic-slice_bitcast_fusion = f32[2,2,32,16,64]{4,3,2,1,0:T(8,128)} fusion(f32[2,2,2,32,16,64]{5,4,3,1,0,2:T(8,128)S(1)} %bitcast_add_fusion, s32[]{:T(128)S(6)} %select_n.91), kind=kLoop, calls=%fused_computation.5 | loop fusion | bytes 1048580 | tf_op jit(solution)/shard_map/jit(dynamic_index_in_dim)/squeeze | solution.py:46
  39.1 0.7 collective-permute-start.5
  39.8 9.8 %collective-permute-done.2 = bf16[4,32,16,64]{3,1,2,0:T(8,128)(2,1)S(1)} collective-permute-done((bf16[4,32,16,64]{3,1,2,0:T(8,128)(2,1)S(1)}, bf16[4,32,16,64]{3,1,2,0:T(8,128)(2,1)S(1)}, u32[]{:S(2)}, u32[]{:S(2)}) %collective-permute-start.2) | collective-permute-done | bytes 262176 | tf_op jit(solution)/shard_map/ppermute | solution.py:23
  49.5 0.1 broadcast_select_fusion.3
  49.7 0.0 copy-done
  49.7 0.0 copy-start.1
  49.7 1.2 %pad_maximum_fusion.1 = bf16[8,32,16,64]{3,1,2,0:T(8,128)(2,1)} fusion(bf16[4,32,16,64]{3,1,2,0:T(8,128)(2,1)S(1)} %get-tuple-element.15, bf16[4,32,16,64]{3,1,2,0:T(8,128)(2,1)S(1)} %get-tuple-element.14), kind=kLoop, calls=%fused_computation.3 | loop fusion | flops 262144 | bytes 1048576 | tf_op jit(solution)/shard_map/concatenate | solution.py:27
  50.9 0.0 collective-permute-start.3
  50.9 19.3 %collective-permute-done.5 = f32[2,2,32,16,64]{4,3,2,1,0:T(8,128)} collective-permute-done((f32[2,2,32,16,64]{4,3,2,1,0:T(8,128)}, f32[2,2,32,16,64]{4,3,2,1,0:T(8,128)}, u32[]{:S(2)}, u32[]{:S(2)}) %collective-permute-start.5) | collective-permute-done | bytes 524320 | tf_op jit(solution)/shard_map/ppermute | solution.py:47
  70.1 0.0 copy-done.1
  70.1 1.4 %bitcast_add_fusion.1 = f32[2,2,32,16,64]{4,3,2,1,0:T(8,128)S(1)} fusion(f32[2,2,32,16,64]{4,3,2,1,0:T(8,128)} %collective-permute-done.5, f32[2,2,2,32,16,64]{5,4,3,1,0,2:T(8,128)S(1)} %copy-done.1, s32[]{:T(128)S(6)} %select_n.90), kind=kLoop, calls=%fused_computation.4 | loop fusion | flops 131072 | bytes 1572868 | tf_op jit(solution)/shard_map/add | solution.py:47
  71.6 1.1 %collective-permute-start.6 = (f32[2,32,16,64]{3,2,1,0:T(8,128)S(1)}, f32[2,32,16,64]{3,2,1,0:T(8,128)S(1)}, u32[]{:S(2)}, u32[]{:S(2)}) collective-permute-start(f32[2,32,16,64]{3,2,1,0:T(8,128)S(1)} %dynamic-slice_bitcast_fusion.1), channel_id=1, source_target_pairs={{0,4},{1,5},{2,6},{3,7},{4,0},{5,1},{6,2},{7,3},{8,12},{9,13},{10,... | collective-permute-start | bytes 786440 | tf_op jit(solution)/shard_map/ppermute | solution.py:47
  72.6 0.0 collective-permute-done.3
  72.6 1.5 %broadcast_select_fusion.1 = (bf16[8,32,16,64]{3,1,2,0:T(8,128)(2,1)S(1)}, bf16[8,32,16,64]{3,1,2,0:T(8,128)(2,1)S(1)}) fusion(bf16[8,32,16,64]{3,1,2,0:T(8,128)(2,1)} %collective-permute-done.3, pred[]{:T(512)S(6)} %eq.16, bf16[4,32,16,64]{3,1,2,0:T(8,128)(2,1)S(1)} %get-tuple-element.15, bf16[4,32,16,64]{3,1,2,0:T(8,128)(2,1)S(1)} %get-tuple-element.14), kind=kLoop, calls=%fused_computation.7 | loop fusion | flops 786432 | bytes 2097153 | tf_op jit(solution)/shard_map/jit(_where)/select_n | solution.py:25
  74.1 0.4 pad_maximum_fusion
  74.5 2.3 %copy.11 = bf16[2,2,2,2,32,16,64]{6,5,4,3,2,1,0:T(8,128)(2,1)} copy(bf16[2,2,2,2,32,16,64]{6,4,5,0,1,2,3:T(8,128)(2,1)S(1)} %bitcast.39) | data formatting | bytes 2097152 | tf_op jit(solution)/shard_map/transpose | solution.py:32
  76.8 7.0 %shard_map.60 = f32[512,64]{1,0:T(8,128)} custom-call(bf16[32,512,256]{2,1,0:T(8,128)(2,1)} %get-tuple-element.4.gm_ref, bf16[16,32,16,64]{3,2,1,0:T(8,128)(2,1)} %bitcast.40), custom_call_target="tpu_custom_call" | custom-call | flops 536870912 | bytes 9437184 | tf_op jit(solution)/shard_map/pallas_call | solution.py:129
  83.8 0.0 copy-start.2
  83.8 0.0 collective-permute-done.6
  83.8 0.1 bitcast_add_fusion.2
  84.0 0.1 copy.24
  84.0 3.5 %collective-permute-start.7 = (f32[32,16,64]{2,0,1:T(8,128)S(1)}, f32[32,16,64]{2,0,1:T(8,128)S(1)}, u32[]{:S(2)}, u32[]{:S(2)}) collective-permute-start(f32[32,16,64]{2,0,1:T(8,128)S(1)} %bitcast.47), channel_id=1, source_target_pairs={{0,8},{1,9},{2,10},{3,11},{4,12},{5,13},{6,14},{7,15},{8,0},{9,1},... | collective-permute-start | bytes 393224 | tf_op jit(solution)/shard_map/ppermute | solution.py:47
  87.5 0.0 copy-done.2
  87.5 0.7 copy.16
  88.3 9.4 %collective-permute-done.7 = f32[32,16,64]{2,0,1:T(8,128)S(1)} collective-permute-done((f32[32,16,64]{2,0,1:T(8,128)S(1)}, f32[32,16,64]{2,0,1:T(8,128)S(1)}, u32[]{:S(2)}, u32[]{:S(2)}) %collective-permute-start.7) | collective-permute-done | bytes 131104 | tf_op jit(solution)/shard_map/ppermute | solution.py:47
  97.6 0.1 fusion
  97.7 0.7 copy.17
  (4 shorter events, 0.1 us)
Async XLA Ops:
  13.3 2.1 %copy-start.3 = (bf16[64,512]{1,0:T(8,128)(2,1)S(1)}, bf16[64,512]{1,0:T(8,128)(2,1)}, u32[]{:S(2)}) copy-start(bf16[64,512]{1,0:T(8,128)(2,1)} %param.5) | copy-start | bytes 196612
  14.9 21.1 %collective-permute-start.4 = (f32[2,2,2,32,16,64]{5,4,3,1,0,2:T(8,128)}, f32[2,2,2,32,16,64]{5,4,3,1,0,2:T(8,128)}, u32[]{:S(2)}, u32[]{:S(2)}) collective-permute-start(f32[2,2,2,32,16,64]{5,4,3,1,0,2:T(8,128)} %bitcast.37), channel_id=1, source_target_pairs={{0,1},{1,0},{2,3},{3,2},{4,5},{5,4},{6,7},{7,6},{8,9},{9,8},{10,11... | collective-permute-start | bytes 3145736 | tf_op jit(solution)/shard_map/ppermute | solution.py:47
  15.5 10.6 %collective-permute-start = (bf16[1,32,16,64]{3,1,2,0:T(8,128)(2,1)S(1)}, bf16[1,32,16,64]{3,1,2,0:T(8,128)(2,1)S(1)}, u32[]{:S(2)}, u32[]{:S(2)}) collective-permute-start(bf16[1,32,16,64]{3,1,2,0:T(8,128)(2,1)S(1)} %bitcast.42), channel_id=1, source_target_pairs={{0,8},{1,9},{2,10},{3,11},{4,12},{5,13},{6,14},{7,15},{8,0},{9,1},... | collective-permute-start | bytes 196616 | tf_op jit(solution)/shard_map/ppermute | solution.py:23
  26.2 8.2 %collective-permute-start.1 = (bf16[2,32,16,64]{3,1,2,0:T(8,128)(2,1)S(1)}, bf16[2,32,16,64]{3,1,2,0:T(8,128)(2,1)S(1)}, u32[]{:S(2)}, u32[]{:S(2)}) collective-permute-start(bf16[2,32,16,64]{3,1,2,0:T(8,128)(2,1)S(1)} %pad_maximum_fusion.3), channel_id=1, source_target_pairs={{0,4},{1,5},{2,6},{3,7},{4,0},{5,1},{6,2},{7,3},{8,12},{9,13},{10,... | collective-permute-start | bytes 393224 | tf_op jit(solution)/shard_map/ppermute | solution.py:23
  34.6 14.9 %collective-permute-start.2 = (bf16[4,32,16,64]{3,1,2,0:T(8,128)(2,1)S(1)}, bf16[4,32,16,64]{3,1,2,0:T(8,128)(2,1)S(1)}, u32[]{:S(2)}, u32[]{:S(2)}) collective-permute-start(bf16[4,32,16,64]{3,1,2,0:T(8,128)(2,1)S(1)} %pad_maximum_fusion.2), channel_id=1, source_target_pairs={{0,2},{1,3},{2,0},{3,1},{4,6},{5,7},{6,4},{7,5},{8,10},{9,11},{10,... | collective-permute-start | bytes 786440 | tf_op jit(solution)/shard_map/ppermute | solution.py:23
  37.9 11.8 %copy-start = (f32[2,2,2,32,16,64]{5,4,3,1,0,2:T(8,128)}, f32[2,2,2,32,16,64]{5,4,3,1,0,2:T(8,128)S(1)}, u32[]{:S(2)}) copy-start(f32[2,2,2,32,16,64]{5,4,3,1,0,2:T(8,128)S(1)} %bitcast_add_fusion) | copy-start | bytes 3145732
  39.1 31.0 %collective-permute-start.5 = (f32[2,2,32,16,64]{4,3,2,1,0:T(8,128)}, f32[2,2,32,16,64]{4,3,2,1,0:T(8,128)}, u32[]{:S(2)}, u32[]{:S(2)}) collective-permute-start(f32[2,2,32,16,64]{4,3,2,1,0:T(8,128)} %dynamic-slice_bitcast_fusion), channel_id=1, source_target_pairs={{0,2},{1,3},{2,0},{3,1},{4,6},{5,7},{6,4},{7,5},{8,10},{9,11},{10,... | collective-permute-start | bytes 1572872 | tf_op jit(solution)/shard_map/ppermute | solution.py:47
  49.7 20.5 %copy-start.1 = (f32[2,2,2,32,16,64]{5,4,3,1,0,2:T(8,128)S(1)}, f32[2,2,2,32,16,64]{5,4,3,1,0,2:T(8,128)}, u32[]{:S(2)}) copy-start(f32[2,2,2,32,16,64]{5,4,3,1,0,2:T(8,128)} %copy-done) | copy-start | bytes 3145732
  50.9 21.7 %collective-permute-start.3 = (bf16[8,32,16,64]{3,1,2,0:T(8,128)(2,1)}, bf16[8,32,16,64]{3,1,2,0:T(8,128)(2,1)}, u32[]{:S(2)}, u32[]{:S(2)}) collective-permute-start(bf16[8,32,16,64]{3,1,2,0:T(8,128)(2,1)} %pad_maximum_fusion.1), channel_id=1, source_target_pairs={{0,1},{1,0},{2,3},{3,2},{4,5},{5,4},{6,7},{7,6},{8,9},{9,8},{10,11... | collective-permute-start | bytes 1572872 | tf_op jit(solution)/shard_map/ppermute | solution.py:23
  71.6 12.3 %collective-permute-start.6 = (f32[2,32,16,64]{3,2,1,0:T(8,128)S(1)}, f32[2,32,16,64]{3,2,1,0:T(8,128)S(1)}, u32[]{:S(2)}, u32[]{:S(2)}) collective-permute-start(f32[2,32,16,64]{3,2,1,0:T(8,128)S(1)} %dynamic-slice_bitcast_fusion.1), channel_id=1, source_target_pairs={{0,4},{1,5},{2,6},{3,7},{4,0},{5,1},{6,2},{7,3},{8,12},{9,13},{10,... | collective-permute-start | bytes 786440 | tf_op jit(solution)/shard_map/ppermute | solution.py:47
  83.8 3.7 %copy-start.2 = (f32[512,64]{1,0:T(8,128)S(1)}, f32[512,64]{1,0:T(8,128)}, u32[]{:S(2)}) copy-start(f32[512,64]{1,0:T(8,128)} %shard_map.60) | copy-start | bytes 393220
  84.0 13.6 %collective-permute-start.7 = (f32[32,16,64]{2,0,1:T(8,128)S(1)}, f32[32,16,64]{2,0,1:T(8,128)S(1)}, u32[]{:S(2)}, u32[]{:S(2)}) collective-permute-start(f32[32,16,64]{2,0,1:T(8,128)S(1)} %bitcast.47), channel_id=1, source_target_pairs={{0,8},{1,9},{2,10},{3,11},{4,12},{5,13},{6,14},{7,15},{8,0},{9,1},... | collective-permute-start | bytes 393224 | tf_op jit(solution)/shard_map/ppermute | solution.py:47

commit v6 on v5

--- a/solution.py
+++ b/solution.py
@@ -95,7 +95,13 @@
     per_dev = right_proj.shape[1] // C
 
     right_t = right_proj.reshape(n_seq, per_dev, C).transpose(2, 1, 0)
-    right_blocks = gather_blocks(right_t, "row", n, bits[::-1])
+    right_blocks = jnp.concatenate(
+        [
+            gather_blocks(right_t[:C // 2], "row", n, bits[::-1]),
+            gather_blocks(right_t[C // 2:], "row", n, (bits[:1] + bits[1:3][::-1] + bits[3:])[::-1]),
+        ],
+        1,
+    )
 
     weight_ec = out_weight.reshape(C, C, p_size).transpose(1, 0, 2).reshape(C * C, p_size)
 
@@ -123,7 +129,15 @@
         ),
     )(pair_cot, weight_ec, left_proj)
 
-    summed = scatter_sum(part_t, "row", n, bits)
+    half = C // 2
+    swapped = bits[:1] + bits[1:3][::-1] + bits[3:]
+    summed = jnp.concatenate(
+        [
+            scatter_sum(part_t[:, :half], "row", n, bits),
+            scatter_sum(part_t[:, half:], "row", n, swapped),
+        ],
+        0,
+    )
     grad_right = summed.transpose(2, 1, 0).reshape(n_seq, per_dev * C).astype(jnp.bfloat16)
 
     left_t = pl.pallas_call(

time: 98.8 us -> 89.7 us (0.908)
  waiting for transfers between devices: 52.8 us -> 33.5 us
  starting transfers between devices: 11.6 us -> 18 us
  local copies, waits for them, and re-layouts: 11.3 us -> 14.1 us
    ppermute x4 -> x8, waiting for transfers between devices: 24.1 us -> 7.22 us  [gather_blocks(): other = lax.ppermute(buf, axis, xor_pairs(n, bit))]
    slice x0 -> x1, local copies, waits for them, and re-layouts: none -> 3.93 us  [per_device(): part_t[:, :half]]
    ppermute x4 -> x8, starting transfers between devices: 5.9 us -> 9.4 us  [gather_blocks(): other = lax.ppermute(buf, axis, xor_pairs(n, bit))]
    ppermute x4 -> x8, starting transfers between devices: 5.65 us -> 8.63 us  [scatter_sum(): buf = keep + lax.ppermute(send, axis, xor_pairs(n, bit))]
    ppermute x4 -> x8, waiting for transfers between devices: 28.6 us -> 26.3 us  [scatter_sum(): buf = keep + lax.ppermute(send, axis, xor_pairs(n, bit))]
    concatenate x0 -> x2, other arithmetic: none -> 1.82 us  [the longest x1 1.79 us: per_device(): jnp.concatenate([gather_blocks(right_t[:C // 2], 'row', n, bits[::-1]), g...]
    transpose x1 -> x2, local copies, waits for them, and re-layouts: 2.27 us -> 0.55 us  [gather_blocks(): buf = buf.transpose(order + list(range(k, k + x.ndim)))]
    add x3 -> x6, other arithmetic: 3.29 us -> 1.7 us  [scatter_sum(): buf = keep + lax.ppermute(send, axis, xor_pairs(n, bit))]
  transfers between devices with their start and end apart: 8 -> 16, of which waited for: 5 -> 7; matrix products, arithmetic and copies ran while one was open for 11% -> 21% of each run, Pallas kernels for 7% -> 17%
where the time goes in v6:
time: 89.7 us; the launch traced here: 89.4 us
  waiting for transfers between devices  33.5 us (37%)
  starting transfers between devices  18 us (20%)
  Pallas kernels  15.3 us (17%)
  local copies, waits for them, and re-layouts  14.1 us (16%)
  other arithmetic  7.59 us (8%)
    ppermute x8, waiting for transfers between devices, scatter_sum(): buf = keep + lax.ppermute(send, axis, xor_pairs(n, bit))  26.3 us
    ppermute x8, starting transfers between devices, gather_blocks(): other = lax.ppermute(buf, axis, xor_pairs(n, bit))  9.4 us
    ppermute x8, starting transfers between devices, scatter_sum(): buf = keep + lax.ppermute(send, axis, xor_pairs(n, bit))  8.63 us
    pallas_call x1, Pallas kernels, per_device(): pl.pallas_call(functools.partial(project_kernel, n_seq=n_seq), grid=(step...  8.17 us
    ppermute x8, waiting for transfers between devices, gather_blocks(): other = lax.ppermute(buf, axis, xor_pairs(n, bit))  7.22 us
    pallas_call x1, Pallas kernels, per_device(): pl.pallas_call(left_kernel, grid=(steps,), in_specs=[pl.BlockSpec((C, own...  7.11 us
    another operation x3, local copies, waits for them, and re-layouts  5.13 us
    slice x1, local copies, waits for them, and re-layouts, per_device(): part_t[:, :half]  3.93 us
  transfers between devices with their start and end apart: 16, of which 7 were waited for; matrix products, arithmetic and copies ran while one was open for 21% of the time, Pallas kernels for 17%

profile of v6, /device:TPU:0, one launch (start us, length us, event | category | flops | bytes accessed | tf_op | source)
XLA Modules:
  0.0 89.4 jit_solution(6894691248210559646)
XLA Ops:
  0.6 1.0 %copy.9 = bf16[64,512]{0,1:T(8,128)(2,1)S(1)} copy(bf16[64,512]{1,0:T(8,128)(2,1)} %param.5) | data formatting | bytes 131072 | tf_op args[1]
  1.6 4.1 %collective-permute-start = (bf16[1,16,16,64]{3,1,2,0:T(8,128)(2,1)S(1)}, bf16[1,16,16,64]{3,1,2,0:T(8,128)(2,1)S(1)}, u32[]{:S(2)}, u32[]{:S(2)}) collective-permute-start(bf16[1,16,16,64]{3,1,2,0:T(8,128)(2,1)S(1)} %get-tuple-element.38), channel_id=1, source_target_pairs={{0,8},{1,9},{2,10},{3,11},{4,12},{5,13},{6,14},{7,15},{8,0},{9,1},... | collective-permute-start | bytes 98312 | tf_op jit(solution)/shard_map/ppermute | solution.py:23
  5.7 0.1 collective-permute-start.4
  5.8 1.8 %copy.8 = bf16[32,32,128]{2,0,1:T(8,128)(2,1)} copy(bf16[32,32,128]{2,1,0:T(8,128)(2,1)} %bitcast.83) | data formatting | bytes 524288 | tf_op jit(solution)/shard_map/reshape | solution.py:106
  7.6 8.2 %shard_map.59 = (bf16[32,512,256]{2,1,0:T(8,128)(2,1)}, f32[16,32,16,64]{3,2,1,0:T(8,128)}) custom-call(bf16[16,256,128]{2,1,0:T(8,128)(2,1)} %p_ref.1, bf16[1024,128]{1,0:T(8,128)(2,1)} %bitcast.84, bf16[64,512]{1,0:T(8,128)(2,1)} %l_ref.1), custom_call_target="tpu_custom_call" | custom-call | flops 1610612736 | bytes 11534336 | tf_op jit(solution)/shard_map/pallas_call | solution.py:108
  15.7 0.0 collective-permute-done
  15.7 0.0 collective-permute-done.4
  15.8 1.8 %collective-permute-start.5 = (bf16[2,16,16,64]{3,1,2,0:T(8,128)(2,1)S(1)}, bf16[2,16,16,64]{3,1,2,0:T(8,128)(2,1)S(1)}, u32[]{:S(2)}, u32[]{:S(2)}) collective-permute-start(bf16[2,16,16,64]{3,1,2,0:T(8,128)(2,1)S(1)} %pad_maximum_fusion.8), channel_id=1, source_target_pairs={{0,2},{1,3},{2,0},{3,1},{4,6},{5,7},{6,4},{7,5},{8,10},{9,11},{10,... | collective-permute-start | bytes 196616 | tf_op jit(solution)/shard_map/ppermute | solution.py:23
  17.7 1.6 %collective-permute-start.1 = (bf16[2,16,16,64]{3,1,2,0:T(8,128)(2,1)S(1)}, bf16[2,16,16,64]{3,1,2,0:T(8,128)(2,1)S(1)}, u32[]{:S(2)}, u32[]{:S(2)}) collective-permute-start(bf16[2,16,16,64]{3,1,2,0:T(8,128)(2,1)S(1)} %pad_maximum_fusion.7), channel_id=1, source_target_pairs={{0,4},{1,5},{2,6},{3,7},{4,0},{5,1},{6,2},{7,3},{8,12},{9,13},{10,... | collective-permute-start | bytes 196616 | tf_op jit(solution)/shard_map/ppermute | solution.py:23
  19.3 3.9 %fusion.2 = (f32[16,16,16,64]{3,2,1,0:T(8,128)S(1)}, f32[16,16,16,64]{3,2,1,0:T(8,128)}) fusion(f32[16,32,16,64]{3,2,1,0:T(8,128)} %get-tuple-element.5), kind=kLoop, calls=%fused_computation.55 | loop fusion | bytes 4194304 | tf_op jit(solution)/shard_map/slice | solution.py:136
  23.3 0.0 collective-permute-done.5
  23.3 0.0 collective-permute-done.1
  23.3 0.1 broadcast_select_fusion.9
  23.3 0.0 copy-start.1
  23.4 0.8 pad_maximum_fusion.5
  24.1 0.5 collective-permute-start.2
  24.7 0.0 copy-done.1
  24.7 2.9 %constant_dynamic-slice_fusion.3 = (f32[2,2,2,1,16,16,64]{6,5,4,3,2,1,0:T(8,128)S(1)}, f32[2,2,2,1,16,16,64]{6,5,4,3,2,1,0:T(8,128)S(1)}, f32[2,2,2,1,16,16,64]{...) fusion(f32[2,2,2,2,16,16,64]{6,5,4,3,2,1,0:T(8,128)} %bitcast.75, s32[]{:T(128)S(6)} %select_n.142, s32[]{:T(128)S(6)} %select_n.143, ...), kind=kLoop, calls=%fused_computation.50 | loop fusion | bytes 4194312 | tf_op jit(solution)/shard_map/dynamic-slice.6
  27.6 1.1 %copy.35 = f32[2,2,2,1,16,16,64]{6,5,4,1,0,2,3:T(8,128)} copy(f32[2,2,2,1,16,16,64]{6,5,4,3,2,1,0:T(8,128)S(1)} %get-tuple-element.42) | data formatting | bytes 1048576 | tf_op jit(solution)/shard_map/dynamic-slice.1
  28.7 0.0 collective-permute-start.8
  28.7 1.1 %copy.34 = f32[2,2,2,1,16,16,64]{6,5,4,2,0,1,3:T(8,128)} copy(f32[2,2,2,1,16,16,64]{6,5,4,3,2,1,0:T(8,128)S(1)} %get-tuple-element.15) | data formatting | bytes 1048576 | tf_op jit(solution)/shard_map/dynamic-slice.7
  29.8 0.5 collective-permute-start.12
  30.3 0.1 pad_maximum_fusion.6
  30.4 1.1 %collective-permute-start.6 = (bf16[4,16,16,64]{3,1,2,0:T(8,128)(2,1)S(1)}, bf16[4,16,16,64]{3,1,2,0:T(8,128)(2,1)S(1)}, u32[]{:S(2)}, u32[]{:S(2)}) collective-permute-start(bf16[4,16,16,64]{3,1,2,0:T(8,128)(2,1)S(1)} %pad_maximum_fusion.6), channel_id=1, source_target_pairs={{0,4},{1,5},{2,6},{3,7},{4,0},{5,1},{6,2},{7,3},{8,12},{9,13},{10,... | collective-permute-start | bytes 393224 | tf_op jit(solution)/shard_map/ppermute | solution.py:23
  31.5 0.0 collective-permute-done.2
  31.5 1.0 %broadcast_select_fusion.7 = (bf16[4,16,16,64]{3,1,2,0:T(8,128)(2,1)S(1)}, bf16[4,16,16,64]{3,1,2,0:T(8,128)(2,1)S(1)}) fusion(bf16[4,16,16,64]{3,1,2,0:T(8,128)(2,1)} %collective-permute-done.2, pred[]{:T(512)S(6)} %eq.9, bf16[2,16,16,64]{3,1,2,0:T(8,128)(2,1)S(1)} %get-tuple-element.40, bf16[2,16,16,64]{3,1,2,0:T(8,128)(2,1)S(1)} %copy-done.2), kind=kLoop, calls=%fused_computation.26 | loop fusion | flops 196608 | bytes 524289 | tf_op jit(solution)/shard_map/jit(_where)/select_n | solution.py:25
  32.5 0.1 pad_maximum_fusion.3
  32.6 0.1 collective-permute-start.3
  32.7 6.0 %collective-permute-done.6 = bf16[4,16,16,64]{3,1,2,0:T(8,128)(2,1)S(1)} collective-permute-done((bf16[4,16,16,64]{3,1,2,0:T(8,128)(2,1)S(1)}, bf16[4,16,16,64]{3,1,2,0:T(8,128)(2,1)S(1)}, u32[]{:S(2)}, u32[]{:S(2)}) %collective-permute-start.6) | collective-permute-done | bytes 131104 | tf_op jit(solution)/shard_map/ppermute | solution.py:23
  38.6 0.1 broadcast_select_fusion.5
  38.7 0.1 pad_maximum_fusion.4
  38.8 0.1 collective-permute-start.7
  38.9 0.0 collective-permute-done.3
  38.9 0.1 broadcast_select_fusion.3
  39.1 0.2 pad_maximum_fusion.1
  39.3 0.3 copy.11
  39.6 1.2 %collective-permute-done.7 = bf16[8,16,16,64]{3,1,2,0:T(8,128)(2,1)S(1)} collective-permute-done((bf16[8,16,16,64]{3,1,2,0:T(8,128)(2,1)S(1)}, bf16[8,16,16,64]{3,1,2,0:T(8,128)(2,1)S(1)}, u32[]{:S(2)}, u32[]{:S(2)}) %collective-permute-start.7) | collective-permute-done | bytes 262176 | tf_op jit(solution)/shard_map/ppermute | solution.py:23
  40.8 0.1 broadcast_select_fusion.1
  41.0 0.2 pad_maximum_fusion.2
  41.2 0.3 copy.13
  41.4 1.8 %pad_maximum_fusion.rt_ref = bf16[16,32,16,64]{3,2,1,0:T(8,128)(2,1)} fusion(bf16[16,16,16,64]{3,2,1,0:T(8,128)(2,1)S(1)} %bitcast.79, bf16[16,16,16,64]{3,2,1,0:T(8,128)(2,1)S(1)} %bitcast.78), kind=kLoop, calls=%fused_computation | loop fusion | flops 524288 | bytes 2097152 | tf_op jit(solution)/shard_map/concatenate | solution.py:98
  43.2 7.1 %shard_map.60 = f32[512,64]{1,0:T(8,128)} custom-call(bf16[32,512,256]{2,1,0:T(8,128)(2,1)} %get-tuple-element.4.gm_ref, bf16[16,32,16,64]{3,2,1,0:T(8,128)(2,1)} %pad_maximum_fusion.rt_ref), custom_call_target="tpu_custom_call" | custom-call | flops 536870912 | bytes 9437184 | tf_op jit(solution)/shard_map/pallas_call | solution.py:143
  50.3 1.0 %convert_bitcast_fusion = bf16[64,512]{0,1:T(8,128)(2,1)S(1)} fusion(f32[512,64]{1,0:T(8,128)} %shard_map.60), kind=kLoop, calls=%fused_computation.36 | loop fusion | flops 32768 | bytes 196608 | tf_op jit(solution)/shard_map/convert_element_type | solution.py:159
  51.3 0.7 copy.22
  52.0 0.0 collective-permute-done.8
  52.0 0.0 copy-done
  52.0 0.1 bitcast_add_fusion.1
  52.2 1.6 %collective-permute-start.9 = (f32[2,2,16,16,64]{4,3,2,1,0:T(8,128)S(1)}, f32[2,2,16,16,64]{4,3,2,1,0:T(8,128)S(1)}, u32[]{:S(2)}, u32[]{:S(2)}) collective-permute-start(f32[2,2,16,16,64]{4,3,2,1,0:T(8,128)S(1)} %dynamic-slice_bitcast_fusion.1), channel_id=1, source_target_pairs={{0,2},{1,3},{2,0},{3,1},{4,6},{5,7},{6,4},{7,5},{8,10},{9,11},{10,... | collective-permute-start | bytes 786440 | tf_op jit(solution)/shard_map/ppermute | solution.py:47
  53.8 0.0 collective-permute-done.12
  53.8 1.4 %bitcast_add_fusion = f32[2,2,2,16,16,64]{5,4,3,2,0,1:T(8,128)S(1)} fusion(f32[2,2,2,16,16,64]{5,4,3,2,0,1:T(8,128)} %collective-permute-done.12, f32[2,2,2,1,16,16,64]{6,5,4,3,2,1,0:T(8,128)S(1)} %get-tuple-element.14), kind=kLoop, calls=%fused_computation.3 | loop fusion | flops 131072 | bytes 1572864 | tf_op jit(solution)/shard_map/add | solution.py:47
  55.2 1.1 %collective-permute-start.13 = (f32[2,2,16,16,64]{4,3,2,1,0:T(8,128)S(1)}, f32[2,2,16,16,64]{4,3,2,1,0:T(8,128)S(1)}, u32[]{:S(2)}, u32[]{:S(2)}) collective-permute-start(f32[2,2,16,16,64]{4,3,2,1,0:T(8,128)S(1)} %dynamic-slice_bitcast_fusion), channel_id=1, source_target_pairs={{0,4},{1,5},{2,6},{3,7},{4,0},{5,1},{6,2},{7,3},{8,12},{9,13},{10,... | collective-permute-start | bytes 786440 | tf_op jit(solution)/shard_map/ppermute | solution.py:47
  56.3 9.9 %collective-permute-done.9 = f32[2,2,16,16,64]{4,3,2,1,0:T(8,128)S(1)} collective-permute-done((f32[2,2,16,16,64]{4,3,2,1,0:T(8,128)S(1)}, f32[2,2,16,16,64]{4,3,2,1,0:T(8,128)S(1)}, u32[]{:S(2)}, u32[]{:S(2)}) %collective-permute-start.9) | collective-permute-done | bytes 262176 | tf_op jit(solution)/shard_map/ppermute | solution.py:47
  66.3 0.1 bitcast_add_fusion.3
  66.4 1.1 %collective-permute-start.10 = (f32[2,16,16,64]{3,2,1,0:T(8,128)S(1)}, f32[2,16,16,64]{3,2,1,0:T(8,128)S(1)}, u32[]{:S(2)}, u32[]{:S(2)}) collective-permute-start(f32[2,16,16,64]{3,2,1,0:T(8,128)S(1)} %dynamic-slice_bitcast_fusion.3), channel_id=1, source_target_pairs={{0,4},{1,5},{2,6},{3,7},{4,0},{5,1},{6,2},{7,3},{8,12},{9,13},{10,... | collective-permute-start | bytes 393224 | tf_op jit(solution)/shard_map/ppermute | solution.py:47
  67.5 2.1 %collective-permute-done.13 = f32[2,2,16,16,64]{4,3,2,1,0:T(8,128)S(1)} collective-permute-done((f32[2,2,16,16,64]{4,3,2,1,0:T(8,128)S(1)}, f32[2,2,16,16,64]{4,3,2,1,0:T(8,128)S(1)}, u32[]{:S(2)}, u32[]{:S(2)}) %collective-permute-start.13) | collective-permute-done | bytes 262176 | tf_op jit(solution)/shard_map/ppermute | solution.py:47
  69.6 0.1 bitcast_add_fusion.2
  69.7 0.1 collective-permute-start.14
  69.8 4.8 %collective-permute-done.10 = f32[2,16,16,64]{3,2,1,0:T(8,128)S(1)} collective-permute-done((f32[2,16,16,64]{3,2,1,0:T(8,128)S(1)}, f32[2,16,16,64]{3,2,1,0:T(8,128)S(1)}, u32[]{:S(2)}, u32[]{:S(2)}) %collective-permute-start.10) | collective-permute-done | bytes 131104 | tf_op jit(solution)/shard_map/ppermute | solution.py:47
  74.7 2.7 %collective-permute-start.11 = (f32[16,16,64]{2,0,1:T(8,128)S(1)}, f32[16,16,64]{2,0,1:T(8,128)S(1)}, u32[]{:S(2)}, u32[]{:S(2)}) collective-permute-start(f32[16,16,64]{2,0,1:T(8,128)S(1)} %bitcast.85), channel_id=1, source_target_pairs={{0,8},{1,9},{2,10},{3,11},{4,12},{5,13},{6,14},{7,15},{8,0},{9,1},... | collective-permute-start | bytes 196616 | tf_op jit(solution)/shard_map/ppermute | solution.py:47
  77.4 0.0 collective-permute-done.14
  77.5 1.6 %collective-permute-start.15 = (f32[16,16,64]{2,0,1:T(8,128)S(1)}, f32[16,16,64]{2,0,1:T(8,128)S(1)}, u32[]{:S(2)}, u32[]{:S(2)}) collective-permute-start(f32[16,16,64]{2,0,1:T(8,128)S(1)} %bitcast.86), channel_id=1, source_target_pairs={{0,8},{1,9},{2,10},{3,11},{4,12},{5,13},{6,14},{7,15},{8,0},{9,1},... | collective-permute-start | bytes 196616 | tf_op jit(solution)/shard_map/ppermute | solution.py:47
  79.2 7.2 %collective-permute-done.11 = f32[16,16,64]{2,0,1:T(8,128)S(1)} collective-permute-done((f32[16,16,64]{2,0,1:T(8,128)S(1)}, f32[16,16,64]{2,0,1:T(8,128)S(1)}, u32[]{:S(2)}, u32[]{:S(2)}) %collective-permute-start.11) | collective-permute-done | bytes 65568 | tf_op jit(solution)/shard_map/ppermute | solution.py:47
  86.4 2.1 %collective-permute-done.15 = f32[16,16,64]{2,0,1:T(8,128)S(1)} collective-permute-done((f32[16,16,64]{2,0,1:T(8,128)S(1)}, f32[16,16,64]{2,0,1:T(8,128)S(1)}, u32[]{:S(2)}, u32[]{:S(2)}) %collective-permute-start.15) | collective-permute-done | bytes 65568 | tf_op jit(solution)/shard_map/ppermute | solution.py:47
  88.7 0.7 copy.23
  (20 shorter events, 0.6 us)
Async XLA Ops:
  1.6 14.1 %collective-permute-start = (bf16[1,16,16,64]{3,1,2,0:T(8,128)(2,1)S(1)}, bf16[1,16,16,64]{3,1,2,0:T(8,128)(2,1)S(1)}, u32[]{:S(2)}, u32[]{:S(2)}) collective-permute-start(bf16[1,16,16,64]{3,1,2,0:T(8,128)(2,1)S(1)} %get-tuple-element.38), channel_id=1, source_target_pairs={{0,8},{1,9},{2,10},{3,11},{4,12},{5,13},{6,14},{7,15},{8,0},{9,1},... | collective-permute-start | bytes 98312 | tf_op jit(solution)/shard_map/ppermute | solution.py:23
  5.7 10.0 %collective-permute-start.4 = (bf16[1,16,16,64]{3,1,2,0:T(8,128)(2,1)S(1)}, bf16[1,16,16,64]{3,1,2,0:T(8,128)(2,1)S(1)}, u32[]{:S(2)}, u32[]{:S(2)}) collective-permute-start(bf16[1,16,16,64]{3,1,2,0:T(8,128)(2,1)S(1)} %get-tuple-element.39), channel_id=1, source_target_pairs={{0,8},{1,9},{2,10},{3,11},{4,12},{5,13},{6,14},{7,15},{8,0},{9,1},... | collective-permute-start | bytes 98312 | tf_op jit(solution)/shard_map/ppermute | solution.py:23
  15.8 7.5 %collective-permute-start.5 = (bf16[2,16,16,64]{3,1,2,0:T(8,128)(2,1)S(1)}, bf16[2,16,16,64]{3,1,2,0:T(8,128)(2,1)S(1)}, u32[]{:S(2)}, u32[]{:S(2)}) collective-permute-start(bf16[2,16,16,64]{3,1,2,0:T(8,128)(2,1)S(1)} %pad_maximum_fusion.8), channel_id=1, source_target_pairs={{0,2},{1,3},{2,0},{3,1},{4,6},{5,7},{6,4},{7,5},{8,10},{9,11},{10,... | collective-permute-start | bytes 196616 | tf_op jit(solution)/shard_map/ppermute | solution.py:23
  17.7 5.6 %collective-permute-start.1 = (bf16[2,16,16,64]{3,1,2,0:T(8,128)(2,1)S(1)}, bf16[2,16,16,64]{3,1,2,0:T(8,128)(2,1)S(1)}, u32[]{:S(2)}, u32[]{:S(2)}) collective-permute-start(bf16[2,16,16,64]{3,1,2,0:T(8,128)(2,1)S(1)} %pad_maximum_fusion.7), channel_id=1, source_target_pairs={{0,4},{1,5},{2,6},{3,7},{4,0},{5,1},{6,2},{7,3},{8,12},{9,13},{10,... | collective-permute-start | bytes 196616 | tf_op jit(solution)/shard_map/ppermute | solution.py:23
  23.3 1.3 %copy-start.1 = (bf16[2,16,16,64]{3,1,2,0:T(8,128)(2,1)}, bf16[2,16,16,64]{3,1,2,0:T(8,128)(2,1)S(1)}, u32[]{:S(2)}) copy-start(bf16[2,16,16,64]{3,1,2,0:T(8,128)(2,1)S(1)} %get-tuple-element.41) | copy-start | bytes 196612
  24.1 7.3 %collective-permute-start.2 = (bf16[4,16,16,64]{3,1,2,0:T(8,128)(2,1)}, bf16[4,16,16,64]{3,1,2,0:T(8,128)(2,1)}, u32[]{:S(2)}, u32[]{:S(2)}) collective-permute-start(bf16[4,16,16,64]{3,1,2,0:T(8,128)(2,1)} %pad_maximum_fusion.5), channel_id=1, source_target_pairs={{0,2},{1,3},{2,0},{3,1},{4,6},{5,7},{6,4},{7,5},{8,10},{9,11},{10,... | collective-permute-start | bytes 393224 | tf_op jit(solution)/shard_map/ppermute | solution.py:23
  27.6 3.9 %copy-start.2 = (bf16[2,16,16,64]{3,1,2,0:T(8,128)(2,1)S(1)}, bf16[2,16,16,64]{3,1,2,0:T(8,128)(2,1)}, u32[]{:S(2)}) copy-start(bf16[2,16,16,64]{3,1,2,0:T(8,128)(2,1)} %copy-done.1) | copy-start | bytes 196612
  28.7 23.4 %collective-permute-start.8 = (f32[2,2,2,16,16,64]{5,4,3,1,0,2:T(8,128)}, f32[2,2,2,16,16,64]{5,4,3,1,0,2:T(8,128)S(1)}, u32[]{:S(2)}, u32[]{:S(2)}) collective-permute-start(f32[2,2,2,16,16,64]{5,4,3,1,0,2:T(8,128)} %bitcast.71), channel_id=1, source_target_pairs={{0,1},{1,0},{2,3},{3,2},{4,5},{5,4},{6,7},{7,6},{8,9},{9,8},{10,11... | collective-permute-start | bytes 1572872 | tf_op jit(solution)/shard_map/ppermute | solution.py:47
  29.8 24.0 %collective-permute-start.12 = (f32[2,2,2,16,16,64]{5,4,3,2,0,1:T(8,128)}, f32[2,2,2,16,16,64]{5,4,3,2,0,1:T(8,128)}, u32[]{:S(2)}, u32[]{:S(2)}) collective-permute-start(f32[2,2,2,16,16,64]{5,4,3,2,0,1:T(8,128)} %bitcast.70), channel_id=1, source_target_pairs={{0,1},{1,0},{2,3},{3,2},{4,5},{5,4},{6,7},{7,6},{8,9},{9,8},{10,11... | collective-permute-start | bytes 1572872 | tf_op jit(solution)/shard_map/ppermute | solution.py:47
  30.4 8.3 %collective-permute-start.6 = (bf16[4,16,16,64]{3,1,2,0:T(8,128)(2,1)S(1)}, bf16[4,16,16,64]{3,1,2,0:T(8,128)(2,1)S(1)}, u32[]{:S(2)}, u32[]{:S(2)}) collective-permute-start(bf16[4,16,16,64]{3,1,2,0:T(8,128)(2,1)S(1)} %pad_maximum_fusion.6), channel_id=1, source_target_pairs={{0,4},{1,5},{2,6},{3,7},{4,0},{5,1},{6,2},{7,3},{8,12},{9,13},{10,... | collective-permute-start | bytes 393224 | tf_op jit(solution)/shard_map/ppermute | solution.py:23
  32.6 6.3 %collective-permute-start.3 = (bf16[8,16,16,64]{3,1,2,0:T(8,128)(2,1)S(1)}, bf16[8,16,16,64]{3,1,2,0:T(8,128)(2,1)S(1)}, u32[]{:S(2)}, u32[]{:S(2)}) collective-permute-start(bf16[8,16,16,64]{3,1,2,0:T(8,128)(2,1)S(1)} %pad_maximum_fusion.3), channel_id=1, source_target_pairs={{0,1},{1,0},{2,3},{3,2},{4,5},{5,4},{6,7},{7,6},{8,9},{9,8},{10,11... | collective-permute-start | bytes 786440 | tf_op jit(solution)/shard_map/ppermute | solution.py:23
  38.8 2.0 %collective-permute-start.7 = (bf16[8,16,16,64]{3,1,2,0:T(8,128)(2,1)S(1)}, bf16[8,16,16,64]{3,1,2,0:T(8,128)(2,1)S(1)}, u32[]{:S(2)}, u32[]{:S(2)}) collective-permute-start(bf16[8,16,16,64]{3,1,2,0:T(8,128)(2,1)S(1)} %pad_maximum_fusion.4), channel_id=1, source_target_pairs={{0,1},{1,0},{2,3},{3,2},{4,5},{5,4},{6,7},{7,6},{8,9},{9,8},{10,11... | collective-permute-start | bytes 786440 | tf_op jit(solution)/shard_map/ppermute | solution.py:23
  43.2 8.8 %copy-start = (f32[2,2,2,1,16,16,64]{6,5,4,3,2,1,0:T(8,128)S(1)}, f32[2,2,2,1,16,16,64]{6,5,4,3,2,1,0:T(8,128)}, u32[]{:S(2)}) copy-start(f32[2,2,2,1,16,16,64]{6,5,4,3,2,1,0:T(8,128)} %get-tuple-element.43) | copy-start | bytes 1572868
  52.2 14.0 %collective-permute-start.9 = (f32[2,2,16,16,64]{4,3,2,1,0:T(8,128)S(1)}, f32[2,2,16,16,64]{4,3,2,1,0:T(8,128)S(1)}, u32[]{:S(2)}, u32[]{:S(2)}) collective-permute-start(f32[2,2,16,16,64]{4,3,2,1,0:T(8,128)S(1)} %dynamic-slice_bitcast_fusion.1), channel_id=1, source_target_pairs={{0,2},{1,3},{2,0},{3,1},{4,6},{5,7},{6,4},{7,5},{8,10},{9,11},{10,... | collective-permute-start | bytes 786440 | tf_op jit(solution)/shard_map/ppermute | solution.py:47
  55.2 14.3 %collective-permute-start.13 = (f32[2,2,16,16,64]{4,3,2,1,0:T(8,128)S(1)}, f32[2,2,16,16,64]{4,3,2,1,0:T(8,128)S(1)}, u32[]{:S(2)}, u32[]{:S(2)}) collective-permute-start(f32[2,2,16,16,64]{4,3,2,1,0:T(8,128)S(1)} %dynamic-slice_bitcast_fusion), channel_id=1, source_target_pairs={{0,4},{1,5},{2,6},{3,7},{4,0},{5,1},{6,2},{7,3},{8,12},{9,13},{10,... | collective-permute-start | bytes 786440 | tf_op jit(solution)/shard_map/ppermute | solution.py:47
  66.4 8.2 %collective-permute-start.10 = (f32[2,16,16,64]{3,2,1,0:T(8,128)S(1)}, f32[2,16,16,64]{3,2,1,0:T(8,128)S(1)}, u32[]{:S(2)}, u32[]{:S(2)}) collective-permute-start(f32[2,16,16,64]{3,2,1,0:T(8,128)S(1)} %dynamic-slice_bitcast_fusion.3), channel_id=1, source_target_pairs={{0,4},{1,5},{2,6},{3,7},{4,0},{5,1},{6,2},{7,3},{8,12},{9,13},{10,... | collective-permute-start | bytes 393224 | tf_op jit(solution)/shard_map/ppermute | solution.py:47
  69.7 7.7 %collective-permute-start.14 = (f32[2,16,16,64]{3,2,1,0:T(8,128)S(1)}, f32[2,16,16,64]{3,2,1,0:T(8,128)S(1)}, u32[]{:S(2)}, u32[]{:S(2)}) collective-permute-start(f32[2,16,16,64]{3,2,1,0:T(8,128)S(1)} %dynamic-slice_bitcast_fusion.2), channel_id=1, source_target_pairs={{0,2},{1,3},{2,0},{3,1},{4,6},{5,7},{6,4},{7,5},{8,10},{9,11},{10,... | collective-permute-start | bytes 393224 | tf_op jit(solution)/shard_map/ppermute | solution.py:47
  74.7 11.6 %collective-permute-start.11 = (f32[16,16,64]{2,0,1:T(8,128)S(1)}, f32[16,16,64]{2,0,1:T(8,128)S(1)}, u32[]{:S(2)}, u32[]{:S(2)}) collective-permute-start(f32[16,16,64]{2,0,1:T(8,128)S(1)} %bitcast.85), channel_id=1, source_target_pairs={{0,8},{1,9},{2,10},{3,11},{4,12},{5,13},{6,14},{7,15},{8,0},{9,1},... | collective-permute-start | bytes 196616 | tf_op jit(solution)/shard_map/ppermute | solution.py:47
  77.5 11.1 %collective-permute-start.15 = (f32[16,16,64]{2,0,1:T(8,128)S(1)}, f32[16,16,64]{2,0,1:T(8,128)S(1)}, u32[]{:S(2)}, u32[]{:S(2)}) collective-permute-start(f32[16,16,64]{2,0,1:T(8,128)S(1)} %bitcast.86), channel_id=1, source_target_pairs={{0,8},{1,9},{2,10},{3,11},{4,12},{5,13},{6,14},{7,15},{8,0},{9,1},... | collective-permute-start | bytes 196616 | tf_op jit(solution)/shard_map/ppermute | solution.py:47

commit v7 on v6

--- a/solution.py
+++ b/solution.py
@@ -129,12 +129,13 @@
         ),
     )(pair_cot, weight_ec, left_proj)
 
-    half = C // 2
+    pieces = 4
+    size = C // pieces
     swapped = bits[:1] + bits[1:3][::-1] + bits[3:]
     summed = jnp.concatenate(
         [
-            scatter_sum(part_t[:, :half], "row", n, bits),
-            scatter_sum(part_t[:, half:], "row", n, swapped),
+            scatter_sum(part_t[:, q * size:(q + 1) * size], "row", n, swapped if q % 2 else bits)
+            for q in range(pieces)
         ],
         0,
     )

time: 89.7 us -> 98.8 us (1.10)
  other arithmetic: 7.59 us -> 15.1 us
  starting transfers between devices: 18 us -> 24 us
  waiting for transfers between devices: 33.5 us -> 27.6 us
  local copies, waits for them, and re-layouts: 14.1 us -> 15.1 us
    ppermute x8 -> x16, waiting for transfers between devices: 26.3 us -> 17.1 us  [scatter_sum(): buf = keep + lax.ppermute(send, axis, xor_pairs(n, bit))]
    ppermute x8 -> x16, starting transfers between devices: 8.63 us -> 14.8 us  [scatter_sum(): buf = keep + lax.ppermute(send, axis, xor_pairs(n, bit))]
    ppermute x8, waiting for transfers between devices: 7.22 us -> 10.6 us  [gather_blocks(): other = lax.ppermute(buf, axis, xor_pairs(n, bit))]
    select_n x6, other arithmetic: 1.48 us -> 4.53 us  [gather_blocks(): low = jnp.where(mine == 0, buf, other)]
    add x6 -> x12, other arithmetic: 1.7 us -> 4.65 us  [scatter_sum(): buf = keep + lax.ppermute(send, axis, xor_pairs(n, bit))]
    concatenate x8, other arithmetic: 1.53 us -> 3.1 us  [gather_blocks(): buf = jnp.concatenate([low, high], 0)]
    another operation x3 -> x6, local copies, waits for them, and re-layouts: 5.13 us -> 5.82 us
    unnamed x9 -> x29, local copies, waits for them, and re-layouts: 2.42 us -> 3.1 us
  transfers between devices with their start and end apart: 16 -> 24, of which waited for: 7 -> 10; matrix products, arithmetic and copies ran while one was open for 21% -> 24% of each run, Pallas kernels for 17% -> 8%
where the time goes in v7:
time: 98.8 us; the launch traced here: 98.1 us
  waiting for transfers between devices  27.6 us (28%)
  starting transfers between devices  24 us (24%)
  Pallas kernels  15.2 us (15%)
  local copies, waits for them, and re-layouts  15.1 us (15%)
  other arithmetic  15.1 us (15%)
  between operations  1.08 us (1%)
    ppermute x16, waiting for transfers between devices, scatter_sum(): buf = keep + lax.ppermute(send, axis, xor_pairs(n, bit))  17.1 us
    ppermute x16, starting transfers between devices, scatter_sum(): buf = keep + lax.ppermute(send, axis, xor_pairs(n, bit))  14.8 us
    ppermute x8, waiting for transfers between devices, gather_blocks(): other = lax.ppermute(buf, axis, xor_pairs(n, bit))  10.6 us
    ppermute x8, starting transfers between devices, gather_blocks(): other = lax.ppermute(buf, axis, xor_pairs(n, bit))  9.13 us
    pallas_call x1, Pallas kernels, per_device(): pl.pallas_call(functools.partial(project_kernel, n_seq=n_seq), grid=(step...  8.23 us
    pallas_call x1, Pallas kernels, per_device(): pl.pallas_call(left_kernel, grid=(steps,), in_specs=[pl.BlockSpec((C, own...  7 us
    another operation x6, local copies, waits for them, and re-layouts  5.82 us
    add x12, other arithmetic, scatter_sum(): buf = keep + lax.ppermute(send, axis, xor_pairs(n, bit))  4.65 us
  transfers between devices with their start and end apart: 24, of which 10 were waited for; matrix products, arithmetic and copies ran while one was open for 24% of the time, Pallas kernels for 8%

profile of v7, /device:TPU:0, one launch (start us, length us, event | category | flops | bytes accessed | tf_op | source)
XLA Modules:
  0.0 98.1 jit_solution(9624559671266109817)
XLA Ops:
  0.6 1.0 copy.9
  1.6 4.1 %collective-permute-start = (bf16[1,16,16,64]{3,1,2,0:T(8,128)(2,1)S(1)}, bf16[1,16,16,64]{3,1,2,0:T(8,128)(2,1)S(1)}, u32[]{:S(2)}, u32[]{:S(2)}) collective-permute-start(bf16[1,16,16,64]{3,1,2,0:T(8,128)(2,1)S(1)} %get-tuple-element.48), channel_id=1, source_target_pairs={{0,8},{1,9},{2,10},{3,11},{4,12},{5,13},{6,14},{7,15},{8,0},{9,1},... | collective-permute-start | bytes 98312 | tf_op jit(solution)/shard_map/ppermute | solution.py:23
  5.7 0.1 collective-permute-start.4
  5.8 1.8 %copy.8 = bf16[32,32,128]{2,0,1:T(8,128)(2,1)} copy(bf16[32,32,128]{2,1,0:T(8,128)(2,1)} %bitcast.127) | data formatting | bytes 524288 | tf_op jit(solution)/shard_map/reshape | solution.py:106
  7.6 8.2 %shard_map.59 = (bf16[32,512,256]{2,1,0:T(8,128)(2,1)}, f32[16,32,16,64]{3,2,1,0:T(8,128)}) custom-call(bf16[16,256,128]{2,1,0:T(8,128)(2,1)} %p_ref.1, bf16[1024,128]{1,0:T(8,128)(2,1)} %bitcast.128, bf16[64,512]{1,0:T(8,128)(2,1)} %l_ref.1), custom_call_target="tpu_custom_call" | custom-call | flops 1610612736 | bytes 11534336 | tf_op jit(solution)/shard_map/pallas_call | solution.py:108
  15.8 3.5 %fusion.4 = (f32[16,8,16,64]{3,2,1,0:T(8,128)S(1)}, f32[16,8,16,64]{3,2,1,0:T(8,128)S(1)}, f32[16,8,16,64]{3,2,1,0:T(8,128)S(1)}, f32[16,8,16,64]{3,2,1,0:T(8,128)}) fusion(f32[16,32,16,64]{3,2,1,0:T(8,128)} %get-tuple-element.5), kind=kLoop, calls=%fused_computation.81 | loop fusion | bytes 4194304 | tf_op jit(solution)/shard_map/slice | solution.py:137
  19.4 1.8 %collective-permute-start.5 = (bf16[2,16,16,64]{3,1,2,0:T(8,128)(2,1)S(1)}, bf16[2,16,16,64]{3,1,2,0:T(8,128)(2,1)S(1)}, u32[]{:S(2)}, u32[]{:S(2)}) collective-permute-start(bf16[2,16,16,64]{3,1,2,0:T(8,128)(2,1)S(1)} %pad_maximum_fusion.8), channel_id=1, source_target_pairs={{0,2},{1,3},{2,0},{3,1},{4,6},{5,7},{6,4},{7,5},{8,10},{9,11},{10,... | collective-permute-start | bytes 196616 | tf_op jit(solution)/shard_map/ppermute | solution.py:23
  21.3 1.6 %collective-permute-start.1 = (bf16[2,16,16,64]{3,1,2,0:T(8,128)(2,1)S(1)}, bf16[2,16,16,64]{3,1,2,0:T(8,128)(2,1)}, u32[]{:S(2)}, u32[]{:S(2)}) collective-permute-start(bf16[2,16,16,64]{3,1,2,0:T(8,128)(2,1)S(1)} %pad_maximum_fusion.7), channel_id=1, source_target_pairs={{0,4},{1,5},{2,6},{3,7},{4,0},{5,1},{6,2},{7,3},{8,12},{9,13},{10,... | collective-permute-start | bytes 196616 | tf_op jit(solution)/shard_map/ppermute | solution.py:23
  23.0 2.3 %constant_dynamic-slice_fusion.11 = (f32[2,2,2,1,8,16,64]{6,5,4,3,2,1,0:T(8,128)}, f32[2,2,2,1,8,16,64]{6,5,4,3,2,1,0:T(8,128)S(1)}, f32[2,2,2,1,8,16,64]{6,5,4,3,2,1,0:T(8,128)S(1)}, f32[2,2,2,1,8,16,64]{6,5,4,3,2,1,0:T(8,128)}) fusion(f32[2,2,2,2,8,16,64]{6,5,4,3,2,1,0:T(8,128)} %bitcast.123, s32[]{:T(128)S(6)} %select_n.158, s32[]{:T(128)S(6)} %select_n.159, ...), kind=kLoop, calls=%fused_computation.76 | loop fusion | bytes 2097160 | tf_op jit(solution)/shard_map/dynamic-slice.6
  25.3 0.8 copy.53
  26.1 0.8 copy.52
  27.0 0.5 collective-permute-start.12
  27.5 0.6 copy-done.12
  28.1 1.0 %broadcast_select_fusion.9 = (bf16[2,16,16,64]{3,1,2,0:T(8,128)(2,1)S(1)}, bf16[2,16,16,64]{3,1,2,0:T(8,128)(2,1)S(1)}, bf16[2,16,16,64]{3,1,2,0:T(8,128)(2,1)S(1)}, bf16[2,16,16,64]{3,1,2,0:T(8,128)(2,1)S(1)}) fusion(bf16[2,16,16,64]{3,1,2,0:T(8,128)(2,1)} %copy-done.12, pred[]{:T(512)S(6)} %eq.9, bf16[1,16,16,64]{3,1,2,0:T(8,128)(2,1)S(1)} %copy-done.9, ...), kind=kLoop, calls=%fused_computation.44 | loop fusion | flops 196608 | bytes 524290 | tf_op jit(solution)/shard_map/jit(_where)/select_n | solution.py:25
  29.2 0.8 pad_maximum_fusion.5
  30.0 0.5 collective-permute-start.2
  30.5 0.2 constant_dynamic-slice_fusion.3
  30.7 0.8 copy.51
  31.5 0.8 copy.50
  32.3 0.5 collective-permute-start.20
  32.9 0.1 pad_maximum_fusion.6
  32.9 5.6 %collective-permute-done.2 = bf16[4,16,16,64]{3,1,2,0:T(8,128)(2,1)} collective-permute-done((bf16[4,16,16,64]{3,1,2,0:T(8,128)(2,1)}, bf16[4,16,16,64]{3,1,2,0:T(8,128)(2,1)}, u32[]{:S(2)}, u32[]{:S(2)}) %collective-permute-start.2) | collective-permute-done | bytes 131104 | tf_op jit(solution)/shard_map/ppermute | solution.py:23
  38.5 0.4 collective-permute-start.6
  39.0 1.0 %broadcast_select_fusion.7 = (bf16[4,16,16,64]{3,1,2,0:T(8,128)(2,1)S(1)}, bf16[4,16,16,64]{3,1,2,0:T(8,128)(2,1)S(1)}) fusion(bf16[4,16,16,64]{3,1,2,0:T(8,128)(2,1)} %collective-permute-done.2, pred[]{:T(512)S(6)} %eq.9, bf16[2,16,16,64]{3,1,2,0:T(8,128)(2,1)S(1)} %get-tuple-element.50, bf16[2,16,16,64]{3,1,2,0:T(8,128)(2,1)S(1)} %copy-done.3), kind=kLoop, calls=%fused_computation.30 | loop fusion | flops 196608 | bytes 524289 | tf_op jit(solution)/shard_map/jit(_where)/select_n | solution.py:25
  40.0 0.9 pad_maximum_fusion.3
  40.9 5.0 %collective-permute-done.6 = bf16[4,16,16,64]{3,1,2,0:T(8,128)(2,1)S(1)} collective-permute-done((bf16[4,16,16,64]{3,1,2,0:T(8,128)(2,1)S(1)}, bf16[4,16,16,64]{3,1,2,0:T(8,128)(2,1)S(1)}, u32[]{:S(2)}, u32[]{:S(2)}) %collective-permute-start.6) | collective-permute-done | bytes 131104 | tf_op jit(solution)/shard_map/ppermute | solution.py:23
  45.9 0.1 broadcast_select_fusion.5
  45.9 0.9 pad_maximum_fusion.4
  46.9 0.5 collective-permute-start.7
  47.4 1.1 %bitcast_add_fusion.3 = f32[2,2,2,8,16,64]{5,4,3,1,0,2:T(8,128)S(1)} fusion(f32[2,2,2,8,16,64]{5,4,3,1,0,2:T(8,128)} %collective-permute-done.8, f32[2,2,2,1,8,16,64]{6,5,4,3,2,1,0:T(8,128)S(1)} %copy-done.1), kind=kLoop, calls=%fused_computation.8 | loop fusion | flops 65536 | bytes 786432 | tf_op jit(solution)/shard_map/add | solution.py:47
  48.5 0.6 collective-permute-start.9
  49.1 1.1 %bitcast_add_fusion.2 = f32[2,2,2,8,16,64]{5,4,3,2,0,1:T(8,128)S(1)} fusion(f32[2,2,2,8,16,64]{5,4,3,2,0,1:T(8,128)} %collective-permute-done.12, f32[2,2,2,1,8,16,64]{6,5,4,3,2,1,0:T(8,128)S(1)} %copy-done), kind=kLoop, calls=%fused_computation.7 | loop fusion | flops 65536 | bytes 786432 | tf_op jit(solution)/shard_map/add | solution.py:47
  50.3 0.3 collective-permute-start.13
  50.6 1.1 %bitcast_add_fusion.1 = f32[2,2,2,8,16,64]{5,4,3,1,0,2:T(8,128)S(1)} fusion(f32[2,2,2,8,16,64]{5,4,3,1,0,2:T(8,128)} %collective-permute-done.16, f32[2,2,2,1,8,16,64]{6,5,4,3,2,1,0:T(8,128)S(1)} %get-tuple-element.53), kind=kLoop, calls=%fused_computation.6 | loop fusion | flops 65536 | bytes 786432 | tf_op jit(solution)/shard_map/add | solution.py:47
  51.8 1.8 %collective-permute-start.17 = (f32[2,2,8,16,64]{4,3,2,1,0:T(8,128)S(1)}, f32[2,2,8,16,64]{4,3,2,1,0:T(8,128)S(1)}, u32[]{:S(2)}, u32[]{:S(2)}) collective-permute-start(f32[2,2,8,16,64]{4,3,2,1,0:T(8,128)S(1)} %dynamic-slice_bitcast_fusion.1), channel_id=1, source_target_pairs={{0,2},{1,3},{2,0},{3,1},{4,6},{5,7},{6,4},{7,5},{8,10},{9,11},{10,... | collective-permute-start | bytes 393224 | tf_op jit(solution)/shard_map/ppermute | solution.py:47
  53.5 1.1 %bitcast_add_fusion = f32[2,2,2,8,16,64]{5,4,3,2,0,1:T(8,128)S(1)} fusion(f32[2,2,2,8,16,64]{5,4,3,2,0,1:T(8,128)} %collective-permute-done.20, f32[2,2,2,1,8,16,64]{6,5,4,3,2,1,0:T(8,128)S(1)} %get-tuple-element.20), kind=kLoop, calls=%fused_computation.5 | loop fusion | flops 65536 | bytes 786432 | tf_op jit(solution)/shard_map/add | solution.py:47
  54.7 3.1 %collective-permute-done.9 = f32[2,2,8,16,64]{4,3,2,1,0:T(8,128)S(1)} collective-permute-done((f32[2,2,8,16,64]{4,3,2,1,0:T(8,128)S(1)}, f32[2,2,8,16,64]{4,3,2,1,0:T(8,128)S(1)}, u32[]{:S(2)}, u32[]{:S(2)}) %collective-permute-start.9) | collective-permute-done | bytes 131104 | tf_op jit(solution)/shard_map/ppermute | solution.py:47
  57.8 0.4 collective-permute-start.21
  58.3 1.6 %collective-permute-start.10 = (f32[2,8,16,64]{3,2,1,0:T(8,128)S(1)}, f32[2,8,16,64]{3,2,1,0:T(8,128)S(1)}, u32[]{:S(2)}, u32[]{:S(2)}) collective-permute-start(f32[2,8,16,64]{3,2,1,0:T(8,128)S(1)} %dynamic-slice_bitcast_fusion.7), channel_id=1, source_target_pairs={{0,4},{1,5},{2,6},{3,7},{4,0},{5,1},{6,2},{7,3},{8,12},{9,13},{10,... | collective-permute-start | bytes 196616 | tf_op jit(solution)/shard_map/ppermute | solution.py:47
  60.0 2.4 %collective-permute-done.17 = f32[2,2,8,16,64]{4,3,2,1,0:T(8,128)S(1)} collective-permute-done((f32[2,2,8,16,64]{4,3,2,1,0:T(8,128)S(1)}, f32[2,2,8,16,64]{4,3,2,1,0:T(8,128)S(1)}, u32[]{:S(2)}, u32[]{:S(2)}) %collective-permute-start.17) | collective-permute-done | bytes 131104 | tf_op jit(solution)/shard_map/ppermute | solution.py:47
  62.4 0.5 collective-permute-start.14
  63.0 3.6 %collective-permute-done.21 = f32[2,2,8,16,64]{4,3,2,1,0:T(8,128)S(1)} collective-permute-done((f32[2,2,8,16,64]{4,3,2,1,0:T(8,128)S(1)}, f32[2,2,8,16,64]{4,3,2,1,0:T(8,128)S(1)}, u32[]{:S(2)}, u32[]{:S(2)}) %collective-permute-start.21) | collective-permute-done | bytes 131104 | tf_op jit(solution)/shard_map/ppermute | solution.py:47
  66.5 0.6 collective-permute-start.18
  67.2 1.2 %collective-permute-done.10 = f32[2,8,16,64]{3,2,1,0:T(8,128)S(1)} collective-permute-done((f32[2,8,16,64]{3,2,1,0:T(8,128)S(1)}, f32[2,8,16,64]{3,2,1,0:T(8,128)S(1)}, u32[]{:S(2)}, u32[]{:S(2)}) %collective-permute-start.10) | collective-permute-done | bytes 65568 | tf_op jit(solution)/shard_map/ppermute | solution.py:47
  68.4 1.2 %collective-permute-start.22 = (f32[2,8,16,64]{3,2,1,0:T(8,128)S(1)}, f32[2,8,16,64]{3,2,1,0:T(8,128)S(1)}, u32[]{:S(2)}, u32[]{:S(2)}) collective-permute-start(f32[2,8,16,64]{3,2,1,0:T(8,128)S(1)} %dynamic-slice_bitcast_fusion.4), channel_id=1, source_target_pairs={{0,2},{1,3},{2,0},{3,1},{4,6},{5,7},{6,4},{7,5},{8,10},{9,11},{10,... | collective-permute-start | bytes 196616 | tf_op jit(solution)/shard_map/ppermute | solution.py:47
  69.7 3.4 %collective-permute-start.11 = (f32[8,16,64]{2,0,1:T(8,128)S(1)}, f32[8,16,64]{2,0,1:T(8,128)S(1)}, u32[]{:S(2)}, u32[]{:S(2)}) collective-permute-start(f32[8,16,64]{2,0,1:T(8,128)S(1)} %bitcast.129), channel_id=1, source_target_pairs={{0,8},{1,9},{2,10},{3,11},{4,12},{5,13},{6,14},{7,15},{8,0},{9,1},... | collective-permute-start | bytes 98312 | tf_op jit(solution)/shard_map/ppermute | solution.py:47
  73.1 2.2 %collective-permute-start.15 = (f32[8,16,64]{2,0,1:T(8,128)S(1)}, f32[8,16,64]{2,0,1:T(8,128)S(1)}, u32[]{:S(2)}, u32[]{:S(2)}) collective-permute-start(f32[8,16,64]{2,0,1:T(8,128)S(1)} %bitcast.130), channel_id=1, source_target_pairs={{0,8},{1,9},{2,10},{3,11},{4,12},{5,13},{6,14},{7,15},{8,0},{9,1},... | collective-permute-start | bytes 98312 | tf_op jit(solution)/shard_map/ppermute | solution.py:47
  75.4 1.0 collective-permute-start.19
  76.5 1.9 %collective-permute-done.11 = f32[8,16,64]{2,0,1:T(8,128)S(1)} collective-permute-done((f32[8,16,64]{2,0,1:T(8,128)S(1)}, f32[8,16,64]{2,0,1:T(8,128)S(1)}, u32[]{:S(2)}, u32[]{:S(2)}) %collective-permute-start.11) | collective-permute-done | bytes 32800 | tf_op jit(solution)/shard_map/ppermute | solution.py:47
  78.4 0.2 collective-permute-start.23
  78.6 0.6 collective-permute-done.15
  79.2 2.7 %collective-permute-done.19 = f32[8,16,64]{2,0,1:T(8,128)S(1)} collective-permute-done((f32[8,16,64]{2,0,1:T(8,128)S(1)}, f32[8,16,64]{2,0,1:T(8,128)S(1)}, u32[]{:S(2)}, u32[]{:S(2)}) %collective-permute-start.19) | collective-permute-done | bytes 32800 | tf_op jit(solution)/shard_map/ppermute | solution.py:47
  82.0 1.6 %collective-permute-done.23 = f32[8,16,64]{2,0,1:T(8,128)S(1)} collective-permute-done((f32[8,16,64]{2,0,1:T(8,128)S(1)}, f32[8,16,64]{2,0,1:T(8,128)S(1)}, u32[]{:S(2)}, u32[]{:S(2)}) %collective-permute-start.23) | collective-permute-done | bytes 32800 | tf_op jit(solution)/shard_map/ppermute | solution.py:47
  83.6 0.7 copy.31
  84.3 1.2 %broadcast_select_fusion.3 = (bf16[8,16,16,64]{3,1,2,0:T(8,128)(2,1)S(1)}, bf16[8,16,16,64]{3,1,2,0:T(8,128)(2,1)S(1)}) fusion(bf16[8,16,16,64]{3,1,2,0:T(8,128)(2,1)} %collective-permute-done.3, pred[]{:T(512)S(6)} %eq.8, bf16[4,16,16,64]{3,1,2,0:T(8,128)(2,1)S(1)} %get-tuple-element.27, bf16[4,16,16,64]{3,1,2,0:T(8,128)(2,1)S(1)} %get-tuple-element.26), kind=kLoop, calls=%fused_computation.16 | loop fusion | flops 393216 | bytes 1048577 | tf_op jit(solution)/shard_map/jit(_where)/select_n | solution.py:25
  85.5 0.2 pad_maximum_fusion.1
  85.7 0.3 copy.11
  86.0 1.2 %broadcast_select_fusion.1 = (bf16[8,16,16,64]{3,1,2,0:T(8,128)(2,1)S(1)}, bf16[8,16,16,64]{3,1,2,0:T(8,128)(2,1)S(1)}) fusion(bf16[8,16,16,64]{3,1,2,0:T(8,128)(2,1)} %collective-permute-done.7, pred[]{:T(512)S(6)} %eq.8, bf16[4,16,16,64]{3,1,2,0:T(8,128)(2,1)S(1)} %get-tuple-element.29, bf16[4,16,16,64]{3,1,2,0:T(8,128)(2,1)S(1)} %get-tuple-element.28), kind=kLoop, calls=%fused_computation.14 | loop fusion | flops 393216 | bytes 1048577 | tf_op jit(solution)/shard_map/jit(_where)/select_n | solution.py:25
  87.2 0.2 pad_maximum_fusion.2
  87.4 0.3 copy.13
  87.7 1.7 %pad_maximum_fusion.rt_ref = bf16[16,32,16,64]{3,2,1,0:T(8,128)(2,1)} fusion(bf16[16,16,16,64]{3,2,1,0:T(8,128)(2,1)S(1)} %bitcast.119, bf16[16,16,16,64]{3,2,1,0:T(8,128)(2,1)S(1)} %bitcast.118), kind=kLoop, calls=%fused_computation | loop fusion | flops 524288 | bytes 2097152 | tf_op jit(solution)/shard_map/concatenate | solution.py:98
  89.4 7.0 %shard_map.60 = f32[512,64]{1,0:T(8,128)} custom-call(bf16[32,512,256]{2,1,0:T(8,128)(2,1)} %get-tuple-element.4.gm_ref, bf16[16,32,16,64]{3,2,1,0:T(8,128)(2,1)} %pad_maximum_fusion.rt_ref), custom_call_target="tpu_custom_call" | custom-call | flops 536870912 | bytes 9437184 | tf_op jit(solution)/shard_map/pallas_call | solution.py:144
  96.4 1.0 convert_bitcast_fusion
  97.4 0.7 copy.30
  (75 shorter events, 0.9 us)
Async XLA Ops:
  1.6 17.7 %collective-permute-start = (bf16[1,16,16,64]{3,1,2,0:T(8,128)(2,1)S(1)}, bf16[1,16,16,64]{3,1,2,0:T(8,128)(2,1)S(1)}, u32[]{:S(2)}, u32[]{:S(2)}) collective-permute-start(bf16[1,16,16,64]{3,1,2,0:T(8,128)(2,1)S(1)} %get-tuple-element.48), channel_id=1, source_target_pairs={{0,8},{1,9},{2,10},{3,11},{4,12},{5,13},{6,14},{7,15},{8,0},{9,1},... | collective-permute-start | bytes 98312 | tf_op jit(solution)/shard_map/ppermute | solution.py:23
  5.7 13.6 %collective-permute-start.4 = (bf16[1,16,16,64]{3,1,2,0:T(8,128)(2,1)S(1)}, bf16[1,16,16,64]{3,1,2,0:T(8,128)(2,1)S(1)}, u32[]{:S(2)}, u32[]{:S(2)}) collective-permute-start(bf16[1,16,16,64]{3,1,2,0:T(8,128)(2,1)S(1)} %get-tuple-element.49), channel_id=1, source_target_pairs={{0,8},{1,9},{2,10},{3,11},{4,12},{5,13},{6,14},{7,15},{8,0},{9,1},... | collective-permute-start | bytes 98312 | tf_op jit(solution)/shard_map/ppermute | solution.py:23
  19.4 3.6 %copy-start.4 = (bf16[1,16,16,64]{3,1,2,0:T(8,128)(2,1)}, bf16[1,16,16,64]{3,1,2,0:T(8,128)(2,1)S(1)}, u32[]{:S(2)}) copy-start(bf16[1,16,16,64]{3,1,2,0:T(8,128)(2,1)S(1)} %get-tuple-element.34) | copy-start | bytes 98308
  19.4 3.6 %copy-start.6 = (bf16[1,16,16,64]{3,1,2,0:T(8,128)(2,1)}, bf16[1,16,16,64]{3,1,2,0:T(8,128)(2,1)S(1)}, u32[]{:S(2)}) copy-start(bf16[1,16,16,64]{3,1,2,0:T(8,128)(2,1)S(1)} %get-tuple-element.35) | copy-start | bytes 98308
  19.4 3.6 %copy-start.8 = (bf16[1,16,16,64]{3,1,2,0:T(8,128)(2,1)}, bf16[1,16,16,64]{3,1,2,0:T(8,128)(2,1)S(1)}, u32[]{:S(2)}) copy-start(bf16[1,16,16,64]{3,1,2,0:T(8,128)(2,1)S(1)} %get-tuple-element.46) | copy-start | bytes 98308
  19.4 3.6 %copy-start.10 = (bf16[1,16,16,64]{3,1,2,0:T(8,128)(2,1)}, bf16[1,16,16,64]{3,1,2,0:T(8,128)(2,1)S(1)}, u32[]{:S(2)}) copy-start(bf16[1,16,16,64]{3,1,2,0:T(8,128)(2,1)S(1)} %get-tuple-element.47) | copy-start | bytes 98308
  19.4 8.0 %collective-permute-start.5 = (bf16[2,16,16,64]{3,1,2,0:T(8,128)(2,1)S(1)}, bf16[2,16,16,64]{3,1,2,0:T(8,128)(2,1)S(1)}, u32[]{:S(2)}, u32[]{:S(2)}) collective-permute-start(bf16[2,16,16,64]{3,1,2,0:T(8,128)(2,1)S(1)} %pad_maximum_fusion.8), channel_id=1, source_target_pairs={{0,2},{1,3},{2,0},{3,1},{4,6},{5,7},{6,4},{7,5},{8,10},{9,11},{10,... | collective-permute-start | bytes 196616 | tf_op jit(solution)/shard_map/ppermute | solution.py:23
  21.3 6.8 %collective-permute-start.1 = (bf16[2,16,16,64]{3,1,2,0:T(8,128)(2,1)S(1)}, bf16[2,16,16,64]{3,1,2,0:T(8,128)(2,1)}, u32[]{:S(2)}, u32[]{:S(2)}) collective-permute-start(bf16[2,16,16,64]{3,1,2,0:T(8,128)(2,1)S(1)} %pad_maximum_fusion.7), channel_id=1, source_target_pairs={{0,4},{1,5},{2,6},{3,7},{4,0},{5,1},{6,2},{7,3},{8,12},{9,13},{10,... | collective-permute-start | bytes 196616 | tf_op jit(solution)/shard_map/ppermute | solution.py:23
  25.3 2.8 %copy-start.5 = (bf16[1,16,16,64]{3,1,2,0:T(8,128)(2,1)S(1)}, bf16[1,16,16,64]{3,1,2,0:T(8,128)(2,1)}, u32[]{:S(2)}) copy-start(bf16[1,16,16,64]{3,1,2,0:T(8,128)(2,1)} %copy-done.4) | copy-start | bytes 98308
  25.3 2.8 %copy-start.7 = (bf16[1,16,16,64]{3,1,2,0:T(8,128)(2,1)S(1)}, bf16[1,16,16,64]{3,1,2,0:T(8,128)(2,1)}, u32[]{:S(2)}) copy-start(bf16[1,16,16,64]{3,1,2,0:T(8,128)(2,1)} %copy-done.6) | copy-start | bytes 98308
  25.3 2.8 %copy-start.9 = (bf16[1,16,16,64]{3,1,2,0:T(8,128)(2,1)S(1)}, bf16[1,16,16,64]{3,1,2,0:T(8,128)(2,1)}, u32[]{:S(2)}) copy-start(bf16[1,16,16,64]{3,1,2,0:T(8,128)(2,1)} %copy-done.8) | copy-start | bytes 98308
  25.3 2.8 %copy-start.11 = (bf16[1,16,16,64]{3,1,2,0:T(8,128)(2,1)S(1)}, bf16[1,16,16,64]{3,1,2,0:T(8,128)(2,1)}, u32[]{:S(2)}) copy-start(bf16[1,16,16,64]{3,1,2,0:T(8,128)(2,1)} %copy-done.10) | copy-start | bytes 98308
  26.1 20.7 %collective-permute-start.8 = (f32[2,2,2,8,16,64]{5,4,3,1,0,2:T(8,128)}, f32[2,2,2,8,16,64]{5,4,3,1,0,2:T(8,128)}, u32[]{:S(2)}, u32[]{:S(2)}) collective-permute-start(f32[2,2,2,8,16,64]{5,4,3,1,0,2:T(8,128)} %bitcast.111), channel_id=1, source_target_pairs={{0,1},{1,0},{2,3},{3,2},{4,5},{5,4},{6,7},{7,6},{8,9},{9,8},{10,11... | collective-permute-start | bytes 786440 | tf_op jit(solution)/shard_map/ppermute | solution.py:47
  27.0 21.6 %collective-permute-start.12 = (f32[2,2,2,8,16,64]{5,4,3,2,0,1:T(8,128)}, f32[2,2,2,8,16,64]{5,4,3,2,0,1:T(8,128)}, u32[]{:S(2)}, u32[]{:S(2)}) collective-permute-start(f32[2,2,2,8,16,64]{5,4,3,2,0,1:T(8,128)} %bitcast.110), channel_id=1, source_target_pairs={{0,1},{1,0},{2,3},{3,2},{4,5},{5,4},{6,7},{7,6},{8,9},{9,8},{10,11... | collective-permute-start | bytes 786440 | tf_op jit(solution)/shard_map/ppermute | solution.py:47
  27.5 0.6 copy-start.12
  29.2 1.3 %copy-start.2 = (bf16[2,16,16,64]{3,1,2,0:T(8,128)(2,1)}, bf16[2,16,16,64]{3,1,2,0:T(8,128)(2,1)S(1)}, u32[]{:S(2)}) copy-start(bf16[2,16,16,64]{3,1,2,0:T(8,128)(2,1)S(1)} %get-tuple-element.51) | copy-start | bytes 196612
  30.0 8.5 %collective-permute-start.2 = (bf16[4,16,16,64]{3,1,2,0:T(8,128)(2,1)}, bf16[4,16,16,64]{3,1,2,0:T(8,128)(2,1)}, u32[]{:S(2)}, u32[]{:S(2)}) collective-permute-start(bf16[4,16,16,64]{3,1,2,0:T(8,128)(2,1)} %pad_maximum_fusion.5), channel_id=1, source_target_pairs={{0,2},{1,3},{2,0},{3,1},{4,6},{5,7},{6,4},{7,5},{8,10},{9,11},{10,... | collective-permute-start | bytes 393224 | tf_op jit(solution)/shard_map/ppermute | solution.py:23
  30.6 8.3 %copy-start.3 = (bf16[2,16,16,64]{3,1,2,0:T(8,128)(2,1)S(1)}, bf16[2,16,16,64]{3,1,2,0:T(8,128)(2,1)}, u32[]{:S(2)}) copy-start(bf16[2,16,16,64]{3,1,2,0:T(8,128)(2,1)} %copy-done.2) | copy-start | bytes 196612
  31.5 18.8 %collective-permute-start.16 = (f32[2,2,2,8,16,64]{5,4,3,1,0,2:T(8,128)}, f32[2,2,2,8,16,64]{5,4,3,1,0,2:T(8,128)}, u32[]{:S(2)}, u32[]{:S(2)}) collective-permute-start(f32[2,2,2,8,16,64]{5,4,3,1,0,2:T(8,128)} %bitcast.109), channel_id=1, source_target_pairs={{0,1},{1,0},{2,3},{3,2},{4,5},{5,4},{6,7},{7,6},{8,9},{9,8},{10,11... | collective-permute-start | bytes 786440 | tf_op jit(solution)/shard_map/ppermute | solution.py:47
  32.3 19.4 %collective-permute-start.20 = (f32[2,2,2,8,16,64]{5,4,3,2,0,1:T(8,128)}, f32[2,2,2,8,16,64]{5,4,3,2,0,1:T(8,128)}, u32[]{:S(2)}, u32[]{:S(2)}) collective-permute-start(f32[2,2,2,8,16,64]{5,4,3,2,0,1:T(8,128)} %bitcast.108), channel_id=1, source_target_pairs={{0,1},{1,0},{2,3},{3,2},{4,5},{5,4},{6,7},{7,6},{8,9},{9,8},{10,11... | collective-permute-start | bytes 786440 | tf_op jit(solution)/shard_map/ppermute | solution.py:47
  32.9 14.5 %copy-start.1 = (f32[2,2,2,1,8,16,64]{6,5,4,3,2,1,0:T(8,128)S(1)}, f32[2,2,2,1,8,16,64]{6,5,4,3,2,1,0:T(8,128)}, u32[]{:S(2)}) copy-start(f32[2,2,2,1,8,16,64]{6,5,4,3,2,1,0:T(8,128)} %get-tuple-element.55) | copy-start | bytes 786436
  38.5 7.4 %collective-permute-start.6 = (bf16[4,16,16,64]{3,1,2,0:T(8,128)(2,1)S(1)}, bf16[4,16,16,64]{3,1,2,0:T(8,128)(2,1)S(1)}, u32[]{:S(2)}, u32[]{:S(2)}) collective-permute-start(bf16[4,16,16,64]{3,1,2,0:T(8,128)(2,1)S(1)} %pad_maximum_fusion.6), channel_id=1, source_target_pairs={{0,4},{1,5},{2,6},{3,7},{4,0},{5,1},{6,2},{7,3},{8,12},{9,13},{10,... | collective-permute-start | bytes 393224 | tf_op jit(solution)/shard_map/ppermute | solution.py:23
  40.9 8.2 %copy-start = (f32[2,2,2,1,8,16,64]{6,5,4,3,2,1,0:T(8,128)S(1)}, f32[2,2,2,1,8,16,64]{6,5,4,3,2,1,0:T(8,128)}, u32[]{:S(2)}) copy-start(f32[2,2,2,1,8,16,64]{6,5,4,3,2,1,0:T(8,128)} %get-tuple-element.16) | copy-start | bytes 786436
  45.9 38.5 %collective-permute-start.3 = (bf16[8,16,16,64]{3,1,2,0:T(8,128)(2,1)}, bf16[8,16,16,64]{3,1,2,0:T(8,128)(2,1)}, u32[]{:S(2)}, u32[]{:S(2)}) collective-permute-start(bf16[8,16,16,64]{3,1,2,0:T(8,128)(2,1)} %pad_maximum_fusion.3), channel_id=1, source_target_pairs={{0,1},{1,0},{2,3},{3,2},{4,5},{5,4},{6,7},{7,6},{8,9},{9,8},{10,11... | collective-permute-start | bytes 786440 | tf_op jit(solution)/shard_map/ppermute | solution.py:23
  46.9 39.2 %collective-permute-start.7 = (bf16[8,16,16,64]{3,1,2,0:T(8,128)(2,1)}, bf16[8,16,16,64]{3,1,2,0:T(8,128)(2,1)}, u32[]{:S(2)}, u32[]{:S(2)}) collective-permute-start(bf16[8,16,16,64]{3,1,2,0:T(8,128)(2,1)} %pad_maximum_fusion.4), channel_id=1, source_target_pairs={{0,1},{1,0},{2,3},{3,2},{4,5},{5,4},{6,7},{7,6},{8,9},{9,8},{10,11... | collective-permute-start | bytes 786440 | tf_op jit(solution)/shard_map/ppermute | solution.py:23
  48.5 9.2 %collective-permute-start.9 = (f32[2,2,8,16,64]{4,3,2,1,0:T(8,128)S(1)}, f32[2,2,8,16,64]{4,3,2,1,0:T(8,128)S(1)}, u32[]{:S(2)}, u32[]{:S(2)}) collective-permute-start(f32[2,2,8,16,64]{4,3,2,1,0:T(8,128)S(1)} %dynamic-slice_bitcast_fusion.3), channel_id=1, source_target_pairs={{0,2},{1,3},{2,0},{3,1},{4,6},{5,7},{6,4},{7,5},{8,10},{9,11},{10,... | collective-permute-start | bytes 393224 | tf_op jit(solution)/shard_map/ppermute | solution.py:47
  50.3 8.0 %collective-permute-start.13 = (f32[2,2,8,16,64]{4,3,2,1,0:T(8,128)S(1)}, f32[2,2,8,16,64]{4,3,2,1,0:T(8,128)S(1)}, u32[]{:S(2)}, u32[]{:S(2)}) collective-permute-start(f32[2,2,8,16,64]{4,3,2,1,0:T(8,128)S(1)} %dynamic-slice_bitcast_fusion.2), channel_id=1, source_target_pairs={{0,4},{1,5},{2,6},{3,7},{4,0},{5,1},{6,2},{7,3},{8,12},{9,13},{10,... | collective-permute-start | bytes 393224 | tf_op jit(solution)/shard_map/ppermute | solution.py:47
  51.8 10.7 %collective-permute-start.17 = (f32[2,2,8,16,64]{4,3,2,1,0:T(8,128)S(1)}, f32[2,2,8,16,64]{4,3,2,1,0:T(8,128)S(1)}, u32[]{:S(2)}, u32[]{:S(2)}) collective-permute-start(f32[2,2,8,16,64]{4,3,2,1,0:T(8,128)S(1)} %dynamic-slice_bitcast_fusion.1), channel_id=1, source_target_pairs={{0,2},{1,3},{2,0},{3,1},{4,6},{5,7},{6,4},{7,5},{8,10},{9,11},{10,... | collective-permute-start | bytes 393224 | tf_op jit(solution)/shard_map/ppermute | solution.py:47
  57.8 8.8 %collective-permute-start.21 = (f32[2,2,8,16,64]{4,3,2,1,0:T(8,128)S(1)}, f32[2,2,8,16,64]{4,3,2,1,0:T(8,128)S(1)}, u32[]{:S(2)}, u32[]{:S(2)}) collective-permute-start(f32[2,2,8,16,64]{4,3,2,1,0:T(8,128)S(1)} %dynamic-slice_bitcast_fusion), channel_id=1, source_target_pairs={{0,4},{1,5},{2,6},{3,7},{4,0},{5,1},{6,2},{7,3},{8,12},{9,13},{10,... | collective-permute-start | bytes 393224 | tf_op jit(solution)/shard_map/ppermute | solution.py:47
  58.3 10.1 %collective-permute-start.10 = (f32[2,8,16,64]{3,2,1,0:T(8,128)S(1)}, f32[2,8,16,64]{3,2,1,0:T(8,128)S(1)}, u32[]{:S(2)}, u32[]{:S(2)}) collective-permute-start(f32[2,8,16,64]{3,2,1,0:T(8,128)S(1)} %dynamic-slice_bitcast_fusion.7), channel_id=1, source_target_pairs={{0,4},{1,5},{2,6},{3,7},{4,0},{5,1},{6,2},{7,3},{8,12},{9,13},{10,... | collective-permute-start | bytes 196616 | tf_op jit(solution)/shard_map/ppermute | solution.py:47
  62.4 7.3 %collective-permute-start.14 = (f32[2,8,16,64]{3,2,1,0:T(8,128)S(1)}, f32[2,8,16,64]{3,2,1,0:T(8,128)S(1)}, u32[]{:S(2)}, u32[]{:S(2)}) collective-permute-start(f32[2,8,16,64]{3,2,1,0:T(8,128)S(1)} %dynamic-slice_bitcast_fusion.6), channel_id=1, source_target_pairs={{0,2},{1,3},{2,0},{3,1},{4,6},{5,7},{6,4},{7,5},{8,10},{9,11},{10,... | collective-permute-start | bytes 196616 | tf_op jit(solution)/shard_map/ppermute | solution.py:47
  66.5 6.6 %collective-permute-start.18 = (f32[2,8,16,64]{3,2,1,0:T(8,128)S(1)}, f32[2,8,16,64]{3,2,1,0:T(8,128)S(1)}, u32[]{:S(2)}, u32[]{:S(2)}) collective-permute-start(f32[2,8,16,64]{3,2,1,0:T(8,128)S(1)} %dynamic-slice_bitcast_fusion.5), channel_id=1, source_target_pairs={{0,4},{1,5},{2,6},{3,7},{4,0},{5,1},{6,2},{7,3},{8,12},{9,13},{10,... | collective-permute-start | bytes 196616 | tf_op jit(solution)/shard_map/ppermute | solution.py:47
  68.4 7.0 %collective-permute-start.22 = (f32[2,8,16,64]{3,2,1,0:T(8,128)S(1)}, f32[2,8,16,64]{3,2,1,0:T(8,128)S(1)}, u32[]{:S(2)}, u32[]{:S(2)}) collective-permute-start(f32[2,8,16,64]{3,2,1,0:T(8,128)S(1)} %dynamic-slice_bitcast_fusion.4), channel_id=1, source_target_pairs={{0,2},{1,3},{2,0},{3,1},{4,6},{5,7},{6,4},{7,5},{8,10},{9,11},{10,... | collective-permute-start | bytes 196616 | tf_op jit(solution)/shard_map/ppermute | solution.py:47
  69.7 8.7 %collective-permute-start.11 = (f32[8,16,64]{2,0,1:T(8,128)S(1)}, f32[8,16,64]{2,0,1:T(8,128)S(1)}, u32[]{:S(2)}, u32[]{:S(2)}) collective-permute-start(f32[8,16,64]{2,0,1:T(8,128)S(1)} %bitcast.129), channel_id=1, source_target_pairs={{0,8},{1,9},{2,10},{3,11},{4,12},{5,13},{6,14},{7,15},{8,0},{9,1},... | collective-permute-start | bytes 98312 | tf_op jit(solution)/shard_map/ppermute | solution.py:47
  73.1 6.1 %collective-permute-start.15 = (f32[8,16,64]{2,0,1:T(8,128)S(1)}, f32[8,16,64]{2,0,1:T(8,128)S(1)}, u32[]{:S(2)}, u32[]{:S(2)}) collective-permute-start(f32[8,16,64]{2,0,1:T(8,128)S(1)} %bitcast.130), channel_id=1, source_target_pairs={{0,8},{1,9},{2,10},{3,11},{4,12},{5,13},{6,14},{7,15},{8,0},{9,1},... | collective-permute-start | bytes 98312 | tf_op jit(solution)/shard_map/ppermute | solution.py:47
  75.4 6.5 %collective-permute-start.19 = (f32[8,16,64]{2,0,1:T(8,128)S(1)}, f32[8,16,64]{2,0,1:T(8,128)S(1)}, u32[]{:S(2)}, u32[]{:S(2)}) collective-permute-start(f32[8,16,64]{2,0,1:T(8,128)S(1)} %bitcast.131), channel_id=1, source_target_pairs={{0,8},{1,9},{2,10},{3,11},{4,12},{5,13},{6,14},{7,15},{8,0},{9,1},... | collective-permute-start | bytes 98312 | tf_op jit(solution)/shard_map/ppermute | solution.py:47
  78.4 5.2 %collective-permute-start.23 = (f32[8,16,64]{2,0,1:T(8,128)S(1)}, f32[8,16,64]{2,0,1:T(8,128)S(1)}, u32[]{:S(2)}, u32[]{:S(2)}) collective-permute-start(f32[8,16,64]{2,0,1:T(8,128)S(1)} %bitcast.132), channel_id=1, source_target_pairs={{0,8},{1,9},{2,10},{3,11},{4,12},{5,13},{6,14},{7,15},{8,0},{9,1},... | collective-permute-start | bytes 98312 | tf_op jit(solution)/shard_map/ppermute | solution.py:47

commit v8 on v6

--- a/solution.py
+++ b/solution.py
@@ -139,6 +139,7 @@
         0,
     )
     grad_right = summed.transpose(2, 1, 0).reshape(n_seq, per_dev * C).astype(jnp.bfloat16)
+    grad_m, grad_right = lax.optimization_barrier((grad_m, grad_right))
 
     left_t = pl.pallas_call(
         left_kernel,

time: 89.7 us -> 90.1 us (level)
  waiting for transfers between devices: 33.5 us -> 35.5 us
  starting transfers between devices: 18 us -> 16.5 us
    ppermute x8, starting transfers between devices: 8.63 us -> 7.11 us  [scatter_sum(): buf = keep + lax.ppermute(send, axis, xor_pairs(n, bit))]
    ppermute x8, waiting for transfers between devices: 26.3 us -> 27.7 us  [scatter_sum(): buf = keep + lax.ppermute(send, axis, xor_pairs(n, bit))]
  transfers between devices with their start and end apart: 16 -> 16, of which waited for: 7 -> 7; matrix products, arithmetic and copies ran while one was open for 21% -> 19% of each run, Pallas kernels for 17% -> 9%
where the time goes in v8:
time: 90.1 us; the launch traced here: 89.7 us
  waiting for transfers between devices  35.5 us (39%)
  starting transfers between devices  16.5 us (18%)
  Pallas kernels  15.2 us (17%)
  local copies, waits for them, and re-layouts  14.1 us (16%)
  other arithmetic  7.6 us (8%)
    ppermute x8, waiting for transfers between devices, scatter_sum(): buf = keep + lax.ppermute(send, axis, xor_pairs(n, bit))  27.7 us
    ppermute x8, starting transfers between devices, gather_blocks(): other = lax.ppermute(buf, axis, xor_pairs(n, bit))  9.4 us
    pallas_call x1, Pallas kernels, per_device(): pl.pallas_call(functools.partial(project_kernel, n_seq=n_seq), grid=(step...  8.17 us
    ppermute x8, waiting for transfers between devices, gather_blocks(): other = lax.ppermute(buf, axis, xor_pairs(n, bit))  7.74 us
    ppermute x8, starting transfers between devices, scatter_sum(): buf = keep + lax.ppermute(send, axis, xor_pairs(n, bit))  7.11 us
    pallas_call x1, Pallas kernels, per_device(): pl.pallas_call(left_kernel, grid=(steps,), in_specs=[pl.BlockSpec((C, own...  7.02 us
    another operation x3, local copies, waits for them, and re-layouts  5.12 us
    slice x1, local copies, waits for them, and re-layouts, per_device(): part_t[:, :half]  3.93 us
  transfers between devices with their start and end apart: 16, of which 7 were waited for; matrix products, arithmetic and copies ran while one was open for 19% of the time, Pallas kernels for 9%

profile of v8, /device:TPU:0, one launch (start us, length us, event | category | flops | bytes accessed | tf_op | source)
XLA Modules:
  0.0 89.7 jit_solution(610149542679274742)
XLA Ops:
  0.6 1.0 %copy.17 = bf16[64,512]{0,1:T(8,128)(2,1)S(1)} copy(bf16[64,512]{1,0:T(8,128)(2,1)} %param.5) | data formatting | bytes 131072 | tf_op args[1]
  1.6 4.1 %collective-permute-start.8 = (bf16[1,16,16,64]{3,1,2,0:T(8,128)(2,1)S(1)}, bf16[1,16,16,64]{3,1,2,0:T(8,128)(2,1)S(1)}, u32[]{:S(2)}, u32[]{:S(2)}) collective-permute-start(bf16[1,16,16,64]{3,1,2,0:T(8,128)(2,1)S(1)} %get-tuple-element.42), channel_id=1, source_target_pairs={{0,8},{1,9},{2,10},{3,11},{4,12},{5,13},{6,14},{7,15},{8,0},{9,1},... | collective-permute-start | bytes 98312 | tf_op jit(solution)/shard_map/ppermute | solution.py:23
  5.7 0.1 collective-permute-start.12
  5.8 1.8 %copy.8 = bf16[32,32,128]{2,0,1:T(8,128)(2,1)} copy(bf16[32,32,128]{2,1,0:T(8,128)(2,1)} %bitcast.83) | data formatting | bytes 524288 | tf_op jit(solution)/shard_map/reshape | solution.py:106
  7.6 8.2 %shard_map.59 = (bf16[32,512,256]{2,1,0:T(8,128)(2,1)}, f32[16,32,16,64]{3,2,1,0:T(8,128)}) custom-call(bf16[16,256,128]{2,1,0:T(8,128)(2,1)} %p_ref.1, bf16[1024,128]{1,0:T(8,128)(2,1)} %bitcast.84, bf16[64,512]{1,0:T(8,128)(2,1)} %l_ref.1), custom_call_target="tpu_custom_call" | custom-call | flops 1610612736 | bytes 11534336 | tf_op jit(solution)/shard_map/pallas_call | solution.py:108
  15.7 0.0 collective-permute-done.8
  15.7 0.0 collective-permute-done.12
  15.8 1.8 %collective-permute-start.13 = (bf16[2,16,16,64]{3,1,2,0:T(8,128)(2,1)S(1)}, bf16[2,16,16,64]{3,1,2,0:T(8,128)(2,1)S(1)}, u32[]{:S(2)}, u32[]{:S(2)}) collective-permute-start(bf16[2,16,16,64]{3,1,2,0:T(8,128)(2,1)S(1)} %pad_maximum_fusion.9), channel_id=1, source_target_pairs={{0,2},{1,3},{2,0},{3,1},{4,6},{5,7},{6,4},{7,5},{8,10},{9,11},{10,... | collective-permute-start | bytes 196616 | tf_op jit(solution)/shard_map/ppermute | solution.py:23
  17.7 1.6 %collective-permute-start.9 = (bf16[2,16,16,64]{3,1,2,0:T(8,128)(2,1)S(1)}, bf16[2,16,16,64]{3,1,2,0:T(8,128)(2,1)S(1)}, u32[]{:S(2)}, u32[]{:S(2)}) collective-permute-start(bf16[2,16,16,64]{3,1,2,0:T(8,128)(2,1)S(1)} %pad_maximum_fusion.8), channel_id=1, source_target_pairs={{0,4},{1,5},{2,6},{3,7},{4,0},{5,1},{6,2},{7,3},{8,12},{9,13},{10,... | collective-permute-start | bytes 196616 | tf_op jit(solution)/shard_map/ppermute | solution.py:23
  19.3 3.9 %fusion.2 = (f32[16,16,16,64]{3,2,1,0:T(8,128)S(1)}, f32[16,16,16,64]{3,2,1,0:T(8,128)}) fusion(f32[16,32,16,64]{3,2,1,0:T(8,128)} %get-tuple-element.7), kind=kLoop, calls=%fused_computation.55 | loop fusion | bytes 4194304 | tf_op jit(solution)/shard_map/slice | solution.py:136
  23.3 0.0 collective-permute-done.13
  23.3 0.0 collective-permute-done.9
  23.3 0.1 broadcast_select_fusion.9
  23.3 0.0 copy-start.1
  23.4 0.8 pad_maximum_fusion.6
  24.1 1.0 %collective-permute-start.14 = (bf16[4,16,16,64]{3,1,2,0:T(8,128)(2,1)}, bf16[4,16,16,64]{3,1,2,0:T(8,128)(2,1)}, u32[]{:S(2)}, u32[]{:S(2)}) collective-permute-start(bf16[4,16,16,64]{3,1,2,0:T(8,128)(2,1)} %pad_maximum_fusion.6), channel_id=1, source_target_pairs={{0,4},{1,5},{2,6},{3,7},{4,0},{5,1},{6,2},{7,3},{8,12},{9,13},{10,... | collective-permute-start | bytes 393224 | tf_op jit(solution)/shard_map/ppermute | solution.py:23
  25.2 0.0 copy-done.1
  25.2 2.9 %constant_dynamic-slice_fusion.3 = (f32[2,2,2,1,16,16,64]{6,5,4,3,2,1,0:T(8,128)}, f32[2,2,2,1,16,16,64]{6,5,4,3,2,1,0:T(8,128)S(1)}, f32[2,2,2,1,16,16,64]{6,5,...) fusion(f32[2,2,2,2,16,16,64]{6,5,4,3,2,1,0:T(8,128)} %bitcast.75, s32[]{:T(128)S(6)} %select_n.120, s32[]{:T(128)S(6)} %select_n.121, ...), kind=kLoop, calls=%fused_computation.50 | loop fusion | bytes 4194312 | tf_op jit(solution)/shard_map/dynamic-slice.6
  28.1 1.1 %copy.34 = f32[2,2,2,1,16,16,64]{6,5,4,2,0,1,3:T(8,128)} copy(f32[2,2,2,1,16,16,64]{6,5,4,3,2,1,0:T(8,128)S(1)} %get-tuple-element.19) | data formatting | bytes 1048576 | tf_op jit(solution)/shard_map/dynamic-slice.7
  29.2 0.0 collective-permute-start.4
  29.2 1.1 %copy.35 = f32[2,2,2,1,16,16,64]{6,5,4,1,0,2,3:T(8,128)} copy(f32[2,2,2,1,16,16,64]{6,5,4,3,2,1,0:T(8,128)S(1)} %get-tuple-element.44) | data formatting | bytes 1048576 | tf_op jit(solution)/shard_map/dynamic-slice.1
  30.3 0.5 collective-permute-start
  30.8 0.1 pad_maximum_fusion.5
  30.9 0.6 collective-permute-start.10
  31.4 0.0 collective-permute-done.14
  31.4 0.0 copy-done.2
  31.4 1.0 %broadcast_select_fusion.5 = (bf16[4,16,16,64]{3,1,2,0:T(8,128)(2,1)S(1)}, bf16[4,16,16,64]{3,1,2,0:T(8,128)(2,1)S(1)}) fusion(bf16[4,16,16,64]{3,1,2,0:T(8,128)(2,1)} %collective-permute-done.14, pred[]{:T(512)S(6)} %eq.10, bf16[2,16,16,64]{3,1,2,0:T(8,128)(2,1)S(1)} %copy-done.2, bf16[2,16,16,64]{3,1,2,0:T(8,128)(2,1)S(1)} %get-tuple-element.30), kind=kLoop, calls=%fused_computation.24 | loop fusion | flops 196608 | bytes 524289 | tf_op jit(solution)/shard_map/jit(_where)/select_n | solution.py:25
  32.5 0.1 pad_maximum_fusion.4
  32.6 0.1 collective-permute-start.15
  32.7 6.5 %collective-permute-done.10 = bf16[4,16,16,64]{3,1,2,0:T(8,128)(2,1)S(1)} collective-permute-done((bf16[4,16,16,64]{3,1,2,0:T(8,128)(2,1)S(1)}, bf16[4,16,16,64]{3,1,2,0:T(8,128)(2,1)S(1)}, u32[]{:S(2)}, u32[]{:S(2)}) %collective-permute-start.10) | collective-permute-done | bytes 131104 | tf_op jit(solution)/shard_map/ppermute | solution.py:23
  39.1 0.1 broadcast_select_fusion.7
  39.2 0.1 pad_maximum_fusion.3
  39.3 0.1 collective-permute-start.11
  39.4 0.0 collective-permute-done.15
  39.4 0.1 broadcast_select_fusion.1
  39.6 0.2 pad_maximum_fusion.2
  39.8 0.3 copy.21
  40.1 1.2 %collective-permute-done.11 = bf16[8,16,16,64]{3,1,2,0:T(8,128)(2,1)S(1)} collective-permute-done((bf16[8,16,16,64]{3,1,2,0:T(8,128)(2,1)S(1)}, bf16[8,16,16,64]{3,1,2,0:T(8,128)(2,1)S(1)}, u32[]{:S(2)}, u32[]{:S(2)}) %collective-permute-start.11) | collective-permute-done | bytes 262176 | tf_op jit(solution)/shard_map/ppermute | solution.py:23
  41.3 0.1 broadcast_select_fusion.3
  41.5 0.2 pad_maximum_fusion.1
  41.7 0.3 copy.19
  42.0 1.8 %pad_maximum_fusion.rt_ref = bf16[16,32,16,64]{3,2,1,0:T(8,128)(2,1)} fusion(bf16[16,16,16,64]{3,2,1,0:T(8,128)(2,1)S(1)} %bitcast.78, bf16[16,16,16,64]{3,2,1,0:T(8,128)(2,1)S(1)} %bitcast.79), kind=kLoop, calls=%fused_computation | loop fusion | flops 524288 | bytes 2097152 | tf_op jit(solution)/shard_map/concatenate | solution.py:98
  43.8 0.0 collective-permute-done.4
  43.8 1.4 %bitcast_add_fusion = f32[2,2,2,16,16,64]{5,4,3,2,0,1:T(8,128)S(1)} fusion(f32[2,2,2,16,16,64]{5,4,3,2,0,1:T(8,128)} %collective-permute-done.4, f32[2,2,2,1,16,16,64]{6,5,4,3,2,1,0:T(8,128)S(1)} %copy-done), kind=kLoop, calls=%fused_computation.3 | loop fusion | flops 131072 | bytes 1572864 | tf_op jit(solution)/shard_map/add | solution.py:47
  45.2 1.1 %collective-permute-start.5 = (f32[2,2,16,16,64]{4,3,2,1,0:T(8,128)S(1)}, f32[2,2,16,16,64]{4,3,2,1,0:T(8,128)S(1)}, u32[]{:S(2)}, u32[]{:S(2)}) collective-permute-start(f32[2,2,16,16,64]{4,3,2,1,0:T(8,128)S(1)} %dynamic-slice_bitcast_fusion), channel_id=1, source_target_pairs={{0,4},{1,5},{2,6},{3,7},{4,0},{5,1},{6,2},{7,3},{8,12},{9,13},{10,... | collective-permute-start | bytes 786440 | tf_op jit(solution)/shard_map/ppermute | solution.py:47
  46.2 0.0 collective-permute-done
  46.2 0.1 bitcast_add_fusion.1
  46.4 0.6 collective-permute-start.1
  47.0 12.2 %collective-permute-done.5 = f32[2,2,16,16,64]{4,3,2,1,0:T(8,128)S(1)} collective-permute-done((f32[2,2,16,16,64]{4,3,2,1,0:T(8,128)S(1)}, f32[2,2,16,16,64]{4,3,2,1,0:T(8,128)S(1)}, u32[]{:S(2)}, u32[]{:S(2)}) %collective-permute-start.5) | collective-permute-done | bytes 262176 | tf_op jit(solution)/shard_map/ppermute | solution.py:47
  59.2 0.1 bitcast_add_fusion.2
  59.3 0.6 collective-permute-start.6
  59.9 0.3 collective-permute-done.1
  60.2 0.1 bitcast_add_fusion.3
  60.3 1.1 %collective-permute-start.2 = (f32[2,16,16,64]{3,2,1,0:T(8,128)S(1)}, f32[2,16,16,64]{3,2,1,0:T(8,128)S(1)}, u32[]{:S(2)}, u32[]{:S(2)}) collective-permute-start(f32[2,16,16,64]{3,2,1,0:T(8,128)S(1)} %dynamic-slice_bitcast_fusion.3), channel_id=1, source_target_pairs={{0,4},{1,5},{2,6},{3,7},{4,0},{5,1},{6,2},{7,3},{8,12},{9,13},{10,... | collective-permute-start | bytes 393224 | tf_op jit(solution)/shard_map/ppermute | solution.py:47
  61.4 5.5 %collective-permute-done.6 = f32[2,16,16,64]{3,2,1,0:T(8,128)S(1)} collective-permute-done((f32[2,16,16,64]{3,2,1,0:T(8,128)S(1)}, f32[2,16,16,64]{3,2,1,0:T(8,128)S(1)}, u32[]{:S(2)}, u32[]{:S(2)}) %collective-permute-start.6) | collective-permute-done | bytes 131104 | tf_op jit(solution)/shard_map/ppermute | solution.py:47
  67.0 2.7 %collective-permute-start.7 = (f32[16,16,64]{2,0,1:T(8,128)S(1)}, f32[16,16,64]{2,0,1:T(8,128)S(1)}, u32[]{:S(2)}, u32[]{:S(2)}) collective-permute-start(f32[16,16,64]{2,0,1:T(8,128)S(1)} %bitcast.85), channel_id=1, source_target_pairs={{0,8},{1,9},{2,10},{3,11},{4,12},{5,13},{6,14},{7,15},{8,0},{9,1},... | collective-permute-start | bytes 196616 | tf_op jit(solution)/shard_map/ppermute | solution.py:47
  69.7 0.0 collective-permute-done.2
  69.8 0.6 collective-permute-start.3
  70.5 8.2 %collective-permute-done.7 = f32[16,16,64]{2,0,1:T(8,128)S(1)} collective-permute-done((f32[16,16,64]{2,0,1:T(8,128)S(1)}, f32[16,16,64]{2,0,1:T(8,128)S(1)}, u32[]{:S(2)}, u32[]{:S(2)}) %collective-permute-start.7) | collective-permute-done | bytes 65568 | tf_op jit(solution)/shard_map/ppermute | solution.py:47
  78.7 1.5 %collective-permute-done.3 = f32[16,16,64]{2,0,1:T(8,128)S(1)} collective-permute-done((f32[16,16,64]{2,0,1:T(8,128)S(1)}, f32[16,16,64]{2,0,1:T(8,128)S(1)}, u32[]{:S(2)}, u32[]{:S(2)}) %collective-permute-start.3) | collective-permute-done | bytes 65568 | tf_op jit(solution)/shard_map/ppermute | solution.py:47
  80.3 7.0 %shard_map.60 = f32[512,64]{1,0:T(8,128)} custom-call(bf16[32,512,256]{2,1,0:T(8,128)(2,1)} %get-tuple-element.8.gm_ref, bf16[16,32,16,64]{3,2,1,0:T(8,128)(2,1)} %pad_maximum_fusion.rt_ref), custom_call_target="tpu_custom_call" | custom-call | flops 536870912 | bytes 9437184 | tf_op jit(solution)/shard_map/pallas_call | solution.py:144
  87.3 1.0 %convert_bitcast_fusion = bf16[64,512]{0,1:T(8,128)(2,1)S(1)} fusion(f32[512,64]{1,0:T(8,128)} %shard_map.60), kind=kLoop, calls=%fused_computation.36 | loop fusion | flops 32768 | bytes 196608 | tf_op jit(solution)/shard_map/convert_element_type | solution.py:160
  88.3 0.7 copy.22
  89.0 0.7 copy.23
  (20 shorter events, 0.6 us)
Async XLA Ops:
  1.6 14.1 %collective-permute-start.8 = (bf16[1,16,16,64]{3,1,2,0:T(8,128)(2,1)S(1)}, bf16[1,16,16,64]{3,1,2,0:T(8,128)(2,1)S(1)}, u32[]{:S(2)}, u32[]{:S(2)}) collective-permute-start(bf16[1,16,16,64]{3,1,2,0:T(8,128)(2,1)S(1)} %get-tuple-element.42), channel_id=1, source_target_pairs={{0,8},{1,9},{2,10},{3,11},{4,12},{5,13},{6,14},{7,15},{8,0},{9,1},... | collective-permute-start | bytes 98312 | tf_op jit(solution)/shard_map/ppermute | solution.py:23
  5.7 10.0 %collective-permute-start.12 = (bf16[1,16,16,64]{3,1,2,0:T(8,128)(2,1)S(1)}, bf16[1,16,16,64]{3,1,2,0:T(8,128)(2,1)S(1)}, u32[]{:S(2)}, u32[]{:S(2)}) collective-permute-start(bf16[1,16,16,64]{3,1,2,0:T(8,128)(2,1)S(1)} %get-tuple-element.43), channel_id=1, source_target_pairs={{0,8},{1,9},{2,10},{3,11},{4,12},{5,13},{6,14},{7,15},{8,0},{9,1},... | collective-permute-start | bytes 98312 | tf_op jit(solution)/shard_map/ppermute | solution.py:23
  15.8 7.5 %collective-permute-start.13 = (bf16[2,16,16,64]{3,1,2,0:T(8,128)(2,1)S(1)}, bf16[2,16,16,64]{3,1,2,0:T(8,128)(2,1)S(1)}, u32[]{:S(2)}, u32[]{:S(2)}) collective-permute-start(bf16[2,16,16,64]{3,1,2,0:T(8,128)(2,1)S(1)} %pad_maximum_fusion.9), channel_id=1, source_target_pairs={{0,2},{1,3},{2,0},{3,1},{4,6},{5,7},{6,4},{7,5},{8,10},{9,11},{10,... | collective-permute-start | bytes 196616 | tf_op jit(solution)/shard_map/ppermute | solution.py:23
  17.7 5.6 %collective-permute-start.9 = (bf16[2,16,16,64]{3,1,2,0:T(8,128)(2,1)S(1)}, bf16[2,16,16,64]{3,1,2,0:T(8,128)(2,1)S(1)}, u32[]{:S(2)}, u32[]{:S(2)}) collective-permute-start(bf16[2,16,16,64]{3,1,2,0:T(8,128)(2,1)S(1)} %pad_maximum_fusion.8), channel_id=1, source_target_pairs={{0,4},{1,5},{2,6},{3,7},{4,0},{5,1},{6,2},{7,3},{8,12},{9,13},{10,... | collective-permute-start | bytes 196616 | tf_op jit(solution)/shard_map/ppermute | solution.py:23
  23.3 1.8 %copy-start.1 = (bf16[2,16,16,64]{3,1,2,0:T(8,128)(2,1)}, bf16[2,16,16,64]{3,1,2,0:T(8,128)(2,1)S(1)}, u32[]{:S(2)}) copy-start(bf16[2,16,16,64]{3,1,2,0:T(8,128)(2,1)S(1)} %get-tuple-element.31) | copy-start | bytes 196612
  24.1 7.3 %collective-permute-start.14 = (bf16[4,16,16,64]{3,1,2,0:T(8,128)(2,1)}, bf16[4,16,16,64]{3,1,2,0:T(8,128)(2,1)}, u32[]{:S(2)}, u32[]{:S(2)}) collective-permute-start(bf16[4,16,16,64]{3,1,2,0:T(8,128)(2,1)} %pad_maximum_fusion.6), channel_id=1, source_target_pairs={{0,4},{1,5},{2,6},{3,7},{4,0},{5,1},{6,2},{7,3},{8,12},{9,13},{10,... | collective-permute-start | bytes 393224 | tf_op jit(solution)/shard_map/ppermute | solution.py:23
  28.1 3.4 %copy-start.2 = (bf16[2,16,16,64]{3,1,2,0:T(8,128)(2,1)S(1)}, bf16[2,16,16,64]{3,1,2,0:T(8,128)(2,1)}, u32[]{:S(2)}) copy-start(bf16[2,16,16,64]{3,1,2,0:T(8,128)(2,1)} %copy-done.1) | copy-start | bytes 196612
  29.2 14.6 %collective-permute-start.4 = (f32[2,2,2,16,16,64]{5,4,3,2,0,1:T(8,128)}, f32[2,2,2,16,16,64]{5,4,3,2,0,1:T(8,128)}, u32[]{:S(2)}, u32[]{:S(2)}) collective-permute-start(f32[2,2,2,16,16,64]{5,4,3,2,0,1:T(8,128)} %bitcast.70), channel_id=1, source_target_pairs={{0,1},{1,0},{2,3},{3,2},{4,5},{5,4},{6,7},{7,6},{8,9},{9,8},{10,11... | collective-permute-start | bytes 1572872 | tf_op jit(solution)/shard_map/ppermute | solution.py:47
  30.3 15.9 %collective-permute-start = (f32[2,2,2,16,16,64]{5,4,3,1,0,2:T(8,128)}, f32[2,2,2,16,16,64]{5,4,3,1,0,2:T(8,128)S(1)}, u32[]{:S(2)}, u32[]{:S(2)}) collective-permute-start(f32[2,2,2,16,16,64]{5,4,3,1,0,2:T(8,128)} %bitcast.71), channel_id=1, source_target_pairs={{0,1},{1,0},{2,3},{3,2},{4,5},{5,4},{6,7},{7,6},{8,9},{9,8},{10,11... | collective-permute-start | bytes 1572872 | tf_op jit(solution)/shard_map/ppermute | solution.py:47
  30.9 8.3 %collective-permute-start.10 = (bf16[4,16,16,64]{3,1,2,0:T(8,128)(2,1)S(1)}, bf16[4,16,16,64]{3,1,2,0:T(8,128)(2,1)S(1)}, u32[]{:S(2)}, u32[]{:S(2)}) collective-permute-start(bf16[4,16,16,64]{3,1,2,0:T(8,128)(2,1)S(1)} %pad_maximum_fusion.5), channel_id=1, source_target_pairs={{0,2},{1,3},{2,0},{3,1},{4,6},{5,7},{6,4},{7,5},{8,10},{9,11},{10,... | collective-permute-start | bytes 393224 | tf_op jit(solution)/shard_map/ppermute | solution.py:23
  32.6 6.8 %collective-permute-start.15 = (bf16[8,16,16,64]{3,1,2,0:T(8,128)(2,1)S(1)}, bf16[8,16,16,64]{3,1,2,0:T(8,128)(2,1)S(1)}, u32[]{:S(2)}, u32[]{:S(2)}) collective-permute-start(bf16[8,16,16,64]{3,1,2,0:T(8,128)(2,1)S(1)} %pad_maximum_fusion.4), channel_id=1, source_target_pairs={{0,1},{1,0},{2,3},{3,2},{4,5},{5,4},{6,7},{7,6},{8,9},{9,8},{10,11... | collective-permute-start | bytes 786440 | tf_op jit(solution)/shard_map/ppermute | solution.py:23
  39.3 2.0 %collective-permute-start.11 = (bf16[8,16,16,64]{3,1,2,0:T(8,128)(2,1)S(1)}, bf16[8,16,16,64]{3,1,2,0:T(8,128)(2,1)S(1)}, u32[]{:S(2)}, u32[]{:S(2)}) collective-permute-start(bf16[8,16,16,64]{3,1,2,0:T(8,128)(2,1)S(1)} %pad_maximum_fusion.3), channel_id=1, source_target_pairs={{0,1},{1,0},{2,3},{3,2},{4,5},{5,4},{6,7},{7,6},{8,9},{9,8},{10,11... | collective-permute-start | bytes 786440 | tf_op jit(solution)/shard_map/ppermute | solution.py:23
  42.0 1.8 %copy-start = (f32[2,2,2,1,16,16,64]{6,5,4,3,2,1,0:T(8,128)S(1)}, f32[2,2,2,1,16,16,64]{6,5,4,3,2,1,0:T(8,128)}, u32[]{:S(2)}) copy-start(f32[2,2,2,1,16,16,64]{6,5,4,3,2,1,0:T(8,128)} %get-tuple-element.18) | copy-start | bytes 1572868
  45.2 14.0 %collective-permute-start.5 = (f32[2,2,16,16,64]{4,3,2,1,0:T(8,128)S(1)}, f32[2,2,16,16,64]{4,3,2,1,0:T(8,128)S(1)}, u32[]{:S(2)}, u32[]{:S(2)}) collective-permute-start(f32[2,2,16,16,64]{4,3,2,1,0:T(8,128)S(1)} %dynamic-slice_bitcast_fusion), channel_id=1, source_target_pairs={{0,4},{1,5},{2,6},{3,7},{4,0},{5,1},{6,2},{7,3},{8,12},{9,13},{10,... | collective-permute-start | bytes 786440 | tf_op jit(solution)/shard_map/ppermute | solution.py:47
  46.4 13.8 %collective-permute-start.1 = (f32[2,2,16,16,64]{4,3,2,1,0:T(8,128)S(1)}, f32[2,2,16,16,64]{4,3,2,1,0:T(8,128)S(1)}, u32[]{:S(2)}, u32[]{:S(2)}) collective-permute-start(f32[2,2,16,16,64]{4,3,2,1,0:T(8,128)S(1)} %dynamic-slice_bitcast_fusion.1), channel_id=1, source_target_pairs={{0,2},{1,3},{2,0},{3,1},{4,6},{5,7},{6,4},{7,5},{8,10},{9,11},{10,... | collective-permute-start | bytes 786440 | tf_op jit(solution)/shard_map/ppermute | solution.py:47
  59.3 7.6 %collective-permute-start.6 = (f32[2,16,16,64]{3,2,1,0:T(8,128)S(1)}, f32[2,16,16,64]{3,2,1,0:T(8,128)S(1)}, u32[]{:S(2)}, u32[]{:S(2)}) collective-permute-start(f32[2,16,16,64]{3,2,1,0:T(8,128)S(1)} %dynamic-slice_bitcast_fusion.2), channel_id=1, source_target_pairs={{0,2},{1,3},{2,0},{3,1},{4,6},{5,7},{6,4},{7,5},{8,10},{9,11},{10,... | collective-permute-start | bytes 393224 | tf_op jit(solution)/shard_map/ppermute | solution.py:47
  60.3 9.4 %collective-permute-start.2 = (f32[2,16,16,64]{3,2,1,0:T(8,128)S(1)}, f32[2,16,16,64]{3,2,1,0:T(8,128)S(1)}, u32[]{:S(2)}, u32[]{:S(2)}) collective-permute-start(f32[2,16,16,64]{3,2,1,0:T(8,128)S(1)} %dynamic-slice_bitcast_fusion.3), channel_id=1, source_target_pairs={{0,4},{1,5},{2,6},{3,7},{4,0},{5,1},{6,2},{7,3},{8,12},{9,13},{10,... | collective-permute-start | bytes 393224 | tf_op jit(solution)/shard_map/ppermute | solution.py:47
  67.0 11.6 %collective-permute-start.7 = (f32[16,16,64]{2,0,1:T(8,128)S(1)}, f32[16,16,64]{2,0,1:T(8,128)S(1)}, u32[]{:S(2)}, u32[]{:S(2)}) collective-permute-start(f32[16,16,64]{2,0,1:T(8,128)S(1)} %bitcast.85), channel_id=1, source_target_pairs={{0,8},{1,9},{2,10},{3,11},{4,12},{5,13},{6,14},{7,15},{8,0},{9,1},... | collective-permute-start | bytes 196616 | tf_op jit(solution)/shard_map/ppermute | solution.py:47
  69.8 10.4 %collective-permute-start.3 = (f32[16,16,64]{2,0,1:T(8,128)S(1)}, f32[16,16,64]{2,0,1:T(8,128)S(1)}, u32[]{:S(2)}, u32[]{:S(2)}) collective-permute-start(f32[16,16,64]{2,0,1:T(8,128)S(1)} %bitcast.86), channel_id=1, source_target_pairs={{0,8},{1,9},{2,10},{3,11},{4,12},{5,13},{6,14},{7,15},{8,0},{9,1},... | collective-permute-start | bytes 196616 | tf_op jit(solution)/shard_map/ppermute | solution.py:47

commit v9 on v6

--- a/solution.py
+++ b/solution.py
@@ -49,13 +49,33 @@
     return buf
 
 
+def scatter_sum_ordered(x, axis, bits):
+    me = lax.axis_index(axis)
+    n = x.shape[0]
+    buf = x
+    for bit in bits:
+        half = buf.shape[0] // 2
+        mine = (me >> bit) & 1
+        keep = lax.dynamic_slice_in_dim(buf, mine * half, half, 0)
+        send = lax.dynamic_slice_in_dim(buf, (1 - mine) * half, half, 0)
+        buf = keep + lax.ppermute(send, axis, xor_pairs(n, bit))
+    return buf[0]
+
+
+def position(d, bits):
+    k = len(bits)
+    return sum(((d >> bit) & 1) << (k - 1 - t) for t, bit in enumerate(bits))
+
+
 def index_bits(n):
     return list(range(n.bit_length() - 1))
 
 
-def project_kernel(p_ref, w_ref, l_ref, gm_ref, pt_ref, *, n_seq):
+def project_kernel(p_ref, w_ref, l_ref, gm_ref, pt_ref, *, n_seq, orders):
     rows = p_ref.shape[0]
     width = p_ref.shape[1]
+    per_block = width // 16
+    half = C // len(orders)
     for i in range(rows):
         prod = lax.dot_general(
             w_ref[...], p_ref[i], (((1,), (1,)), ((), ())), preferred_element_type=jnp.float32
@@ -63,11 +83,15 @@
         grad = (prod / n_seq).astype(jnp.bfloat16)
         for e in range(C):
             gm_ref[e, i * C:(i + 1) * C, :] = grad[e * C:(e + 1) * C, :]
+    first = pl.program_id(0) * per_block
     for e in range(C):
         part = lax.dot_general(
             gm_ref[e], l_ref[...], (((0,), (1,)), ((), ())), preferred_element_type=jnp.float32
         )
-        pt_ref[:, e, :, :] = part.reshape(width // 16, 16, part.shape[1])
+        part = part.reshape(per_block, 16, part.shape[1])
+        h = e // half
+        for local in range(per_block):
+            pt_ref[h, position(first + local, orders[h]), e % half] = part[local]
 
 
 def left_kernel(gm_ref, rt_ref, out_ref):
@@ -105,8 +129,11 @@
 
     weight_ec = out_weight.reshape(C, C, p_size).transpose(1, 0, 2).reshape(C * C, p_size)
 
+    swapped = bits[:1] + bits[1:3][::-1] + bits[3:]
+    orders = (tuple(bits), tuple(swapped))
+    half = C // len(orders)
     grad_m, part_t = pl.pallas_call(
-        functools.partial(project_kernel, n_seq=n_seq),
+        functools.partial(project_kernel, n_seq=n_seq, orders=orders),
         grid=(steps,),
         in_specs=[
             pl.BlockSpec((own_rows, block, p_size), lambda b: (0, b, 0)),
@@ -115,11 +142,11 @@
         ],
         out_specs=[
             pl.BlockSpec((C, own_rows * C, block), lambda b: (0, 0, b)),
-            pl.BlockSpec((block // 16, C, 16, n_seq), lambda b: (b, 0, 0, 0)),
+            pl.BlockSpec((len(orders), total // 16, half, 16, n_seq), lambda b: (0, 0, 0, 0, 0)),
         ],
         out_shape=[
             jax.ShapeDtypeStruct((C, own_rows * C, total), jnp.bfloat16),
-            jax.ShapeDtypeStruct((total // 16, C, 16, n_seq), jnp.float32),
+            jax.ShapeDtypeStruct((len(orders), total // 16, half, 16, n_seq), jnp.float32),
         ],
         compiler_params=pltpu.CompilerParams(vmem_limit_bytes=56 * 1024 * 1024),
         cost_estimate=pl.CostEstimate(
@@ -129,14 +156,8 @@
         ),
     )(pair_cot, weight_ec, left_proj)
 
-    half = C // 2
-    swapped = bits[:1] + bits[1:3][::-1] + bits[3:]
     summed = jnp.concatenate(
-        [
-            scatter_sum(part_t[:, :half], "row", n, bits),
-            scatter_sum(part_t[:, half:], "row", n, swapped),
-        ],
-        0,
+        [scatter_sum_ordered(part_t[h], "row", list(orders[h])) for h in range(len(orders))], 0
     )
     grad_right = summed.transpose(2, 1, 0).reshape(n_seq, per_dev * C).astype(jnp.bfloat16)
 

time: 89.7 us -> 90.4 us (level)
  local copies, waits for them, and re-layouts: 14.1 us -> 11.1 us
  other arithmetic: 7.59 us -> 10.3 us
  starting transfers between devices: 18 us -> 20.4 us
  waiting for transfers between devices: 33.5 us -> 32.3 us
    another operation x3 -> x0, local copies, waits for them, and re-layouts: 5.13 us -> none
    dynamic_slice x4 -> x8, local copies, waits for them, and re-layouts: 0.15 us -> 2.29 us  [scatter_sum_ordered(): send = lax.dynamic_slice_in_dim(buf, (1 - mine) * half, half, 0)]
    add x6, other arithmetic: 1.7 us -> 3.3 us  [scatter_sum_ordered(): buf = keep + lax.ppermute(send, axis, xor_pairs(n, bit))]
    ppermute x8, starting transfers between devices: 8.63 us -> 9.88 us  [scatter_sum_ordered(): buf = keep + lax.ppermute(send, axis, xor_pairs(n, bit))]
    ppermute x8, starting transfers between devices: 9.4 us -> 10.5 us  [gather_blocks(): other = lax.ppermute(buf, axis, xor_pairs(n, bit))]
    unnamed x9 -> x5, local copies, waits for them, and re-layouts: 2.42 us -> 2.42 us
  transfers between devices with their start and end apart: 16 -> 16, of which waited for: 7 -> 9; matrix products, arithmetic and copies ran while one was open for 21% -> 22% of each run, Pallas kernels for 17% -> 17%
where the time goes in v9:
time: 90.4 us; the launch traced here: 90.1 us
  waiting for transfers between devices  32.3 us (36%)
  starting transfers between devices  20.4 us (23%)
  Pallas kernels  15.2 us (17%)
  local copies, waits for them, and re-layouts  11.1 us (12%)
  other arithmetic  10.3 us (11%)
    ppermute x8, waiting for transfers between devices, scatter_sum_ordered(): buf = keep + lax.ppermute(send, axis, xor_pairs(n, bit))  25.7 us
    ppermute x8, starting transfers between devices, gather_blocks(): other = lax.ppermute(buf, axis, xor_pairs(n, bit))  10.5 us
    ppermute x8, starting transfers between devices, scatter_sum_ordered(): buf = keep + lax.ppermute(send, axis, xor_pairs(n, bit))  9.88 us
    pallas_call x1, Pallas kernels, per_device(): pl.pallas_call(functools.partial(project_kernel, n_seq=n_seq, orders=orde...  8.18 us
    pallas_call x1, Pallas kernels, per_device(): pl.pallas_call(left_kernel, grid=(steps,), in_specs=[pl.BlockSpec((C, own...  7.02 us
    ppermute x8, waiting for transfers between devices, gather_blocks(): other = lax.ppermute(buf, axis, xor_pairs(n, bit))  6.61 us
    slice x1, local copies, waits for them, and re-layouts, per_device(): part_t[h]  3.99 us
    add x6, other arithmetic, scatter_sum_ordered(): buf = keep + lax.ppermute(send, axis, xor_pairs(n, bit))  3.3 us
  transfers between devices with their start and end apart: 16, of which 9 were waited for; matrix products, arithmetic and copies ran while one was open for 22% of the time, Pallas kernels for 17%

profile of v9, /device:TPU:0, one launch (start us, length us, event | category | flops | bytes accessed | tf_op | source)
XLA Modules:
  0.0 90.1 jit_solution(5121024436493845309)
XLA Ops:
  0.6 1.0 %copy.10 = bf16[64,512]{0,1:T(8,128)(2,1)S(1)} copy(bf16[64,512]{1,0:T(8,128)(2,1)} %param.5) | data formatting | bytes 131072 | tf_op args[1]
  1.6 4.1 %collective-permute-start = (bf16[1,16,16,64]{3,1,2,0:T(8,128)(2,1)S(1)}, bf16[1,16,16,64]{3,1,2,0:T(8,128)(2,1)S(1)}, u32[]{:S(2)}, u32[]{:S(2)}) collective-permute-start(bf16[1,16,16,64]{3,1,2,0:T(8,128)(2,1)S(1)} %get-tuple-element.30), channel_id=1, source_target_pairs={{0,8},{1,9},{2,10},{3,11},{4,12},{5,13},{6,14},{7,15},{8,0},{9,1},... | collective-permute-start | bytes 98312 | tf_op jit(solution)/shard_map/ppermute | solution.py:23
  5.7 0.1 collective-permute-start.4
  5.8 1.8 %copy.9 = bf16[32,32,128]{2,0,1:T(8,128)(2,1)} copy(bf16[32,32,128]{2,1,0:T(8,128)(2,1)} %bitcast.51) | data formatting | bytes 524288 | tf_op jit(solution)/shard_map/reshape | solution.py:130
  7.6 8.2 %shard_map.59 = (bf16[32,512,256]{2,1,0:T(8,128)(2,1)}, f32[2,16,16,16,64]{4,3,2,1,0:T(8,128)}) custom-call(bf16[16,256,128]{2,1,0:T(8,128)(2,1)} %p_ref.1, bf16[1024,128]{1,0:T(8,128)(2,1)} %bitcast.52, bf16[64,512]{1,0:T(8,128)(2,1)} %l_ref.1), custom_call_target="tpu_custom_call" | custom-call | flops 1610612736 | bytes 11534336 | tf_op jit(solution)/shard_map/pallas_call | solution.py:135
  15.7 4.0 %fusion.2 = (f32[1,16,16,16,64]{4,3,2,1,0:T(8,128)S(1)}, f32[1,16,16,16,64]{4,3,2,1,0:T(8,128)}) fusion(f32[2,16,16,16,64]{4,3,2,1,0:T(8,128)} %get-tuple-element.5), kind=kLoop, calls=%fused_computation.47 | loop fusion | bytes 4194304 | tf_op jit(solution)/shard_map/slice | solution.py:160
  19.7 0.0 collective-permute-done
  19.7 0.0 collective-permute-done.4
  19.8 1.8 %collective-permute-start.5 = (bf16[2,16,16,64]{3,1,2,0:T(8,128)(2,1)S(1)}, bf16[2,16,16,64]{3,1,2,0:T(8,128)(2,1)S(1)}, u32[]{:S(2)}, u32[]{:S(2)}) collective-permute-start(bf16[2,16,16,64]{3,1,2,0:T(8,128)(2,1)S(1)} %pad_maximum_fusion.8), channel_id=1, source_target_pairs={{0,2},{1,3},{2,0},{3,1},{4,6},{5,7},{6,4},{7,5},{8,10},{9,11},{10,... | collective-permute-start | bytes 196616 | tf_op jit(solution)/shard_map/ppermute | solution.py:23
  21.7 1.6 %collective-permute-start.1 = (bf16[2,16,16,64]{3,1,2,0:T(8,128)(2,1)S(1)}, bf16[2,16,16,64]{3,1,2,0:T(8,128)(2,1)S(1)}, u32[]{:S(2)}, u32[]{:S(2)}) collective-permute-start(bf16[2,16,16,64]{3,1,2,0:T(8,128)(2,1)S(1)} %pad_maximum_fusion.7), channel_id=1, source_target_pairs={{0,4},{1,5},{2,6},{3,7},{4,0},{5,1},{6,2},{7,3},{8,12},{9,13},{10,... | collective-permute-start | bytes 196616 | tf_op jit(solution)/shard_map/ppermute | solution.py:23
  23.3 1.5 %collective-permute-done.5 = bf16[2,16,16,64]{3,1,2,0:T(8,128)(2,1)S(1)} collective-permute-done((bf16[2,16,16,64]{3,1,2,0:T(8,128)(2,1)S(1)}, bf16[2,16,16,64]{3,1,2,0:T(8,128)(2,1)S(1)}, u32[]{:S(2)}, u32[]{:S(2)}) %collective-permute-start.5) | collective-permute-done | bytes 65568 | tf_op jit(solution)/shard_map/ppermute | solution.py:23
  24.9 0.1 pad_maximum_fusion.6
  24.9 1.9 %collective-permute-start.6 = (bf16[4,16,16,64]{3,1,2,0:T(8,128)(2,1)S(1)}, bf16[4,16,16,64]{3,1,2,0:T(8,128)(2,1)S(1)}, u32[]{:S(2)}, u32[]{:S(2)}) collective-permute-start(bf16[4,16,16,64]{3,1,2,0:T(8,128)(2,1)S(1)} %pad_maximum_fusion.6), channel_id=1, source_target_pairs={{0,4},{1,5},{2,6},{3,7},{4,0},{5,1},{6,2},{7,3},{8,12},{9,13},{10,... | collective-permute-start | bytes 393224 | tf_op jit(solution)/shard_map/ppermute | solution.py:23
  26.8 0.6 collective-permute-done.1
  27.5 0.1 pad_maximum_fusion.5
  27.6 0.0 copy-start
  27.6 1.0 %collective-permute-start.2 = (bf16[4,16,16,64]{3,1,2,0:T(8,128)(2,1)S(1)}, bf16[4,16,16,64]{3,1,2,0:T(8,128)(2,1)S(1)}, u32[]{:S(2)}, u32[]{:S(2)}) collective-permute-start(bf16[4,16,16,64]{3,1,2,0:T(8,128)(2,1)S(1)} %pad_maximum_fusion.5), channel_id=1, source_target_pairs={{0,2},{1,3},{2,0},{3,1},{4,6},{5,7},{6,4},{7,5},{8,10},{9,11},{10,... | collective-permute-start | bytes 393224 | tf_op jit(solution)/shard_map/ppermute | solution.py:23
  28.5 3.8 %collective-permute-done.6 = bf16[4,16,16,64]{3,1,2,0:T(8,128)(2,1)S(1)} collective-permute-done((bf16[4,16,16,64]{3,1,2,0:T(8,128)(2,1)S(1)}, bf16[4,16,16,64]{3,1,2,0:T(8,128)(2,1)S(1)}, u32[]{:S(2)}, u32[]{:S(2)}) %collective-permute-start.6) | collective-permute-done | bytes 131104 | tf_op jit(solution)/shard_map/ppermute | solution.py:23
  32.3 0.1 broadcast_select_fusion.5
  32.4 0.9 %pad_maximum_fusion.4 = bf16[8,16,16,64]{3,1,2,0:T(8,128)(2,1)} fusion(bf16[4,16,16,64]{3,1,2,0:T(8,128)(2,1)S(1)} %get-tuple-element.19, bf16[4,16,16,64]{3,1,2,0:T(8,128)(2,1)S(1)} %get-tuple-element.18), kind=kLoop, calls=%fused_computation.8 | loop fusion | flops 131072 | bytes 524288 | tf_op jit(solution)/shard_map/concatenate | solution.py:27
  33.3 0.0 collective-permute-start.7
  33.3 0.7 collective-permute-done.2
  34.0 0.1 broadcast_select_fusion.7
  34.1 0.9 %pad_maximum_fusion.3 = bf16[8,16,16,64]{3,1,2,0:T(8,128)(2,1)} fusion(bf16[4,16,16,64]{3,1,2,0:T(8,128)(2,1)S(1)} %get-tuple-element.17, bf16[4,16,16,64]{3,1,2,0:T(8,128)(2,1)S(1)} %get-tuple-element.16), kind=kLoop, calls=%fused_computation.7 | loop fusion | flops 131072 | bytes 524288 | tf_op jit(solution)/shard_map/concatenate | solution.py:27
  35.0 0.0 collective-permute-start.3
  35.0 0.0 copy-done
  35.0 1.0 %dynamic-slice_bitcast_fusion = f32[8,16,16,64]{3,2,1,0:T(8,128)} fusion(f32[1,16,16,16,64]{4,3,2,1,0:T(8,128)S(1)} %copy-done, s32[]{:T(128)S(6)} %select_n.147), kind=kLoop, calls=%fused_computation.5 | loop fusion | bytes 1048580 | tf_op jit(solution)/shard_map/dynamic_slice | solution.py:60
  36.1 0.5 collective-permute-start.12
  36.6 1.1 %dynamic-slice_bitcast_fusion.1 = f32[8,16,16,64]{3,2,1,0:T(8,128)} fusion(f32[1,16,16,16,64]{4,3,2,1,0:T(8,128)S(1)} %get-tuple-element.10, s32[]{:T(128)S(6)} %select_n.147), kind=kLoop, calls=%fused_computation.6 | loop fusion | bytes 1048580 | tf_op jit(solution)/shard_map/dynamic_slice | solution.py:60
  37.6 0.0 collective-permute-start.8
  37.6 0.0 collective-permute-done.7
  37.6 0.0 collective-permute-done.3
  37.6 1.5 %broadcast_select_fusion.1 = (bf16[8,16,16,64]{3,1,2,0:T(8,128)(2,1)S(1)}, bf16[8,16,16,64]{3,1,2,0:T(8,128)(2,1)S(1)}, bf16[8,16,16,64]{3,1,2,0:T(8,128)(2,1)S(1)}, bf16[8,16,16,64]{3,1,2,0:T(8,128)(2,1)S(1)}) fusion(bf16[8,16,16,64]{3,1,2,0:T(8,128)(2,1)} %collective-permute-done.7, pred[]{:T(512)S(6)} %eq.8, ...), kind=kLoop, calls=%fused_computation.12 | loop fusion | flops 786432 | bytes 2097153 | tf_op jit(solution)/shard_map/jit(_where)/select_n | solution.py:25
  39.1 0.2 pad_maximum_fusion.2
  39.3 0.3 copy.14
  39.6 0.2 pad_maximum_fusion.1
  39.8 0.3 copy.12
  40.1 1.8 %pad_maximum_fusion.rt_ref = bf16[16,32,16,64]{3,2,1,0:T(8,128)(2,1)} fusion(bf16[16,16,16,64]{3,2,1,0:T(8,128)(2,1)S(1)} %bitcast.46, bf16[16,16,16,64]{3,2,1,0:T(8,128)(2,1)S(1)} %bitcast.47), kind=kLoop, calls=%fused_computation | loop fusion | flops 524288 | bytes 2097152 | tf_op jit(solution)/shard_map/concatenate | solution.py:122
  41.9 7.0 %shard_map.60 = f32[512,64]{1,0:T(8,128)} custom-call(bf16[32,512,256]{2,1,0:T(8,128)(2,1)} %get-tuple-element.4.gm_ref, bf16[16,32,16,64]{3,2,1,0:T(8,128)(2,1)} %pad_maximum_fusion.rt_ref), custom_call_target="tpu_custom_call" | custom-call | flops 536870912 | bytes 9437184 | tf_op jit(solution)/shard_map/pallas_call | solution.py:164
  49.0 1.0 %convert_bitcast_fusion = bf16[64,512]{0,1:T(8,128)(2,1)S(1)} fusion(f32[512,64]{1,0:T(8,128)} %shard_map.60), kind=kLoop, calls=%fused_computation.28 | loop fusion | flops 32768 | bytes 196608 | tf_op jit(solution)/shard_map/convert_element_type | solution.py:180
  49.9 0.7 copy.16
  50.6 0.0 collective-permute-done.12
  50.6 1.7 %bitcast_add_fusion = f32[8,16,16,64]{3,2,1,0:T(8,128)S(1)} fusion(f32[8,16,16,64]{3,2,1,0:T(8,128)} %collective-permute-done.12, f32[1,16,16,16,64]{4,3,2,1,0:T(8,128)} %get-tuple-element.11, s32[]{:T(128)S(6)} %select_n.146), kind=kLoop, calls=%fused_computation.3 | loop fusion | flops 131072 | bytes 1572868 | tf_op jit(solution)/shard_map/add | solution.py:61
  52.4 1.6 %collective-permute-start.13 = (f32[4,16,16,64]{3,2,1,0:T(8,128)S(1)}, f32[4,16,16,64]{3,2,1,0:T(8,128)S(1)}, u32[]{:S(2)}, u32[]{:S(2)}) collective-permute-start(f32[4,16,16,64]{3,2,1,0:T(8,128)S(1)} %constant_dynamic-slice_fusion.2), channel_id=1, source_target_pairs={{0,4},{1,5},{2,6},{3,7},{4,0},{5,1},{6,2},{7,3},{8,12},{9,13},{10,... | collective-permute-start | bytes 786440 | tf_op jit(solution)/shard_map/ppermute | solution.py:61
  54.1 0.0 collective-permute-done.8
  54.1 1.4 %bitcast_add_fusion.1 = f32[8,16,16,64]{3,2,1,0:T(8,128)S(1)} fusion(f32[8,16,16,64]{3,2,1,0:T(8,128)} %collective-permute-done.8, f32[1,16,16,16,64]{4,3,2,1,0:T(8,128)S(1)} %get-tuple-element.10, s32[]{:T(128)S(6)} %select_n.146), kind=kLoop, calls=%fused_computation.4 | loop fusion | flops 131072 | bytes 1572868 | tf_op jit(solution)/shard_map/add | solution.py:61
  55.5 0.7 collective-permute-start.9
  56.2 10.6 %collective-permute-done.13 = f32[4,16,16,64]{3,2,1,0:T(8,128)S(1)} collective-permute-done((f32[4,16,16,64]{3,2,1,0:T(8,128)S(1)}, f32[4,16,16,64]{3,2,1,0:T(8,128)S(1)}, u32[]{:S(2)}, u32[]{:S(2)}) %collective-permute-start.13) | collective-permute-done | bytes 262176 | tf_op jit(solution)/shard_map/ppermute | solution.py:61
  66.8 0.1 dynamic-slice_add_fusion
  66.9 1.0 %collective-permute-start.14 = (f32[2,16,16,64]{3,2,1,0:T(8,128)S(1)}, f32[2,16,16,64]{3,2,1,0:T(8,128)S(1)}, u32[]{:S(2)}, u32[]{:S(2)}) collective-permute-start(f32[2,16,16,64]{3,2,1,0:T(8,128)S(1)} %constant_dynamic-slice_fusion.1), channel_id=1, source_target_pairs={{0,2},{1,3},{2,0},{3,1},{4,6},{5,7},{6,4},{7,5},{8,10},{9,11},{10,... | collective-permute-start | bytes 393224 | tf_op jit(solution)/shard_map/ppermute | solution.py:61
  67.9 2.0 %collective-permute-done.9 = f32[4,16,16,64]{3,2,1,0:T(8,128)S(1)} collective-permute-done((f32[4,16,16,64]{3,2,1,0:T(8,128)S(1)}, f32[4,16,16,64]{3,2,1,0:T(8,128)S(1)}, u32[]{:S(2)}, u32[]{:S(2)}) %collective-permute-start.9) | collective-permute-done | bytes 262176 | tf_op jit(solution)/shard_map/ppermute | solution.py:61
  69.9 0.1 dynamic-slice_add_fusion.1
  70.0 0.3 collective-permute-start.10
  70.2 5.0 %collective-permute-done.14 = f32[2,16,16,64]{3,2,1,0:T(8,128)S(1)} collective-permute-done((f32[2,16,16,64]{3,2,1,0:T(8,128)S(1)}, f32[2,16,16,64]{3,2,1,0:T(8,128)S(1)}, u32[]{:S(2)}, u32[]{:S(2)}) %collective-permute-start.14) | collective-permute-done | bytes 131104 | tf_op jit(solution)/shard_map/ppermute | solution.py:61
  75.3 2.7 %collective-permute-start.15 = (f32[1,16,16,64]{3,2,1,0:T(8,128)S(1)}, f32[1,16,16,64]{3,2,1,0:T(8,128)S(1)}, u32[]{:S(2)}, u32[]{:S(2)}) collective-permute-start(f32[1,16,16,64]{3,2,1,0:T(8,128)S(1)} %constant_dynamic-slice_fusion), channel_id=1, source_target_pairs={{0,8},{1,9},{2,10},{3,11},{4,12},{5,13},{6,14},{7,15},{8,0},{9,1},... | collective-permute-start | bytes 196616 | tf_op jit(solution)/shard_map/ppermute | solution.py:61
  78.0 0.0 collective-permute-done.10
  78.1 3.1 %collective-permute-start.11 = (f32[1,16,16,64]{3,2,1,0:T(8,128)S(1)}, f32[1,16,16,64]{3,2,1,0:T(8,128)S(1)}, u32[]{:S(2)}, u32[]{:S(2)}) collective-permute-start(f32[1,16,16,64]{3,2,1,0:T(8,128)S(1)} %constant_dynamic-slice_fusion.3), channel_id=1, source_target_pairs={{0,8},{1,9},{2,10},{3,11},{4,12},{5,13},{6,14},{7,15},{8,0},{9,1},... | collective-permute-start | bytes 196616 | tf_op jit(solution)/shard_map/ppermute | solution.py:61
  81.2 6.5 %collective-permute-done.15 = f32[1,16,16,64]{3,2,1,0:T(8,128)S(1)} collective-permute-done((f32[1,16,16,64]{3,2,1,0:T(8,128)S(1)}, f32[1,16,16,64]{3,2,1,0:T(8,128)S(1)}, u32[]{:S(2)}, u32[]{:S(2)}) %collective-permute-start.15) | collective-permute-done | bytes 65568 | tf_op jit(solution)/shard_map/ppermute | solution.py:61
  87.7 1.6 %collective-permute-done.11 = f32[1,16,16,64]{3,2,1,0:T(8,128)S(1)} collective-permute-done((f32[1,16,16,64]{3,2,1,0:T(8,128)S(1)}, f32[1,16,16,64]{3,2,1,0:T(8,128)S(1)}, u32[]{:S(2)}, u32[]{:S(2)}) %collective-permute-start.11) | collective-permute-done | bytes 65568 | tf_op jit(solution)/shard_map/ppermute | solution.py:61
  89.4 0.7 copy.17
  (18 shorter events, 0.5 us)
Async XLA Ops:
  1.6 18.1 %collective-permute-start = (bf16[1,16,16,64]{3,1,2,0:T(8,128)(2,1)S(1)}, bf16[1,16,16,64]{3,1,2,0:T(8,128)(2,1)S(1)}, u32[]{:S(2)}, u32[]{:S(2)}) collective-permute-start(bf16[1,16,16,64]{3,1,2,0:T(8,128)(2,1)S(1)} %get-tuple-element.30), channel_id=1, source_target_pairs={{0,8},{1,9},{2,10},{3,11},{4,12},{5,13},{6,14},{7,15},{8,0},{9,1},... | collective-permute-start | bytes 98312 | tf_op jit(solution)/shard_map/ppermute | solution.py:23
  5.7 14.0 %collective-permute-start.4 = (bf16[1,16,16,64]{3,1,2,0:T(8,128)(2,1)S(1)}, bf16[1,16,16,64]{3,1,2,0:T(8,128)(2,1)S(1)}, u32[]{:S(2)}, u32[]{:S(2)}) collective-permute-start(bf16[1,16,16,64]{3,1,2,0:T(8,128)(2,1)S(1)} %get-tuple-element.31), channel_id=1, source_target_pairs={{0,8},{1,9},{2,10},{3,11},{4,12},{5,13},{6,14},{7,15},{8,0},{9,1},... | collective-permute-start | bytes 98312 | tf_op jit(solution)/shard_map/ppermute | solution.py:23
  19.8 5.0 %collective-permute-start.5 = (bf16[2,16,16,64]{3,1,2,0:T(8,128)(2,1)S(1)}, bf16[2,16,16,64]{3,1,2,0:T(8,128)(2,1)S(1)}, u32[]{:S(2)}, u32[]{:S(2)}) collective-permute-start(bf16[2,16,16,64]{3,1,2,0:T(8,128)(2,1)S(1)} %pad_maximum_fusion.8), channel_id=1, source_target_pairs={{0,2},{1,3},{2,0},{3,1},{4,6},{5,7},{6,4},{7,5},{8,10},{9,11},{10,... | collective-permute-start | bytes 196616 | tf_op jit(solution)/shard_map/ppermute | solution.py:23
  21.7 5.8 %collective-permute-start.1 = (bf16[2,16,16,64]{3,1,2,0:T(8,128)(2,1)S(1)}, bf16[2,16,16,64]{3,1,2,0:T(8,128)(2,1)S(1)}, u32[]{:S(2)}, u32[]{:S(2)}) collective-permute-start(bf16[2,16,16,64]{3,1,2,0:T(8,128)(2,1)S(1)} %pad_maximum_fusion.7), channel_id=1, source_target_pairs={{0,4},{1,5},{2,6},{3,7},{4,0},{5,1},{6,2},{7,3},{8,12},{9,13},{10,... | collective-permute-start | bytes 196616 | tf_op jit(solution)/shard_map/ppermute | solution.py:23
  24.9 7.4 %collective-permute-start.6 = (bf16[4,16,16,64]{3,1,2,0:T(8,128)(2,1)S(1)}, bf16[4,16,16,64]{3,1,2,0:T(8,128)(2,1)S(1)}, u32[]{:S(2)}, u32[]{:S(2)}) collective-permute-start(bf16[4,16,16,64]{3,1,2,0:T(8,128)(2,1)S(1)} %pad_maximum_fusion.6), channel_id=1, source_target_pairs={{0,4},{1,5},{2,6},{3,7},{4,0},{5,1},{6,2},{7,3},{8,12},{9,13},{10,... | collective-permute-start | bytes 393224 | tf_op jit(solution)/shard_map/ppermute | solution.py:23
  27.6 7.5 %copy-start = (f32[1,16,16,16,64]{4,3,2,1,0:T(8,128)S(1)}, f32[1,16,16,16,64]{4,3,2,1,0:T(8,128)}, u32[]{:S(2)}) copy-start(f32[1,16,16,16,64]{4,3,2,1,0:T(8,128)} %get-tuple-element.11) | copy-start | bytes 3145732
  27.6 6.4 %collective-permute-start.2 = (bf16[4,16,16,64]{3,1,2,0:T(8,128)(2,1)S(1)}, bf16[4,16,16,64]{3,1,2,0:T(8,128)(2,1)S(1)}, u32[]{:S(2)}, u32[]{:S(2)}) collective-permute-start(bf16[4,16,16,64]{3,1,2,0:T(8,128)(2,1)S(1)} %pad_maximum_fusion.5), channel_id=1, source_target_pairs={{0,2},{1,3},{2,0},{3,1},{4,6},{5,7},{6,4},{7,5},{8,10},{9,11},{10,... | collective-permute-start | bytes 393224 | tf_op jit(solution)/shard_map/ppermute | solution.py:23
  33.3 4.3 %collective-permute-start.7 = (bf16[8,16,16,64]{3,1,2,0:T(8,128)(2,1)}, bf16[8,16,16,64]{3,1,2,0:T(8,128)(2,1)}, u32[]{:S(2)}, u32[]{:S(2)}) collective-permute-start(bf16[8,16,16,64]{3,1,2,0:T(8,128)(2,1)} %pad_maximum_fusion.4), channel_id=1, source_target_pairs={{0,1},{1,0},{2,3},{3,2},{4,5},{5,4},{6,7},{7,6},{8,9},{9,8},{10,11... | collective-permute-start | bytes 786440 | tf_op jit(solution)/shard_map/ppermute | solution.py:23
  35.0 2.6 %collective-permute-start.3 = (bf16[8,16,16,64]{3,1,2,0:T(8,128)(2,1)}, bf16[8,16,16,64]{3,1,2,0:T(8,128)(2,1)}, u32[]{:S(2)}, u32[]{:S(2)}) collective-permute-start(bf16[8,16,16,64]{3,1,2,0:T(8,128)(2,1)} %pad_maximum_fusion.3), channel_id=1, source_target_pairs={{0,1},{1,0},{2,3},{3,2},{4,5},{5,4},{6,7},{7,6},{8,9},{9,8},{10,11... | collective-permute-start | bytes 786440 | tf_op jit(solution)/shard_map/ppermute | solution.py:23
  36.1 14.6 %collective-permute-start.12 = (f32[8,16,16,64]{3,2,1,0:T(8,128)}, f32[8,16,16,64]{3,2,1,0:T(8,128)}, u32[]{:S(2)}, u32[]{:S(2)}) collective-permute-start(f32[8,16,16,64]{3,2,1,0:T(8,128)} %dynamic-slice_bitcast_fusion), channel_id=1, source_target_pairs={{0,1},{1,0},{2,3},{3,2},{4,5},{5,4},{6,7},{7,6},{8,9},{9,8},{10,11... | collective-permute-start | bytes 1572872 | tf_op jit(solution)/shard_map/ppermute | solution.py:61
  37.6 16.4 %collective-permute-start.8 = (f32[8,16,16,64]{3,2,1,0:T(8,128)}, f32[8,16,16,64]{3,2,1,0:T(8,128)}, u32[]{:S(2)}, u32[]{:S(2)}) collective-permute-start(f32[8,16,16,64]{3,2,1,0:T(8,128)} %dynamic-slice_bitcast_fusion.1), channel_id=1, source_target_pairs={{0,1},{1,0},{2,3},{3,2},{4,5},{5,4},{6,7},{7,6},{8,9},{9,8},{10,11... | collective-permute-start | bytes 1572872 | tf_op jit(solution)/shard_map/ppermute | solution.py:61
  52.4 14.4 %collective-permute-start.13 = (f32[4,16,16,64]{3,2,1,0:T(8,128)S(1)}, f32[4,16,16,64]{3,2,1,0:T(8,128)S(1)}, u32[]{:S(2)}, u32[]{:S(2)}) collective-permute-start(f32[4,16,16,64]{3,2,1,0:T(8,128)S(1)} %constant_dynamic-slice_fusion.2), channel_id=1, source_target_pairs={{0,4},{1,5},{2,6},{3,7},{4,0},{5,1},{6,2},{7,3},{8,12},{9,13},{10,... | collective-permute-start | bytes 786440 | tf_op jit(solution)/shard_map/ppermute | solution.py:61
  55.5 14.4 %collective-permute-start.9 = (f32[4,16,16,64]{3,2,1,0:T(8,128)S(1)}, f32[4,16,16,64]{3,2,1,0:T(8,128)S(1)}, u32[]{:S(2)}, u32[]{:S(2)}) collective-permute-start(f32[4,16,16,64]{3,2,1,0:T(8,128)S(1)} %constant_dynamic-slice_fusion.5), channel_id=1, source_target_pairs={{0,2},{1,3},{2,0},{3,1},{4,6},{5,7},{6,4},{7,5},{8,10},{9,11},{10,... | collective-permute-start | bytes 786440 | tf_op jit(solution)/shard_map/ppermute | solution.py:61
  66.9 8.3 %collective-permute-start.14 = (f32[2,16,16,64]{3,2,1,0:T(8,128)S(1)}, f32[2,16,16,64]{3,2,1,0:T(8,128)S(1)}, u32[]{:S(2)}, u32[]{:S(2)}) collective-permute-start(f32[2,16,16,64]{3,2,1,0:T(8,128)S(1)} %constant_dynamic-slice_fusion.1), channel_id=1, source_target_pairs={{0,2},{1,3},{2,0},{3,1},{4,6},{5,7},{6,4},{7,5},{8,10},{9,11},{10,... | collective-permute-start | bytes 393224 | tf_op jit(solution)/shard_map/ppermute | solution.py:61
  70.0 8.0 %collective-permute-start.10 = (f32[2,16,16,64]{3,2,1,0:T(8,128)S(1)}, f32[2,16,16,64]{3,2,1,0:T(8,128)S(1)}, u32[]{:S(2)}, u32[]{:S(2)}) collective-permute-start(f32[2,16,16,64]{3,2,1,0:T(8,128)S(1)} %constant_dynamic-slice_fusion.4), channel_id=1, source_target_pairs={{0,4},{1,5},{2,6},{3,7},{4,0},{5,1},{6,2},{7,3},{8,12},{9,13},{10,... | collective-permute-start | bytes 393224 | tf_op jit(solution)/shard_map/ppermute | solution.py:61
  75.3 12.3 %collective-permute-start.15 = (f32[1,16,16,64]{3,2,1,0:T(8,128)S(1)}, f32[1,16,16,64]{3,2,1,0:T(8,128)S(1)}, u32[]{:S(2)}, u32[]{:S(2)}) collective-permute-start(f32[1,16,16,64]{3,2,1,0:T(8,128)S(1)} %constant_dynamic-slice_fusion), channel_id=1, source_target_pairs={{0,8},{1,9},{2,10},{3,11},{4,12},{5,13},{6,14},{7,15},{8,0},{9,1},... | collective-permute-start | bytes 196616 | tf_op jit(solution)/shard_map/ppermute | solution.py:61
  78.1 11.2 %collective-permute-start.11 = (f32[1,16,16,64]{3,2,1,0:T(8,128)S(1)}, f32[1,16,16,64]{3,2,1,0:T(8,128)S(1)}, u32[]{:S(2)}, u32[]{:S(2)}) collective-permute-start(f32[1,16,16,64]{3,2,1,0:T(8,128)S(1)} %constant_dynamic-slice_fusion.3), channel_id=1, source_target_pairs={{0,8},{1,9},{2,10},{3,11},{4,12},{5,13},{6,14},{7,15},{8,0},{9,1},... | collective-permute-start | bytes 196616 | tf_op jit(solution)/shard_map/ppermute | solution.py:61

commit v10 on v9

--- a/solution.py
+++ b/solution.py
@@ -47,6 +47,34 @@
         buf = keep + lax.ppermute(send, axis, xor_pairs(n, bit))
         left.pop(t)
     return buf
+
+
+def gather_step(state, axis, n, bit):
+    buf, done = state
+    me = lax.axis_index(axis)
+    other = lax.ppermute(buf, axis, xor_pairs(n, bit))
+    mine = (me >> bit) & 1
+    low = jnp.where(mine == 0, buf, other)
+    high = jnp.where(mine == 0, other, buf)
+    return jnp.concatenate([low, high], 0), [bit] + done
+
+
+def gather_finish(state, n, shape):
+    buf, done = state
+    k = len(done)
+    buf = buf.reshape((2,) * k + shape)
+    order = sorted(range(k), key=lambda t: -done[t])
+    buf = buf.transpose(order + list(range(k, k + len(shape))))
+    return buf.reshape((n,) + shape)
+
+
+def scatter_step(buf, axis, n, bit):
+    me = lax.axis_index(axis)
+    half = buf.shape[0] // 2
+    mine = (me >> bit) & 1
+    keep = lax.dynamic_slice_in_dim(buf, mine * half, half, 0)
+    send = lax.dynamic_slice_in_dim(buf, (1 - mine) * half, half, 0)
+    return keep + lax.ppermute(send, axis, xor_pairs(n, bit))
 
 
 def scatter_sum_ordered(x, axis, bits):
@@ -119,19 +147,17 @@
     per_dev = right_proj.shape[1] // C
 
     right_t = right_proj.reshape(n_seq, per_dev, C).transpose(2, 1, 0)
-    right_blocks = jnp.concatenate(
-        [
-            gather_blocks(right_t[:C // 2], "row", n, bits[::-1]),
-            gather_blocks(right_t[C // 2:], "row", n, (bits[:1] + bits[1:3][::-1] + bits[3:])[::-1]),
-        ],
-        1,
-    )
-
-    weight_ec = out_weight.reshape(C, C, p_size).transpose(1, 0, 2).reshape(C * C, p_size)
-
     swapped = bits[:1] + bits[1:3][::-1] + bits[3:]
     orders = (tuple(bits), tuple(swapped))
     half = C // len(orders)
+    early = 2
+    gathers = [(right_t[h * half:(h + 1) * half][None], []) for h in range(len(orders))]
+    for h in range(len(orders)):
+        for bit in orders[h][::-1][:early]:
+            gathers[h] = gather_step(gathers[h], "row", n, bit)
+
+    weight_ec = out_weight.reshape(C, C, p_size).transpose(1, 0, 2).reshape(C * C, p_size)
+
     grad_m, part_t = pl.pallas_call(
         functools.partial(project_kernel, n_seq=n_seq, orders=orders),
         grid=(steps,),
@@ -156,9 +182,20 @@
         ),
     )(pair_cot, weight_ec, left_proj)
 
-    summed = jnp.concatenate(
-        [scatter_sum_ordered(part_t[h], "row", list(orders[h])) for h in range(len(orders))], 0
+    scatters = [scatter_step(part_t[h], "row", n, orders[h][0]) for h in range(len(orders))]
+    bufs = [g[0] for g in gathers]
+    scatters, bufs = lax.optimization_barrier((scatters, bufs))
+    gathers = [(bufs[h], gathers[h][1]) for h in range(len(orders))]
+    for h in range(len(orders)):
+        for bit in orders[h][::-1][early:]:
+            gathers[h] = gather_step(gathers[h], "row", n, bit)
+    right_blocks = jnp.concatenate(
+        [gather_finish(gathers[h], n, right_t[:half].shape) for h in range(len(orders))], 1
     )
+    for h in range(len(orders)):
+        for bit in orders[h][1:]:
+            scatters[h] = scatter_step(scatters[h], "row", n, bit)
+    summed = jnp.concatenate([scatters[h][0] for h in range(len(orders))], 0)
     grad_right = summed.transpose(2, 1, 0).reshape(n_seq, per_dev * C).astype(jnp.bfloat16)
 
     left_t = pl.pallas_call(

time: 90.4 us -> 79 us (0.87)
  waiting for transfers between devices: 32.3 us -> 22.5 us
  starting transfers between devices: 20.4 us -> 17.9 us
    ppermute x16, waiting for transfers between devices: 32.3 us -> 22.5 us  [the longest x8 12.9 us: scatter_step(): return keep + lax.ppermute(send, axis, xor_pairs(n, bit))]
    ppermute x16, starting transfers between devices: 20.4 us -> 17.9 us  [the longest x8 9.82 us: gather_step(): other = lax.ppermute(buf, axis, xor_pairs(n, bit))]
    unnamed x5 -> x7, local copies, waits for them, and re-layouts: 2.42 us -> 3.04 us
  transfers between devices with their start and end apart: 16 -> 16, of which waited for: 9 -> 7; matrix products, arithmetic and copies ran while one was open for 22% -> 23% of each run, Pallas kernels for 17% -> 19%
where the time goes in v10:
time: 79 us; the launch traced here: 78.6 us
  waiting for transfers between devices  22.5 us (28%)
  starting transfers between devices  17.9 us (23%)
  Pallas kernels  15.2 us (19%)
  local copies, waits for them, and re-layouts  11.9 us (15%)
  other arithmetic  10.1 us (13%)
  between operations  0.93 us (1%)
    ppermute x8, waiting for transfers between devices, scatter_step(): return keep + lax.ppermute(send, axis, xor_pairs(n, bit))  12.9 us
    ppermute x8, starting transfers between devices, gather_step(): other = lax.ppermute(buf, axis, xor_pairs(n, bit))  9.82 us
    ppermute x8, waiting for transfers between devices, gather_step(): other = lax.ppermute(buf, axis, xor_pairs(n, bit))  9.6 us
    pallas_call x1, Pallas kernels, per_device(): pl.pallas_call(functools.partial(project_kernel, n_seq=n_seq, orders=orde...  8.17 us
    ppermute x8, starting transfers between devices, scatter_step(): return keep + lax.ppermute(send, axis, xor_pairs(n, bit))  8.03 us
    pallas_call x1, Pallas kernels, per_device(): pl.pallas_call(left_kernel, grid=(steps,), in_specs=[pl.BlockSpec((C, own...  7 us
    slice x1, local copies, waits for them, and re-layouts, per_device(): part_t[h]  3.99 us
    unnamed x7, local copies, waits for them, and re-layouts  3.04 us
  transfers between devices with their start and end apart: 16, of which 7 were waited for; matrix products, arithmetic and copies ran while one was open for 23% of the time, Pallas kernels for 19%

profile of v10, /device:TPU:0, one launch (start us, length us, event | category | flops | bytes accessed | tf_op | source)
XLA Modules:
  0.0 78.6 jit_solution(12315718690151439561)
XLA Ops:
  0.6 1.0 %copy.10 = bf16[64,512]{0,1:T(8,128)(2,1)S(1)} copy(bf16[64,512]{1,0:T(8,128)(2,1)} %param.5) | data formatting | bytes 131072 | tf_op args[1]
  1.6 4.1 %collective-permute-start.4 = (bf16[1,16,16,64]{3,1,2,0:T(8,128)(2,1)S(1)}, bf16[1,16,16,64]{3,1,2,0:T(8,128)(2,1)S(1)}, u32[]{:S(2)}, u32[]{:S(2)}) collective-permute-start(bf16[1,16,16,64]{3,1,2,0:T(8,128)(2,1)S(1)} %get-tuple-element.38), channel_id=1, source_target_pairs={{0,8},{1,9},{2,10},{3,11},{4,12},{5,13},{6,14},{7,15},{8,0},{9,1},... | collective-permute-start | bytes 98312 | tf_op jit(solution)/shard_map/ppermute | solution.py:55
  5.7 0.1 collective-permute-start.2
  5.8 1.8 %copy.9 = bf16[32,32,128]{2,0,1:T(8,128)(2,1)} copy(bf16[32,32,128]{2,1,0:T(8,128)(2,1)} %bitcast.51) | data formatting | bytes 524288 | tf_op jit(solution)/shard_map/reshape | solution.py:159
  7.6 8.2 %shard_map.59 = (bf16[32,512,256]{2,1,0:T(8,128)(2,1)}, f32[2,16,16,16,64]{4,3,2,1,0:T(8,128)}) custom-call(bf16[16,256,128]{2,1,0:T(8,128)(2,1)} %p_ref.1, bf16[1024,128]{1,0:T(8,128)(2,1)} %bitcast.52, bf16[64,512]{1,0:T(8,128)(2,1)} %l_ref.1), custom_call_target="tpu_custom_call" | custom-call | flops 1610612736 | bytes 11534336 | tf_op jit(solution)/shard_map/pallas_call | solution.py:161
  15.7 4.0 %fusion.2 = (f32[1,16,16,16,64]{4,3,2,1,0:T(8,128)S(1)}, f32[1,16,16,16,64]{4,3,2,1,0:T(8,128)}) fusion(f32[2,16,16,16,64]{4,3,2,1,0:T(8,128)} %get-tuple-element.9), kind=kLoop, calls=%fused_computation.47 | loop fusion | bytes 4194304 | tf_op jit(solution)/shard_map/slice | solution.py:185
  19.7 1.3 %dynamic-slice_bitcast_fusion.1 = f32[8,16,16,64]{3,2,1,0:T(8,128)S(1)} fusion(f32[1,16,16,16,64]{4,3,2,1,0:T(8,128)} %get-tuple-element.19, s32[]{:T(128)S(6)} %select_n.127), kind=kLoop, calls=%fused_computation.6 | loop fusion | bytes 1048580 | tf_op jit(solution)/shard_map/dynamic_slice | solution.py:76
  21.0 0.1 collective-permute-start
  21.1 0.0 collective-permute-done.4
  21.1 0.0 copy-start.1
  21.2 0.6 copy-done.1
  21.8 0.0 collective-permute-done.2
  21.8 0.9 %broadcast_select_fusion.13 = (bf16[1,16,16,64]{3,1,2,0:T(8,128)(2,1)S(1)}, bf16[1,16,16,64]{3,1,2,0:T(8,128)(2,1)S(1)}, bf16[1,16,16,64]{3,1,2,0:T(8,128)(2,1)S(1)}, bf16[1,16,16,64]{3,1,2,0:T(8,128)(2,1)S(1)}) fusion(bf16[1,16,16,64]{3,1,2,0:T(8,128)(2,1)} %copy-done.1, pred[]{:T(512)S(6)} %eq.11, bf16[32,16,64]{2,0,1:T(8,128)(2,1)S(1)} %bitcast.49, ...), kind=kLoop, calls=%fused_computation.38 | loop fusion | flops 65536 | bytes 262145 | tf_op jit(solution)/shard_map/jit(_where)/select_n | solution.py:57
  22.7 0.7 pad_maximum_fusion.8
  23.4 1.8 %collective-permute-start.5 = (bf16[2,16,16,64]{3,1,2,0:T(8,128)(2,1)}, bf16[2,16,16,64]{3,1,2,0:T(8,128)(2,1)S(1)}, u32[]{:S(2)}, u32[]{:S(2)}) collective-permute-start(bf16[2,16,16,64]{3,1,2,0:T(8,128)(2,1)} %pad_maximum_fusion.8), channel_id=1, source_target_pairs={{0,2},{1,3},{2,0},{3,1},{4,6},{5,7},{6,4},{7,5},{8,10},{9,11},{10,... | collective-permute-start | bytes 196616 | tf_op jit(solution)/shard_map/ppermute | solution.py:55
  25.1 0.7 pad_maximum_fusion.7
  25.8 1.6 %collective-permute-start.3 = (bf16[2,16,16,64]{3,1,2,0:T(8,128)(2,1)}, bf16[2,16,16,64]{3,1,2,0:T(8,128)(2,1)}, u32[]{:S(2)}, u32[]{:S(2)}) collective-permute-start(bf16[2,16,16,64]{3,1,2,0:T(8,128)(2,1)} %pad_maximum_fusion.7), channel_id=1, source_target_pairs={{0,4},{1,5},{2,6},{3,7},{4,0},{5,1},{6,2},{7,3},{8,12},{9,13},{10,... | collective-permute-start | bytes 196616 | tf_op jit(solution)/shard_map/ppermute | solution.py:55
  27.4 1.1 %dynamic-slice_bitcast_fusion = f32[8,16,16,64]{3,2,1,0:T(8,128)} fusion(f32[1,16,16,16,64]{4,3,2,1,0:T(8,128)S(1)} %get-tuple-element.18, s32[]{:T(128)S(6)} %select_n.127), kind=kLoop, calls=%fused_computation.5 | loop fusion | bytes 1048580 | tf_op jit(solution)/shard_map/dynamic_slice | solution.py:76
  28.5 0.0 collective-permute-start.1
  28.5 1.0 %collective-permute-done.5 = bf16[2,16,16,64]{3,1,2,0:T(8,128)(2,1)S(1)} collective-permute-done((bf16[2,16,16,64]{3,1,2,0:T(8,128)(2,1)}, bf16[2,16,16,64]{3,1,2,0:T(8,128)(2,1)S(1)}, u32[]{:S(2)}, u32[]{:S(2)}) %collective-permute-start.5) | collective-permute-done | bytes 65568 | tf_op jit(solution)/shard_map/ppermute | solution.py:55
  29.5 2.2 %collective-permute-done.3 = bf16[2,16,16,64]{3,1,2,0:T(8,128)(2,1)} collective-permute-done((bf16[2,16,16,64]{3,1,2,0:T(8,128)(2,1)}, bf16[2,16,16,64]{3,1,2,0:T(8,128)(2,1)}, u32[]{:S(2)}, u32[]{:S(2)}) %collective-permute-start.3) | collective-permute-done | bytes 65568 | tf_op jit(solution)/shard_map/ppermute | solution.py:55
  31.7 1.0 %broadcast_select_fusion.9 = (bf16[2,16,16,64]{3,1,2,0:T(8,128)(2,1)S(1)}, bf16[2,16,16,64]{3,1,2,0:T(8,128)(2,1)S(1)}, bf16[2,16,16,64]{3,1,2,0:T(8,128)(2,1)S(1)}, bf16[2,16,16,64]{3,1,2,0:T(8,128)(2,1)S(1)}) fusion(bf16[2,16,16,64]{3,1,2,0:T(8,128)(2,1)S(1)} %collective-permute-done.5, pred[]{:T(512)S(6)} %eq.9, ...), kind=kLoop, calls=%fused_computation.30 | loop fusion | flops 196608 | bytes 524290 | tf_op jit(solution)/shard_map/jit(_where)/select_n | solution.py:57
  32.7 0.1 pad_maximum_fusion.5
  32.8 0.1 pad_maximum_fusion.6
  32.8 0.0 collective-permute-done
  32.9 0.0 copy-done
  32.9 1.4 %bitcast_add_fusion.1 = f32[8,16,16,64]{3,2,1,0:T(8,128)S(1)} fusion(f32[8,16,16,64]{3,2,1,0:T(8,128)} %collective-permute-done, f32[1,16,16,16,64]{4,3,2,1,0:T(8,128)S(1)} %copy-done, s32[]{:T(128)S(6)} %select_n.126), kind=kLoop, calls=%fused_computation.4 | loop fusion | flops 131072 | bytes 1572868 | tf_op jit(solution)/shard_map/add | solution.py:77
  34.2 0.0 collective-permute-done.1
  34.2 1.4 %bitcast_add_fusion = f32[8,16,16,64]{3,2,1,0:T(8,128)S(1)} fusion(f32[8,16,16,64]{3,2,1,0:T(8,128)} %collective-permute-done.1, f32[1,16,16,16,64]{4,3,2,1,0:T(8,128)S(1)} %get-tuple-element.18, s32[]{:T(128)S(6)} %select_n.126), kind=kLoop, calls=%fused_computation.3 | loop fusion | flops 131072 | bytes 1572868 | tf_op jit(solution)/shard_map/add | solution.py:77
  35.6 1.6 %collective-permute-start.8 = (bf16[4,16,16,64]{3,1,2,0:T(8,128)(2,1)S(1)}, bf16[4,16,16,64]{3,1,2,0:T(8,128)(2,1)S(1)}, u32[]{:S(2)}, u32[]{:S(2)}) collective-permute-start(bf16[4,16,16,64]{3,1,2,0:T(8,128)(2,1)S(1)} %pad_maximum_fusion.6), channel_id=1, source_target_pairs={{0,4},{1,5},{2,6},{3,7},{4,0},{5,1},{6,2},{7,3},{8,12},{9,13},{10,... | collective-permute-start | bytes 393224 | tf_op jit(solution)/shard_map/ppermute | solution.py:55
  37.3 0.5 collective-permute-start.6
  37.8 0.3 collective-permute-start.13
  38.2 1.8 %collective-permute-start.10 = (f32[4,16,16,64]{3,2,1,0:T(8,128)S(1)}, f32[4,16,16,64]{3,2,1,0:T(8,128)S(1)}, u32[]{:S(2)}, u32[]{:S(2)}) collective-permute-start(f32[4,16,16,64]{3,2,1,0:T(8,128)S(1)} %constant_dynamic-slice_fusion.5), channel_id=1, source_target_pairs={{0,2},{1,3},{2,0},{3,1},{4,6},{5,7},{6,4},{7,5},{8,10},{9,11},{10,... | collective-permute-start | bytes 786440 | tf_op jit(solution)/shard_map/ppermute | solution.py:77
  39.9 5.0 %collective-permute-done.8 = bf16[4,16,16,64]{3,1,2,0:T(8,128)(2,1)S(1)} collective-permute-done((bf16[4,16,16,64]{3,1,2,0:T(8,128)(2,1)S(1)}, bf16[4,16,16,64]{3,1,2,0:T(8,128)(2,1)S(1)}, u32[]{:S(2)}, u32[]{:S(2)}) %collective-permute-start.8) | collective-permute-done | bytes 131104 | tf_op jit(solution)/shard_map/ppermute | solution.py:55
  45.0 0.1 pad_maximum_fusion.4
  45.1 0.1 collective-permute-start.9
  45.2 1.3 %collective-permute-done.6 = bf16[4,16,16,64]{3,1,2,0:T(8,128)(2,1)S(1)} collective-permute-done((bf16[4,16,16,64]{3,1,2,0:T(8,128)(2,1)S(1)}, bf16[4,16,16,64]{3,1,2,0:T(8,128)(2,1)S(1)}, u32[]{:S(2)}, u32[]{:S(2)}) %collective-permute-start.6) | collective-permute-done | bytes 131104 | tf_op jit(solution)/shard_map/ppermute | solution.py:55
  46.5 0.1 pad_maximum_fusion.3
  46.7 0.1 collective-permute-start.7
  46.7 7.8 %collective-permute-done.13 = f32[4,16,16,64]{3,2,1,0:T(8,128)S(1)} collective-permute-done((f32[4,16,16,64]{3,2,1,0:T(8,128)S(1)}, f32[4,16,16,64]{3,2,1,0:T(8,128)S(1)}, u32[]{:S(2)}, u32[]{:S(2)}) %collective-permute-start.13) | collective-permute-done | bytes 262176 | tf_op jit(solution)/shard_map/ppermute | solution.py:77
  54.5 0.1 dynamic-slice_add_fusion
  54.6 0.5 collective-permute-start.14
  55.1 0.7 collective-permute-done.10
  55.8 0.1 dynamic-slice_add_fusion.1
  55.9 1.0 %collective-permute-start.11 = (f32[2,16,16,64]{3,2,1,0:T(8,128)S(1)}, f32[2,16,16,64]{3,2,1,0:T(8,128)S(1)}, u32[]{:S(2)}, u32[]{:S(2)}) collective-permute-start(f32[2,16,16,64]{3,2,1,0:T(8,128)S(1)} %constant_dynamic-slice_fusion.4), channel_id=1, source_target_pairs={{0,4},{1,5},{2,6},{3,7},{4,0},{5,1},{6,2},{7,3},{8,12},{9,13},{10,... | collective-permute-start | bytes 393224 | tf_op jit(solution)/shard_map/ppermute | solution.py:77
  56.9 4.5 %collective-permute-done.14 = f32[2,16,16,64]{3,2,1,0:T(8,128)S(1)} collective-permute-done((f32[2,16,16,64]{3,2,1,0:T(8,128)S(1)}, f32[2,16,16,64]{3,2,1,0:T(8,128)S(1)}, u32[]{:S(2)}, u32[]{:S(2)}) %collective-permute-start.14) | collective-permute-done | bytes 131104 | tf_op jit(solution)/shard_map/ppermute | solution.py:77
  61.5 2.7 %collective-permute-start.15 = (f32[1,16,16,64]{3,2,1,0:T(8,128)S(1)}, f32[1,16,16,64]{3,2,1,0:T(8,128)S(1)}, u32[]{:S(2)}, u32[]{:S(2)}) collective-permute-start(f32[1,16,16,64]{3,2,1,0:T(8,128)S(1)} %constant_dynamic-slice_fusion), channel_id=1, source_target_pairs={{0,8},{1,9},{2,10},{3,11},{4,12},{5,13},{6,14},{7,15},{8,0},{9,1},... | collective-permute-start | bytes 196616 | tf_op jit(solution)/shard_map/ppermute | solution.py:77
  64.1 0.0 collective-permute-done.11
  64.2 1.7 %collective-permute-start.12 = (f32[1,16,16,64]{3,2,1,0:T(8,128)S(1)}, f32[1,16,16,64]{3,2,1,0:T(8,128)S(1)}, u32[]{:S(2)}, u32[]{:S(2)}) collective-permute-start(f32[1,16,16,64]{3,2,1,0:T(8,128)S(1)} %constant_dynamic-slice_fusion.3), channel_id=1, source_target_pairs={{0,8},{1,9},{2,10},{3,11},{4,12},{5,13},{6,14},{7,15},{8,0},{9,1},... | collective-permute-start | bytes 196616 | tf_op jit(solution)/shard_map/ppermute | solution.py:77
  65.9 0.0 collective-permute-done.9
  65.9 0.1 broadcast_select_fusion.1
  66.0 0.2 pad_maximum_fusion.2
  66.2 0.3 copy.14
  66.5 0.0 collective-permute-done.7
  66.5 0.1 broadcast_select_fusion.3
  66.7 0.2 pad_maximum_fusion.1
  66.9 0.3 copy.12
  67.2 1.8 %pad_maximum_fusion.rt_ref = bf16[16,32,16,64]{3,2,1,0:T(8,128)(2,1)} fusion(bf16[16,16,16,64]{3,2,1,0:T(8,128)(2,1)S(1)} %bitcast.46, bf16[16,16,16,64]{3,2,1,0:T(8,128)(2,1)S(1)} %bitcast.47), kind=kLoop, calls=%fused_computation | loop fusion | flops 524288 | bytes 2097152 | tf_op jit(solution)/shard_map/concatenate | solution.py:192
  69.0 7.0 %shard_map.60 = f32[512,64]{1,0:T(8,128)} custom-call(bf16[32,512,256]{2,1,0:T(8,128)(2,1)} %get-tuple-element.8.gm_ref, bf16[16,32,16,64]{3,2,1,0:T(8,128)(2,1)} %pad_maximum_fusion.rt_ref), custom_call_target="tpu_custom_call" | custom-call | flops 536870912 | bytes 9437184 | tf_op jit(solution)/shard_map/pallas_call | solution.py:201
  76.0 1.0 %convert_bitcast_fusion = bf16[64,512]{0,1:T(8,128)(2,1)S(1)} fusion(f32[512,64]{1,0:T(8,128)} %shard_map.60), kind=kLoop, calls=%fused_computation.28 | loop fusion | flops 32768 | bytes 196608 | tf_op jit(solution)/shard_map/convert_element_type | solution.py:217
  77.0 0.7 copy.16
  77.7 0.0 collective-permute-done.15
  77.7 0.0 collective-permute-done.12
  77.8 0.7 copy.17
  (16 shorter events, 0.4 us)
Async XLA Ops:
  1.6 19.5 %collective-permute-start.4 = (bf16[1,16,16,64]{3,1,2,0:T(8,128)(2,1)S(1)}, bf16[1,16,16,64]{3,1,2,0:T(8,128)(2,1)S(1)}, u32[]{:S(2)}, u32[]{:S(2)}) collective-permute-start(bf16[1,16,16,64]{3,1,2,0:T(8,128)(2,1)S(1)} %get-tuple-element.38), channel_id=1, source_target_pairs={{0,8},{1,9},{2,10},{3,11},{4,12},{5,13},{6,14},{7,15},{8,0},{9,1},... | collective-permute-start | bytes 98312 | tf_op jit(solution)/shard_map/ppermute | solution.py:55
  5.7 16.1 %collective-permute-start.2 = (bf16[1,16,16,64]{3,1,2,0:T(8,128)(2,1)S(1)}, bf16[1,16,16,64]{3,1,2,0:T(8,128)(2,1)}, u32[]{:S(2)}, u32[]{:S(2)}) collective-permute-start(bf16[1,16,16,64]{3,1,2,0:T(8,128)(2,1)S(1)} %get-tuple-element.39), channel_id=1, source_target_pairs={{0,8},{1,9},{2,10},{3,11},{4,12},{5,13},{6,14},{7,15},{8,0},{9,1},... | collective-permute-start | bytes 98312 | tf_op jit(solution)/shard_map/ppermute | solution.py:55
  21.0 11.8 %collective-permute-start = (f32[8,16,16,64]{3,2,1,0:T(8,128)S(1)}, f32[8,16,16,64]{3,2,1,0:T(8,128)}, u32[]{:S(2)}, u32[]{:S(2)}) collective-permute-start(f32[8,16,16,64]{3,2,1,0:T(8,128)S(1)} %dynamic-slice_bitcast_fusion.1), channel_id=1, source_target_pairs={{0,1},{1,0},{2,3},{3,2},{4,5},{5,4},{6,7},{7,6},{8,9},{9,8},{10,11... | collective-permute-start | bytes 1572872 | tf_op jit(solution)/shard_map/ppermute | solution.py:77
  21.1 0.6 copy-start.1
  23.4 6.1 %collective-permute-start.5 = (bf16[2,16,16,64]{3,1,2,0:T(8,128)(2,1)}, bf16[2,16,16,64]{3,1,2,0:T(8,128)(2,1)S(1)}, u32[]{:S(2)}, u32[]{:S(2)}) collective-permute-start(bf16[2,16,16,64]{3,1,2,0:T(8,128)(2,1)} %pad_maximum_fusion.8), channel_id=1, source_target_pairs={{0,2},{1,3},{2,0},{3,1},{4,6},{5,7},{6,4},{7,5},{8,10},{9,11},{10,... | collective-permute-start | bytes 196616 | tf_op jit(solution)/shard_map/ppermute | solution.py:55
  25.8 5.9 %collective-permute-start.3 = (bf16[2,16,16,64]{3,1,2,0:T(8,128)(2,1)}, bf16[2,16,16,64]{3,1,2,0:T(8,128)(2,1)}, u32[]{:S(2)}, u32[]{:S(2)}) collective-permute-start(bf16[2,16,16,64]{3,1,2,0:T(8,128)(2,1)} %pad_maximum_fusion.7), channel_id=1, source_target_pairs={{0,4},{1,5},{2,6},{3,7},{4,0},{5,1},{6,2},{7,3},{8,12},{9,13},{10,... | collective-permute-start | bytes 196616 | tf_op jit(solution)/shard_map/ppermute | solution.py:55
  28.5 5.8 %collective-permute-start.1 = (f32[8,16,16,64]{3,2,1,0:T(8,128)}, f32[8,16,16,64]{3,2,1,0:T(8,128)}, u32[]{:S(2)}, u32[]{:S(2)}) collective-permute-start(f32[8,16,16,64]{3,2,1,0:T(8,128)} %dynamic-slice_bitcast_fusion), channel_id=1, source_target_pairs={{0,1},{1,0},{2,3},{3,2},{4,5},{5,4},{6,7},{7,6},{8,9},{9,8},{10,11... | collective-permute-start | bytes 1572872 | tf_op jit(solution)/shard_map/ppermute | solution.py:77
  28.5 4.4 %copy-start = (f32[1,16,16,16,64]{4,3,2,1,0:T(8,128)S(1)}, f32[1,16,16,16,64]{4,3,2,1,0:T(8,128)}, u32[]{:S(2)}) copy-start(f32[1,16,16,16,64]{4,3,2,1,0:T(8,128)} %get-tuple-element.19) | copy-start | bytes 3145732
  35.6 9.3 %collective-permute-start.8 = (bf16[4,16,16,64]{3,1,2,0:T(8,128)(2,1)S(1)}, bf16[4,16,16,64]{3,1,2,0:T(8,128)(2,1)S(1)}, u32[]{:S(2)}, u32[]{:S(2)}) collective-permute-start(bf16[4,16,16,64]{3,1,2,0:T(8,128)(2,1)S(1)} %pad_maximum_fusion.6), channel_id=1, source_target_pairs={{0,4},{1,5},{2,6},{3,7},{4,0},{5,1},{6,2},{7,3},{8,12},{9,13},{10,... | collective-permute-start | bytes 393224 | tf_op jit(solution)/shard_map/ppermute | solution.py:55
  37.3 9.2 %collective-permute-start.6 = (bf16[4,16,16,64]{3,1,2,0:T(8,128)(2,1)S(1)}, bf16[4,16,16,64]{3,1,2,0:T(8,128)(2,1)S(1)}, u32[]{:S(2)}, u32[]{:S(2)}) collective-permute-start(bf16[4,16,16,64]{3,1,2,0:T(8,128)(2,1)S(1)} %pad_maximum_fusion.5), channel_id=1, source_target_pairs={{0,2},{1,3},{2,0},{3,1},{4,6},{5,7},{6,4},{7,5},{8,10},{9,11},{10,... | collective-permute-start | bytes 393224 | tf_op jit(solution)/shard_map/ppermute | solution.py:55
  37.8 16.7 %collective-permute-start.13 = (f32[4,16,16,64]{3,2,1,0:T(8,128)S(1)}, f32[4,16,16,64]{3,2,1,0:T(8,128)S(1)}, u32[]{:S(2)}, u32[]{:S(2)}) collective-permute-start(f32[4,16,16,64]{3,2,1,0:T(8,128)S(1)} %constant_dynamic-slice_fusion.2), channel_id=1, source_target_pairs={{0,4},{1,5},{2,6},{3,7},{4,0},{5,1},{6,2},{7,3},{8,12},{9,13},{10,... | collective-permute-start | bytes 786440 | tf_op jit(solution)/shard_map/ppermute | solution.py:77
  38.2 17.6 %collective-permute-start.10 = (f32[4,16,16,64]{3,2,1,0:T(8,128)S(1)}, f32[4,16,16,64]{3,2,1,0:T(8,128)S(1)}, u32[]{:S(2)}, u32[]{:S(2)}) collective-permute-start(f32[4,16,16,64]{3,2,1,0:T(8,128)S(1)} %constant_dynamic-slice_fusion.5), channel_id=1, source_target_pairs={{0,2},{1,3},{2,0},{3,1},{4,6},{5,7},{6,4},{7,5},{8,10},{9,11},{10,... | collective-permute-start | bytes 786440 | tf_op jit(solution)/shard_map/ppermute | solution.py:77
  45.1 20.8 %collective-permute-start.9 = (bf16[8,16,16,64]{3,1,2,0:T(8,128)(2,1)S(1)}, bf16[8,16,16,64]{3,1,2,0:T(8,128)(2,1)S(1)}, u32[]{:S(2)}, u32[]{:S(2)}) collective-permute-start(bf16[8,16,16,64]{3,1,2,0:T(8,128)(2,1)S(1)} %pad_maximum_fusion.4), channel_id=1, source_target_pairs={{0,1},{1,0},{2,3},{3,2},{4,5},{5,4},{6,7},{7,6},{8,9},{9,8},{10,11... | collective-permute-start | bytes 786440 | tf_op jit(solution)/shard_map/ppermute | solution.py:55
  46.7 19.9 %collective-permute-start.7 = (bf16[8,16,16,64]{3,1,2,0:T(8,128)(2,1)S(1)}, bf16[8,16,16,64]{3,1,2,0:T(8,128)(2,1)S(1)}, u32[]{:S(2)}, u32[]{:S(2)}) collective-permute-start(bf16[8,16,16,64]{3,1,2,0:T(8,128)(2,1)S(1)} %pad_maximum_fusion.3), channel_id=1, source_target_pairs={{0,1},{1,0},{2,3},{3,2},{4,5},{5,4},{6,7},{7,6},{8,9},{9,8},{10,11... | collective-permute-start | bytes 786440 | tf_op jit(solution)/shard_map/ppermute | solution.py:55
  54.6 6.8 %collective-permute-start.14 = (f32[2,16,16,64]{3,2,1,0:T(8,128)S(1)}, f32[2,16,16,64]{3,2,1,0:T(8,128)S(1)}, u32[]{:S(2)}, u32[]{:S(2)}) collective-permute-start(f32[2,16,16,64]{3,2,1,0:T(8,128)S(1)} %constant_dynamic-slice_fusion.1), channel_id=1, source_target_pairs={{0,2},{1,3},{2,0},{3,1},{4,6},{5,7},{6,4},{7,5},{8,10},{9,11},{10,... | collective-permute-start | bytes 393224 | tf_op jit(solution)/shard_map/ppermute | solution.py:77
  55.9 8.2 %collective-permute-start.11 = (f32[2,16,16,64]{3,2,1,0:T(8,128)S(1)}, f32[2,16,16,64]{3,2,1,0:T(8,128)S(1)}, u32[]{:S(2)}, u32[]{:S(2)}) collective-permute-start(f32[2,16,16,64]{3,2,1,0:T(8,128)S(1)} %constant_dynamic-slice_fusion.4), channel_id=1, source_target_pairs={{0,4},{1,5},{2,6},{3,7},{4,0},{5,1},{6,2},{7,3},{8,12},{9,13},{10,... | collective-permute-start | bytes 393224 | tf_op jit(solution)/shard_map/ppermute | solution.py:77
  61.5 16.2 %collective-permute-start.15 = (f32[1,16,16,64]{3,2,1,0:T(8,128)S(1)}, f32[1,16,16,64]{3,2,1,0:T(8,128)S(1)}, u32[]{:S(2)}, u32[]{:S(2)}) collective-permute-start(f32[1,16,16,64]{3,2,1,0:T(8,128)S(1)} %constant_dynamic-slice_fusion), channel_id=1, source_target_pairs={{0,8},{1,9},{2,10},{3,11},{4,12},{5,13},{6,14},{7,15},{8,0},{9,1},... | collective-permute-start | bytes 196616 | tf_op jit(solution)/shard_map/ppermute | solution.py:77
  64.2 13.5 %collective-permute-start.12 = (f32[1,16,16,64]{3,2,1,0:T(8,128)S(1)}, f32[1,16,16,64]{3,2,1,0:T(8,128)S(1)}, u32[]{:S(2)}, u32[]{:S(2)}) collective-permute-start(f32[1,16,16,64]{3,2,1,0:T(8,128)S(1)} %constant_dynamic-slice_fusion.3), channel_id=1, source_target_pairs={{0,8},{1,9},{2,10},{3,11},{4,12},{5,13},{6,14},{7,15},{8,0},{9,1},... | collective-permute-start | bytes 196616 | tf_op jit(solution)/shard_map/ppermute | solution.py:77

commit v11 on v10

--- a/solution.py
+++ b/solution.py
@@ -99,7 +99,7 @@
     return list(range(n.bit_length() - 1))
 
 
-def project_kernel(p_ref, w_ref, l_ref, gm_ref, pt_ref, *, n_seq, orders):
+def project_kernel(p_ref, w_ref, l_ref, gm_ref, *pt_refs, n_seq, orders):
     rows = p_ref.shape[0]
     width = p_ref.shape[1]
     per_block = width // 16
@@ -119,7 +119,7 @@
         part = part.reshape(per_block, 16, part.shape[1])
         h = e // half
         for local in range(per_block):
-            pt_ref[h, position(first + local, orders[h]), e % half] = part[local]
+            pt_refs[h][position(first + local, orders[h]), e % half] = part[local]
 
 
 def left_kernel(gm_ref, rt_ref, out_ref):
@@ -129,7 +129,7 @@
 
     width = gm_ref.shape[2]
     acc = out_ref[...]
-    for e in range(C):
+    for e in range(gm_ref.shape[0]):
         right_e = rt_ref[:, e, :, :].reshape(width, rt_ref.shape[3])
         acc = acc + jnp.dot(gm_ref[e], right_e, preferred_element_type=jnp.float32)
     out_ref[...] = acc
@@ -158,7 +158,7 @@
 
     weight_ec = out_weight.reshape(C, C, p_size).transpose(1, 0, 2).reshape(C * C, p_size)
 
-    grad_m, part_t = pl.pallas_call(
+    grad_m, *part_t = pl.pallas_call(
         functools.partial(project_kernel, n_seq=n_seq, orders=orders),
         grid=(steps,),
         in_specs=[
@@ -168,12 +168,12 @@
         ],
         out_specs=[
             pl.BlockSpec((C, own_rows * C, block), lambda b: (0, 0, b)),
-            pl.BlockSpec((len(orders), total // 16, half, 16, n_seq), lambda b: (0, 0, 0, 0, 0)),
-        ],
+        ]
+        + [pl.BlockSpec((total // 16, half, 16, n_seq), lambda b: (0, 0, 0, 0))] * len(orders),
         out_shape=[
             jax.ShapeDtypeStruct((C, own_rows * C, total), jnp.bfloat16),
-            jax.ShapeDtypeStruct((len(orders), total // 16, half, 16, n_seq), jnp.float32),
-        ],
+        ]
+        + [jax.ShapeDtypeStruct((total // 16, half, 16, n_seq), jnp.float32)] * len(orders),
         compiler_params=pltpu.CompilerParams(vmem_limit_bytes=56 * 1024 * 1024),
         cost_estimate=pl.CostEstimate(
             flops=2 * own_rows * total * C * C * (p_size + n_seq),
@@ -189,31 +189,32 @@
     for h in range(len(orders)):
         for bit in orders[h][::-1][early:]:
             gathers[h] = gather_step(gathers[h], "row", n, bit)
-    right_blocks = jnp.concatenate(
-        [gather_finish(gathers[h], n, right_t[:half].shape) for h in range(len(orders))], 1
-    )
+    right_halves = [gather_finish(gathers[h], n, right_t[:half].shape) for h in range(len(orders))]
     for h in range(len(orders)):
         for bit in orders[h][1:]:
             scatters[h] = scatter_step(scatters[h], "row", n, bit)
     summed = jnp.concatenate([scatters[h][0] for h in range(len(orders))], 0)
     grad_right = summed.transpose(2, 1, 0).reshape(n_seq, per_dev * C).astype(jnp.bfloat16)
 
-    left_t = pl.pallas_call(
-        left_kernel,
-        grid=(steps,),
-        in_specs=[
-            pl.BlockSpec((C, own_rows * C, block), lambda b: (0, 0, b)),
-            pl.BlockSpec((block // 16, C, 16, n_seq), lambda b: (b, 0, 0, 0)),
-        ],
-        out_specs=pl.BlockSpec((own_rows * C, n_seq), lambda b: (0, 0)),
-        out_shape=jax.ShapeDtypeStruct((own_rows * C, n_seq), jnp.float32),
-        compiler_params=pltpu.CompilerParams(vmem_limit_bytes=56 * 1024 * 1024),
-        cost_estimate=pl.CostEstimate(
-            flops=2 * own_rows * total * C * C * n_seq,
-            transcendentals=0,
-            bytes_accessed=2 * own_rows * total * C * C + 2 * total * C * n_seq,
-        ),
-    )(grad_m, right_blocks)
+    left_t = None
+    for h in range(len(orders)):
+        piece = pl.pallas_call(
+            left_kernel,
+            grid=(steps,),
+            in_specs=[
+                pl.BlockSpec((half, own_rows * C, block), lambda b, h=h: (h, 0, b)),
+                pl.BlockSpec((block // 16, half, 16, n_seq), lambda b: (b, 0, 0, 0)),
+            ],
+            out_specs=pl.BlockSpec((own_rows * C, n_seq), lambda b: (0, 0)),
+            out_shape=jax.ShapeDtypeStruct((own_rows * C, n_seq), jnp.float32),
+            compiler_params=pltpu.CompilerParams(vmem_limit_bytes=56 * 1024 * 1024),
+            cost_estimate=pl.CostEstimate(
+                flops=2 * own_rows * total * C * half * n_seq,
+                transcendentals=0,
+                bytes_accessed=2 * own_rows * total * C * half + 2 * total * half * n_seq,
+            ),
+        )(grad_m, right_halves[h])
+        left_t = piece if left_t is None else left_t + piece
     grad_left = left_t.T.astype(jnp.bfloat16)
     return (grad_left, grad_right)
 

time: 79 us -> 79.2 us (level)
  starting transfers between devices: 17.9 us -> 21.8 us
  waiting for transfers between devices: 22.5 us -> 20.5 us
  Pallas kernels: 15.2 us -> 17.1 us
  other arithmetic: 10.1 us -> 8.32 us
  local copies, waits for them, and re-layouts: 11.9 us -> 10.2 us
    slice x1 -> x0, local copies, waits for them, and re-layouts: 3.99 us -> none  [per_device(): part_t[h]]
    ppermute x8, starting transfers between devices: 8.03 us -> 11.6 us  [scatter_step(): return keep + lax.ppermute(send, axis, xor_pairs(n, bit))]
    transpose x2, local copies, waits for them, and re-layouts: 0.55 us -> 2.61 us  [gather_finish(): buf = buf.transpose(order + list(range(k, k + len(shape))))]
    pallas_call x1 -> x2, Pallas kernels: 7 us -> 8.92 us  [per_device(): pl.pallas_call(left_kernel, grid=(steps,), in_specs=[pl.BlockSpec((half,...]
    concatenate x1 -> x0, other arithmetic: 1.81 us -> none  [per_device(): jnp.concatenate([gather_finish(gathers[h], n, right_t[:half].shape) for h...]
    ppermute x8, waiting for transfers between devices: 9.6 us -> 8.34 us  [gather_step(): other = lax.ppermute(buf, axis, xor_pairs(n, bit))]
    ppermute x8, waiting for transfers between devices: 12.9 us -> 12.1 us  [scatter_step(): return keep + lax.ppermute(send, axis, xor_pairs(n, bit))]
    unnamed x7 -> x11, local copies, waits for them, and re-layouts: 3.04 us -> 3.05 us
  transfers between devices with their start and end apart: 16 -> 16, of which waited for: 7 -> 7; matrix products, arithmetic and copies ran while one was open for 23% -> 19% of each run, Pallas kernels for 19% -> 22%
where the time goes in v11:
time: 79.2 us; the launch traced here: 78.8 us
  starting transfers between devices  21.8 us (28%)
  waiting for transfers between devices  20.5 us (26%)
  Pallas kernels  17.1 us (22%)
  local copies, waits for them, and re-layouts  10.2 us (13%)
  other arithmetic  8.32 us (11%)
  between operations  0.9 us (1%)
    ppermute x8, waiting for transfers between devices, scatter_step(): return keep + lax.ppermute(send, axis, xor_pairs(n, bit))  12.1 us
    ppermute x8, starting transfers between devices, scatter_step(): return keep + lax.ppermute(send, axis, xor_pairs(n, bit))  11.6 us
    ppermute x8, starting transfers between devices, gather_step(): other = lax.ppermute(buf, axis, xor_pairs(n, bit))  10.2 us
    pallas_call x2, Pallas kernels, per_device(): pl.pallas_call(left_kernel, grid=(steps,), in_specs=[pl.BlockSpec((half,...  8.92 us
    ppermute x8, waiting for transfers between devices, gather_step(): other = lax.ppermute(buf, axis, xor_pairs(n, bit))  8.34 us
    pallas_call x1, Pallas kernels, per_device(): pl.pallas_call(functools.partial(project_kernel, n_seq=n_seq, orders=orde...  8.19 us
    unnamed x11, local copies, waits for them, and re-layouts  3.05 us
    add x6, other arithmetic, scatter_step(): return keep + lax.ppermute(send, axis, xor_pairs(n, bit))  2.94 us
  transfers between devices with their start and end apart: 16, of which 7 were waited for; matrix products, arithmetic and copies ran while one was open for 19% of the time, Pallas kernels for 22%

profile of v11, /device:TPU:0, one launch (start us, length us, event | category | flops | bytes accessed | tf_op | source)
XLA Modules:
  0.0 78.8 jit_solution(17019419841200142138)
XLA Ops:
  0.6 1.0 %copy.9 = bf16[64,512]{0,1:T(8,128)(2,1)S(1)} copy(bf16[64,512]{1,0:T(8,128)(2,1)} %param.5) | data formatting | bytes 131072 | tf_op args[1]
  1.6 4.1 %collective-permute-start.4 = (bf16[1,16,16,64]{3,1,2,0:T(8,128)(2,1)S(1)}, bf16[1,16,16,64]{3,1,2,0:T(8,128)(2,1)S(1)}, u32[]{:S(2)}, u32[]{:S(2)}) collective-permute-start(bf16[1,16,16,64]{3,1,2,0:T(8,128)(2,1)S(1)} %get-tuple-element.38), channel_id=1, source_target_pairs={{0,8},{1,9},{2,10},{3,11},{4,12},{5,13},{6,14},{7,15},{8,0},{9,1},... | collective-permute-start | bytes 98312 | tf_op jit(solution)/shard_map/ppermute | solution.py:55
  5.7 0.1 collective-permute-start.2
  5.8 1.8 %copy.8 = bf16[32,32,128]{2,0,1:T(8,128)(2,1)} copy(bf16[32,32,128]{2,1,0:T(8,128)(2,1)} %bitcast.43) | data formatting | bytes 524288 | tf_op jit(solution)/shard_map/reshape | solution.py:159
  7.6 8.2 %shard_map.59 = (bf16[32,512,256]{2,1,0:T(8,128)(2,1)}, f32[16,16,16,64]{3,2,1,0:T(8,128)}, f32[16,16,16,64]{3,2,1,0:T(8,128)}) custom-call(bf16[16,256,128]{2,1,0:T(8,128)(2,1)} %p_ref.1, bf16[1024,128]{1,0:T(8,128)(2,1)} %bitcast.44, bf16[64,512]{1,0:T(8,128)(2,1)} %l_ref.1), custom_call_target="tpu_custom_call" | custom-call | flops 1610612736 | bytes 11534336 | tf_op jit(solution)/shard_map/pallas_call | solution.py:161
  15.8 1.5 %constant_dynamic-slice_fusion.7 = f32[8,16,16,64]{3,2,1,0:T(8,128)S(1)} fusion(f32[16,16,16,64]{3,2,1,0:T(8,128)} %get-tuple-element.10, s32[]{:T(128)S(6)} %select_n.127), kind=kLoop, calls=%fused_computation.46 | loop fusion | bytes 1048580 | tf_op jit(solution)/shard_map/dynamic_slice | solution.py:76
  17.2 0.1 collective-permute-start
  17.3 0.0 collective-permute-done.4
  17.3 0.0 copy-start.3
  17.3 0.6 copy-done.3
  18.0 0.0 collective-permute-done.2
  18.0 0.9 %broadcast_select_fusion.13 = (bf16[1,16,16,64]{3,1,2,0:T(8,128)(2,1)S(1)}, bf16[1,16,16,64]{3,1,2,0:T(8,128)(2,1)S(1)}, bf16[1,16,16,64]{3,1,2,0:T(8,128)(2,1)S(1)}, bf16[1,16,16,64]{3,1,2,0:T(8,128)(2,1)S(1)}) fusion(bf16[1,16,16,64]{3,1,2,0:T(8,128)(2,1)} %copy-done.3, pred[]{:T(512)S(6)} %eq.11, bf16[32,16,64]{2,0,1:T(8,128)(2,1)S(1)} %bitcast.41, ...), kind=kLoop, calls=%fused_computation.36 | loop fusion | flops 65536 | bytes 262145 | tf_op jit(solution)/shard_map/jit(_where)/select_n | solution.py:57
  18.9 0.7 pad_maximum_fusion.7
  19.5 1.8 %collective-permute-start.5 = (bf16[2,16,16,64]{3,1,2,0:T(8,128)(2,1)}, bf16[2,16,16,64]{3,1,2,0:T(8,128)(2,1)S(1)}, u32[]{:S(2)}, u32[]{:S(2)}) collective-permute-start(bf16[2,16,16,64]{3,1,2,0:T(8,128)(2,1)} %pad_maximum_fusion.7), channel_id=1, source_target_pairs={{0,2},{1,3},{2,0},{3,1},{4,6},{5,7},{6,4},{7,5},{8,10},{9,11},{10,... | collective-permute-start | bytes 196616 | tf_op jit(solution)/shard_map/ppermute | solution.py:55
  21.3 0.7 pad_maximum_fusion.6
  22.0 1.6 %collective-permute-start.3 = (bf16[2,16,16,64]{3,1,2,0:T(8,128)(2,1)}, bf16[2,16,16,64]{3,1,2,0:T(8,128)(2,1)}, u32[]{:S(2)}, u32[]{:S(2)}) collective-permute-start(bf16[2,16,16,64]{3,1,2,0:T(8,128)(2,1)} %pad_maximum_fusion.6), channel_id=1, source_target_pairs={{0,4},{1,5},{2,6},{3,7},{4,0},{5,1},{6,2},{7,3},{8,12},{9,13},{10,... | collective-permute-start | bytes 196616 | tf_op jit(solution)/shard_map/ppermute | solution.py:55
  23.6 0.0 copy-done
  23.6 1.1 %constant_dynamic-slice_fusion.6 = f32[8,16,16,64]{3,2,1,0:T(8,128)} fusion(f32[16,16,16,64]{3,2,1,0:T(8,128)S(1)} %copy-done, s32[]{:T(128)S(6)} %select_n.127), kind=kLoop, calls=%fused_computation.45 | loop fusion | bytes 1048580 | tf_op jit(solution)/shard_map/dynamic_slice | solution.py:76
  24.7 0.0 collective-permute-start.1
  24.7 1.0 %collective-permute-done.5 = bf16[2,16,16,64]{3,1,2,0:T(8,128)(2,1)S(1)} collective-permute-done((bf16[2,16,16,64]{3,1,2,0:T(8,128)(2,1)}, bf16[2,16,16,64]{3,1,2,0:T(8,128)(2,1)S(1)}, u32[]{:S(2)}, u32[]{:S(2)}) %collective-permute-start.5) | collective-permute-done | bytes 65568 | tf_op jit(solution)/shard_map/ppermute | solution.py:55
  25.7 2.2 %collective-permute-done.3 = bf16[2,16,16,64]{3,1,2,0:T(8,128)(2,1)} collective-permute-done((bf16[2,16,16,64]{3,1,2,0:T(8,128)(2,1)}, bf16[2,16,16,64]{3,1,2,0:T(8,128)(2,1)}, u32[]{:S(2)}, u32[]{:S(2)}) %collective-permute-start.3) | collective-permute-done | bytes 65568 | tf_op jit(solution)/shard_map/ppermute | solution.py:55
  27.9 1.0 %broadcast_select_fusion.9 = (bf16[2,16,16,64]{3,1,2,0:T(8,128)(2,1)S(1)}, bf16[2,16,16,64]{3,1,2,0:T(8,128)(2,1)S(1)}, bf16[2,16,16,64]{3,1,2,0:T(8,128)(2,1)S(1)}, bf16[2,16,16,64]{3,1,2,0:T(8,128)(2,1)S(1)}) fusion(bf16[2,16,16,64]{3,1,2,0:T(8,128)(2,1)S(1)} %collective-permute-done.5, pred[]{:T(512)S(6)} %eq.9, ...), kind=kLoop, calls=%fused_computation.28 | loop fusion | flops 196608 | bytes 524290 | tf_op jit(solution)/shard_map/jit(_where)/select_n | solution.py:57
  28.9 0.1 pad_maximum_fusion.4
  29.0 0.1 pad_maximum_fusion.5
  29.0 0.0 collective-permute-done
  29.0 0.0 copy-done.1
  29.0 1.4 %dynamic-slice_add_fusion.1 = f32[8,16,16,64]{3,2,1,0:T(8,128)S(1)} fusion(f32[8,16,16,64]{3,2,1,0:T(8,128)} %collective-permute-done, f32[16,16,16,64]{3,2,1,0:T(8,128)S(1)} %copy-done.1, s32[]{:T(128)S(6)} %select_n.126), kind=kLoop, calls=%fused_computation.3 | loop fusion | flops 131072 | bytes 1572868 | tf_op jit(solution)/shard_map/add | solution.py:77
  30.4 0.0 collective-permute-done.1
  30.4 1.4 %dynamic-slice_add_fusion = f32[8,16,16,64]{3,2,1,0:T(8,128)S(1)} fusion(f32[8,16,16,64]{3,2,1,0:T(8,128)} %collective-permute-done.1, f32[16,16,16,64]{3,2,1,0:T(8,128)S(1)} %copy-done, s32[]{:T(128)S(6)} %select_n.126), kind=kLoop, calls=%fused_computation.2 | loop fusion | flops 131072 | bytes 1572868 | tf_op jit(solution)/shard_map/add | solution.py:77
  31.8 0.4 collective-permute-start.6
  32.2 1.7 %collective-permute-start.8 = (bf16[4,16,16,64]{3,1,2,0:T(8,128)(2,1)S(1)}, bf16[4,16,16,64]{3,1,2,0:T(8,128)(2,1)S(1)}, u32[]{:S(2)}, u32[]{:S(2)}) collective-permute-start(bf16[4,16,16,64]{3,1,2,0:T(8,128)(2,1)S(1)} %pad_maximum_fusion.5), channel_id=1, source_target_pairs={{0,4},{1,5},{2,6},{3,7},{4,0},{5,1},{6,2},{7,3},{8,12},{9,13},{10,... | collective-permute-start | bytes 393224 | tf_op jit(solution)/shard_map/ppermute | solution.py:55
  34.0 0.3 collective-permute-start.13
  34.4 1.8 %collective-permute-start.10 = (f32[4,16,16,64]{3,2,1,0:T(8,128)S(1)}, f32[4,16,16,64]{3,2,1,0:T(8,128)S(1)}, u32[]{:S(2)}, u32[]{:S(2)}) collective-permute-start(f32[4,16,16,64]{3,2,1,0:T(8,128)S(1)} %constant_dynamic-slice_fusion.5), channel_id=1, source_target_pairs={{0,2},{1,3},{2,0},{3,1},{4,6},{5,7},{6,4},{7,5},{8,10},{9,11},{10,... | collective-permute-start | bytes 786440 | tf_op jit(solution)/shard_map/ppermute | solution.py:77
  36.1 5.0 %collective-permute-done.6 = bf16[4,16,16,64]{3,1,2,0:T(8,128)(2,1)S(1)} collective-permute-done((bf16[4,16,16,64]{3,1,2,0:T(8,128)(2,1)S(1)}, bf16[4,16,16,64]{3,1,2,0:T(8,128)(2,1)S(1)}, u32[]{:S(2)}, u32[]{:S(2)}) %collective-permute-start.6) | collective-permute-done | bytes 131104 | tf_op jit(solution)/shard_map/ppermute | solution.py:55
  41.2 0.1 pad_maximum_fusion.2
  41.3 0.1 collective-permute-start.7
  41.3 0.1 collective-permute-done.8
  41.5 0.1 pad_maximum_fusion.3
  41.6 0.5 collective-permute-start.9
  42.1 8.8 %collective-permute-done.13 = f32[4,16,16,64]{3,2,1,0:T(8,128)S(1)} collective-permute-done((f32[4,16,16,64]{3,2,1,0:T(8,128)S(1)}, f32[4,16,16,64]{3,2,1,0:T(8,128)S(1)}, u32[]{:S(2)}, u32[]{:S(2)}) %collective-permute-start.13) | collective-permute-done | bytes 262176 | tf_op jit(solution)/shard_map/ppermute | solution.py:77
  50.9 0.1 dynamic-slice_add_fusion.2
  51.0 1.6 %collective-permute-start.14 = (f32[2,16,16,64]{3,2,1,0:T(8,128)S(1)}, f32[2,16,16,64]{3,2,1,0:T(8,128)S(1)}, u32[]{:S(2)}, u32[]{:S(2)}) collective-permute-start(f32[2,16,16,64]{3,2,1,0:T(8,128)S(1)} %constant_dynamic-slice_fusion.1), channel_id=1, source_target_pairs={{0,2},{1,3},{2,0},{3,1},{4,6},{5,7},{6,4},{7,5},{8,10},{9,11},{10,... | collective-permute-start | bytes 393224 | tf_op jit(solution)/shard_map/ppermute | solution.py:77
  52.6 0.0 collective-permute-done.10
  52.6 0.1 dynamic-slice_add_fusion.3
  52.7 1.6 %collective-permute-start.11 = (f32[2,16,16,64]{3,2,1,0:T(8,128)S(1)}, f32[2,16,16,64]{3,2,1,0:T(8,128)S(1)}, u32[]{:S(2)}, u32[]{:S(2)}) collective-permute-start(f32[2,16,16,64]{3,2,1,0:T(8,128)S(1)} %constant_dynamic-slice_fusion.4), channel_id=1, source_target_pairs={{0,4},{1,5},{2,6},{3,7},{4,0},{5,1},{6,2},{7,3},{8,12},{9,13},{10,... | collective-permute-start | bytes 393224 | tf_op jit(solution)/shard_map/ppermute | solution.py:77
  54.4 3.2 %collective-permute-done.14 = f32[2,16,16,64]{3,2,1,0:T(8,128)S(1)} collective-permute-done((f32[2,16,16,64]{3,2,1,0:T(8,128)S(1)}, f32[2,16,16,64]{3,2,1,0:T(8,128)S(1)}, u32[]{:S(2)}, u32[]{:S(2)}) %collective-permute-start.14) | collective-permute-done | bytes 131104 | tf_op jit(solution)/shard_map/ppermute | solution.py:77
  57.6 2.6 %collective-permute-start.15 = (f32[1,16,16,64]{3,2,1,0:T(8,128)S(1)}, f32[1,16,16,64]{3,2,1,0:T(8,128)S(1)}, u32[]{:S(2)}, u32[]{:S(2)}) collective-permute-start(f32[1,16,16,64]{3,2,1,0:T(8,128)S(1)} %constant_dynamic-slice_fusion), channel_id=1, source_target_pairs={{0,8},{1,9},{2,10},{3,11},{4,12},{5,13},{6,14},{7,15},{8,0},{9,1},... | collective-permute-start | bytes 196616 | tf_op jit(solution)/shard_map/ppermute | solution.py:77
  60.2 0.2 collective-permute-done.11
  60.4 3.5 %collective-permute-start.12 = (f32[1,16,16,64]{3,2,1,0:T(8,128)S(1)}, f32[1,16,16,64]{3,2,1,0:T(8,128)S(1)}, u32[]{:S(2)}, u32[]{:S(2)}) collective-permute-start(f32[1,16,16,64]{3,2,1,0:T(8,128)S(1)} %constant_dynamic-slice_fusion.3), channel_id=1, source_target_pairs={{0,8},{1,9},{2,10},{3,11},{4,12},{5,13},{6,14},{7,15},{8,0},{9,1},... | collective-permute-start | bytes 196616 | tf_op jit(solution)/shard_map/ppermute | solution.py:77
  64.0 0.0 collective-permute-done.7
  64.0 0.1 broadcast_select_fusion.3
  64.1 0.2 pad_maximum_fusion
  64.3 1.3 %copy.11 = bf16[2,2,2,2,16,16,64]{6,5,4,3,2,1,0:T(8,128)(2,1)} copy(bf16[2,2,2,2,16,16,64]{6,4,5,0,1,2,3:T(8,128)(2,1)S(1)} %bitcast.38) | data formatting | bytes 1048576 | tf_op jit(solution)/shard_map/transpose | solution.py:67
  65.6 0.0 collective-permute-done.9
  65.6 0.1 broadcast_select_fusion.1
  65.8 0.2 pad_maximum_fusion.1
  66.0 1.3 %copy.13 = bf16[2,2,2,2,16,16,64]{6,5,4,3,2,1,0:T(8,128)(2,1)} copy(bf16[2,2,2,2,16,16,64]{6,4,5,0,2,1,3:T(8,128)(2,1)S(1)} %bitcast.39) | data formatting | bytes 1048576 | tf_op jit(solution)/shard_map/transpose | solution.py:67
  67.3 4.4 %shard_map.60 = f32[512,64]{1,0:T(8,128)} custom-call(bf16[32,512,256]{2,1,0:T(8,128)(2,1)} %get-tuple-element.9.gm_ref, bf16[16,16,16,64]{3,2,1,0:T(8,128)(2,1)} %bitcast.36), custom_call_target="tpu_custom_call" | custom-call | flops 268435456 | bytes 4718592 | tf_op jit(solution)/shard_map/pallas_call | solution.py:201
  71.8 4.5 %shard_map.61 = f32[512,64]{1,0:T(8,128)} custom-call(bf16[32,512,256]{2,1,0:T(8,128)(2,1)} %get-tuple-element.9.gm_ref, bf16[16,16,16,64]{3,2,1,0:T(8,128)(2,1)} %bitcast.37), custom_call_target="tpu_custom_call" | custom-call | flops 268435456 | bytes 4718592 | tf_op jit(solution)/shard_map/pallas_call | solution.py:201
  76.2 1.0 %fusion = bf16[64,512]{0,1:T(8,128)(2,1)S(1)} fusion(f32[512,64]{1,0:T(8,128)S(1)} %copy-done.2, f32[512,64]{1,0:T(8,128)} %shard_map.61), kind=kLoop, calls=%fused_computation.21 | loop fusion | flops 65536 | bytes 327680 | tf_op jit(solution)/shard_map/convert_element_type | solution.py:218
  77.2 0.7 copy.15
  78.0 0.0 collective-permute-done.15
  78.0 0.0 collective-permute-done.12
  78.1 0.7 copy.16
  (19 shorter events, 0.4 us)
Async XLA Ops:
  1.6 15.7 %collective-permute-start.4 = (bf16[1,16,16,64]{3,1,2,0:T(8,128)(2,1)S(1)}, bf16[1,16,16,64]{3,1,2,0:T(8,128)(2,1)S(1)}, u32[]{:S(2)}, u32[]{:S(2)}) collective-permute-start(bf16[1,16,16,64]{3,1,2,0:T(8,128)(2,1)S(1)} %get-tuple-element.38), channel_id=1, source_target_pairs={{0,8},{1,9},{2,10},{3,11},{4,12},{5,13},{6,14},{7,15},{8,0},{9,1},... | collective-permute-start | bytes 98312 | tf_op jit(solution)/shard_map/ppermute | solution.py:55
  5.7 12.3 %collective-permute-start.2 = (bf16[1,16,16,64]{3,1,2,0:T(8,128)(2,1)S(1)}, bf16[1,16,16,64]{3,1,2,0:T(8,128)(2,1)}, u32[]{:S(2)}, u32[]{:S(2)}) collective-permute-start(bf16[1,16,16,64]{3,1,2,0:T(8,128)(2,1)S(1)} %get-tuple-element.39), channel_id=1, source_target_pairs={{0,8},{1,9},{2,10},{3,11},{4,12},{5,13},{6,14},{7,15},{8,0},{9,1},... | collective-permute-start | bytes 98312 | tf_op jit(solution)/shard_map/ppermute | solution.py:55
  15.8 7.8 %copy-start = (f32[16,16,16,64]{3,2,1,0:T(8,128)S(1)}, f32[16,16,16,64]{3,2,1,0:T(8,128)}, u32[]{:S(2)}) copy-start(f32[16,16,16,64]{3,2,1,0:T(8,128)} %get-tuple-element.11) | copy-start | bytes 3145732
  17.2 11.8 %collective-permute-start = (f32[8,16,16,64]{3,2,1,0:T(8,128)S(1)}, f32[8,16,16,64]{3,2,1,0:T(8,128)}, u32[]{:S(2)}, u32[]{:S(2)}) collective-permute-start(f32[8,16,16,64]{3,2,1,0:T(8,128)S(1)} %constant_dynamic-slice_fusion.7), channel_id=1, source_target_pairs={{0,1},{1,0},{2,3},{3,2},{4,5},{5,4},{6,7},{7,6},{8,9},{9,8},{10,11... | collective-permute-start | bytes 1572872 | tf_op jit(solution)/shard_map/ppermute | solution.py:77
  17.3 0.6 copy-start.3
  19.5 6.1 %collective-permute-start.5 = (bf16[2,16,16,64]{3,1,2,0:T(8,128)(2,1)}, bf16[2,16,16,64]{3,1,2,0:T(8,128)(2,1)S(1)}, u32[]{:S(2)}, u32[]{:S(2)}) collective-permute-start(bf16[2,16,16,64]{3,1,2,0:T(8,128)(2,1)} %pad_maximum_fusion.7), channel_id=1, source_target_pairs={{0,2},{1,3},{2,0},{3,1},{4,6},{5,7},{6,4},{7,5},{8,10},{9,11},{10,... | collective-permute-start | bytes 196616 | tf_op jit(solution)/shard_map/ppermute | solution.py:55
  22.0 5.9 %collective-permute-start.3 = (bf16[2,16,16,64]{3,1,2,0:T(8,128)(2,1)}, bf16[2,16,16,64]{3,1,2,0:T(8,128)(2,1)}, u32[]{:S(2)}, u32[]{:S(2)}) collective-permute-start(bf16[2,16,16,64]{3,1,2,0:T(8,128)(2,1)} %pad_maximum_fusion.6), channel_id=1, source_target_pairs={{0,4},{1,5},{2,6},{3,7},{4,0},{5,1},{6,2},{7,3},{8,12},{9,13},{10,... | collective-permute-start | bytes 196616 | tf_op jit(solution)/shard_map/ppermute | solution.py:55
  24.7 5.8 %collective-permute-start.1 = (f32[8,16,16,64]{3,2,1,0:T(8,128)}, f32[8,16,16,64]{3,2,1,0:T(8,128)}, u32[]{:S(2)}, u32[]{:S(2)}) collective-permute-start(f32[8,16,16,64]{3,2,1,0:T(8,128)} %constant_dynamic-slice_fusion.6), channel_id=1, source_target_pairs={{0,1},{1,0},{2,3},{3,2},{4,5},{5,4},{6,7},{7,6},{8,9},{9,8},{10,11... | collective-permute-start | bytes 1572872 | tf_op jit(solution)/shard_map/ppermute | solution.py:77
  24.7 4.4 %copy-start.1 = (f32[16,16,16,64]{3,2,1,0:T(8,128)S(1)}, f32[16,16,16,64]{3,2,1,0:T(8,128)}, u32[]{:S(2)}) copy-start(f32[16,16,16,64]{3,2,1,0:T(8,128)} %get-tuple-element.10) | copy-start | bytes 3145732
  31.8 9.3 %collective-permute-start.6 = (bf16[4,16,16,64]{3,1,2,0:T(8,128)(2,1)S(1)}, bf16[4,16,16,64]{3,1,2,0:T(8,128)(2,1)S(1)}, u32[]{:S(2)}, u32[]{:S(2)}) collective-permute-start(bf16[4,16,16,64]{3,1,2,0:T(8,128)(2,1)S(1)} %pad_maximum_fusion.4), channel_id=1, source_target_pairs={{0,2},{1,3},{2,0},{3,1},{4,6},{5,7},{6,4},{7,5},{8,10},{9,11},{10,... | collective-permute-start | bytes 393224 | tf_op jit(solution)/shard_map/ppermute | solution.py:55
  32.2 9.2 %collective-permute-start.8 = (bf16[4,16,16,64]{3,1,2,0:T(8,128)(2,1)S(1)}, bf16[4,16,16,64]{3,1,2,0:T(8,128)(2,1)S(1)}, u32[]{:S(2)}, u32[]{:S(2)}) collective-permute-start(bf16[4,16,16,64]{3,1,2,0:T(8,128)(2,1)S(1)} %pad_maximum_fusion.5), channel_id=1, source_target_pairs={{0,4},{1,5},{2,6},{3,7},{4,0},{5,1},{6,2},{7,3},{8,12},{9,13},{10,... | collective-permute-start | bytes 393224 | tf_op jit(solution)/shard_map/ppermute | solution.py:55
  34.0 16.9 %collective-permute-start.13 = (f32[4,16,16,64]{3,2,1,0:T(8,128)S(1)}, f32[4,16,16,64]{3,2,1,0:T(8,128)S(1)}, u32[]{:S(2)}, u32[]{:S(2)}) collective-permute-start(f32[4,16,16,64]{3,2,1,0:T(8,128)S(1)} %constant_dynamic-slice_fusion.2), channel_id=1, source_target_pairs={{0,4},{1,5},{2,6},{3,7},{4,0},{5,1},{6,2},{7,3},{8,12},{9,13},{10,... | collective-permute-start | bytes 786440 | tf_op jit(solution)/shard_map/ppermute | solution.py:77
  34.4 18.2 %collective-permute-start.10 = (f32[4,16,16,64]{3,2,1,0:T(8,128)S(1)}, f32[4,16,16,64]{3,2,1,0:T(8,128)S(1)}, u32[]{:S(2)}, u32[]{:S(2)}) collective-permute-start(f32[4,16,16,64]{3,2,1,0:T(8,128)S(1)} %constant_dynamic-slice_fusion.5), channel_id=1, source_target_pairs={{0,2},{1,3},{2,0},{3,1},{4,6},{5,7},{6,4},{7,5},{8,10},{9,11},{10,... | collective-permute-start | bytes 786440 | tf_op jit(solution)/shard_map/ppermute | solution.py:77
  41.3 22.7 %collective-permute-start.7 = (bf16[8,16,16,64]{3,1,2,0:T(8,128)(2,1)S(1)}, bf16[8,16,16,64]{3,1,2,0:T(8,128)(2,1)S(1)}, u32[]{:S(2)}, u32[]{:S(2)}) collective-permute-start(bf16[8,16,16,64]{3,1,2,0:T(8,128)(2,1)S(1)} %pad_maximum_fusion.2), channel_id=1, source_target_pairs={{0,1},{1,0},{2,3},{3,2},{4,5},{5,4},{6,7},{7,6},{8,9},{9,8},{10,11... | collective-permute-start | bytes 786440 | tf_op jit(solution)/shard_map/ppermute | solution.py:55
  41.6 24.0 %collective-permute-start.9 = (bf16[8,16,16,64]{3,1,2,0:T(8,128)(2,1)S(1)}, bf16[8,16,16,64]{3,1,2,0:T(8,128)(2,1)S(1)}, u32[]{:S(2)}, u32[]{:S(2)}) collective-permute-start(bf16[8,16,16,64]{3,1,2,0:T(8,128)(2,1)S(1)} %pad_maximum_fusion.3), channel_id=1, source_target_pairs={{0,1},{1,0},{2,3},{3,2},{4,5},{5,4},{6,7},{7,6},{8,9},{9,8},{10,11... | collective-permute-start | bytes 786440 | tf_op jit(solution)/shard_map/ppermute | solution.py:55
  51.0 6.6 %collective-permute-start.14 = (f32[2,16,16,64]{3,2,1,0:T(8,128)S(1)}, f32[2,16,16,64]{3,2,1,0:T(8,128)S(1)}, u32[]{:S(2)}, u32[]{:S(2)}) collective-permute-start(f32[2,16,16,64]{3,2,1,0:T(8,128)S(1)} %constant_dynamic-slice_fusion.1), channel_id=1, source_target_pairs={{0,2},{1,3},{2,0},{3,1},{4,6},{5,7},{6,4},{7,5},{8,10},{9,11},{10,... | collective-permute-start | bytes 393224 | tf_op jit(solution)/shard_map/ppermute | solution.py:77
  52.7 7.7 %collective-permute-start.11 = (f32[2,16,16,64]{3,2,1,0:T(8,128)S(1)}, f32[2,16,16,64]{3,2,1,0:T(8,128)S(1)}, u32[]{:S(2)}, u32[]{:S(2)}) collective-permute-start(f32[2,16,16,64]{3,2,1,0:T(8,128)S(1)} %constant_dynamic-slice_fusion.4), channel_id=1, source_target_pairs={{0,4},{1,5},{2,6},{3,7},{4,0},{5,1},{6,2},{7,3},{8,12},{9,13},{10,... | collective-permute-start | bytes 393224 | tf_op jit(solution)/shard_map/ppermute | solution.py:77
  57.6 20.4 %collective-permute-start.15 = (f32[1,16,16,64]{3,2,1,0:T(8,128)S(1)}, f32[1,16,16,64]{3,2,1,0:T(8,128)S(1)}, u32[]{:S(2)}, u32[]{:S(2)}) collective-permute-start(f32[1,16,16,64]{3,2,1,0:T(8,128)S(1)} %constant_dynamic-slice_fusion), channel_id=1, source_target_pairs={{0,8},{1,9},{2,10},{3,11},{4,12},{5,13},{6,14},{7,15},{8,0},{9,1},... | collective-permute-start | bytes 196616 | tf_op jit(solution)/shard_map/ppermute | solution.py:77
  60.4 17.5 %collective-permute-start.12 = (f32[1,16,16,64]{3,2,1,0:T(8,128)S(1)}, f32[1,16,16,64]{3,2,1,0:T(8,128)S(1)}, u32[]{:S(2)}, u32[]{:S(2)}) collective-permute-start(f32[1,16,16,64]{3,2,1,0:T(8,128)S(1)} %constant_dynamic-slice_fusion.3), channel_id=1, source_target_pairs={{0,8},{1,9},{2,10},{3,11},{4,12},{5,13},{6,14},{7,15},{8,0},{9,1},... | collective-permute-start | bytes 196616 | tf_op jit(solution)/shard_map/ppermute | solution.py:77
  71.8 4.5 %copy-start.2 = (f32[512,64]{1,0:T(8,128)S(1)}, f32[512,64]{1,0:T(8,128)}, u32[]{:S(2)}) copy-start(f32[512,64]{1,0:T(8,128)} %shard_map.60) | copy-start | bytes 393220

commit v12 on v11

--- a/solution.py
+++ b/solution.py
@@ -150,7 +150,7 @@
     swapped = bits[:1] + bits[1:3][::-1] + bits[3:]
     orders = (tuple(bits), tuple(swapped))
     half = C // len(orders)
-    early = 2
+    early = 1
     gathers = [(right_t[h * half:(h + 1) * half][None], []) for h in range(len(orders))]
     for h in range(len(orders)):
         for bit in orders[h][::-1][:early]:

time: 79.2 us -> 79.7 us (level)
  waiting for transfers between devices: 20.5 us -> 26.5 us
  other arithmetic: 8.32 us -> 5.62 us
  local copies, waits for them, and re-layouts: 10.2 us -> 8.73 us
  starting transfers between devices: 21.8 us -> 20.6 us
    ppermute x8, waiting for transfers between devices: 8.34 us -> 21 us  [gather_step(): other = lax.ppermute(buf, axis, xor_pairs(n, bit))]
    ppermute x8, waiting for transfers between devices: 12.1 us -> 5.45 us  [scatter_step(): return keep + lax.ppermute(send, axis, xor_pairs(n, bit))]
    select_n x6 -> x7, other arithmetic: 2.24 us -> 0.49 us  [gather_step(): low = jnp.where(mine == 0, buf, other)]
    unnamed x11 -> x9, local copies, waits for them, and re-layouts: 3.05 us -> 1.58 us
    concatenate x8 -> x7, other arithmetic: 2.09 us -> 0.79 us  [gather_step(): return (jnp.concatenate([low, high], 0), [bit] + done)]
  transfers between devices with their start and end apart: 16 -> 16, of which waited for: 7 -> 5; matrix products, arithmetic and copies ran while one was open for 19% -> 11% of each run, Pallas kernels for 22% -> 11%
where the time goes in v12:
time: 79.7 us; the launch traced here: 79.4 us
  waiting for transfers between devices  26.5 us (33%)
  starting transfers between devices  20.6 us (26%)
  Pallas kernels  17.1 us (21%)
  local copies, waits for them, and re-layouts  8.73 us (11%)
  other arithmetic  5.62 us (7%)
  between operations  0.9 us (1%)
    ppermute x8, waiting for transfers between devices, gather_step(): other = lax.ppermute(buf, axis, xor_pairs(n, bit))  21 us
    ppermute x8, starting transfers between devices, scatter_step(): return keep + lax.ppermute(send, axis, xor_pairs(n, bit))  11 us
    ppermute x8, starting transfers between devices, gather_step(): other = lax.ppermute(buf, axis, xor_pairs(n, bit))  9.63 us
    pallas_call x2, Pallas kernels, per_device(): pl.pallas_call(left_kernel, grid=(steps,), in_specs=[pl.BlockSpec((half,...  8.94 us
    pallas_call x1, Pallas kernels, per_device(): pl.pallas_call(functools.partial(project_kernel, n_seq=n_seq, orders=orde...  8.21 us
    ppermute x8, waiting for transfers between devices, scatter_step(): return keep + lax.ppermute(send, axis, xor_pairs(n, bit))  5.45 us
    add x6, other arithmetic, scatter_step(): return keep + lax.ppermute(send, axis, xor_pairs(n, bit))  3.29 us
    dynamic_slice x8, local copies, waits for them, and re-layouts, scatter_step(): send = lax.dynamic_slice_in_dim(buf, (1 - mine) * half, half, 0)  2.72 us
  transfers between devices with their start and end apart: 16, of which 5 were waited for; matrix products, arithmetic and copies ran while one was open for 11% of the time, Pallas kernels for 11%

profile of v12, /device:TPU:0, one launch (start us, length us, event | category | flops | bytes accessed | tf_op | source)
XLA Modules:
  0.0 79.4 jit_solution(14049417967299052360)
XLA Ops:
  0.6 1.8 %copy.8 = bf16[32,32,128]{2,0,1:T(8,128)(2,1)} copy(bf16[32,32,128]{2,1,0:T(8,128)(2,1)} %bitcast.43) | data formatting | bytes 524288 | tf_op jit(solution)/shard_map/reshape | solution.py:159
  2.4 0.0 copy-start.2
  2.4 8.2 %shard_map.59 = (bf16[32,512,256]{2,1,0:T(8,128)(2,1)}, f32[16,16,16,64]{3,2,1,0:T(8,128)}, f32[16,16,16,64]{3,2,1,0:T(8,128)}) custom-call(bf16[16,256,128]{2,1,0:T(8,128)(2,1)} %p_ref.1, bf16[1024,128]{1,0:T(8,128)(2,1)} %bitcast.44, bf16[64,512]{1,0:T(8,128)(2,1)} %l_ref.1), custom_call_target="tpu_custom_call" | custom-call | flops 1610612736 | bytes 11534336 | tf_op jit(solution)/shard_map/pallas_call | solution.py:161
  10.6 0.0 copy-start
  10.6 1.5 %constant_dynamic-slice_fusion.7 = f32[8,16,16,64]{3,2,1,0:T(8,128)S(1)} fusion(f32[16,16,16,64]{3,2,1,0:T(8,128)} %get-tuple-element.10, s32[]{:T(128)S(6)} %select_n.128), kind=kLoop, calls=%fused_computation.46 | loop fusion | bytes 1048580 | tf_op jit(solution)/shard_map/dynamic_slice | solution.py:76
  12.1 0.5 collective-permute-start
  12.6 0.0 copy-done.2
  12.6 0.1 copy.9
  12.8 3.7 %collective-permute-start.3 = (bf16[1,16,16,64]{3,1,2,0:T(8,128)(2,1)S(1)}, bf16[1,16,16,64]{3,1,2,0:T(8,128)(2,1)S(1)}, u32[]{:S(2)}, u32[]{:S(2)}) collective-permute-start(bf16[1,16,16,64]{3,1,2,0:T(8,128)(2,1)S(1)} %get-tuple-element.38), channel_id=1, source_target_pairs={{0,8},{1,9},{2,10},{3,11},{4,12},{5,13},{6,14},{7,15},{8,0},{9,1},... | collective-permute-start | bytes 98312 | tf_op jit(solution)/shard_map/ppermute | solution.py:55
  16.4 0.1 collective-permute-start.2
  16.5 0.0 copy-done
  16.5 1.1 %constant_dynamic-slice_fusion.6 = f32[8,16,16,64]{3,2,1,0:T(8,128)} fusion(f32[16,16,16,64]{3,2,1,0:T(8,128)S(1)} %copy-done, s32[]{:T(128)S(6)} %select_n.128), kind=kLoop, calls=%fused_computation.45 | loop fusion | bytes 1048580 | tf_op jit(solution)/shard_map/dynamic_slice | solution.py:76
  17.6 0.2 collective-permute-start.1
  17.8 3.0 %collective-permute-done.3 = bf16[1,16,16,64]{3,1,2,0:T(8,128)(2,1)S(1)} collective-permute-done((bf16[1,16,16,64]{3,1,2,0:T(8,128)(2,1)S(1)}, bf16[1,16,16,64]{3,1,2,0:T(8,128)(2,1)S(1)}, u32[]{:S(2)}, u32[]{:S(2)}) %collective-permute-start.3) | collective-permute-done | bytes 32800 | tf_op jit(solution)/shard_map/ppermute | solution.py:55
  20.8 2.6 %collective-permute-done.2 = bf16[1,16,16,64]{3,1,2,0:T(8,128)(2,1)S(1)} collective-permute-done((bf16[1,16,16,64]{3,1,2,0:T(8,128)(2,1)S(1)}, bf16[1,16,16,64]{3,1,2,0:T(8,128)(2,1)S(1)}, u32[]{:S(2)}, u32[]{:S(2)}) %collective-permute-start.2) | collective-permute-done | bytes 32800 | tf_op jit(solution)/shard_map/ppermute | solution.py:55
  23.4 0.1 pad_maximum_fusion.6
  23.5 0.0 collective-permute-done
  23.5 1.7 %dynamic-slice_add_fusion.1 = f32[8,16,16,64]{3,2,1,0:T(8,128)S(1)} fusion(f32[8,16,16,64]{3,2,1,0:T(8,128)} %collective-permute-done, f32[16,16,16,64]{3,2,1,0:T(8,128)} %get-tuple-element.10, s32[]{:T(128)S(6)} %select_n.127), kind=kLoop, calls=%fused_computation.3 | loop fusion | flops 131072 | bytes 1572868 | tf_op jit(solution)/shard_map/add | solution.py:77
  25.2 0.0 collective-permute-done.1
  25.2 1.4 %dynamic-slice_add_fusion = f32[8,16,16,64]{3,2,1,0:T(8,128)S(1)} fusion(f32[8,16,16,64]{3,2,1,0:T(8,128)} %collective-permute-done.1, f32[16,16,16,64]{3,2,1,0:T(8,128)S(1)} %copy-done, s32[]{:T(128)S(6)} %select_n.127), kind=kLoop, calls=%fused_computation.2 | loop fusion | flops 131072 | bytes 1572868 | tf_op jit(solution)/shard_map/add | solution.py:77
  26.6 0.8 %collective-permute-start.4 = (bf16[2,16,16,64]{3,1,2,0:T(8,128)(2,1)S(1)}, bf16[2,16,16,64]{3,1,2,0:T(8,128)(2,1)S(1)}, u32[]{:S(2)}, u32[]{:S(2)}) collective-permute-start(bf16[2,16,16,64]{3,1,2,0:T(8,128)(2,1)S(1)} %get-tuple-element.12), channel_id=1, source_target_pairs={{0,4},{1,5},{2,6},{3,7},{4,0},{5,1},{6,2},{7,3},{8,12},{9,13},{10,... | collective-permute-start | bytes 196616 | tf_op jit(solution)/shard_map/ppermute | solution.py:55
  27.4 1.5 %collective-permute-start.7 = (bf16[2,16,16,64]{3,1,2,0:T(8,128)(2,1)S(1)}, bf16[2,16,16,64]{3,1,2,0:T(8,128)(2,1)S(1)}, u32[]{:S(2)}, u32[]{:S(2)}) collective-permute-start(bf16[2,16,16,64]{3,1,2,0:T(8,128)(2,1)S(1)} %get-tuple-element.13), channel_id=1, source_target_pairs={{0,2},{1,3},{2,0},{3,1},{4,6},{5,7},{6,4},{7,5},{8,10},{9,11},{10,... | collective-permute-start | bytes 196616 | tf_op jit(solution)/shard_map/ppermute | solution.py:55
  29.0 1.4 %collective-permute-start.13 = (f32[4,16,16,64]{3,2,1,0:T(8,128)S(1)}, f32[4,16,16,64]{3,2,1,0:T(8,128)S(1)}, u32[]{:S(2)}, u32[]{:S(2)}) collective-permute-start(f32[4,16,16,64]{3,2,1,0:T(8,128)S(1)} %constant_dynamic-slice_fusion.2), channel_id=1, source_target_pairs={{0,4},{1,5},{2,6},{3,7},{4,0},{5,1},{6,2},{7,3},{8,12},{9,13},{10,... | collective-permute-start | bytes 786440 | tf_op jit(solution)/shard_map/ppermute | solution.py:77
  30.4 0.5 collective-permute-start.10
  30.9 1.6 %collective-permute-done.4 = bf16[2,16,16,64]{3,1,2,0:T(8,128)(2,1)S(1)} collective-permute-done((bf16[2,16,16,64]{3,1,2,0:T(8,128)(2,1)S(1)}, bf16[2,16,16,64]{3,1,2,0:T(8,128)(2,1)S(1)}, u32[]{:S(2)}, u32[]{:S(2)}) %collective-permute-start.4) | collective-permute-done | bytes 65568 | tf_op jit(solution)/shard_map/ppermute | solution.py:55
  32.5 0.1 pad_maximum_fusion.4
  32.6 2.2 %collective-permute-start.5 = (bf16[4,16,16,64]{3,1,2,0:T(8,128)(2,1)S(1)}, bf16[4,16,16,64]{3,1,2,0:T(8,128)(2,1)S(1)}, u32[]{:S(2)}, u32[]{:S(2)}) collective-permute-start(bf16[4,16,16,64]{3,1,2,0:T(8,128)(2,1)S(1)} %pad_maximum_fusion.4), channel_id=1, source_target_pairs={{0,2},{1,3},{2,0},{3,1},{4,6},{5,7},{6,4},{7,5},{8,10},{9,11},{10,... | collective-permute-start | bytes 393224 | tf_op jit(solution)/shard_map/ppermute | solution.py:55
  34.8 0.0 collective-permute-done.7
  34.8 0.1 pad_maximum_fusion.5
  34.9 0.7 collective-permute-start.8
  35.6 13.8 %collective-permute-done.5 = bf16[4,16,16,64]{3,1,2,0:T(8,128)(2,1)S(1)} collective-permute-done((bf16[4,16,16,64]{3,1,2,0:T(8,128)(2,1)S(1)}, bf16[4,16,16,64]{3,1,2,0:T(8,128)(2,1)S(1)}, u32[]{:S(2)}, u32[]{:S(2)}) %collective-permute-start.5) | collective-permute-done | bytes 131104 | tf_op jit(solution)/shard_map/ppermute | solution.py:55
  49.4 0.1 broadcast_select_fusion.7
  49.5 0.1 pad_maximum_fusion.2
  49.6 0.1 collective-permute-start.6
  49.7 0.0 collective-permute-done.8
  49.7 0.1 broadcast_select_fusion.5
  49.8 0.1 pad_maximum_fusion.3
  49.9 0.5 collective-permute-start.9
  50.5 0.0 collective-permute-done.13
  50.5 0.1 dynamic-slice_add_fusion.2
  50.6 1.6 %collective-permute-start.14 = (f32[2,16,16,64]{3,2,1,0:T(8,128)S(1)}, f32[2,16,16,64]{3,2,1,0:T(8,128)S(1)}, u32[]{:S(2)}, u32[]{:S(2)}) collective-permute-start(f32[2,16,16,64]{3,2,1,0:T(8,128)S(1)} %constant_dynamic-slice_fusion.1), channel_id=1, source_target_pairs={{0,2},{1,3},{2,0},{3,1},{4,6},{5,7},{6,4},{7,5},{8,10},{9,11},{10,... | collective-permute-start | bytes 393224 | tf_op jit(solution)/shard_map/ppermute | solution.py:77
  52.1 0.0 collective-permute-done.10
  52.1 0.1 dynamic-slice_add_fusion.3
  52.2 1.2 %collective-permute-start.11 = (f32[2,16,16,64]{3,2,1,0:T(8,128)S(1)}, f32[2,16,16,64]{3,2,1,0:T(8,128)S(1)}, u32[]{:S(2)}, u32[]{:S(2)}) collective-permute-start(f32[2,16,16,64]{3,2,1,0:T(8,128)S(1)} %constant_dynamic-slice_fusion.4), channel_id=1, source_target_pairs={{0,4},{1,5},{2,6},{3,7},{4,0},{5,1},{6,2},{7,3},{8,12},{9,13},{10,... | collective-permute-start | bytes 393224 | tf_op jit(solution)/shard_map/ppermute | solution.py:77
  53.5 5.4 %collective-permute-done.14 = f32[2,16,16,64]{3,2,1,0:T(8,128)S(1)} collective-permute-done((f32[2,16,16,64]{3,2,1,0:T(8,128)S(1)}, f32[2,16,16,64]{3,2,1,0:T(8,128)S(1)}, u32[]{:S(2)}, u32[]{:S(2)}) %collective-permute-start.14) | collective-permute-done | bytes 131104 | tf_op jit(solution)/shard_map/ppermute | solution.py:77
  58.9 3.4 %collective-permute-start.15 = (f32[1,16,16,64]{3,2,1,0:T(8,128)S(1)}, f32[1,16,16,64]{3,2,1,0:T(8,128)S(1)}, u32[]{:S(2)}, u32[]{:S(2)}) collective-permute-start(f32[1,16,16,64]{3,2,1,0:T(8,128)S(1)} %constant_dynamic-slice_fusion), channel_id=1, source_target_pairs={{0,8},{1,9},{2,10},{3,11},{4,12},{5,13},{6,14},{7,15},{8,0},{9,1},... | collective-permute-start | bytes 196616 | tf_op jit(solution)/shard_map/ppermute | solution.py:77
  62.4 0.0 collective-permute-done.11
  62.5 2.1 %collective-permute-start.12 = (f32[1,16,16,64]{3,2,1,0:T(8,128)S(1)}, f32[1,16,16,64]{3,2,1,0:T(8,128)S(1)}, u32[]{:S(2)}, u32[]{:S(2)}) collective-permute-start(f32[1,16,16,64]{3,2,1,0:T(8,128)S(1)} %constant_dynamic-slice_fusion.3), channel_id=1, source_target_pairs={{0,8},{1,9},{2,10},{3,11},{4,12},{5,13},{6,14},{7,15},{8,0},{9,1},... | collective-permute-start | bytes 196616 | tf_op jit(solution)/shard_map/ppermute | solution.py:77
  64.6 0.0 collective-permute-done.6
  64.6 0.1 broadcast_select_fusion.3
  64.7 0.2 pad_maximum_fusion
  64.9 1.3 %copy.11 = bf16[2,2,2,2,16,16,64]{6,5,4,3,2,1,0:T(8,128)(2,1)} copy(bf16[2,2,2,2,16,16,64]{6,4,5,0,1,2,3:T(8,128)(2,1)S(1)} %bitcast.38) | data formatting | bytes 1048576 | tf_op jit(solution)/shard_map/transpose | solution.py:67
  66.2 0.0 collective-permute-done.9
  66.2 0.1 broadcast_select_fusion.1
  66.4 0.2 pad_maximum_fusion.1
  66.6 1.3 %copy.13 = bf16[2,2,2,2,16,16,64]{6,5,4,3,2,1,0:T(8,128)(2,1)} copy(bf16[2,2,2,2,16,16,64]{6,4,5,0,2,1,3:T(8,128)(2,1)S(1)} %bitcast.39) | data formatting | bytes 1048576 | tf_op jit(solution)/shard_map/transpose | solution.py:67
  67.9 4.4 %shard_map.60 = f32[512,64]{1,0:T(8,128)} custom-call(bf16[32,512,256]{2,1,0:T(8,128)(2,1)} %get-tuple-element.9.gm_ref, bf16[16,16,16,64]{3,2,1,0:T(8,128)(2,1)} %bitcast.36), custom_call_target="tpu_custom_call" | custom-call | flops 268435456 | bytes 4718592 | tf_op jit(solution)/shard_map/pallas_call | solution.py:201
  72.4 4.5 %shard_map.61 = f32[512,64]{1,0:T(8,128)} custom-call(bf16[32,512,256]{2,1,0:T(8,128)(2,1)} %get-tuple-element.9.gm_ref, bf16[16,16,16,64]{3,2,1,0:T(8,128)(2,1)} %bitcast.37), custom_call_target="tpu_custom_call" | custom-call | flops 268435456 | bytes 4718592 | tf_op jit(solution)/shard_map/pallas_call | solution.py:201
  76.9 0.0 copy-done.1
  76.9 1.0 %fusion = bf16[64,512]{0,1:T(8,128)(2,1)S(1)} fusion(f32[512,64]{1,0:T(8,128)S(1)} %copy-done.1, f32[512,64]{1,0:T(8,128)} %shard_map.61), kind=kLoop, calls=%fused_computation.21 | loop fusion | flops 65536 | bytes 327680 | tf_op jit(solution)/shard_map/convert_element_type | solution.py:218
  77.8 0.0 collective-permute-done.15
  77.9 0.7 copy.15
  78.6 0.0 collective-permute-done.12
  78.7 0.7 copy.16
  (17 shorter events, 0.4 us)
Async XLA Ops:
  2.4 10.2 %copy-start.2 = (bf16[64,512]{1,0:T(8,128)(2,1)S(1)}, bf16[64,512]{1,0:T(8,128)(2,1)}, u32[]{:S(2)}) copy-start(bf16[64,512]{1,0:T(8,128)(2,1)} %param.5) | copy-start | bytes 196612
  10.6 5.9 %copy-start = (f32[16,16,16,64]{3,2,1,0:T(8,128)S(1)}, f32[16,16,16,64]{3,2,1,0:T(8,128)}, u32[]{:S(2)}) copy-start(f32[16,16,16,64]{3,2,1,0:T(8,128)} %get-tuple-element.11) | copy-start | bytes 3145732
  12.1 11.4 %collective-permute-start = (f32[8,16,16,64]{3,2,1,0:T(8,128)S(1)}, f32[8,16,16,64]{3,2,1,0:T(8,128)}, u32[]{:S(2)}, u32[]{:S(2)}) collective-permute-start(f32[8,16,16,64]{3,2,1,0:T(8,128)S(1)} %constant_dynamic-slice_fusion.7), channel_id=1, source_target_pairs={{0,1},{1,0},{2,3},{3,2},{4,5},{5,4},{6,7},{7,6},{8,9},{9,8},{10,11... | collective-permute-start | bytes 1572872 | tf_op jit(solution)/shard_map/ppermute | solution.py:77
  12.8 8.0 %collective-permute-start.3 = (bf16[1,16,16,64]{3,1,2,0:T(8,128)(2,1)S(1)}, bf16[1,16,16,64]{3,1,2,0:T(8,128)(2,1)S(1)}, u32[]{:S(2)}, u32[]{:S(2)}) collective-permute-start(bf16[1,16,16,64]{3,1,2,0:T(8,128)(2,1)S(1)} %get-tuple-element.38), channel_id=1, source_target_pairs={{0,8},{1,9},{2,10},{3,11},{4,12},{5,13},{6,14},{7,15},{8,0},{9,1},... | collective-permute-start | bytes 98312 | tf_op jit(solution)/shard_map/ppermute | solution.py:55
  16.4 7.0 %collective-permute-start.2 = (bf16[1,16,16,64]{3,1,2,0:T(8,128)(2,1)S(1)}, bf16[1,16,16,64]{3,1,2,0:T(8,128)(2,1)S(1)}, u32[]{:S(2)}, u32[]{:S(2)}) collective-permute-start(bf16[1,16,16,64]{3,1,2,0:T(8,128)(2,1)S(1)} %get-tuple-element.39), channel_id=1, source_target_pairs={{0,8},{1,9},{2,10},{3,11},{4,12},{5,13},{6,14},{7,15},{8,0},{9,1},... | collective-permute-start | bytes 98312 | tf_op jit(solution)/shard_map/ppermute | solution.py:55
  17.6 7.6 %collective-permute-start.1 = (f32[8,16,16,64]{3,2,1,0:T(8,128)}, f32[8,16,16,64]{3,2,1,0:T(8,128)}, u32[]{:S(2)}, u32[]{:S(2)}) collective-permute-start(f32[8,16,16,64]{3,2,1,0:T(8,128)} %constant_dynamic-slice_fusion.6), channel_id=1, source_target_pairs={{0,1},{1,0},{2,3},{3,2},{4,5},{5,4},{6,7},{7,6},{8,9},{9,8},{10,11... | collective-permute-start | bytes 1572872 | tf_op jit(solution)/shard_map/ppermute | solution.py:77
  26.6 5.9 %collective-permute-start.4 = (bf16[2,16,16,64]{3,1,2,0:T(8,128)(2,1)S(1)}, bf16[2,16,16,64]{3,1,2,0:T(8,128)(2,1)S(1)}, u32[]{:S(2)}, u32[]{:S(2)}) collective-permute-start(bf16[2,16,16,64]{3,1,2,0:T(8,128)(2,1)S(1)} %get-tuple-element.12), channel_id=1, source_target_pairs={{0,4},{1,5},{2,6},{3,7},{4,0},{5,1},{6,2},{7,3},{8,12},{9,13},{10,... | collective-permute-start | bytes 196616 | tf_op jit(solution)/shard_map/ppermute | solution.py:55
  27.4 7.3 %collective-permute-start.7 = (bf16[2,16,16,64]{3,1,2,0:T(8,128)(2,1)S(1)}, bf16[2,16,16,64]{3,1,2,0:T(8,128)(2,1)S(1)}, u32[]{:S(2)}, u32[]{:S(2)}) collective-permute-start(bf16[2,16,16,64]{3,1,2,0:T(8,128)(2,1)S(1)} %get-tuple-element.13), channel_id=1, source_target_pairs={{0,2},{1,3},{2,0},{3,1},{4,6},{5,7},{6,4},{7,5},{8,10},{9,11},{10,... | collective-permute-start | bytes 196616 | tf_op jit(solution)/shard_map/ppermute | solution.py:55
  29.0 21.5 %collective-permute-start.13 = (f32[4,16,16,64]{3,2,1,0:T(8,128)S(1)}, f32[4,16,16,64]{3,2,1,0:T(8,128)S(1)}, u32[]{:S(2)}, u32[]{:S(2)}) collective-permute-start(f32[4,16,16,64]{3,2,1,0:T(8,128)S(1)} %constant_dynamic-slice_fusion.2), channel_id=1, source_target_pairs={{0,4},{1,5},{2,6},{3,7},{4,0},{5,1},{6,2},{7,3},{8,12},{9,13},{10,... | collective-permute-start | bytes 786440 | tf_op jit(solution)/shard_map/ppermute | solution.py:77
  30.4 21.8 %collective-permute-start.10 = (f32[4,16,16,64]{3,2,1,0:T(8,128)S(1)}, f32[4,16,16,64]{3,2,1,0:T(8,128)S(1)}, u32[]{:S(2)}, u32[]{:S(2)}) collective-permute-start(f32[4,16,16,64]{3,2,1,0:T(8,128)S(1)} %constant_dynamic-slice_fusion.5), channel_id=1, source_target_pairs={{0,2},{1,3},{2,0},{3,1},{4,6},{5,7},{6,4},{7,5},{8,10},{9,11},{10,... | collective-permute-start | bytes 786440 | tf_op jit(solution)/shard_map/ppermute | solution.py:77
  32.6 16.9 %collective-permute-start.5 = (bf16[4,16,16,64]{3,1,2,0:T(8,128)(2,1)S(1)}, bf16[4,16,16,64]{3,1,2,0:T(8,128)(2,1)S(1)}, u32[]{:S(2)}, u32[]{:S(2)}) collective-permute-start(bf16[4,16,16,64]{3,1,2,0:T(8,128)(2,1)S(1)} %pad_maximum_fusion.4), channel_id=1, source_target_pairs={{0,2},{1,3},{2,0},{3,1},{4,6},{5,7},{6,4},{7,5},{8,10},{9,11},{10,... | collective-permute-start | bytes 393224 | tf_op jit(solution)/shard_map/ppermute | solution.py:55
  34.9 14.9 %collective-permute-start.8 = (bf16[4,16,16,64]{3,1,2,0:T(8,128)(2,1)S(1)}, bf16[4,16,16,64]{3,1,2,0:T(8,128)(2,1)S(1)}, u32[]{:S(2)}, u32[]{:S(2)}) collective-permute-start(bf16[4,16,16,64]{3,1,2,0:T(8,128)(2,1)S(1)} %pad_maximum_fusion.5), channel_id=1, source_target_pairs={{0,4},{1,5},{2,6},{3,7},{4,0},{5,1},{6,2},{7,3},{8,12},{9,13},{10,... | collective-permute-start | bytes 393224 | tf_op jit(solution)/shard_map/ppermute | solution.py:55
  49.6 15.0 %collective-permute-start.6 = (bf16[8,16,16,64]{3,1,2,0:T(8,128)(2,1)S(1)}, bf16[8,16,16,64]{3,1,2,0:T(8,128)(2,1)S(1)}, u32[]{:S(2)}, u32[]{:S(2)}) collective-permute-start(bf16[8,16,16,64]{3,1,2,0:T(8,128)(2,1)S(1)} %pad_maximum_fusion.2), channel_id=1, source_target_pairs={{0,1},{1,0},{2,3},{3,2},{4,5},{5,4},{6,7},{7,6},{8,9},{9,8},{10,11... | collective-permute-start | bytes 786440 | tf_op jit(solution)/shard_map/ppermute | solution.py:55
  49.9 16.3 %collective-permute-start.9 = (bf16[8,16,16,64]{3,1,2,0:T(8,128)(2,1)S(1)}, bf16[8,16,16,64]{3,1,2,0:T(8,128)(2,1)S(1)}, u32[]{:S(2)}, u32[]{:S(2)}) collective-permute-start(bf16[8,16,16,64]{3,1,2,0:T(8,128)(2,1)S(1)} %pad_maximum_fusion.3), channel_id=1, source_target_pairs={{0,1},{1,0},{2,3},{3,2},{4,5},{5,4},{6,7},{7,6},{8,9},{9,8},{10,11... | collective-permute-start | bytes 786440 | tf_op jit(solution)/shard_map/ppermute | solution.py:55
  50.6 8.3 %collective-permute-start.14 = (f32[2,16,16,64]{3,2,1,0:T(8,128)S(1)}, f32[2,16,16,64]{3,2,1,0:T(8,128)S(1)}, u32[]{:S(2)}, u32[]{:S(2)}) collective-permute-start(f32[2,16,16,64]{3,2,1,0:T(8,128)S(1)} %constant_dynamic-slice_fusion.1), channel_id=1, source_target_pairs={{0,2},{1,3},{2,0},{3,1},{4,6},{5,7},{6,4},{7,5},{8,10},{9,11},{10,... | collective-permute-start | bytes 393224 | tf_op jit(solution)/shard_map/ppermute | solution.py:77
  52.2 10.1 %collective-permute-start.11 = (f32[2,16,16,64]{3,2,1,0:T(8,128)S(1)}, f32[2,16,16,64]{3,2,1,0:T(8,128)S(1)}, u32[]{:S(2)}, u32[]{:S(2)}) collective-permute-start(f32[2,16,16,64]{3,2,1,0:T(8,128)S(1)} %constant_dynamic-slice_fusion.4), channel_id=1, source_target_pairs={{0,4},{1,5},{2,6},{3,7},{4,0},{5,1},{6,2},{7,3},{8,12},{9,13},{10,... | collective-permute-start | bytes 393224 | tf_op jit(solution)/shard_map/ppermute | solution.py:77
  58.9 18.9 %collective-permute-start.15 = (f32[1,16,16,64]{3,2,1,0:T(8,128)S(1)}, f32[1,16,16,64]{3,2,1,0:T(8,128)S(1)}, u32[]{:S(2)}, u32[]{:S(2)}) collective-permute-start(f32[1,16,16,64]{3,2,1,0:T(8,128)S(1)} %constant_dynamic-slice_fusion), channel_id=1, source_target_pairs={{0,8},{1,9},{2,10},{3,11},{4,12},{5,13},{6,14},{7,15},{8,0},{9,1},... | collective-permute-start | bytes 196616 | tf_op jit(solution)/shard_map/ppermute | solution.py:77
  62.5 16.2 %collective-permute-start.12 = (f32[1,16,16,64]{3,2,1,0:T(8,128)S(1)}, f32[1,16,16,64]{3,2,1,0:T(8,128)S(1)}, u32[]{:S(2)}, u32[]{:S(2)}) collective-permute-start(f32[1,16,16,64]{3,2,1,0:T(8,128)S(1)} %constant_dynamic-slice_fusion.3), channel_id=1, source_target_pairs={{0,8},{1,9},{2,10},{3,11},{4,12},{5,13},{6,14},{7,15},{8,0},{9,1},... | collective-permute-start | bytes 196616 | tf_op jit(solution)/shard_map/ppermute | solution.py:77
  72.4 4.5 %copy-start.1 = (f32[512,64]{1,0:T(8,128)S(1)}, f32[512,64]{1,0:T(8,128)}, u32[]{:S(2)}) copy-start(f32[512,64]{1,0:T(8,128)} %shard_map.60) | copy-start | bytes 393220

commit v13 on v11

--- a/solution.py
+++ b/solution.py
@@ -69,12 +69,8 @@
 
 
 def scatter_step(buf, axis, n, bit):
-    me = lax.axis_index(axis)
     half = buf.shape[0] // 2
-    mine = (me >> bit) & 1
-    keep = lax.dynamic_slice_in_dim(buf, mine * half, half, 0)
-    send = lax.dynamic_slice_in_dim(buf, (1 - mine) * half, half, 0)
-    return keep + lax.ppermute(send, axis, xor_pairs(n, bit))
+    return buf[:half] + lax.ppermute(buf[half:], axis, xor_pairs(n, bit))
 
 
 def scatter_sum_ordered(x, axis, bits):
@@ -99,7 +95,7 @@
     return list(range(n.bit_length() - 1))
 
 
-def project_kernel(p_ref, w_ref, l_ref, gm_ref, *pt_refs, n_seq, orders):
+def project_kernel(me_ref, p_ref, w_ref, l_ref, gm_ref, *pt_refs, n_seq, orders):
     rows = p_ref.shape[0]
     width = p_ref.shape[1]
     per_block = width // 16
@@ -112,6 +108,7 @@
         for e in range(C):
             gm_ref[e, i * C:(i + 1) * C, :] = grad[e * C:(e + 1) * C, :]
     first = pl.program_id(0) * per_block
+    me = me_ref[0]
     for e in range(C):
         part = lax.dot_general(
             gm_ref[e], l_ref[...], (((0,), (1,)), ((), ())), preferred_element_type=jnp.float32
@@ -119,7 +116,7 @@
         part = part.reshape(per_block, 16, part.shape[1])
         h = e // half
         for local in range(per_block):
-            pt_refs[h][position(first + local, orders[h]), e % half] = part[local]
+            pt_refs[h][position((first + local) ^ me, orders[h]), e % half] = part[local]
 
 
 def left_kernel(gm_ref, rt_ref, out_ref):
@@ -162,6 +159,7 @@
         functools.partial(project_kernel, n_seq=n_seq, orders=orders),
         grid=(steps,),
         in_specs=[
+            pl.BlockSpec(memory_space=pltpu.SMEM),
             pl.BlockSpec((own_rows, block, p_size), lambda b: (0, b, 0)),
             pl.BlockSpec((C * C, p_size), lambda b: (0, 0)),
             pl.BlockSpec((n_seq, own_rows * C), lambda b: (0, 0)),
@@ -180,7 +178,7 @@
             transcendentals=0,
             bytes_accessed=2 * own_rows * total * (p_size + C * C) + 4 * total * C * n_seq,
         ),
-    )(pair_cot, weight_ec, left_proj)
+    )(lax.axis_index("row").astype(jnp.int32).reshape(1), pair_cot, weight_ec, left_proj)
 
     scatters = [scatter_step(part_t[h], "row", n, orders[h][0]) for h in range(len(orders))]
     bufs = [g[0] for g in gathers]

time: 79.2 us -> 81.8 us (1.033)
  waiting for transfers between devices: 20.5 us -> 22.6 us
  Pallas kernels: 17.1 us -> 18.4 us
  starting transfers between devices: 21.8 us -> 20.6 us
    dynamic_slice x8 -> x0, local copies, waits for them, and re-layouts: 2.72 us -> none  [scatter_step(): send = lax.dynamic_slice_in_dim(buf, (1 - mine) * half, half, 0)]
    slice x0 -> x8, local copies, waits for them, and re-layouts: none -> 2.64 us  [scatter_step(): return buf[:half] + lax.ppermute(buf[half:], axis, xor_pairs(n, bit))]
    ppermute x8, waiting for transfers between devices: 8.34 us -> 9.7 us  [gather_step(): other = lax.ppermute(buf, axis, xor_pairs(n, bit))]
    ppermute x8, starting transfers between devices: 10.2 us -> 8.92 us  [gather_step(): other = lax.ppermute(buf, axis, xor_pairs(n, bit))]
    pallas_call x1, Pallas kernels: 8.19 us -> 9.45 us  [per_device(): pl.pallas_call(functools.partial(project_kernel, n_seq=n_seq, orders=orde...]
  transfers between devices with their start and end apart: 16 -> 16, of which waited for: 7 -> 5; matrix products, arithmetic and copies ran while one was open for 19% -> 18% of each run, Pallas kernels for 22% -> 23%
where the time goes in v13:
time: 81.8 us; the launch traced here: 81.4 us
  waiting for transfers between devices  22.6 us (28%)
  starting transfers between devices  20.6 us (25%)
  Pallas kernels  18.4 us (22%)
  local copies, waits for them, and re-layouts  9.84 us (12%)
  other arithmetic  9.12 us (11%)
  between operations  0.89 us (1%)
    ppermute x8, waiting for transfers between devices, scatter_step(): return buf[:half] + lax.ppermute(buf[half:], axis, xor_pairs(n, bit))  12.9 us
    ppermute x8, starting transfers between devices, scatter_step(): return buf[:half] + lax.ppermute(buf[half:], axis, xor_pairs(n, bit))  11.7 us
    ppermute x8, waiting for transfers between devices, gather_step(): other = lax.ppermute(buf, axis, xor_pairs(n, bit))  9.7 us
    pallas_call x1, Pallas kernels, per_device(): pl.pallas_call(functools.partial(project_kernel, n_seq=n_seq, orders=orde...  9.45 us
    pallas_call x2, Pallas kernels, per_device(): pl.pallas_call(left_kernel, grid=(steps,), in_specs=[pl.BlockSpec((half,...  8.93 us
    ppermute x8, starting transfers between devices, gather_step(): other = lax.ppermute(buf, axis, xor_pairs(n, bit))  8.92 us
    add x6, other arithmetic, scatter_step(): return buf[:half] + lax.ppermute(buf[half:], axis, xor_pairs(n, bit))  2.94 us
    concatenate x8, other arithmetic, gather_step(): return (jnp.concatenate([low, high], 0), [bit] + done)  2.82 us
  transfers between devices with their start and end apart: 16, of which 5 were waited for; matrix products, arithmetic and copies ran while one was open for 18% of the time, Pallas kernels for 23%

profile of v13, /device:TPU:0, one launch (start us, length us, event | category | flops | bytes accessed | tf_op | source)
XLA Modules:
  0.0 81.4 jit_solution(3975246367444259896)
XLA Ops:
  0.6 1.0 %copy.9 = bf16[64,512]{0,1:T(8,128)(2,1)S(1)} copy(bf16[64,512]{1,0:T(8,128)(2,1)} %param.5) | data formatting | bytes 131072 | tf_op args[1]
  1.6 4.1 %collective-permute-start.4 = (bf16[1,16,16,64]{3,1,2,0:T(8,128)(2,1)S(1)}, bf16[1,16,16,64]{3,1,2,0:T(8,128)(2,1)S(1)}, u32[]{:S(2)}, u32[]{:S(2)}) collective-permute-start(bf16[1,16,16,64]{3,1,2,0:T(8,128)(2,1)S(1)} %get-tuple-element.38), channel_id=1, source_target_pairs={{0,8},{1,9},{2,10},{3,11},{4,12},{5,13},{6,14},{7,15},{8,0},{9,1},... | collective-permute-start | bytes 98312 | tf_op jit(solution)/shard_map/ppermute | solution.py:55
  5.7 0.1 collective-permute-start.2
  5.8 1.8 %copy.8 = bf16[32,32,128]{2,0,1:T(8,128)(2,1)} copy(bf16[32,32,128]{2,1,0:T(8,128)(2,1)} %bitcast.44) | data formatting | bytes 524288 | tf_op jit(solution)/shard_map/reshape | solution.py:156
  7.6 1.8 %collective-permute-done.4 = bf16[1,16,16,64]{3,1,2,0:T(8,128)(2,1)S(1)} collective-permute-done((bf16[1,16,16,64]{3,1,2,0:T(8,128)(2,1)S(1)}, bf16[1,16,16,64]{3,1,2,0:T(8,128)(2,1)S(1)}, u32[]{:S(2)}, u32[]{:S(2)}) %collective-permute-start.4) | collective-permute-done | bytes 32800 | tf_op jit(solution)/shard_map/ppermute | solution.py:55
  9.4 2.8 %collective-permute-done.2 = bf16[1,16,16,64]{3,1,2,0:T(8,128)(2,1)S(1)} collective-permute-done((bf16[1,16,16,64]{3,1,2,0:T(8,128)(2,1)S(1)}, bf16[1,16,16,64]{3,1,2,0:T(8,128)(2,1)S(1)}, u32[]{:S(2)}, u32[]{:S(2)}) %collective-permute-start.2) | collective-permute-done | bytes 32800 | tf_op jit(solution)/shard_map/ppermute | solution.py:55
  12.2 0.7 pad_maximum_fusion.7
  12.9 1.7 %collective-permute-start.5 = (bf16[2,16,16,64]{3,1,2,0:T(8,128)(2,1)}, bf16[2,16,16,64]{3,1,2,0:T(8,128)(2,1)S(1)}, u32[]{:S(2)}, u32[]{:S(2)}) collective-permute-start(bf16[2,16,16,64]{3,1,2,0:T(8,128)(2,1)} %pad_maximum_fusion.7), channel_id=1, source_target_pairs={{0,2},{1,3},{2,0},{3,1},{4,6},{5,7},{6,4},{7,5},{8,10},{9,11},{10,... | collective-permute-start | bytes 196616 | tf_op jit(solution)/shard_map/ppermute | solution.py:55
  14.6 0.7 pad_maximum_fusion.6
  15.3 0.4 collective-permute-start.3
  15.6 9.5 %shard_map.59 = (bf16[32,512,256]{2,1,0:T(8,128)(2,1)}, f32[16,16,16,64]{3,2,1,0:T(8,128)}, f32[16,16,16,64]{3,2,1,0:T(8,128)}) custom-call(s32[1]{0:T(128)} %bitcast.me_ref, bf16[16,256,128]{2,1,0:T(8,128)(2,1)} %p_ref.1, bf16[1024,128]{1,0:T(8,128)(2,1)} %bitcast.45, bf16[64,512]{1,0:T(8,128)(2,1)} %l_ref.1), custom_call_target="tpu_custom_call" | custom-call | flops 1610612736 | bytes 11534336 | tf_op jit(solution)/shard_map/pallas_call | solution.py:158
  25.1 1.5 %slice.55 = f32[8,16,16,64]{3,2,1,0:T(8,128)S(1)} slice(f32[16,16,16,64]{3,2,1,0:T(8,128)} %get-tuple-element.10), slice={[8:16], [0:16], [0:16], [0:64]} | slice | bytes 1048576 | tf_op jit(solution)/shard_map/slice | solution.py:73
  26.6 0.1 collective-permute-start
  26.7 0.3 copy-done
  27.0 1.0 %slice.57 = f32[8,16,16,64]{3,2,1,0:T(8,128)} slice(f32[16,16,16,64]{3,2,1,0:T(8,128)S(1)} %copy-done), slice={[8:16], [0:16], [0:16], [0:64]} | slice | bytes 1048576 | tf_op jit(solution)/shard_map/slice | solution.py:73
  28.1 0.2 collective-permute-start.1
  28.2 0.0 collective-permute-done.5
  28.2 0.0 collective-permute-done.3
  28.2 1.0 %broadcast_select_fusion.9 = (bf16[2,16,16,64]{3,1,2,0:T(8,128)(2,1)S(1)}, bf16[2,16,16,64]{3,1,2,0:T(8,128)(2,1)S(1)}, bf16[2,16,16,64]{3,1,2,0:T(8,128)(2,1)S(1)}, bf16[2,16,16,64]{3,1,2,0:T(8,128)(2,1)S(1)}) fusion(bf16[2,16,16,64]{3,1,2,0:T(8,128)(2,1)S(1)} %collective-permute-done.5, pred[]{:T(512)S(6)} %eq.9, ...), kind=kLoop, calls=%fused_computation.30 | loop fusion | flops 196608 | bytes 524290 | tf_op jit(solution)/shard_map/jit(_where)/select_n | solution.py:57
  29.2 0.0 copy-start.1
  29.2 0.8 pad_maximum_fusion.4
  30.0 0.1 pad_maximum_fusion.5
  30.0 0.0 collective-permute-done
  30.1 0.0 copy-done.2
  30.1 1.4 %slice_add_fusion.1 = f32[8,16,16,64]{3,2,1,0:T(8,128)S(1)} fusion(f32[8,16,16,64]{3,2,1,0:T(8,128)} %collective-permute-done, f32[16,16,16,64]{3,2,1,0:T(8,128)S(1)} %copy-done.2), kind=kLoop, calls=%fused_computation.3 | loop fusion | flops 131072 | bytes 1572864 | tf_op jit(solution)/shard_map/add | solution.py:73
  31.4 0.0 collective-permute-done.1
  31.5 1.4 %slice_add_fusion = f32[8,16,16,64]{3,2,1,0:T(8,128)S(1)} fusion(f32[8,16,16,64]{3,2,1,0:T(8,128)} %collective-permute-done.1, f32[16,16,16,64]{3,2,1,0:T(8,128)S(1)} %copy-done.1), kind=kLoop, calls=%fused_computation.2 | loop fusion | flops 131072 | bytes 1572864 | tf_op jit(solution)/shard_map/add | solution.py:73
  32.8 0.6 collective-permute-start.6
  33.4 1.5 %collective-permute-start.8 = (bf16[4,16,16,64]{3,1,2,0:T(8,128)(2,1)S(1)}, bf16[4,16,16,64]{3,1,2,0:T(8,128)(2,1)S(1)}, u32[]{:S(2)}, u32[]{:S(2)}) collective-permute-start(bf16[4,16,16,64]{3,1,2,0:T(8,128)(2,1)S(1)} %pad_maximum_fusion.5), channel_id=1, source_target_pairs={{0,4},{1,5},{2,6},{3,7},{4,0},{5,1},{6,2},{7,3},{8,12},{9,13},{10,... | collective-permute-start | bytes 393224 | tf_op jit(solution)/shard_map/ppermute | solution.py:55
  34.9 0.6 collective-permute-start.13
  35.6 1.6 %collective-permute-start.10 = (f32[4,16,16,64]{3,2,1,0:T(8,128)S(1)}, f32[4,16,16,64]{3,2,1,0:T(8,128)S(1)}, u32[]{:S(2)}, u32[]{:S(2)}) collective-permute-start(f32[4,16,16,64]{3,2,1,0:T(8,128)S(1)} %slice.61), channel_id=1, source_target_pairs={{0,2},{1,3},{2,0},{3,1},{4,6},{5,7},{6,4},{7,5},{8,10},{9,11},{10,... | collective-permute-start | bytes 786440 | tf_op jit(solution)/shard_map/ppermute | solution.py:73
  37.1 5.1 %collective-permute-done.6 = bf16[4,16,16,64]{3,1,2,0:T(8,128)(2,1)S(1)} collective-permute-done((bf16[4,16,16,64]{3,1,2,0:T(8,128)(2,1)}, bf16[4,16,16,64]{3,1,2,0:T(8,128)(2,1)S(1)}, u32[]{:S(2)}, u32[]{:S(2)}) %collective-permute-start.6) | collective-permute-done | bytes 131104 | tf_op jit(solution)/shard_map/ppermute | solution.py:55
  42.2 1.0 %broadcast_select_fusion.7 = (bf16[4,16,16,64]{3,1,2,0:T(8,128)(2,1)S(1)}, bf16[4,16,16,64]{3,1,2,0:T(8,128)(2,1)S(1)}) fusion(bf16[4,16,16,64]{3,1,2,0:T(8,128)(2,1)} %pad_maximum_fusion.4, bf16[4,16,16,64]{3,1,2,0:T(8,128)(2,1)S(1)} %collective-permute-done.6, pred[]{:T(512)S(6)} %eq.9), kind=kLoop, calls=%fused_computation.20 | loop fusion | flops 131072 | bytes 524289 | tf_op jit(solution)/shard_map/jit(_where)/select_n | solution.py:57
  43.2 0.1 pad_maximum_fusion.2
  43.3 0.1 collective-permute-start.7
  43.4 0.0 collective-permute-done.8
  43.5 0.1 pad_maximum_fusion.3
  43.6 0.5 collective-permute-start.9
  44.1 8.8 %collective-permute-done.13 = f32[4,16,16,64]{3,2,1,0:T(8,128)S(1)} collective-permute-done((f32[4,16,16,64]{3,2,1,0:T(8,128)S(1)}, f32[4,16,16,64]{3,2,1,0:T(8,128)S(1)}, u32[]{:S(2)}, u32[]{:S(2)}) %collective-permute-start.13) | collective-permute-done | bytes 262176 | tf_op jit(solution)/shard_map/ppermute | solution.py:73
  52.9 0.1 slice_add_fusion.2
  53.0 1.6 %collective-permute-start.14 = (f32[2,16,16,64]{3,2,1,0:T(8,128)S(1)}, f32[2,16,16,64]{3,2,1,0:T(8,128)S(1)}, u32[]{:S(2)}, u32[]{:S(2)}) collective-permute-start(f32[2,16,16,64]{3,2,1,0:T(8,128)S(1)} %slice.79), channel_id=1, source_target_pairs={{0,2},{1,3},{2,0},{3,1},{4,6},{5,7},{6,4},{7,5},{8,10},{9,11},{10,... | collective-permute-start | bytes 393224 | tf_op jit(solution)/shard_map/ppermute | solution.py:73
  54.6 0.0 collective-permute-done.10
  54.6 0.1 slice_add_fusion.3
  54.7 1.7 %collective-permute-start.11 = (f32[2,16,16,64]{3,2,1,0:T(8,128)S(1)}, f32[2,16,16,64]{3,2,1,0:T(8,128)S(1)}, u32[]{:S(2)}, u32[]{:S(2)}) collective-permute-start(f32[2,16,16,64]{3,2,1,0:T(8,128)S(1)} %slice.75), channel_id=1, source_target_pairs={{0,4},{1,5},{2,6},{3,7},{4,0},{5,1},{6,2},{7,3},{8,12},{9,13},{10,... | collective-permute-start | bytes 393224 | tf_op jit(solution)/shard_map/ppermute | solution.py:73
  56.4 4.1 %collective-permute-done.14 = f32[2,16,16,64]{3,2,1,0:T(8,128)S(1)} collective-permute-done((f32[2,16,16,64]{3,2,1,0:T(8,128)S(1)}, f32[2,16,16,64]{3,2,1,0:T(8,128)S(1)}, u32[]{:S(2)}, u32[]{:S(2)}) %collective-permute-start.14) | collective-permute-done | bytes 131104 | tf_op jit(solution)/shard_map/ppermute | solution.py:73
  60.6 3.4 %collective-permute-start.15 = (f32[1,16,16,64]{3,2,1,0:T(8,128)S(1)}, f32[1,16,16,64]{3,2,1,0:T(8,128)S(1)}, u32[]{:S(2)}, u32[]{:S(2)}) collective-permute-start(f32[1,16,16,64]{3,2,1,0:T(8,128)S(1)} %slice.81), channel_id=1, source_target_pairs={{0,8},{1,9},{2,10},{3,11},{4,12},{5,13},{6,14},{7,15},{8,0},{9,1},... | collective-permute-start | bytes 196616 | tf_op jit(solution)/shard_map/ppermute | solution.py:73
  64.0 0.0 collective-permute-done.11
  64.1 2.5 %collective-permute-start.12 = (f32[1,16,16,64]{3,2,1,0:T(8,128)S(1)}, f32[1,16,16,64]{3,2,1,0:T(8,128)S(1)}, u32[]{:S(2)}, u32[]{:S(2)}) collective-permute-start(f32[1,16,16,64]{3,2,1,0:T(8,128)S(1)} %slice.77), channel_id=1, source_target_pairs={{0,8},{1,9},{2,10},{3,11},{4,12},{5,13},{6,14},{7,15},{8,0},{9,1},... | collective-permute-start | bytes 196616 | tf_op jit(solution)/shard_map/ppermute | solution.py:73
  66.6 0.0 collective-permute-done.7
  66.6 0.1 broadcast_select_fusion.3
  66.7 0.2 pad_maximum_fusion
  66.9 1.3 %copy.11 = bf16[2,2,2,2,16,16,64]{6,5,4,3,2,1,0:T(8,128)(2,1)} copy(bf16[2,2,2,2,16,16,64]{6,4,5,0,1,2,3:T(8,128)(2,1)S(1)} %bitcast.39) | data formatting | bytes 1048576 | tf_op jit(solution)/shard_map/transpose | solution.py:67
  68.2 0.0 collective-permute-done.9
  68.2 0.1 broadcast_select_fusion.1
  68.3 0.2 pad_maximum_fusion.1
  68.6 1.3 %copy.13 = bf16[2,2,2,2,16,16,64]{6,5,4,3,2,1,0:T(8,128)(2,1)} copy(bf16[2,2,2,2,16,16,64]{6,4,5,0,2,1,3:T(8,128)(2,1)S(1)} %bitcast.40) | data formatting | bytes 1048576 | tf_op jit(solution)/shard_map/transpose | solution.py:67
  69.9 4.4 %shard_map.60 = f32[512,64]{1,0:T(8,128)} custom-call(bf16[32,512,256]{2,1,0:T(8,128)(2,1)} %get-tuple-element.9.gm_ref, bf16[16,16,16,64]{3,2,1,0:T(8,128)(2,1)} %bitcast.37), custom_call_target="tpu_custom_call" | custom-call | flops 268435456 | bytes 4718592 | tf_op jit(solution)/shard_map/pallas_call | solution.py:199
  74.3 4.5 %shard_map.61 = f32[512,64]{1,0:T(8,128)} custom-call(bf16[32,512,256]{2,1,0:T(8,128)(2,1)} %get-tuple-element.9.gm_ref, bf16[16,16,16,64]{3,2,1,0:T(8,128)(2,1)} %bitcast.38), custom_call_target="tpu_custom_call" | custom-call | flops 268435456 | bytes 4718592 | tf_op jit(solution)/shard_map/pallas_call | solution.py:199
  78.8 0.0 copy-done.3
  78.8 1.0 %fusion = bf16[64,512]{0,1:T(8,128)(2,1)S(1)} fusion(f32[512,64]{1,0:T(8,128)S(1)} %copy-done.3, f32[512,64]{1,0:T(8,128)} %shard_map.61), kind=kLoop, calls=%fused_computation.21 | loop fusion | flops 65536 | bytes 327680 | tf_op jit(solution)/shard_map/convert_element_type | solution.py:216
  79.8 0.7 copy.15
  80.5 0.0 collective-permute-done.15
  80.6 0.0 collective-permute-done.12
  80.7 0.7 copy.16
  (19 shorter events, 0.4 us)
Async XLA Ops:
  1.6 7.8 %collective-permute-start.4 = (bf16[1,16,16,64]{3,1,2,0:T(8,128)(2,1)S(1)}, bf16[1,16,16,64]{3,1,2,0:T(8,128)(2,1)S(1)}, u32[]{:S(2)}, u32[]{:S(2)}) collective-permute-start(bf16[1,16,16,64]{3,1,2,0:T(8,128)(2,1)S(1)} %get-tuple-element.38), channel_id=1, source_target_pairs={{0,8},{1,9},{2,10},{3,11},{4,12},{5,13},{6,14},{7,15},{8,0},{9,1},... | collective-permute-start | bytes 98312 | tf_op jit(solution)/shard_map/ppermute | solution.py:55
  5.7 6.5 %collective-permute-start.2 = (bf16[1,16,16,64]{3,1,2,0:T(8,128)(2,1)S(1)}, bf16[1,16,16,64]{3,1,2,0:T(8,128)(2,1)S(1)}, u32[]{:S(2)}, u32[]{:S(2)}) collective-permute-start(bf16[1,16,16,64]{3,1,2,0:T(8,128)(2,1)S(1)} %get-tuple-element.39), channel_id=1, source_target_pairs={{0,8},{1,9},{2,10},{3,11},{4,12},{5,13},{6,14},{7,15},{8,0},{9,1},... | collective-permute-start | bytes 98312 | tf_op jit(solution)/shard_map/ppermute | solution.py:55
  12.9 15.3 %collective-permute-start.5 = (bf16[2,16,16,64]{3,1,2,0:T(8,128)(2,1)}, bf16[2,16,16,64]{3,1,2,0:T(8,128)(2,1)S(1)}, u32[]{:S(2)}, u32[]{:S(2)}) collective-permute-start(bf16[2,16,16,64]{3,1,2,0:T(8,128)(2,1)} %pad_maximum_fusion.7), channel_id=1, source_target_pairs={{0,2},{1,3},{2,0},{3,1},{4,6},{5,7},{6,4},{7,5},{8,10},{9,11},{10,... | collective-permute-start | bytes 196616 | tf_op jit(solution)/shard_map/ppermute | solution.py:55
  15.3 12.9 %collective-permute-start.3 = (bf16[2,16,16,64]{3,1,2,0:T(8,128)(2,1)}, bf16[2,16,16,64]{3,1,2,0:T(8,128)(2,1)}, u32[]{:S(2)}, u32[]{:S(2)}) collective-permute-start(bf16[2,16,16,64]{3,1,2,0:T(8,128)(2,1)} %pad_maximum_fusion.6), channel_id=1, source_target_pairs={{0,4},{1,5},{2,6},{3,7},{4,0},{5,1},{6,2},{7,3},{8,12},{9,13},{10,... | collective-permute-start | bytes 196616 | tf_op jit(solution)/shard_map/ppermute | solution.py:55
  25.1 1.9 %copy-start = (f32[16,16,16,64]{3,2,1,0:T(8,128)S(1)}, f32[16,16,16,64]{3,2,1,0:T(8,128)}, u32[]{:S(2)}) copy-start(f32[16,16,16,64]{3,2,1,0:T(8,128)} %get-tuple-element.11) | copy-start | bytes 3145732
  26.6 3.5 %collective-permute-start = (f32[8,16,16,64]{3,2,1,0:T(8,128)S(1)}, f32[8,16,16,64]{3,2,1,0:T(8,128)}, u32[]{:S(2)}, u32[]{:S(2)}) collective-permute-start(f32[8,16,16,64]{3,2,1,0:T(8,128)S(1)} %slice.55), channel_id=1, source_target_pairs={{0,1},{1,0},{2,3},{3,2},{4,5},{5,4},{6,7},{7,6},{8,9},{9,8},{10,11... | collective-permute-start | bytes 1572872 | tf_op jit(solution)/shard_map/ppermute | solution.py:73
  27.0 3.1 %copy-start.2 = (f32[16,16,16,64]{3,2,1,0:T(8,128)S(1)}, f32[16,16,16,64]{3,2,1,0:T(8,128)}, u32[]{:S(2)}) copy-start(f32[16,16,16,64]{3,2,1,0:T(8,128)} %get-tuple-element.10) | copy-start | bytes 3145732
  28.1 3.4 %collective-permute-start.1 = (f32[8,16,16,64]{3,2,1,0:T(8,128)}, f32[8,16,16,64]{3,2,1,0:T(8,128)}, u32[]{:S(2)}, u32[]{:S(2)}) collective-permute-start(f32[8,16,16,64]{3,2,1,0:T(8,128)} %slice.57), channel_id=1, source_target_pairs={{0,1},{1,0},{2,3},{3,2},{4,5},{5,4},{6,7},{7,6},{8,9},{9,8},{10,11... | collective-permute-start | bytes 1572872 | tf_op jit(solution)/shard_map/ppermute | solution.py:73
  29.2 2.2 %copy-start.1 = (f32[16,16,16,64]{3,2,1,0:T(8,128)S(1)}, f32[16,16,16,64]{3,2,1,0:T(8,128)}, u32[]{:S(2)}) copy-start(f32[16,16,16,64]{3,2,1,0:T(8,128)} %get-tuple-element.11) | copy-start | bytes 3145732
  32.8 9.4 %collective-permute-start.6 = (bf16[4,16,16,64]{3,1,2,0:T(8,128)(2,1)}, bf16[4,16,16,64]{3,1,2,0:T(8,128)(2,1)S(1)}, u32[]{:S(2)}, u32[]{:S(2)}) collective-permute-start(bf16[4,16,16,64]{3,1,2,0:T(8,128)(2,1)} %pad_maximum_fusion.4), channel_id=1, source_target_pairs={{0,2},{1,3},{2,0},{3,1},{4,6},{5,7},{6,4},{7,5},{8,10},{9,11},{10,... | collective-permute-start | bytes 393224 | tf_op jit(solution)/shard_map/ppermute | solution.py:55
  33.4 10.0 %collective-permute-start.8 = (bf16[4,16,16,64]{3,1,2,0:T(8,128)(2,1)S(1)}, bf16[4,16,16,64]{3,1,2,0:T(8,128)(2,1)S(1)}, u32[]{:S(2)}, u32[]{:S(2)}) collective-permute-start(bf16[4,16,16,64]{3,1,2,0:T(8,128)(2,1)S(1)} %pad_maximum_fusion.5), channel_id=1, source_target_pairs={{0,4},{1,5},{2,6},{3,7},{4,0},{5,1},{6,2},{7,3},{8,12},{9,13},{10,... | collective-permute-start | bytes 393224 | tf_op jit(solution)/shard_map/ppermute | solution.py:55
  34.9 18.0 %collective-permute-start.13 = (f32[4,16,16,64]{3,2,1,0:T(8,128)S(1)}, f32[4,16,16,64]{3,2,1,0:T(8,128)S(1)}, u32[]{:S(2)}, u32[]{:S(2)}) collective-permute-start(f32[4,16,16,64]{3,2,1,0:T(8,128)S(1)} %slice.67), channel_id=1, source_target_pairs={{0,4},{1,5},{2,6},{3,7},{4,0},{5,1},{6,2},{7,3},{8,12},{9,13},{10,... | collective-permute-start | bytes 786440 | tf_op jit(solution)/shard_map/ppermute | solution.py:73
  35.6 19.0 %collective-permute-start.10 = (f32[4,16,16,64]{3,2,1,0:T(8,128)S(1)}, f32[4,16,16,64]{3,2,1,0:T(8,128)S(1)}, u32[]{:S(2)}, u32[]{:S(2)}) collective-permute-start(f32[4,16,16,64]{3,2,1,0:T(8,128)S(1)} %slice.61), channel_id=1, source_target_pairs={{0,2},{1,3},{2,0},{3,1},{4,6},{5,7},{6,4},{7,5},{8,10},{9,11},{10,... | collective-permute-start | bytes 786440 | tf_op jit(solution)/shard_map/ppermute | solution.py:73
  43.3 23.2 %collective-permute-start.7 = (bf16[8,16,16,64]{3,1,2,0:T(8,128)(2,1)S(1)}, bf16[8,16,16,64]{3,1,2,0:T(8,128)(2,1)S(1)}, u32[]{:S(2)}, u32[]{:S(2)}) collective-permute-start(bf16[8,16,16,64]{3,1,2,0:T(8,128)(2,1)S(1)} %pad_maximum_fusion.2), channel_id=1, source_target_pairs={{0,1},{1,0},{2,3},{3,2},{4,5},{5,4},{6,7},{7,6},{8,9},{9,8},{10,11... | collective-permute-start | bytes 786440 | tf_op jit(solution)/shard_map/ppermute | solution.py:55
  43.6 24.6 %collective-permute-start.9 = (bf16[8,16,16,64]{3,1,2,0:T(8,128)(2,1)S(1)}, bf16[8,16,16,64]{3,1,2,0:T(8,128)(2,1)S(1)}, u32[]{:S(2)}, u32[]{:S(2)}) collective-permute-start(bf16[8,16,16,64]{3,1,2,0:T(8,128)(2,1)S(1)} %pad_maximum_fusion.3), channel_id=1, source_target_pairs={{0,1},{1,0},{2,3},{3,2},{4,5},{5,4},{6,7},{7,6},{8,9},{9,8},{10,11... | collective-permute-start | bytes 786440 | tf_op jit(solution)/shard_map/ppermute | solution.py:55
  53.0 7.5 %collective-permute-start.14 = (f32[2,16,16,64]{3,2,1,0:T(8,128)S(1)}, f32[2,16,16,64]{3,2,1,0:T(8,128)S(1)}, u32[]{:S(2)}, u32[]{:S(2)}) collective-permute-start(f32[2,16,16,64]{3,2,1,0:T(8,128)S(1)} %slice.79), channel_id=1, source_target_pairs={{0,2},{1,3},{2,0},{3,1},{4,6},{5,7},{6,4},{7,5},{8,10},{9,11},{10,... | collective-permute-start | bytes 393224 | tf_op jit(solution)/shard_map/ppermute | solution.py:73
  54.7 9.3 %collective-permute-start.11 = (f32[2,16,16,64]{3,2,1,0:T(8,128)S(1)}, f32[2,16,16,64]{3,2,1,0:T(8,128)S(1)}, u32[]{:S(2)}, u32[]{:S(2)}) collective-permute-start(f32[2,16,16,64]{3,2,1,0:T(8,128)S(1)} %slice.75), channel_id=1, source_target_pairs={{0,4},{1,5},{2,6},{3,7},{4,0},{5,1},{6,2},{7,3},{8,12},{9,13},{10,... | collective-permute-start | bytes 393224 | tf_op jit(solution)/shard_map/ppermute | solution.py:73
  60.6 20.0 %collective-permute-start.15 = (f32[1,16,16,64]{3,2,1,0:T(8,128)S(1)}, f32[1,16,16,64]{3,2,1,0:T(8,128)S(1)}, u32[]{:S(2)}, u32[]{:S(2)}) collective-permute-start(f32[1,16,16,64]{3,2,1,0:T(8,128)S(1)} %slice.81), channel_id=1, source_target_pairs={{0,8},{1,9},{2,10},{3,11},{4,12},{5,13},{6,14},{7,15},{8,0},{9,1},... | collective-permute-start | bytes 196616 | tf_op jit(solution)/shard_map/ppermute | solution.py:73
  64.1 16.5 %collective-permute-start.12 = (f32[1,16,16,64]{3,2,1,0:T(8,128)S(1)}, f32[1,16,16,64]{3,2,1,0:T(8,128)S(1)}, u32[]{:S(2)}, u32[]{:S(2)}) collective-permute-start(f32[1,16,16,64]{3,2,1,0:T(8,128)S(1)} %slice.77), channel_id=1, source_target_pairs={{0,8},{1,9},{2,10},{3,11},{4,12},{5,13},{6,14},{7,15},{8,0},{9,1},... | collective-permute-start | bytes 196616 | tf_op jit(solution)/shard_map/ppermute | solution.py:73
  74.3 4.5 %copy-start.3 = (f32[512,64]{1,0:T(8,128)S(1)}, f32[512,64]{1,0:T(8,128)}, u32[]{:S(2)}) copy-start(f32[512,64]{1,0:T(8,128)} %shard_map.60) | copy-start | bytes 393220

commit v14 on v10

--- a/solution.py
+++ b/solution.py
@@ -99,7 +99,7 @@
     return list(range(n.bit_length() - 1))
 
 
-def project_kernel(p_ref, w_ref, l_ref, gm_ref, pt_ref, *, n_seq, orders):
+def project_kernel(p_ref, w_ref, l_ref, gm_ref, *pt_refs, n_seq, orders):
     rows = p_ref.shape[0]
     width = p_ref.shape[1]
     per_block = width // 16
@@ -119,7 +119,7 @@
         part = part.reshape(per_block, 16, part.shape[1])
         h = e // half
         for local in range(per_block):
-            pt_ref[h, position(first + local, orders[h]), e % half] = part[local]
+            pt_refs[h][position(first + local, orders[h]), e % half] = part[local]
 
 
 def left_kernel(gm_ref, rt_ref, out_ref):
@@ -129,7 +129,7 @@
 
     width = gm_ref.shape[2]
     acc = out_ref[...]
-    for e in range(C):
+    for e in range(gm_ref.shape[0]):
         right_e = rt_ref[:, e, :, :].reshape(width, rt_ref.shape[3])
         acc = acc + jnp.dot(gm_ref[e], right_e, preferred_element_type=jnp.float32)
     out_ref[...] = acc
@@ -158,7 +158,7 @@
 
     weight_ec = out_weight.reshape(C, C, p_size).transpose(1, 0, 2).reshape(C * C, p_size)
 
-    grad_m, part_t = pl.pallas_call(
+    grad_m, *part_t = pl.pallas_call(
         functools.partial(project_kernel, n_seq=n_seq, orders=orders),
         grid=(steps,),
         in_specs=[
@@ -168,12 +168,12 @@
         ],
         out_specs=[
             pl.BlockSpec((C, own_rows * C, block), lambda b: (0, 0, b)),
-            pl.BlockSpec((len(orders), total // 16, half, 16, n_seq), lambda b: (0, 0, 0, 0, 0)),
-        ],
+        ]
+        + [pl.BlockSpec((total // 16, half, 16, n_seq), lambda b: (0, 0, 0, 0))] * len(orders),
         out_shape=[
             jax.ShapeDtypeStruct((C, own_rows * C, total), jnp.bfloat16),
-            jax.ShapeDtypeStruct((len(orders), total // 16, half, 16, n_seq), jnp.float32),
-        ],
+        ]
+        + [jax.ShapeDtypeStruct((total // 16, half, 16, n_seq), jnp.float32)] * len(orders),
         compiler_params=pltpu.CompilerParams(vmem_limit_bytes=56 * 1024 * 1024),
         cost_estimate=pl.CostEstimate(
             flops=2 * own_rows * total * C * C * (p_size + n_seq),

time: 79 us -> 75.2 us (0.952)
  local copies, waits for them, and re-layouts: 11.9 us -> 8.13 us
    slice x1 -> x0, local copies, waits for them, and re-layouts: 3.99 us -> none  [per_device(): part_t[h]]
    unnamed x7 -> x9, local copies, waits for them, and re-layouts: 3.04 us -> 3.04 us
  transfers between devices with their start and end apart: 16 -> 16, of which waited for: 7 -> 7; matrix products, arithmetic and copies ran while one was open for 23% -> 19% of each run, Pallas kernels for 19% -> 20%
where the time goes in v14:
time: 75.2 us; the launch traced here: 74.8 us
  waiting for transfers between devices  22.5 us (30%)
  starting transfers between devices  17.9 us (24%)
  Pallas kernels  15.2 us (20%)
  other arithmetic  10.1 us (13%)
  local copies, waits for them, and re-layouts  8.13 us (11%)
  between operations  0.93 us (1%)
    ppermute x8, waiting for transfers between devices, scatter_step(): return keep + lax.ppermute(send, axis, xor_pairs(n, bit))  13 us
    ppermute x8, starting transfers between devices, gather_step(): other = lax.ppermute(buf, axis, xor_pairs(n, bit))  9.82 us
    ppermute x8, waiting for transfers between devices, gather_step(): other = lax.ppermute(buf, axis, xor_pairs(n, bit))  9.57 us
    pallas_call x1, Pallas kernels, per_device(): pl.pallas_call(functools.partial(project_kernel, n_seq=n_seq, orders=orde...  8.17 us
    ppermute x8, starting transfers between devices, scatter_step(): return keep + lax.ppermute(send, axis, xor_pairs(n, bit))  8.03 us
    pallas_call x1, Pallas kernels, per_device(): pl.pallas_call(left_kernel, grid=(steps,), in_specs=[pl.BlockSpec((C, own...  7 us
    unnamed x9, local copies, waits for them, and re-layouts  3.04 us
    add x6, other arithmetic, scatter_step(): return keep + lax.ppermute(send, axis, xor_pairs(n, bit))  2.94 us
  transfers between devices with their start and end apart: 16, of which 7 were waited for; matrix products, arithmetic and copies ran while one was open for 19% of the time, Pallas kernels for 20%

profile of v14, /device:TPU:0, one launch (start us, length us, event | category | flops | bytes accessed | tf_op | source)
XLA Modules:
  0.0 74.8 jit_solution(17656479774838847655)
XLA Ops:
  0.6 1.0 %copy.9 = bf16[64,512]{0,1:T(8,128)(2,1)S(1)} copy(bf16[64,512]{1,0:T(8,128)(2,1)} %param.5) | data formatting | bytes 131072 | tf_op args[1]
  1.6 4.1 %collective-permute-start.4 = (bf16[1,16,16,64]{3,1,2,0:T(8,128)(2,1)S(1)}, bf16[1,16,16,64]{3,1,2,0:T(8,128)(2,1)S(1)}, u32[]{:S(2)}, u32[]{:S(2)}) collective-permute-start(bf16[1,16,16,64]{3,1,2,0:T(8,128)(2,1)S(1)} %get-tuple-element.38), channel_id=1, source_target_pairs={{0,8},{1,9},{2,10},{3,11},{4,12},{5,13},{6,14},{7,15},{8,0},{9,1},... | collective-permute-start | bytes 98312 | tf_op jit(solution)/shard_map/ppermute | solution.py:55
  5.7 0.1 collective-permute-start.2
  5.8 1.8 %copy.8 = bf16[32,32,128]{2,0,1:T(8,128)(2,1)} copy(bf16[32,32,128]{2,1,0:T(8,128)(2,1)} %bitcast.43) | data formatting | bytes 524288 | tf_op jit(solution)/shard_map/reshape | solution.py:159
  7.6 8.2 %shard_map.59 = (bf16[32,512,256]{2,1,0:T(8,128)(2,1)}, f32[16,16,16,64]{3,2,1,0:T(8,128)}, f32[16,16,16,64]{3,2,1,0:T(8,128)}) custom-call(bf16[16,256,128]{2,1,0:T(8,128)(2,1)} %p_ref.1, bf16[1024,128]{1,0:T(8,128)(2,1)} %bitcast.44, bf16[64,512]{1,0:T(8,128)(2,1)} %l_ref.1), custom_call_target="tpu_custom_call" | custom-call | flops 1610612736 | bytes 11534336 | tf_op jit(solution)/shard_map/pallas_call | solution.py:161
  15.7 1.5 %constant_dynamic-slice_fusion.7 = f32[8,16,16,64]{3,2,1,0:T(8,128)S(1)} fusion(f32[16,16,16,64]{3,2,1,0:T(8,128)} %get-tuple-element.10, s32[]{:T(128)S(6)} %select_n.127), kind=kLoop, calls=%fused_computation.46 | loop fusion | bytes 1048580 | tf_op jit(solution)/shard_map/dynamic_slice | solution.py:76
  17.2 0.1 collective-permute-start
  17.3 0.0 collective-permute-done.4
  17.3 0.0 copy-start.2
  17.3 0.6 copy-done.2
  17.9 0.0 collective-permute-done.2
  17.9 0.9 %broadcast_select_fusion.13 = (bf16[1,16,16,64]{3,1,2,0:T(8,128)(2,1)S(1)}, bf16[1,16,16,64]{3,1,2,0:T(8,128)(2,1)S(1)}, bf16[1,16,16,64]{3,1,2,0:T(8,128)(2,1)S(1)}, bf16[1,16,16,64]{3,1,2,0:T(8,128)(2,1)S(1)}) fusion(bf16[1,16,16,64]{3,1,2,0:T(8,128)(2,1)} %copy-done.2, pred[]{:T(512)S(6)} %eq.11, bf16[32,16,64]{2,0,1:T(8,128)(2,1)S(1)} %bitcast.41, ...), kind=kLoop, calls=%fused_computation.36 | loop fusion | flops 65536 | bytes 262145 | tf_op jit(solution)/shard_map/jit(_where)/select_n | solution.py:57
  18.8 0.7 pad_maximum_fusion.8
  19.5 1.8 %collective-permute-start.5 = (bf16[2,16,16,64]{3,1,2,0:T(8,128)(2,1)}, bf16[2,16,16,64]{3,1,2,0:T(8,128)(2,1)S(1)}, u32[]{:S(2)}, u32[]{:S(2)}) collective-permute-start(bf16[2,16,16,64]{3,1,2,0:T(8,128)(2,1)} %pad_maximum_fusion.8), channel_id=1, source_target_pairs={{0,2},{1,3},{2,0},{3,1},{4,6},{5,7},{6,4},{7,5},{8,10},{9,11},{10,... | collective-permute-start | bytes 196616 | tf_op jit(solution)/shard_map/ppermute | solution.py:55
  21.3 0.7 pad_maximum_fusion.7
  22.0 1.6 %collective-permute-start.3 = (bf16[2,16,16,64]{3,1,2,0:T(8,128)(2,1)}, bf16[2,16,16,64]{3,1,2,0:T(8,128)(2,1)}, u32[]{:S(2)}, u32[]{:S(2)}) collective-permute-start(bf16[2,16,16,64]{3,1,2,0:T(8,128)(2,1)} %pad_maximum_fusion.7), channel_id=1, source_target_pairs={{0,4},{1,5},{2,6},{3,7},{4,0},{5,1},{6,2},{7,3},{8,12},{9,13},{10,... | collective-permute-start | bytes 196616 | tf_op jit(solution)/shard_map/ppermute | solution.py:55
  23.6 0.0 copy-done
  23.6 1.1 %constant_dynamic-slice_fusion.6 = f32[8,16,16,64]{3,2,1,0:T(8,128)} fusion(f32[16,16,16,64]{3,2,1,0:T(8,128)S(1)} %copy-done, s32[]{:T(128)S(6)} %select_n.127), kind=kLoop, calls=%fused_computation.45 | loop fusion | bytes 1048580 | tf_op jit(solution)/shard_map/dynamic_slice | solution.py:76
  24.7 0.0 collective-permute-start.1
  24.7 1.0 %collective-permute-done.5 = bf16[2,16,16,64]{3,1,2,0:T(8,128)(2,1)S(1)} collective-permute-done((bf16[2,16,16,64]{3,1,2,0:T(8,128)(2,1)}, bf16[2,16,16,64]{3,1,2,0:T(8,128)(2,1)S(1)}, u32[]{:S(2)}, u32[]{:S(2)}) %collective-permute-start.5) | collective-permute-done | bytes 65568 | tf_op jit(solution)/shard_map/ppermute | solution.py:55
  25.7 2.3 %collective-permute-done.3 = bf16[2,16,16,64]{3,1,2,0:T(8,128)(2,1)} collective-permute-done((bf16[2,16,16,64]{3,1,2,0:T(8,128)(2,1)}, bf16[2,16,16,64]{3,1,2,0:T(8,128)(2,1)}, u32[]{:S(2)}, u32[]{:S(2)}) %collective-permute-start.3) | collective-permute-done | bytes 65568 | tf_op jit(solution)/shard_map/ppermute | solution.py:55
  27.9 1.0 %broadcast_select_fusion.9 = (bf16[2,16,16,64]{3,1,2,0:T(8,128)(2,1)S(1)}, bf16[2,16,16,64]{3,1,2,0:T(8,128)(2,1)S(1)}, bf16[2,16,16,64]{3,1,2,0:T(8,128)(2,1)S(1)}, bf16[2,16,16,64]{3,1,2,0:T(8,128)(2,1)S(1)}) fusion(bf16[2,16,16,64]{3,1,2,0:T(8,128)(2,1)S(1)} %collective-permute-done.5, pred[]{:T(512)S(6)} %eq.9, ...), kind=kLoop, calls=%fused_computation.28 | loop fusion | flops 196608 | bytes 524290 | tf_op jit(solution)/shard_map/jit(_where)/select_n | solution.py:57
  28.9 0.1 pad_maximum_fusion.5
  29.0 0.1 pad_maximum_fusion.6
  29.0 0.0 collective-permute-done
  29.0 0.0 copy-done.1
  29.1 1.4 %dynamic-slice_add_fusion.1 = f32[8,16,16,64]{3,2,1,0:T(8,128)S(1)} fusion(f32[8,16,16,64]{3,2,1,0:T(8,128)} %collective-permute-done, f32[16,16,16,64]{3,2,1,0:T(8,128)S(1)} %copy-done.1, s32[]{:T(128)S(6)} %select_n.126), kind=kLoop, calls=%fused_computation.4 | loop fusion | flops 131072 | bytes 1572868 | tf_op jit(solution)/shard_map/add | solution.py:77
  30.4 0.0 collective-permute-done.1
  30.4 1.4 %dynamic-slice_add_fusion = f32[8,16,16,64]{3,2,1,0:T(8,128)S(1)} fusion(f32[8,16,16,64]{3,2,1,0:T(8,128)} %collective-permute-done.1, f32[16,16,16,64]{3,2,1,0:T(8,128)S(1)} %copy-done, s32[]{:T(128)S(6)} %select_n.126), kind=kLoop, calls=%fused_computation.3 | loop fusion | flops 131072 | bytes 1572868 | tf_op jit(solution)/shard_map/add | solution.py:77
  31.8 1.6 %collective-permute-start.8 = (bf16[4,16,16,64]{3,1,2,0:T(8,128)(2,1)S(1)}, bf16[4,16,16,64]{3,1,2,0:T(8,128)(2,1)S(1)}, u32[]{:S(2)}, u32[]{:S(2)}) collective-permute-start(bf16[4,16,16,64]{3,1,2,0:T(8,128)(2,1)S(1)} %pad_maximum_fusion.6), channel_id=1, source_target_pairs={{0,4},{1,5},{2,6},{3,7},{4,0},{5,1},{6,2},{7,3},{8,12},{9,13},{10,... | collective-permute-start | bytes 393224 | tf_op jit(solution)/shard_map/ppermute | solution.py:55
  33.4 0.5 collective-permute-start.6
  34.0 0.3 collective-permute-start.13
  34.4 1.8 %collective-permute-start.10 = (f32[4,16,16,64]{3,2,1,0:T(8,128)S(1)}, f32[4,16,16,64]{3,2,1,0:T(8,128)S(1)}, u32[]{:S(2)}, u32[]{:S(2)}) collective-permute-start(f32[4,16,16,64]{3,2,1,0:T(8,128)S(1)} %constant_dynamic-slice_fusion.5), channel_id=1, source_target_pairs={{0,2},{1,3},{2,0},{3,1},{4,6},{5,7},{6,4},{7,5},{8,10},{9,11},{10,... | collective-permute-start | bytes 786440 | tf_op jit(solution)/shard_map/ppermute | solution.py:77
  36.1 5.0 %collective-permute-done.8 = bf16[4,16,16,64]{3,1,2,0:T(8,128)(2,1)S(1)} collective-permute-done((bf16[4,16,16,64]{3,1,2,0:T(8,128)(2,1)S(1)}, bf16[4,16,16,64]{3,1,2,0:T(8,128)(2,1)S(1)}, u32[]{:S(2)}, u32[]{:S(2)}) %collective-permute-start.8) | collective-permute-done | bytes 131104 | tf_op jit(solution)/shard_map/ppermute | solution.py:55
  41.2 0.1 pad_maximum_fusion.4
  41.3 0.1 collective-permute-start.9
  41.4 1.3 %collective-permute-done.6 = bf16[4,16,16,64]{3,1,2,0:T(8,128)(2,1)S(1)} collective-permute-done((bf16[4,16,16,64]{3,1,2,0:T(8,128)(2,1)S(1)}, bf16[4,16,16,64]{3,1,2,0:T(8,128)(2,1)S(1)}, u32[]{:S(2)}, u32[]{:S(2)}) %collective-permute-start.6) | collective-permute-done | bytes 131104 | tf_op jit(solution)/shard_map/ppermute | solution.py:55
  42.7 0.1 pad_maximum_fusion.3
  42.8 0.1 collective-permute-start.7
  42.9 7.8 %collective-permute-done.13 = f32[4,16,16,64]{3,2,1,0:T(8,128)S(1)} collective-permute-done((f32[4,16,16,64]{3,2,1,0:T(8,128)S(1)}, f32[4,16,16,64]{3,2,1,0:T(8,128)S(1)}, u32[]{:S(2)}, u32[]{:S(2)}) %collective-permute-start.13) | collective-permute-done | bytes 262176 | tf_op jit(solution)/shard_map/ppermute | solution.py:77
  50.7 0.1 dynamic-slice_add_fusion.2
  50.8 0.5 collective-permute-start.14
  51.3 0.7 collective-permute-done.10
  52.0 0.1 dynamic-slice_add_fusion.3
  52.1 1.0 %collective-permute-start.11 = (f32[2,16,16,64]{3,2,1,0:T(8,128)S(1)}, f32[2,16,16,64]{3,2,1,0:T(8,128)S(1)}, u32[]{:S(2)}, u32[]{:S(2)}) collective-permute-start(f32[2,16,16,64]{3,2,1,0:T(8,128)S(1)} %constant_dynamic-slice_fusion.4), channel_id=1, source_target_pairs={{0,4},{1,5},{2,6},{3,7},{4,0},{5,1},{6,2},{7,3},{8,12},{9,13},{10,... | collective-permute-start | bytes 393224 | tf_op jit(solution)/shard_map/ppermute | solution.py:77
  53.1 4.5 %collective-permute-done.14 = f32[2,16,16,64]{3,2,1,0:T(8,128)S(1)} collective-permute-done((f32[2,16,16,64]{3,2,1,0:T(8,128)S(1)}, f32[2,16,16,64]{3,2,1,0:T(8,128)S(1)}, u32[]{:S(2)}, u32[]{:S(2)}) %collective-permute-start.14) | collective-permute-done | bytes 131104 | tf_op jit(solution)/shard_map/ppermute | solution.py:77
  57.7 2.7 %collective-permute-start.15 = (f32[1,16,16,64]{3,2,1,0:T(8,128)S(1)}, f32[1,16,16,64]{3,2,1,0:T(8,128)S(1)}, u32[]{:S(2)}, u32[]{:S(2)}) collective-permute-start(f32[1,16,16,64]{3,2,1,0:T(8,128)S(1)} %constant_dynamic-slice_fusion), channel_id=1, source_target_pairs={{0,8},{1,9},{2,10},{3,11},{4,12},{5,13},{6,14},{7,15},{8,0},{9,1},... | collective-permute-start | bytes 196616 | tf_op jit(solution)/shard_map/ppermute | solution.py:77
  60.3 0.0 collective-permute-done.11
  60.4 1.7 %collective-permute-start.12 = (f32[1,16,16,64]{3,2,1,0:T(8,128)S(1)}, f32[1,16,16,64]{3,2,1,0:T(8,128)S(1)}, u32[]{:S(2)}, u32[]{:S(2)}) collective-permute-start(f32[1,16,16,64]{3,2,1,0:T(8,128)S(1)} %constant_dynamic-slice_fusion.3), channel_id=1, source_target_pairs={{0,8},{1,9},{2,10},{3,11},{4,12},{5,13},{6,14},{7,15},{8,0},{9,1},... | collective-permute-start | bytes 196616 | tf_op jit(solution)/shard_map/ppermute | solution.py:77
  62.1 0.0 collective-permute-done.9
  62.1 0.1 broadcast_select_fusion.1
  62.2 0.2 pad_maximum_fusion.2
  62.4 0.3 copy.13
  62.7 0.0 collective-permute-done.7
  62.7 0.1 broadcast_select_fusion.3
  62.9 0.2 pad_maximum_fusion.1
  63.1 0.3 copy.11
  63.4 1.8 %pad_maximum_fusion.rt_ref = bf16[16,32,16,64]{3,2,1,0:T(8,128)(2,1)} fusion(bf16[16,16,16,64]{3,2,1,0:T(8,128)(2,1)S(1)} %bitcast.38, bf16[16,16,16,64]{3,2,1,0:T(8,128)(2,1)S(1)} %bitcast.39), kind=kLoop, calls=%fused_computation | loop fusion | flops 524288 | bytes 2097152 | tf_op jit(solution)/shard_map/concatenate | solution.py:192
  65.2 7.0 %shard_map.60 = f32[512,64]{1,0:T(8,128)} custom-call(bf16[32,512,256]{2,1,0:T(8,128)(2,1)} %get-tuple-element.9.gm_ref, bf16[16,32,16,64]{3,2,1,0:T(8,128)(2,1)} %pad_maximum_fusion.rt_ref), custom_call_target="tpu_custom_call" | custom-call | flops 536870912 | bytes 9437184 | tf_op jit(solution)/shard_map/pallas_call | solution.py:201
  72.2 1.0 %convert_bitcast_fusion = bf16[64,512]{0,1:T(8,128)(2,1)S(1)} fusion(f32[512,64]{1,0:T(8,128)} %shard_map.60), kind=kLoop, calls=%fused_computation.26 | loop fusion | flops 32768 | bytes 196608 | tf_op jit(solution)/shard_map/convert_element_type | solution.py:217
  73.2 0.7 copy.15
  73.9 0.0 collective-permute-done.15
  73.9 0.0 collective-permute-done.12
  74.0 0.7 copy.16
  (17 shorter events, 0.4 us)
Async XLA Ops:
  1.6 15.7 %collective-permute-start.4 = (bf16[1,16,16,64]{3,1,2,0:T(8,128)(2,1)S(1)}, bf16[1,16,16,64]{3,1,2,0:T(8,128)(2,1)S(1)}, u32[]{:S(2)}, u32[]{:S(2)}) collective-permute-start(bf16[1,16,16,64]{3,1,2,0:T(8,128)(2,1)S(1)} %get-tuple-element.38), channel_id=1, source_target_pairs={{0,8},{1,9},{2,10},{3,11},{4,12},{5,13},{6,14},{7,15},{8,0},{9,1},... | collective-permute-start | bytes 98312 | tf_op jit(solution)/shard_map/ppermute | solution.py:55
  5.7 12.2 %collective-permute-start.2 = (bf16[1,16,16,64]{3,1,2,0:T(8,128)(2,1)S(1)}, bf16[1,16,16,64]{3,1,2,0:T(8,128)(2,1)}, u32[]{:S(2)}, u32[]{:S(2)}) collective-permute-start(bf16[1,16,16,64]{3,1,2,0:T(8,128)(2,1)S(1)} %get-tuple-element.39), channel_id=1, source_target_pairs={{0,8},{1,9},{2,10},{3,11},{4,12},{5,13},{6,14},{7,15},{8,0},{9,1},... | collective-permute-start | bytes 98312 | tf_op jit(solution)/shard_map/ppermute | solution.py:55
  15.7 7.8 %copy-start = (f32[16,16,16,64]{3,2,1,0:T(8,128)S(1)}, f32[16,16,16,64]{3,2,1,0:T(8,128)}, u32[]{:S(2)}) copy-start(f32[16,16,16,64]{3,2,1,0:T(8,128)} %get-tuple-element.11) | copy-start | bytes 3145732
  17.2 11.8 %collective-permute-start = (f32[8,16,16,64]{3,2,1,0:T(8,128)S(1)}, f32[8,16,16,64]{3,2,1,0:T(8,128)}, u32[]{:S(2)}, u32[]{:S(2)}) collective-permute-start(f32[8,16,16,64]{3,2,1,0:T(8,128)S(1)} %constant_dynamic-slice_fusion.7), channel_id=1, source_target_pairs={{0,1},{1,0},{2,3},{3,2},{4,5},{5,4},{6,7},{7,6},{8,9},{9,8},{10,11... | collective-permute-start | bytes 1572872 | tf_op jit(solution)/shard_map/ppermute | solution.py:77
  17.3 0.6 copy-start.2
  19.5 6.1 %collective-permute-start.5 = (bf16[2,16,16,64]{3,1,2,0:T(8,128)(2,1)}, bf16[2,16,16,64]{3,1,2,0:T(8,128)(2,1)S(1)}, u32[]{:S(2)}, u32[]{:S(2)}) collective-permute-start(bf16[2,16,16,64]{3,1,2,0:T(8,128)(2,1)} %pad_maximum_fusion.8), channel_id=1, source_target_pairs={{0,2},{1,3},{2,0},{3,1},{4,6},{5,7},{6,4},{7,5},{8,10},{9,11},{10,... | collective-permute-start | bytes 196616 | tf_op jit(solution)/shard_map/ppermute | solution.py:55
  22.0 5.9 %collective-permute-start.3 = (bf16[2,16,16,64]{3,1,2,0:T(8,128)(2,1)}, bf16[2,16,16,64]{3,1,2,0:T(8,128)(2,1)}, u32[]{:S(2)}, u32[]{:S(2)}) collective-permute-start(bf16[2,16,16,64]{3,1,2,0:T(8,128)(2,1)} %pad_maximum_fusion.7), channel_id=1, source_target_pairs={{0,4},{1,5},{2,6},{3,7},{4,0},{5,1},{6,2},{7,3},{8,12},{9,13},{10,... | collective-permute-start | bytes 196616 | tf_op jit(solution)/shard_map/ppermute | solution.py:55
  24.7 5.7 %collective-permute-start.1 = (f32[8,16,16,64]{3,2,1,0:T(8,128)}, f32[8,16,16,64]{3,2,1,0:T(8,128)}, u32[]{:S(2)}, u32[]{:S(2)}) collective-permute-start(f32[8,16,16,64]{3,2,1,0:T(8,128)} %constant_dynamic-slice_fusion.6), channel_id=1, source_target_pairs={{0,1},{1,0},{2,3},{3,2},{4,5},{5,4},{6,7},{7,6},{8,9},{9,8},{10,11... | collective-permute-start | bytes 1572872 | tf_op jit(solution)/shard_map/ppermute | solution.py:77
  24.7 4.4 %copy-start.1 = (f32[16,16,16,64]{3,2,1,0:T(8,128)S(1)}, f32[16,16,16,64]{3,2,1,0:T(8,128)}, u32[]{:S(2)}) copy-start(f32[16,16,16,64]{3,2,1,0:T(8,128)} %get-tuple-element.10) | copy-start | bytes 3145732
  31.8 9.3 %collective-permute-start.8 = (bf16[4,16,16,64]{3,1,2,0:T(8,128)(2,1)S(1)}, bf16[4,16,16,64]{3,1,2,0:T(8,128)(2,1)S(1)}, u32[]{:S(2)}, u32[]{:S(2)}) collective-permute-start(bf16[4,16,16,64]{3,1,2,0:T(8,128)(2,1)S(1)} %pad_maximum_fusion.6), channel_id=1, source_target_pairs={{0,4},{1,5},{2,6},{3,7},{4,0},{5,1},{6,2},{7,3},{8,12},{9,13},{10,... | collective-permute-start | bytes 393224 | tf_op jit(solution)/shard_map/ppermute | solution.py:55
  33.4 9.2 %collective-permute-start.6 = (bf16[4,16,16,64]{3,1,2,0:T(8,128)(2,1)S(1)}, bf16[4,16,16,64]{3,1,2,0:T(8,128)(2,1)S(1)}, u32[]{:S(2)}, u32[]{:S(2)}) collective-permute-start(bf16[4,16,16,64]{3,1,2,0:T(8,128)(2,1)S(1)} %pad_maximum_fusion.5), channel_id=1, source_target_pairs={{0,2},{1,3},{2,0},{3,1},{4,6},{5,7},{6,4},{7,5},{8,10},{9,11},{10,... | collective-permute-start | bytes 393224 | tf_op jit(solution)/shard_map/ppermute | solution.py:55
  34.0 16.7 %collective-permute-start.13 = (f32[4,16,16,64]{3,2,1,0:T(8,128)S(1)}, f32[4,16,16,64]{3,2,1,0:T(8,128)S(1)}, u32[]{:S(2)}, u32[]{:S(2)}) collective-permute-start(f32[4,16,16,64]{3,2,1,0:T(8,128)S(1)} %constant_dynamic-slice_fusion.2), channel_id=1, source_target_pairs={{0,4},{1,5},{2,6},{3,7},{4,0},{5,1},{6,2},{7,3},{8,12},{9,13},{10,... | collective-permute-start | bytes 786440 | tf_op jit(solution)/shard_map/ppermute | solution.py:77
  34.4 17.6 %collective-permute-start.10 = (f32[4,16,16,64]{3,2,1,0:T(8,128)S(1)}, f32[4,16,16,64]{3,2,1,0:T(8,128)S(1)}, u32[]{:S(2)}, u32[]{:S(2)}) collective-permute-start(f32[4,16,16,64]{3,2,1,0:T(8,128)S(1)} %constant_dynamic-slice_fusion.5), channel_id=1, source_target_pairs={{0,2},{1,3},{2,0},{3,1},{4,6},{5,7},{6,4},{7,5},{8,10},{9,11},{10,... | collective-permute-start | bytes 786440 | tf_op jit(solution)/shard_map/ppermute | solution.py:77
  41.3 20.8 %collective-permute-start.9 = (bf16[8,16,16,64]{3,1,2,0:T(8,128)(2,1)S(1)}, bf16[8,16,16,64]{3,1,2,0:T(8,128)(2,1)S(1)}, u32[]{:S(2)}, u32[]{:S(2)}) collective-permute-start(bf16[8,16,16,64]{3,1,2,0:T(8,128)(2,1)S(1)} %pad_maximum_fusion.4), channel_id=1, source_target_pairs={{0,1},{1,0},{2,3},{3,2},{4,5},{5,4},{6,7},{7,6},{8,9},{9,8},{10,11... | collective-permute-start | bytes 786440 | tf_op jit(solution)/shard_map/ppermute | solution.py:55
  42.8 19.9 %collective-permute-start.7 = (bf16[8,16,16,64]{3,1,2,0:T(8,128)(2,1)S(1)}, bf16[8,16,16,64]{3,1,2,0:T(8,128)(2,1)S(1)}, u32[]{:S(2)}, u32[]{:S(2)}) collective-permute-start(bf16[8,16,16,64]{3,1,2,0:T(8,128)(2,1)S(1)} %pad_maximum_fusion.3), channel_id=1, source_target_pairs={{0,1},{1,0},{2,3},{3,2},{4,5},{5,4},{6,7},{7,6},{8,9},{9,8},{10,11... | collective-permute-start | bytes 786440 | tf_op jit(solution)/shard_map/ppermute | solution.py:55
  50.8 6.8 %collective-permute-start.14 = (f32[2,16,16,64]{3,2,1,0:T(8,128)S(1)}, f32[2,16,16,64]{3,2,1,0:T(8,128)S(1)}, u32[]{:S(2)}, u32[]{:S(2)}) collective-permute-start(f32[2,16,16,64]{3,2,1,0:T(8,128)S(1)} %constant_dynamic-slice_fusion.1), channel_id=1, source_target_pairs={{0,2},{1,3},{2,0},{3,1},{4,6},{5,7},{6,4},{7,5},{8,10},{9,11},{10,... | collective-permute-start | bytes 393224 | tf_op jit(solution)/shard_map/ppermute | solution.py:77
  52.1 8.2 %collective-permute-start.11 = (f32[2,16,16,64]{3,2,1,0:T(8,128)S(1)}, f32[2,16,16,64]{3,2,1,0:T(8,128)S(1)}, u32[]{:S(2)}, u32[]{:S(2)}) collective-permute-start(f32[2,16,16,64]{3,2,1,0:T(8,128)S(1)} %constant_dynamic-slice_fusion.4), channel_id=1, source_target_pairs={{0,4},{1,5},{2,6},{3,7},{4,0},{5,1},{6,2},{7,3},{8,12},{9,13},{10,... | collective-permute-start | bytes 393224 | tf_op jit(solution)/shard_map/ppermute | solution.py:77
  57.7 16.2 %collective-permute-start.15 = (f32[1,16,16,64]{3,2,1,0:T(8,128)S(1)}, f32[1,16,16,64]{3,2,1,0:T(8,128)S(1)}, u32[]{:S(2)}, u32[]{:S(2)}) collective-permute-start(f32[1,16,16,64]{3,2,1,0:T(8,128)S(1)} %constant_dynamic-slice_fusion), channel_id=1, source_target_pairs={{0,8},{1,9},{2,10},{3,11},{4,12},{5,13},{6,14},{7,15},{8,0},{9,1},... | collective-permute-start | bytes 196616 | tf_op jit(solution)/shard_map/ppermute | solution.py:77
  60.4 13.5 %collective-permute-start.12 = (f32[1,16,16,64]{3,2,1,0:T(8,128)S(1)}, f32[1,16,16,64]{3,2,1,0:T(8,128)S(1)}, u32[]{:S(2)}, u32[]{:S(2)}) collective-permute-start(f32[1,16,16,64]{3,2,1,0:T(8,128)S(1)} %constant_dynamic-slice_fusion.3), channel_id=1, source_target_pairs={{0,8},{1,9},{2,10},{3,11},{4,12},{5,13},{6,14},{7,15},{8,0},{9,1},... | collective-permute-start | bytes 196616 | tf_op jit(solution)/shard_map/ppermute | solution.py:77

commit v15 on v14

--- a/solution.py
+++ b/solution.py
@@ -150,7 +150,7 @@
     swapped = bits[:1] + bits[1:3][::-1] + bits[3:]
     orders = (tuple(bits), tuple(swapped))
     half = C // len(orders)
-    early = 2
+    early = 0
     gathers = [(right_t[h * half:(h + 1) * half][None], []) for h in range(len(orders))]
     for h in range(len(orders)):
         for bit in orders[h][::-1][:early]:

time: 75.2 us -> 90.5 us (1.20)
  waiting for transfers between devices: 22.5 us -> 40.2 us
  other arithmetic: 10.1 us -> 7.44 us
  starting transfers between devices: 17.9 us -> 19.8 us
  local copies, waits for them, and re-layouts: 8.13 us -> 6.6 us
    ppermute x8, waiting for transfers between devices: 9.57 us -> 20.1 us  [gather_step(): other = lax.ppermute(buf, axis, xor_pairs(n, bit))]
    ppermute x8, waiting for transfers between devices: 13 us -> 20.1 us  [scatter_step(): return keep + lax.ppermute(send, axis, xor_pairs(n, bit))]
    ppermute x8, starting transfers between devices: 8.03 us -> 11.2 us  [scatter_step(): return keep + lax.ppermute(send, axis, xor_pairs(n, bit))]
    select_n x6 -> x7, other arithmetic: 2.24 us -> 0.52 us  [gather_step(): low = jnp.where(mine == 0, buf, other)]
    unnamed x9 -> x7, local copies, waits for them, and re-layouts: 3.04 us -> 1.58 us
    concatenate x8, other arithmetic: 2.12 us -> 0.8 us  [gather_step(): return (jnp.concatenate([low, high], 0), [bit] + done)]
    ppermute x8, starting transfers between devices: 9.82 us -> 8.61 us  [gather_step(): other = lax.ppermute(buf, axis, xor_pairs(n, bit))]
  transfers between devices with their start and end apart: 16 -> 16, of which waited for: 7 -> 10; matrix products, arithmetic and copies ran while one was open for 19% -> 4% of each run, Pallas kernels for 20% -> 0%
where the time goes in v15:
time: 90.5 us; the launch traced here: 90.2 us
  waiting for transfers between devices  40.2 us (44%)
  starting transfers between devices  19.8 us (22%)
  Pallas kernels  15.2 us (17%)
  other arithmetic  7.44 us (8%)
  local copies, waits for them, and re-layouts  6.6 us (7%)
  between operations  0.91 us (1%)
    ppermute x8, waiting for transfers between devices, scatter_step(): return keep + lax.ppermute(send, axis, xor_pairs(n, bit))  20.1 us
    ppermute x8, waiting for transfers between devices, gather_step(): other = lax.ppermute(buf, axis, xor_pairs(n, bit))  20.1 us
    ppermute x8, starting transfers between devices, scatter_step(): return keep + lax.ppermute(send, axis, xor_pairs(n, bit))  11.2 us
    ppermute x8, starting transfers between devices, gather_step(): other = lax.ppermute(buf, axis, xor_pairs(n, bit))  8.61 us
    pallas_call x1, Pallas kernels, per_device(): pl.pallas_call(functools.partial(project_kernel, n_seq=n_seq, orders=orde...  8.2 us
    pallas_call x1, Pallas kernels, per_device(): pl.pallas_call(left_kernel, grid=(steps,), in_specs=[pl.BlockSpec((C, own...  7 us
    add x6, other arithmetic, scatter_step(): return keep + lax.ppermute(send, axis, xor_pairs(n, bit))  3.28 us
    dynamic_slice x8, local copies, waits for them, and re-layouts, scatter_step(): send = lax.dynamic_slice_in_dim(buf, (1 - mine) * half, half, 0)  2.66 us
  transfers between devices with their start and end apart: 16, of which 10 were waited for; matrix products, arithmetic and copies ran while one was open for 4% of the time, Pallas kernels for 0%

profile of v15, /device:TPU:0, one launch (start us, length us, event | category | flops | bytes accessed | tf_op | source)
XLA Modules:
  0.0 90.2 jit_solution(13860515617299755526)
XLA Ops:
  0.6 1.8 %copy.8 = bf16[32,32,128]{2,0,1:T(8,128)(2,1)} copy(bf16[32,32,128]{2,1,0:T(8,128)(2,1)} %bitcast.34) | data formatting | bytes 524288 | tf_op jit(solution)/shard_map/reshape | solution.py:159
  2.4 8.2 %shard_map.59 = (bf16[32,512,256]{2,1,0:T(8,128)(2,1)}, f32[16,16,16,64]{3,2,1,0:T(8,128)}, f32[16,16,16,64]{3,2,1,0:T(8,128)}) custom-call(bf16[16,256,128]{2,1,0:T(8,128)(2,1)} %p_ref.1, bf16[1024,128]{1,0:T(8,128)(2,1)} %bitcast.35, bf16[64,512]{1,0:T(8,128)(2,1)} %l_ref.1), custom_call_target="tpu_custom_call" | custom-call | flops 1610612736 | bytes 11534336 | tf_op jit(solution)/shard_map/pallas_call | solution.py:161
  10.6 0.0 copy-start
  10.6 0.0 copy-start.1
  10.6 2.4 %constant_dynamic-slice_fusion.6 = f32[8,16,16,64]{3,2,1,0:T(8,128)} fusion(f32[16,16,16,64]{3,2,1,0:T(8,128)} %get-tuple-element.11, s32[]{:T(128)S(6)} %select_n.129), kind=kLoop, calls=%fused_computation.45 | loop fusion | bytes 1048580 | tf_op jit(solution)/shard_map/dynamic_slice | solution.py:76
  13.0 0.5 collective-permute-start.1
  13.5 0.0 copy-done
  13.5 0.1 constant_dynamic-slice_fusion.7
  13.6 0.1 collective-permute-start
  13.7 0.0 copy-done.1
  13.7 0.1 copy.9
  13.8 2.3 %collective-permute-done.1 = f32[8,16,16,64]{3,2,1,0:T(8,128)} collective-permute-done((f32[8,16,16,64]{3,2,1,0:T(8,128)}, f32[8,16,16,64]{3,2,1,0:T(8,128)}, u32[]{:S(2)}, u32[]{:S(2)}) %collective-permute-start.1) | collective-permute-done | bytes 524320 | tf_op jit(solution)/shard_map/ppermute | solution.py:77
  16.1 1.7 %dynamic-slice_add_fusion = f32[8,16,16,64]{3,2,1,0:T(8,128)S(1)} fusion(f32[8,16,16,64]{3,2,1,0:T(8,128)} %collective-permute-done.1, f32[16,16,16,64]{3,2,1,0:T(8,128)} %get-tuple-element.11, s32[]{:T(128)S(6)} %select_n.128), kind=kLoop, calls=%fused_computation.3 | loop fusion | flops 131072 | bytes 1572868 | tf_op jit(solution)/shard_map/add | solution.py:77
  17.8 0.0 collective-permute-done
  17.8 1.4 %dynamic-slice_add_fusion.1 = f32[8,16,16,64]{3,2,1,0:T(8,128)S(1)} fusion(f32[8,16,16,64]{3,2,1,0:T(8,128)} %collective-permute-done, f32[16,16,16,64]{3,2,1,0:T(8,128)S(1)} %copy-done, s32[]{:T(128)S(6)} %select_n.128), kind=kLoop, calls=%fused_computation.4 | loop fusion | flops 131072 | bytes 1572868 | tf_op jit(solution)/shard_map/add | solution.py:77
  19.3 3.0 %collective-permute-start.10 = (f32[4,16,16,64]{3,2,1,0:T(8,128)S(1)}, f32[4,16,16,64]{3,2,1,0:T(8,128)S(1)}, u32[]{:S(2)}, u32[]{:S(2)}) collective-permute-start(f32[4,16,16,64]{3,2,1,0:T(8,128)S(1)} %constant_dynamic-slice_fusion.5), channel_id=1, source_target_pairs={{0,2},{1,3},{2,0},{3,1},{4,6},{5,7},{6,4},{7,5},{8,10},{9,11},{10,... | collective-permute-start | bytes 786440 | tf_op jit(solution)/shard_map/ppermute | solution.py:77
  22.2 2.6 %collective-permute-start.2 = (bf16[1,16,16,64]{3,1,2,0:T(8,128)(2,1)S(1)}, bf16[1,16,16,64]{3,1,2,0:T(8,128)(2,1)S(1)}, u32[]{:S(2)}, u32[]{:S(2)}) collective-permute-start(bf16[1,16,16,64]{3,1,2,0:T(8,128)(2,1)S(1)} %get-tuple-element.12), channel_id=1, source_target_pairs={{0,8},{1,9},{2,10},{3,11},{4,12},{5,13},{6,14},{7,15},{8,0},{9,1},... | collective-permute-start | bytes 98312 | tf_op jit(solution)/shard_map/ppermute | solution.py:55
  24.8 1.6 %collective-permute-start.13 = (f32[4,16,16,64]{3,2,1,0:T(8,128)S(1)}, f32[4,16,16,64]{3,2,1,0:T(8,128)S(1)}, u32[]{:S(2)}, u32[]{:S(2)}) collective-permute-start(f32[4,16,16,64]{3,2,1,0:T(8,128)S(1)} %constant_dynamic-slice_fusion.2), channel_id=1, source_target_pairs={{0,4},{1,5},{2,6},{3,7},{4,0},{5,1},{6,2},{7,3},{8,12},{9,13},{10,... | collective-permute-start | bytes 786440 | tf_op jit(solution)/shard_map/ppermute | solution.py:77
  26.5 0.3 collective-permute-start.6
  26.8 1.4 %collective-permute-done.2 = bf16[1,16,16,64]{3,1,2,0:T(8,128)(2,1)S(1)} collective-permute-done((bf16[1,16,16,64]{3,1,2,0:T(8,128)(2,1)S(1)}, bf16[1,16,16,64]{3,1,2,0:T(8,128)(2,1)S(1)}, u32[]{:S(2)}, u32[]{:S(2)}) %collective-permute-start.2) | collective-permute-done | bytes 32800 | tf_op jit(solution)/shard_map/ppermute | solution.py:55
  28.3 1.5 %collective-permute-start.3 = (bf16[2,16,16,64]{3,1,2,0:T(8,128)(2,1)S(1)}, bf16[2,16,16,64]{3,1,2,0:T(8,128)(2,1)S(1)}, u32[]{:S(2)}, u32[]{:S(2)}) collective-permute-start(bf16[2,16,16,64]{3,1,2,0:T(8,128)(2,1)S(1)} %pad_maximum_fusion.7), channel_id=1, source_target_pairs={{0,4},{1,5},{2,6},{3,7},{4,0},{5,1},{6,2},{7,3},{8,12},{9,13},{10,... | collective-permute-start | bytes 196616 | tf_op jit(solution)/shard_map/ppermute | solution.py:55
  29.8 10.5 %collective-permute-done.6 = bf16[1,16,16,64]{3,1,2,0:T(8,128)(2,1)S(1)} collective-permute-done((bf16[1,16,16,64]{3,1,2,0:T(8,128)(2,1)S(1)}, bf16[1,16,16,64]{3,1,2,0:T(8,128)(2,1)S(1)}, u32[]{:S(2)}, u32[]{:S(2)}) %collective-permute-start.6) | collective-permute-done | bytes 32800 | tf_op jit(solution)/shard_map/ppermute | solution.py:55
  40.3 0.6 collective-permute-start.7
  40.9 2.3 %collective-permute-done.3 = bf16[2,16,16,64]{3,1,2,0:T(8,128)(2,1)S(1)} collective-permute-done((bf16[2,16,16,64]{3,1,2,0:T(8,128)(2,1)S(1)}, bf16[2,16,16,64]{3,1,2,0:T(8,128)(2,1)S(1)}, u32[]{:S(2)}, u32[]{:S(2)}) %collective-permute-start.3) | collective-permute-done | bytes 65568 | tf_op jit(solution)/shard_map/ppermute | solution.py:55
  43.2 0.1 pad_maximum_fusion.5
  43.3 0.3 collective-permute-start.4
  43.6 1.8 %collective-permute-done.7 = bf16[2,16,16,64]{3,1,2,0:T(8,128)(2,1)S(1)} collective-permute-done((bf16[2,16,16,64]{3,1,2,0:T(8,128)(2,1)S(1)}, bf16[2,16,16,64]{3,1,2,0:T(8,128)(2,1)S(1)}, u32[]{:S(2)}, u32[]{:S(2)}) %collective-permute-start.7) | collective-permute-done | bytes 65568 | tf_op jit(solution)/shard_map/ppermute | solution.py:55
  45.4 0.1 pad_maximum_fusion.6
  45.5 3.2 %collective-permute-start.8 = (bf16[4,16,16,64]{3,1,2,0:T(8,128)(2,1)S(1)}, bf16[4,16,16,64]{3,1,2,0:T(8,128)(2,1)S(1)}, u32[]{:S(2)}, u32[]{:S(2)}) collective-permute-start(bf16[4,16,16,64]{3,1,2,0:T(8,128)(2,1)S(1)} %pad_maximum_fusion.6), channel_id=1, source_target_pairs={{0,4},{1,5},{2,6},{3,7},{4,0},{5,1},{6,2},{7,3},{8,12},{9,13},{10,... | collective-permute-start | bytes 393224 | tf_op jit(solution)/shard_map/ppermute | solution.py:55
  48.7 2.3 %collective-permute-done.4 = bf16[4,16,16,64]{3,1,2,0:T(8,128)(2,1)S(1)} collective-permute-done((bf16[4,16,16,64]{3,1,2,0:T(8,128)(2,1)S(1)}, bf16[4,16,16,64]{3,1,2,0:T(8,128)(2,1)S(1)}, u32[]{:S(2)}, u32[]{:S(2)}) %collective-permute-start.4) | collective-permute-done | bytes 131104 | tf_op jit(solution)/shard_map/ppermute | solution.py:55
  51.0 0.1 broadcast_select_fusion.7
  51.0 0.1 pad_maximum_fusion.3
  51.1 0.1 collective-permute-start.5
  51.2 1.8 %collective-permute-done.8 = bf16[4,16,16,64]{3,1,2,0:T(8,128)(2,1)S(1)} collective-permute-done((bf16[4,16,16,64]{3,1,2,0:T(8,128)(2,1)S(1)}, bf16[4,16,16,64]{3,1,2,0:T(8,128)(2,1)S(1)}, u32[]{:S(2)}, u32[]{:S(2)}) %collective-permute-start.8) | collective-permute-done | bytes 131104 | tf_op jit(solution)/shard_map/ppermute | solution.py:55
  53.0 0.1 broadcast_select_fusion.5
  53.1 0.1 pad_maximum_fusion.4
  53.2 0.1 collective-permute-start.9
  53.3 0.0 collective-permute-done.10
  53.3 0.1 dynamic-slice_add_fusion.3
  53.4 2.1 %collective-permute-start.11 = (f32[2,16,16,64]{3,2,1,0:T(8,128)S(1)}, f32[2,16,16,64]{3,2,1,0:T(8,128)S(1)}, u32[]{:S(2)}, u32[]{:S(2)}) collective-permute-start(f32[2,16,16,64]{3,2,1,0:T(8,128)S(1)} %constant_dynamic-slice_fusion.4), channel_id=1, source_target_pairs={{0,4},{1,5},{2,6},{3,7},{4,0},{5,1},{6,2},{7,3},{8,12},{9,13},{10,... | collective-permute-start | bytes 393224 | tf_op jit(solution)/shard_map/ppermute | solution.py:77
  55.5 0.0 collective-permute-done.13
  55.5 0.1 dynamic-slice_add_fusion.2
  55.6 0.6 collective-permute-start.14
  56.2 6.3 %collective-permute-done.11 = f32[2,16,16,64]{3,2,1,0:T(8,128)S(1)} collective-permute-done((f32[2,16,16,64]{3,2,1,0:T(8,128)S(1)}, f32[2,16,16,64]{3,2,1,0:T(8,128)S(1)}, u32[]{:S(2)}, u32[]{:S(2)}) %collective-permute-start.11) | collective-permute-done | bytes 131104 | tf_op jit(solution)/shard_map/ppermute | solution.py:77
  62.5 3.3 %collective-permute-start.12 = (f32[1,16,16,64]{3,2,1,0:T(8,128)S(1)}, f32[1,16,16,64]{3,2,1,0:T(8,128)S(1)}, u32[]{:S(2)}, u32[]{:S(2)}) collective-permute-start(f32[1,16,16,64]{3,2,1,0:T(8,128)S(1)} %constant_dynamic-slice_fusion.3), channel_id=1, source_target_pairs={{0,8},{1,9},{2,10},{3,11},{4,12},{5,13},{6,14},{7,15},{8,0},{9,1},... | collective-permute-start | bytes 196616 | tf_op jit(solution)/shard_map/ppermute | solution.py:77
  65.8 0.0 collective-permute-done.14
  65.8 0.1 collective-permute-start.15
  66.0 9.5 %collective-permute-done.12 = f32[1,16,16,64]{3,2,1,0:T(8,128)S(1)} collective-permute-done((f32[1,16,16,64]{3,2,1,0:T(8,128)S(1)}, f32[1,16,16,64]{3,2,1,0:T(8,128)S(1)}, u32[]{:S(2)}, u32[]{:S(2)}) %collective-permute-start.12) | collective-permute-done | bytes 65568 | tf_op jit(solution)/shard_map/ppermute | solution.py:77
  75.5 2.1 %collective-permute-done.15 = f32[1,16,16,64]{3,2,1,0:T(8,128)S(1)} collective-permute-done((f32[1,16,16,64]{3,2,1,0:T(8,128)S(1)}, f32[1,16,16,64]{3,2,1,0:T(8,128)S(1)}, u32[]{:S(2)}, u32[]{:S(2)}) %collective-permute-start.15) | collective-permute-done | bytes 65568 | tf_op jit(solution)/shard_map/ppermute | solution.py:77
  77.7 0.7 copy.16
  78.4 0.0 collective-permute-done.5
  78.4 0.0 collective-permute-done.9
  78.4 0.3 broadcast_select_fusion.1
  78.7 0.2 pad_maximum_fusion.1
  78.9 0.3 copy.11
  79.2 0.2 pad_maximum_fusion.2
  79.4 0.3 copy.13
  79.7 1.8 %pad_maximum_fusion.rt_ref = bf16[16,32,16,64]{3,2,1,0:T(8,128)(2,1)} fusion(bf16[16,16,16,64]{3,2,1,0:T(8,128)(2,1)S(1)} %bitcast.31, bf16[16,16,16,64]{3,2,1,0:T(8,128)(2,1)S(1)} %bitcast.30), kind=kLoop, calls=%fused_computation | loop fusion | flops 524288 | bytes 2097152 | tf_op jit(solution)/shard_map/concatenate | solution.py:192
  81.5 7.0 %shard_map.60 = f32[512,64]{1,0:T(8,128)} custom-call(bf16[32,512,256]{2,1,0:T(8,128)(2,1)} %get-tuple-element.9.gm_ref, bf16[16,32,16,64]{3,2,1,0:T(8,128)(2,1)} %pad_maximum_fusion.rt_ref), custom_call_target="tpu_custom_call" | custom-call | flops 536870912 | bytes 9437184 | tf_op jit(solution)/shard_map/pallas_call | solution.py:201
  88.5 1.0 %convert_bitcast_fusion = bf16[64,512]{0,1:T(8,128)(2,1)S(1)} fusion(f32[512,64]{1,0:T(8,128)} %shard_map.60), kind=kLoop, calls=%fused_computation.26 | loop fusion | flops 32768 | bytes 196608 | tf_op jit(solution)/shard_map/convert_element_type | solution.py:217
  89.5 0.7 copy.15
  (19 shorter events, 0.5 us)
Async XLA Ops:
  10.6 2.9 %copy-start = (f32[16,16,16,64]{3,2,1,0:T(8,128)S(1)}, f32[16,16,16,64]{3,2,1,0:T(8,128)}, u32[]{:S(2)}) copy-start(f32[16,16,16,64]{3,2,1,0:T(8,128)} %get-tuple-element.10) | copy-start | bytes 3145732
  10.6 3.1 %copy-start.1 = (bf16[64,512]{1,0:T(8,128)(2,1)S(1)}, bf16[64,512]{1,0:T(8,128)(2,1)}, u32[]{:S(2)}) copy-start(bf16[64,512]{1,0:T(8,128)(2,1)} %param.5) | copy-start | bytes 196612
  13.0 3.1 %collective-permute-start.1 = (f32[8,16,16,64]{3,2,1,0:T(8,128)}, f32[8,16,16,64]{3,2,1,0:T(8,128)}, u32[]{:S(2)}, u32[]{:S(2)}) collective-permute-start(f32[8,16,16,64]{3,2,1,0:T(8,128)} %constant_dynamic-slice_fusion.6), channel_id=1, source_target_pairs={{0,1},{1,0},{2,3},{3,2},{4,5},{5,4},{6,7},{7,6},{8,9},{9,8},{10,11... | collective-permute-start | bytes 1572872 | tf_op jit(solution)/shard_map/ppermute | solution.py:77
  13.6 4.3 %collective-permute-start = (f32[8,16,16,64]{3,2,1,0:T(8,128)S(1)}, f32[8,16,16,64]{3,2,1,0:T(8,128)}, u32[]{:S(2)}, u32[]{:S(2)}) collective-permute-start(f32[8,16,16,64]{3,2,1,0:T(8,128)S(1)} %constant_dynamic-slice_fusion.7), channel_id=1, source_target_pairs={{0,1},{1,0},{2,3},{3,2},{4,5},{5,4},{6,7},{7,6},{8,9},{9,8},{10,11... | collective-permute-start | bytes 1572872 | tf_op jit(solution)/shard_map/ppermute | solution.py:77
  19.3 34.0 %collective-permute-start.10 = (f32[4,16,16,64]{3,2,1,0:T(8,128)S(1)}, f32[4,16,16,64]{3,2,1,0:T(8,128)S(1)}, u32[]{:S(2)}, u32[]{:S(2)}) collective-permute-start(f32[4,16,16,64]{3,2,1,0:T(8,128)S(1)} %constant_dynamic-slice_fusion.5), channel_id=1, source_target_pairs={{0,2},{1,3},{2,0},{3,1},{4,6},{5,7},{6,4},{7,5},{8,10},{9,11},{10,... | collective-permute-start | bytes 786440 | tf_op jit(solution)/shard_map/ppermute | solution.py:77
  22.2 6.0 %collective-permute-start.2 = (bf16[1,16,16,64]{3,1,2,0:T(8,128)(2,1)S(1)}, bf16[1,16,16,64]{3,1,2,0:T(8,128)(2,1)S(1)}, u32[]{:S(2)}, u32[]{:S(2)}) collective-permute-start(bf16[1,16,16,64]{3,1,2,0:T(8,128)(2,1)S(1)} %get-tuple-element.12), channel_id=1, source_target_pairs={{0,8},{1,9},{2,10},{3,11},{4,12},{5,13},{6,14},{7,15},{8,0},{9,1},... | collective-permute-start | bytes 98312 | tf_op jit(solution)/shard_map/ppermute | solution.py:55
  24.8 30.7 %collective-permute-start.13 = (f32[4,16,16,64]{3,2,1,0:T(8,128)S(1)}, f32[4,16,16,64]{3,2,1,0:T(8,128)S(1)}, u32[]{:S(2)}, u32[]{:S(2)}) collective-permute-start(f32[4,16,16,64]{3,2,1,0:T(8,128)S(1)} %constant_dynamic-slice_fusion.2), channel_id=1, source_target_pairs={{0,4},{1,5},{2,6},{3,7},{4,0},{5,1},{6,2},{7,3},{8,12},{9,13},{10,... | collective-permute-start | bytes 786440 | tf_op jit(solution)/shard_map/ppermute | solution.py:77
  26.5 13.8 %collective-permute-start.6 = (bf16[1,16,16,64]{3,1,2,0:T(8,128)(2,1)S(1)}, bf16[1,16,16,64]{3,1,2,0:T(8,128)(2,1)S(1)}, u32[]{:S(2)}, u32[]{:S(2)}) collective-permute-start(bf16[1,16,16,64]{3,1,2,0:T(8,128)(2,1)S(1)} %get-tuple-element.13), channel_id=1, source_target_pairs={{0,8},{1,9},{2,10},{3,11},{4,12},{5,13},{6,14},{7,15},{8,0},{9,1},... | collective-permute-start | bytes 98312 | tf_op jit(solution)/shard_map/ppermute | solution.py:55
  28.3 14.9 %collective-permute-start.3 = (bf16[2,16,16,64]{3,1,2,0:T(8,128)(2,1)S(1)}, bf16[2,16,16,64]{3,1,2,0:T(8,128)(2,1)S(1)}, u32[]{:S(2)}, u32[]{:S(2)}) collective-permute-start(bf16[2,16,16,64]{3,1,2,0:T(8,128)(2,1)S(1)} %pad_maximum_fusion.7), channel_id=1, source_target_pairs={{0,4},{1,5},{2,6},{3,7},{4,0},{5,1},{6,2},{7,3},{8,12},{9,13},{10,... | collective-permute-start | bytes 196616 | tf_op jit(solution)/shard_map/ppermute | solution.py:55
  40.3 5.0 %collective-permute-start.7 = (bf16[2,16,16,64]{3,1,2,0:T(8,128)(2,1)S(1)}, bf16[2,16,16,64]{3,1,2,0:T(8,128)(2,1)S(1)}, u32[]{:S(2)}, u32[]{:S(2)}) collective-permute-start(bf16[2,16,16,64]{3,1,2,0:T(8,128)(2,1)S(1)} %pad_maximum_fusion.8), channel_id=1, source_target_pairs={{0,2},{1,3},{2,0},{3,1},{4,6},{5,7},{6,4},{7,5},{8,10},{9,11},{10,... | collective-permute-start | bytes 196616 | tf_op jit(solution)/shard_map/ppermute | solution.py:55
  43.3 7.7 %collective-permute-start.4 = (bf16[4,16,16,64]{3,1,2,0:T(8,128)(2,1)S(1)}, bf16[4,16,16,64]{3,1,2,0:T(8,128)(2,1)S(1)}, u32[]{:S(2)}, u32[]{:S(2)}) collective-permute-start(bf16[4,16,16,64]{3,1,2,0:T(8,128)(2,1)S(1)} %pad_maximum_fusion.5), channel_id=1, source_target_pairs={{0,2},{1,3},{2,0},{3,1},{4,6},{5,7},{6,4},{7,5},{8,10},{9,11},{10,... | collective-permute-start | bytes 393224 | tf_op jit(solution)/shard_map/ppermute | solution.py:55
  45.5 7.6 %collective-permute-start.8 = (bf16[4,16,16,64]{3,1,2,0:T(8,128)(2,1)S(1)}, bf16[4,16,16,64]{3,1,2,0:T(8,128)(2,1)S(1)}, u32[]{:S(2)}, u32[]{:S(2)}) collective-permute-start(bf16[4,16,16,64]{3,1,2,0:T(8,128)(2,1)S(1)} %pad_maximum_fusion.6), channel_id=1, source_target_pairs={{0,4},{1,5},{2,6},{3,7},{4,0},{5,1},{6,2},{7,3},{8,12},{9,13},{10,... | collective-permute-start | bytes 393224 | tf_op jit(solution)/shard_map/ppermute | solution.py:55
  51.1 27.2 %collective-permute-start.5 = (bf16[8,16,16,64]{3,1,2,0:T(8,128)(2,1)S(1)}, bf16[8,16,16,64]{3,1,2,0:T(8,128)(2,1)S(1)}, u32[]{:S(2)}, u32[]{:S(2)}) collective-permute-start(bf16[8,16,16,64]{3,1,2,0:T(8,128)(2,1)S(1)} %pad_maximum_fusion.3), channel_id=1, source_target_pairs={{0,1},{1,0},{2,3},{3,2},{4,5},{5,4},{6,7},{7,6},{8,9},{9,8},{10,11... | collective-permute-start | bytes 786440 | tf_op jit(solution)/shard_map/ppermute | solution.py:55
  53.2 25.2 %collective-permute-start.9 = (bf16[8,16,16,64]{3,1,2,0:T(8,128)(2,1)S(1)}, bf16[8,16,16,64]{3,1,2,0:T(8,128)(2,1)S(1)}, u32[]{:S(2)}, u32[]{:S(2)}) collective-permute-start(bf16[8,16,16,64]{3,1,2,0:T(8,128)(2,1)S(1)} %pad_maximum_fusion.4), channel_id=1, source_target_pairs={{0,1},{1,0},{2,3},{3,2},{4,5},{5,4},{6,7},{7,6},{8,9},{9,8},{10,11... | collective-permute-start | bytes 786440 | tf_op jit(solution)/shard_map/ppermute | solution.py:55
  53.4 9.0 %collective-permute-start.11 = (f32[2,16,16,64]{3,2,1,0:T(8,128)S(1)}, f32[2,16,16,64]{3,2,1,0:T(8,128)S(1)}, u32[]{:S(2)}, u32[]{:S(2)}) collective-permute-start(f32[2,16,16,64]{3,2,1,0:T(8,128)S(1)} %constant_dynamic-slice_fusion.4), channel_id=1, source_target_pairs={{0,4},{1,5},{2,6},{3,7},{4,0},{5,1},{6,2},{7,3},{8,12},{9,13},{10,... | collective-permute-start | bytes 393224 | tf_op jit(solution)/shard_map/ppermute | solution.py:77
  55.6 10.2 %collective-permute-start.14 = (f32[2,16,16,64]{3,2,1,0:T(8,128)S(1)}, f32[2,16,16,64]{3,2,1,0:T(8,128)S(1)}, u32[]{:S(2)}, u32[]{:S(2)}) collective-permute-start(f32[2,16,16,64]{3,2,1,0:T(8,128)S(1)} %constant_dynamic-slice_fusion.1), channel_id=1, source_target_pairs={{0,2},{1,3},{2,0},{3,1},{4,6},{5,7},{6,4},{7,5},{8,10},{9,11},{10,... | collective-permute-start | bytes 393224 | tf_op jit(solution)/shard_map/ppermute | solution.py:77
  62.5 12.9 %collective-permute-start.12 = (f32[1,16,16,64]{3,2,1,0:T(8,128)S(1)}, f32[1,16,16,64]{3,2,1,0:T(8,128)S(1)}, u32[]{:S(2)}, u32[]{:S(2)}) collective-permute-start(f32[1,16,16,64]{3,2,1,0:T(8,128)S(1)} %constant_dynamic-slice_fusion.3), channel_id=1, source_target_pairs={{0,8},{1,9},{2,10},{3,11},{4,12},{5,13},{6,14},{7,15},{8,0},{9,1},... | collective-permute-start | bytes 196616 | tf_op jit(solution)/shard_map/ppermute | solution.py:77
  65.8 11.7 %collective-permute-start.15 = (f32[1,16,16,64]{3,2,1,0:T(8,128)S(1)}, f32[1,16,16,64]{3,2,1,0:T(8,128)S(1)}, u32[]{:S(2)}, u32[]{:S(2)}) collective-permute-start(f32[1,16,16,64]{3,2,1,0:T(8,128)S(1)} %constant_dynamic-slice_fusion), channel_id=1, source_target_pairs={{0,8},{1,9},{2,10},{3,11},{4,12},{5,13},{6,14},{7,15},{8,0},{9,1},... | collective-permute-start | bytes 196616 | tf_op jit(solution)/shard_map/ppermute | solution.py:77

commit v16 on v15

--- a/solution.py
+++ b/solution.py
@@ -150,7 +150,7 @@
     swapped = bits[:1] + bits[1:3][::-1] + bits[3:]
     orders = (tuple(bits), tuple(swapped))
     half = C // len(orders)
-    early = 0
+    early = 3
     gathers = [(right_t[h * half:(h + 1) * half][None], []) for h in range(len(orders))]
     for h in range(len(orders)):
         for bit in orders[h][::-1][:early]:

time: 90.5 us -> 83.3 us (0.920)
  waiting for transfers between devices: 40.2 us -> 28.5 us
  local copies, waits for them, and re-layouts: 6.6 us -> 8.55 us
  starting transfers between devices: 19.8 us -> 21.6 us
    ppermute x8, waiting for transfers between devices: 20.1 us -> 8.03 us  [gather_step(): other = lax.ppermute(buf, axis, xor_pairs(n, bit))]
    ppermute x8, starting transfers between devices: 8.61 us -> 10.4 us  [gather_step(): other = lax.ppermute(buf, axis, xor_pairs(n, bit))]
    unnamed x7 -> x9, local copies, waits for them, and re-layouts: 1.58 us -> 2.68 us
    select_n x7 -> x6, other arithmetic: 0.52 us -> 1.43 us  [gather_step(): low = jnp.where(mine == 0, buf, other)]
  transfers between devices with their start and end apart: 16 -> 16, of which waited for: 10 -> 6; matrix products, arithmetic and copies ran while one was open for 4% -> 16% of each run, Pallas kernels for 0% -> 18%
where the time goes in v16:
time: 83.3 us; the launch traced here: 82.9 us
  waiting for transfers between devices  28.5 us (34%)
  starting transfers between devices  21.6 us (26%)
  Pallas kernels  15.2 us (18%)
  local copies, waits for them, and re-layouts  8.55 us (10%)
  other arithmetic  8.13 us (10%)
  between operations  0.92 us (1%)
    ppermute x8, waiting for transfers between devices, scatter_step(): return keep + lax.ppermute(send, axis, xor_pairs(n, bit))  20.4 us
    ppermute x8, starting transfers between devices, scatter_step(): return keep + lax.ppermute(send, axis, xor_pairs(n, bit))  11.2 us
    ppermute x8, starting transfers between devices, gather_step(): other = lax.ppermute(buf, axis, xor_pairs(n, bit))  10.4 us
    pallas_call x1, Pallas kernels, per_device(): pl.pallas_call(functools.partial(project_kernel, n_seq=n_seq, orders=orde...  8.2 us
    ppermute x8, waiting for transfers between devices, gather_step(): other = lax.ppermute(buf, axis, xor_pairs(n, bit))  8.03 us
    pallas_call x1, Pallas kernels, per_device(): pl.pallas_call(left_kernel, grid=(steps,), in_specs=[pl.BlockSpec((C, own...  7 us
    dynamic_slice x8, local copies, waits for them, and re-layouts, scatter_step(): send = lax.dynamic_slice_in_dim(buf, (1 - mine) * half, half, 0)  3.52 us
    add x6, other arithmetic, scatter_step(): return keep + lax.ppermute(send, axis, xor_pairs(n, bit))  3.06 us
  transfers between devices with their start and end apart: 16, of which 6 were waited for; matrix products, arithmetic and copies ran while one was open for 16% of the time, Pallas kernels for 18%

profile of v16, /device:TPU:0, one launch (start us, length us, event | category | flops | bytes accessed | tf_op | source)
XLA Modules:
  0.0 82.9 jit_solution(4175750123789539817)
XLA Ops:
  0.6 1.0 %copy.9 = bf16[64,512]{0,1:T(8,128)(2,1)S(1)} copy(bf16[64,512]{1,0:T(8,128)(2,1)} %param.5) | data formatting | bytes 131072 | tf_op args[1]
  1.6 4.1 %collective-permute-start.5 = (bf16[1,16,16,64]{3,1,2,0:T(8,128)(2,1)S(1)}, bf16[1,16,16,64]{3,1,2,0:T(8,128)(2,1)S(1)}, u32[]{:S(2)}, u32[]{:S(2)}) collective-permute-start(bf16[1,16,16,64]{3,1,2,0:T(8,128)(2,1)S(1)} %get-tuple-element.38), channel_id=1, source_target_pairs={{0,8},{1,9},{2,10},{3,11},{4,12},{5,13},{6,14},{7,15},{8,0},{9,1},... | collective-permute-start | bytes 98312 | tf_op jit(solution)/shard_map/ppermute | solution.py:55
  5.7 0.1 collective-permute-start.2
  5.8 1.8 %copy.8 = bf16[32,32,128]{2,0,1:T(8,128)(2,1)} copy(bf16[32,32,128]{2,1,0:T(8,128)(2,1)} %bitcast.43) | data formatting | bytes 524288 | tf_op jit(solution)/shard_map/reshape | solution.py:159
  7.6 8.2 %shard_map.59 = (bf16[32,512,256]{2,1,0:T(8,128)(2,1)}, f32[16,16,16,64]{3,2,1,0:T(8,128)}, f32[16,16,16,64]{3,2,1,0:T(8,128)}) custom-call(bf16[16,256,128]{2,1,0:T(8,128)(2,1)} %p_ref.1, bf16[1024,128]{1,0:T(8,128)(2,1)} %bitcast.44, bf16[64,512]{1,0:T(8,128)(2,1)} %l_ref.1), custom_call_target="tpu_custom_call" | custom-call | flops 1610612736 | bytes 11534336 | tf_op jit(solution)/shard_map/pallas_call | solution.py:161
  15.8 0.0 collective-permute-done.5
  15.8 0.0 collective-permute-done.2
  15.8 0.0 copy-start
  15.8 1.8 %collective-permute-start.6 = (bf16[2,16,16,64]{3,1,2,0:T(8,128)(2,1)S(1)}, bf16[2,16,16,64]{3,1,2,0:T(8,128)(2,1)S(1)}, u32[]{:S(2)}, u32[]{:S(2)}) collective-permute-start(bf16[2,16,16,64]{3,1,2,0:T(8,128)(2,1)S(1)} %pad_maximum_fusion.8), channel_id=1, source_target_pairs={{0,2},{1,3},{2,0},{3,1},{4,6},{5,7},{6,4},{7,5},{8,10},{9,11},{10,... | collective-permute-start | bytes 196616 | tf_op jit(solution)/shard_map/ppermute | solution.py:55
  17.7 1.6 %collective-permute-start.3 = (bf16[2,16,16,64]{3,1,2,0:T(8,128)(2,1)S(1)}, bf16[2,16,16,64]{3,1,2,0:T(8,128)(2,1)S(1)}, u32[]{:S(2)}, u32[]{:S(2)}) collective-permute-start(bf16[2,16,16,64]{3,1,2,0:T(8,128)(2,1)S(1)} %pad_maximum_fusion.7), channel_id=1, source_target_pairs={{0,4},{1,5},{2,6},{3,7},{4,0},{5,1},{6,2},{7,3},{8,12},{9,13},{10,... | collective-permute-start | bytes 196616 | tf_op jit(solution)/shard_map/ppermute | solution.py:55
  19.3 2.3 %constant_dynamic-slice_fusion.7 = f32[8,16,16,64]{3,2,1,0:T(8,128)} fusion(f32[16,16,16,64]{3,2,1,0:T(8,128)} %get-tuple-element.10, s32[]{:T(128)S(6)} %select_n.126), kind=kLoop, calls=%fused_computation.46 | loop fusion | bytes 1048580 | tf_op jit(solution)/shard_map/dynamic_slice | solution.py:76
  21.6 0.0 collective-permute-start
  21.6 0.0 collective-permute-done.6
  21.6 1.1 %collective-permute-done.3 = bf16[2,16,16,64]{3,1,2,0:T(8,128)(2,1)S(1)} collective-permute-done((bf16[2,16,16,64]{3,1,2,0:T(8,128)(2,1)S(1)}, bf16[2,16,16,64]{3,1,2,0:T(8,128)(2,1)S(1)}, u32[]{:S(2)}, u32[]{:S(2)}) %collective-permute-start.3) | collective-permute-done | bytes 65568 | tf_op jit(solution)/shard_map/ppermute | solution.py:55
  22.7 0.1 broadcast_select_fusion.9
  22.8 0.1 pad_maximum_fusion.5
  22.9 0.3 collective-permute-start.4
  23.2 0.0 copy-done
  23.2 1.1 %constant_dynamic-slice_fusion.6 = f32[8,16,16,64]{3,2,1,0:T(8,128)} fusion(f32[16,16,16,64]{3,2,1,0:T(8,128)S(1)} %copy-done, s32[]{:T(128)S(6)} %select_n.126), kind=kLoop, calls=%fused_computation.45 | loop fusion | bytes 1048580 | tf_op jit(solution)/shard_map/dynamic_slice | solution.py:76
  24.3 0.0 collective-permute-start.1
  24.3 0.1 pad_maximum_fusion.6
  24.4 0.0 copy-start.2
  24.4 1.9 %collective-permute-start.7 = (bf16[4,16,16,64]{3,1,2,0:T(8,128)(2,1)S(1)}, bf16[4,16,16,64]{3,1,2,0:T(8,128)(2,1)S(1)}, u32[]{:S(2)}, u32[]{:S(2)}) collective-permute-start(bf16[4,16,16,64]{3,1,2,0:T(8,128)(2,1)S(1)} %pad_maximum_fusion.6), channel_id=1, source_target_pairs={{0,4},{1,5},{2,6},{3,7},{4,0},{5,1},{6,2},{7,3},{8,12},{9,13},{10,... | collective-permute-start | bytes 393224 | tf_op jit(solution)/shard_map/ppermute | solution.py:55
  26.3 4.3 %collective-permute-done.4 = bf16[4,16,16,64]{3,1,2,0:T(8,128)(2,1)S(1)} collective-permute-done((bf16[4,16,16,64]{3,1,2,0:T(8,128)(2,1)S(1)}, bf16[4,16,16,64]{3,1,2,0:T(8,128)(2,1)S(1)}, u32[]{:S(2)}, u32[]{:S(2)}) %collective-permute-start.4) | collective-permute-done | bytes 131104 | tf_op jit(solution)/shard_map/ppermute | solution.py:55
  30.6 0.1 broadcast_select_fusion.7
  30.6 2.6 %collective-permute-done.7 = bf16[4,16,16,64]{3,1,2,0:T(8,128)(2,1)S(1)} collective-permute-done((bf16[4,16,16,64]{3,1,2,0:T(8,128)(2,1)S(1)}, bf16[4,16,16,64]{3,1,2,0:T(8,128)(2,1)S(1)}, u32[]{:S(2)}, u32[]{:S(2)}) %collective-permute-start.7) | collective-permute-done | bytes 131104 | tf_op jit(solution)/shard_map/ppermute | solution.py:55
  33.2 0.1 broadcast_select_fusion.5
  33.3 0.1 pad_maximum_fusion.3
  33.4 0.0 copy-start.1
  33.4 0.1 pad_maximum_fusion.4
  33.6 0.0 collective-permute-done
  33.6 1.5 %dynamic-slice_add_fusion.1 = f32[8,16,16,64]{3,2,1,0:T(8,128)S(1)} fusion(f32[8,16,16,64]{3,2,1,0:T(8,128)} %collective-permute-done, f32[16,16,16,64]{3,2,1,0:T(8,128)S(1)} %copy-done.2, s32[]{:T(128)S(6)} %select_n.125), kind=kLoop, calls=%fused_computation.4 | loop fusion | flops 131072 | bytes 1572868 | tf_op jit(solution)/shard_map/add | solution.py:77
  35.1 0.0 collective-permute-done.1
  35.1 0.3 copy-done.1
  35.3 1.4 %dynamic-slice_add_fusion = f32[8,16,16,64]{3,2,1,0:T(8,128)S(1)} fusion(f32[8,16,16,64]{3,2,1,0:T(8,128)} %collective-permute-done.1, f32[16,16,16,64]{3,2,1,0:T(8,128)S(1)} %copy-done.1, s32[]{:T(128)S(6)} %select_n.125), kind=kLoop, calls=%fused_computation.3 | loop fusion | flops 131072 | bytes 1572868 | tf_op jit(solution)/shard_map/add | solution.py:77
  36.7 0.1 collective-permute-start.9
  36.8 0.5 collective-permute-start.8
  37.3 1.8 %collective-permute-start.13 = (f32[4,16,16,64]{3,2,1,0:T(8,128)S(1)}, f32[4,16,16,64]{3,2,1,0:T(8,128)S(1)}, u32[]{:S(2)}, u32[]{:S(2)}) collective-permute-start(f32[4,16,16,64]{3,2,1,0:T(8,128)S(1)} %constant_dynamic-slice_fusion.2), channel_id=1, source_target_pairs={{0,4},{1,5},{2,6},{3,7},{4,0},{5,1},{6,2},{7,3},{8,12},{9,13},{10,... | collective-permute-start | bytes 786440 | tf_op jit(solution)/shard_map/ppermute | solution.py:77
  39.2 1.6 %collective-permute-start.10 = (f32[4,16,16,64]{3,2,1,0:T(8,128)S(1)}, f32[4,16,16,64]{3,2,1,0:T(8,128)S(1)}, u32[]{:S(2)}, u32[]{:S(2)}) collective-permute-start(f32[4,16,16,64]{3,2,1,0:T(8,128)S(1)} %constant_dynamic-slice_fusion.5), channel_id=1, source_target_pairs={{0,2},{1,3},{2,0},{3,1},{4,6},{5,7},{6,4},{7,5},{8,10},{9,11},{10,... | collective-permute-start | bytes 786440 | tf_op jit(solution)/shard_map/ppermute | solution.py:77
  40.8 0.0 collective-permute-done.9
  40.8 1.1 %broadcast_select_fusion.1 = (bf16[8,16,16,64]{3,1,2,0:T(8,128)(2,1)S(1)}, bf16[8,16,16,64]{3,1,2,0:T(8,128)(2,1)S(1)}) fusion(bf16[8,16,16,64]{3,1,2,0:T(8,128)(2,1)S(1)} %pad_maximum_fusion.4, bf16[8,16,16,64]{3,1,2,0:T(8,128)(2,1)} %collective-permute-done.9, pred[]{:T(512)S(6)} %eq.8), kind=kLoop, calls=%fused_computation.10 | loop fusion | flops 262144 | bytes 1048577 | tf_op jit(solution)/shard_map/jit(_where)/select_n | solution.py:57
  41.9 0.0 collective-permute-done.8
  41.9 0.1 broadcast_select_fusion.3
  42.0 0.2 pad_maximum_fusion.2
  42.2 0.2 pad_maximum_fusion.1
  42.4 8.9 %collective-permute-done.13 = f32[4,16,16,64]{3,2,1,0:T(8,128)S(1)} collective-permute-done((f32[4,16,16,64]{3,2,1,0:T(8,128)S(1)}, f32[4,16,16,64]{3,2,1,0:T(8,128)S(1)}, u32[]{:S(2)}, u32[]{:S(2)}) %collective-permute-start.13) | collective-permute-done | bytes 262176 | tf_op jit(solution)/shard_map/ppermute | solution.py:77
  51.3 0.1 dynamic-slice_add_fusion.2
  51.4 0.3 copy.13
  51.7 0.3 copy.11
  52.0 1.8 %collective-permute-start.14 = (f32[2,16,16,64]{3,2,1,0:T(8,128)S(1)}, f32[2,16,16,64]{3,2,1,0:T(8,128)S(1)}, u32[]{:S(2)}, u32[]{:S(2)}) collective-permute-start(f32[2,16,16,64]{3,2,1,0:T(8,128)S(1)} %constant_dynamic-slice_fusion.1), channel_id=1, source_target_pairs={{0,2},{1,3},{2,0},{3,1},{4,6},{5,7},{6,4},{7,5},{8,10},{9,11},{10,... | collective-permute-start | bytes 393224 | tf_op jit(solution)/shard_map/ppermute | solution.py:77
  53.7 1.8 %pad_maximum_fusion.rt_ref = bf16[16,32,16,64]{3,2,1,0:T(8,128)(2,1)} fusion(bf16[16,16,16,64]{3,2,1,0:T(8,128)(2,1)S(1)} %bitcast.38, bf16[16,16,16,64]{3,2,1,0:T(8,128)(2,1)S(1)} %bitcast.39), kind=kLoop, calls=%fused_computation | loop fusion | flops 524288 | bytes 2097152 | tf_op jit(solution)/shard_map/concatenate | solution.py:192
  55.5 7.0 %shard_map.60 = f32[512,64]{1,0:T(8,128)} custom-call(bf16[32,512,256]{2,1,0:T(8,128)(2,1)} %get-tuple-element.9.gm_ref, bf16[16,32,16,64]{3,2,1,0:T(8,128)(2,1)} %pad_maximum_fusion.rt_ref), custom_call_target="tpu_custom_call" | custom-call | flops 536870912 | bytes 9437184 | tf_op jit(solution)/shard_map/pallas_call | solution.py:201
  62.5 0.0 collective-permute-done.10
  62.5 0.1 dynamic-slice_add_fusion.3
  62.6 1.0 %convert_bitcast_fusion = bf16[64,512]{0,1:T(8,128)(2,1)S(1)} fusion(f32[512,64]{1,0:T(8,128)} %shard_map.60), kind=kLoop, calls=%fused_computation.26 | loop fusion | flops 32768 | bytes 196608 | tf_op jit(solution)/shard_map/convert_element_type | solution.py:217
  63.6 0.7 copy.15
  64.3 1.6 %collective-permute-start.11 = (f32[2,16,16,64]{3,2,1,0:T(8,128)S(1)}, f32[2,16,16,64]{3,2,1,0:T(8,128)S(1)}, u32[]{:S(2)}, u32[]{:S(2)}) collective-permute-start(f32[2,16,16,64]{3,2,1,0:T(8,128)S(1)} %constant_dynamic-slice_fusion.4), channel_id=1, source_target_pairs={{0,4},{1,5},{2,6},{3,7},{4,0},{5,1},{6,2},{7,3},{8,12},{9,13},{10,... | collective-permute-start | bytes 393224 | tf_op jit(solution)/shard_map/ppermute | solution.py:77
  66.0 0.0 collective-permute-done.14
  66.0 2.7 %collective-permute-start.15 = (f32[1,16,16,64]{3,2,1,0:T(8,128)S(1)}, f32[1,16,16,64]{3,2,1,0:T(8,128)S(1)}, u32[]{:S(2)}, u32[]{:S(2)}) collective-permute-start(f32[1,16,16,64]{3,2,1,0:T(8,128)S(1)} %constant_dynamic-slice_fusion), channel_id=1, source_target_pairs={{0,8},{1,9},{2,10},{3,11},{4,12},{5,13},{6,14},{7,15},{8,0},{9,1},... | collective-permute-start | bytes 196616 | tf_op jit(solution)/shard_map/ppermute | solution.py:77
  68.7 5.7 %collective-permute-done.11 = f32[2,16,16,64]{3,2,1,0:T(8,128)S(1)} collective-permute-done((f32[2,16,16,64]{3,2,1,0:T(8,128)S(1)}, f32[2,16,16,64]{3,2,1,0:T(8,128)S(1)}, u32[]{:S(2)}, u32[]{:S(2)}) %collective-permute-start.11) | collective-permute-done | bytes 131104 | tf_op jit(solution)/shard_map/ppermute | solution.py:77
  74.5 1.7 %collective-permute-start.12 = (f32[1,16,16,64]{3,2,1,0:T(8,128)S(1)}, f32[1,16,16,64]{3,2,1,0:T(8,128)S(1)}, u32[]{:S(2)}, u32[]{:S(2)}) collective-permute-start(f32[1,16,16,64]{3,2,1,0:T(8,128)S(1)} %constant_dynamic-slice_fusion.3), channel_id=1, source_target_pairs={{0,8},{1,9},{2,10},{3,11},{4,12},{5,13},{6,14},{7,15},{8,0},{9,1},... | collective-permute-start | bytes 196616 | tf_op jit(solution)/shard_map/ppermute | solution.py:77
  76.2 0.0 collective-permute-done.15
  76.2 5.8 %collective-permute-done.12 = f32[1,16,16,64]{3,2,1,0:T(8,128)S(1)} collective-permute-done((f32[1,16,16,64]{3,2,1,0:T(8,128)S(1)}, f32[1,16,16,64]{3,2,1,0:T(8,128)S(1)}, u32[]{:S(2)}, u32[]{:S(2)}) %collective-permute-start.12) | collective-permute-done | bytes 65568 | tf_op jit(solution)/shard_map/ppermute | solution.py:77
  82.1 0.7 copy.16
  (17 shorter events, 0.4 us)
Async XLA Ops:
  1.6 14.1 %collective-permute-start.5 = (bf16[1,16,16,64]{3,1,2,0:T(8,128)(2,1)S(1)}, bf16[1,16,16,64]{3,1,2,0:T(8,128)(2,1)S(1)}, u32[]{:S(2)}, u32[]{:S(2)}) collective-permute-start(bf16[1,16,16,64]{3,1,2,0:T(8,128)(2,1)S(1)} %get-tuple-element.38), channel_id=1, source_target_pairs={{0,8},{1,9},{2,10},{3,11},{4,12},{5,13},{6,14},{7,15},{8,0},{9,1},... | collective-permute-start | bytes 98312 | tf_op jit(solution)/shard_map/ppermute | solution.py:55
  5.7 10.0 %collective-permute-start.2 = (bf16[1,16,16,64]{3,1,2,0:T(8,128)(2,1)S(1)}, bf16[1,16,16,64]{3,1,2,0:T(8,128)(2,1)S(1)}, u32[]{:S(2)}, u32[]{:S(2)}) collective-permute-start(bf16[1,16,16,64]{3,1,2,0:T(8,128)(2,1)S(1)} %get-tuple-element.39), channel_id=1, source_target_pairs={{0,8},{1,9},{2,10},{3,11},{4,12},{5,13},{6,14},{7,15},{8,0},{9,1},... | collective-permute-start | bytes 98312 | tf_op jit(solution)/shard_map/ppermute | solution.py:55
  15.8 7.4 %copy-start = (f32[16,16,16,64]{3,2,1,0:T(8,128)S(1)}, f32[16,16,16,64]{3,2,1,0:T(8,128)}, u32[]{:S(2)}) copy-start(f32[16,16,16,64]{3,2,1,0:T(8,128)} %get-tuple-element.11) | copy-start | bytes 3145732
  15.8 5.8 %collective-permute-start.6 = (bf16[2,16,16,64]{3,1,2,0:T(8,128)(2,1)S(1)}, bf16[2,16,16,64]{3,1,2,0:T(8,128)(2,1)S(1)}, u32[]{:S(2)}, u32[]{:S(2)}) collective-permute-start(bf16[2,16,16,64]{3,1,2,0:T(8,128)(2,1)S(1)} %pad_maximum_fusion.8), channel_id=1, source_target_pairs={{0,2},{1,3},{2,0},{3,1},{4,6},{5,7},{6,4},{7,5},{8,10},{9,11},{10,... | collective-permute-start | bytes 196616 | tf_op jit(solution)/shard_map/ppermute | solution.py:55
  17.7 5.0 %collective-permute-start.3 = (bf16[2,16,16,64]{3,1,2,0:T(8,128)(2,1)S(1)}, bf16[2,16,16,64]{3,1,2,0:T(8,128)(2,1)S(1)}, u32[]{:S(2)}, u32[]{:S(2)}) collective-permute-start(bf16[2,16,16,64]{3,1,2,0:T(8,128)(2,1)S(1)} %pad_maximum_fusion.7), channel_id=1, source_target_pairs={{0,4},{1,5},{2,6},{3,7},{4,0},{5,1},{6,2},{7,3},{8,12},{9,13},{10,... | collective-permute-start | bytes 196616 | tf_op jit(solution)/shard_map/ppermute | solution.py:55
  21.6 11.9 %collective-permute-start = (f32[8,16,16,64]{3,2,1,0:T(8,128)}, f32[8,16,16,64]{3,2,1,0:T(8,128)}, u32[]{:S(2)}, u32[]{:S(2)}) collective-permute-start(f32[8,16,16,64]{3,2,1,0:T(8,128)} %constant_dynamic-slice_fusion.7), channel_id=1, source_target_pairs={{0,1},{1,0},{2,3},{3,2},{4,5},{5,4},{6,7},{7,6},{8,9},{9,8},{10,11... | collective-permute-start | bytes 1572872 | tf_op jit(solution)/shard_map/ppermute | solution.py:77
  22.9 7.7 %collective-permute-start.4 = (bf16[4,16,16,64]{3,1,2,0:T(8,128)(2,1)S(1)}, bf16[4,16,16,64]{3,1,2,0:T(8,128)(2,1)S(1)}, u32[]{:S(2)}, u32[]{:S(2)}) collective-permute-start(bf16[4,16,16,64]{3,1,2,0:T(8,128)(2,1)S(1)} %pad_maximum_fusion.5), channel_id=1, source_target_pairs={{0,2},{1,3},{2,0},{3,1},{4,6},{5,7},{6,4},{7,5},{8,10},{9,11},{10,... | collective-permute-start | bytes 393224 | tf_op jit(solution)/shard_map/ppermute | solution.py:55
  24.3 10.8 %collective-permute-start.1 = (f32[8,16,16,64]{3,2,1,0:T(8,128)}, f32[8,16,16,64]{3,2,1,0:T(8,128)}, u32[]{:S(2)}, u32[]{:S(2)}) collective-permute-start(f32[8,16,16,64]{3,2,1,0:T(8,128)} %constant_dynamic-slice_fusion.6), channel_id=1, source_target_pairs={{0,1},{1,0},{2,3},{3,2},{4,5},{5,4},{6,7},{7,6},{8,9},{9,8},{10,11... | collective-permute-start | bytes 1572872 | tf_op jit(solution)/shard_map/ppermute | solution.py:77
  24.4 9.2 %copy-start.2 = (f32[16,16,16,64]{3,2,1,0:T(8,128)S(1)}, f32[16,16,16,64]{3,2,1,0:T(8,128)}, u32[]{:S(2)}) copy-start(f32[16,16,16,64]{3,2,1,0:T(8,128)} %get-tuple-element.10) | copy-start | bytes 3145732
  24.4 8.9 %collective-permute-start.7 = (bf16[4,16,16,64]{3,1,2,0:T(8,128)(2,1)S(1)}, bf16[4,16,16,64]{3,1,2,0:T(8,128)(2,1)S(1)}, u32[]{:S(2)}, u32[]{:S(2)}) collective-permute-start(bf16[4,16,16,64]{3,1,2,0:T(8,128)(2,1)S(1)} %pad_maximum_fusion.6), channel_id=1, source_target_pairs={{0,4},{1,5},{2,6},{3,7},{4,0},{5,1},{6,2},{7,3},{8,12},{9,13},{10,... | collective-permute-start | bytes 393224 | tf_op jit(solution)/shard_map/ppermute | solution.py:55
  33.4 1.9 %copy-start.1 = (f32[16,16,16,64]{3,2,1,0:T(8,128)S(1)}, f32[16,16,16,64]{3,2,1,0:T(8,128)}, u32[]{:S(2)}) copy-start(f32[16,16,16,64]{3,2,1,0:T(8,128)} %get-tuple-element.11) | copy-start | bytes 3145732
  36.7 4.0 %collective-permute-start.9 = (bf16[8,16,16,64]{3,1,2,0:T(8,128)(2,1)S(1)}, bf16[8,16,16,64]{3,1,2,0:T(8,128)(2,1)}, u32[]{:S(2)}, u32[]{:S(2)}) collective-permute-start(bf16[8,16,16,64]{3,1,2,0:T(8,128)(2,1)S(1)} %pad_maximum_fusion.4), channel_id=1, source_target_pairs={{0,1},{1,0},{2,3},{3,2},{4,5},{5,4},{6,7},{7,6},{8,9},{9,8},{10,11... | collective-permute-start | bytes 786440 | tf_op jit(solution)/shard_map/ppermute | solution.py:55
  36.8 5.1 %collective-permute-start.8 = (bf16[8,16,16,64]{3,1,2,0:T(8,128)(2,1)S(1)}, bf16[8,16,16,64]{3,1,2,0:T(8,128)(2,1)S(1)}, u32[]{:S(2)}, u32[]{:S(2)}) collective-permute-start(bf16[8,16,16,64]{3,1,2,0:T(8,128)(2,1)S(1)} %pad_maximum_fusion.3), channel_id=1, source_target_pairs={{0,1},{1,0},{2,3},{3,2},{4,5},{5,4},{6,7},{7,6},{8,9},{9,8},{10,11... | collective-permute-start | bytes 786440 | tf_op jit(solution)/shard_map/ppermute | solution.py:55
  37.3 14.0 %collective-permute-start.13 = (f32[4,16,16,64]{3,2,1,0:T(8,128)S(1)}, f32[4,16,16,64]{3,2,1,0:T(8,128)S(1)}, u32[]{:S(2)}, u32[]{:S(2)}) collective-permute-start(f32[4,16,16,64]{3,2,1,0:T(8,128)S(1)} %constant_dynamic-slice_fusion.2), channel_id=1, source_target_pairs={{0,4},{1,5},{2,6},{3,7},{4,0},{5,1},{6,2},{7,3},{8,12},{9,13},{10,... | collective-permute-start | bytes 786440 | tf_op jit(solution)/shard_map/ppermute | solution.py:77
  39.2 23.4 %collective-permute-start.10 = (f32[4,16,16,64]{3,2,1,0:T(8,128)S(1)}, f32[4,16,16,64]{3,2,1,0:T(8,128)S(1)}, u32[]{:S(2)}, u32[]{:S(2)}) collective-permute-start(f32[4,16,16,64]{3,2,1,0:T(8,128)S(1)} %constant_dynamic-slice_fusion.5), channel_id=1, source_target_pairs={{0,2},{1,3},{2,0},{3,1},{4,6},{5,7},{6,4},{7,5},{8,10},{9,11},{10,... | collective-permute-start | bytes 786440 | tf_op jit(solution)/shard_map/ppermute | solution.py:77
  52.0 14.0 %collective-permute-start.14 = (f32[2,16,16,64]{3,2,1,0:T(8,128)S(1)}, f32[2,16,16,64]{3,2,1,0:T(8,128)S(1)}, u32[]{:S(2)}, u32[]{:S(2)}) collective-permute-start(f32[2,16,16,64]{3,2,1,0:T(8,128)S(1)} %constant_dynamic-slice_fusion.1), channel_id=1, source_target_pairs={{0,2},{1,3},{2,0},{3,1},{4,6},{5,7},{6,4},{7,5},{8,10},{9,11},{10,... | collective-permute-start | bytes 393224 | tf_op jit(solution)/shard_map/ppermute | solution.py:77
  64.3 10.1 %collective-permute-start.11 = (f32[2,16,16,64]{3,2,1,0:T(8,128)S(1)}, f32[2,16,16,64]{3,2,1,0:T(8,128)S(1)}, u32[]{:S(2)}, u32[]{:S(2)}) collective-permute-start(f32[2,16,16,64]{3,2,1,0:T(8,128)S(1)} %constant_dynamic-slice_fusion.4), channel_id=1, source_target_pairs={{0,4},{1,5},{2,6},{3,7},{4,0},{5,1},{6,2},{7,3},{8,12},{9,13},{10,... | collective-permute-start | bytes 393224 | tf_op jit(solution)/shard_map/ppermute | solution.py:77
  66.0 10.2 %collective-permute-start.15 = (f32[1,16,16,64]{3,2,1,0:T(8,128)S(1)}, f32[1,16,16,64]{3,2,1,0:T(8,128)S(1)}, u32[]{:S(2)}, u32[]{:S(2)}) collective-permute-start(f32[1,16,16,64]{3,2,1,0:T(8,128)S(1)} %constant_dynamic-slice_fusion), channel_id=1, source_target_pairs={{0,8},{1,9},{2,10},{3,11},{4,12},{5,13},{6,14},{7,15},{8,0},{9,1},... | collective-permute-start | bytes 196616 | tf_op jit(solution)/shard_map/ppermute | solution.py:77
  74.5 7.6 %collective-permute-start.12 = (f32[1,16,16,64]{3,2,1,0:T(8,128)S(1)}, f32[1,16,16,64]{3,2,1,0:T(8,128)S(1)}, u32[]{:S(2)}, u32[]{:S(2)}) collective-permute-start(f32[1,16,16,64]{3,2,1,0:T(8,128)S(1)} %constant_dynamic-slice_fusion.3), channel_id=1, source_target_pairs={{0,8},{1,9},{2,10},{3,11},{4,12},{5,13},{6,14},{7,15},{8,0},{9,1},... | collective-permute-start | bytes 196616 | tf_op jit(solution)/shard_map/ppermute | solution.py:77

commit v17 on v14

--- a/solution.py
+++ b/solution.py
@@ -151,12 +151,12 @@
     orders = (tuple(bits), tuple(swapped))
     half = C // len(orders)
     early = 2
+    weight_ec = out_weight.reshape(C, C, p_size).transpose(1, 0, 2).reshape(C * C, p_size)
+    right_t, weight_ec = lax.optimization_barrier((right_t, weight_ec))
     gathers = [(right_t[h * half:(h + 1) * half][None], []) for h in range(len(orders))]
     for h in range(len(orders)):
         for bit in orders[h][::-1][:early]:
             gathers[h] = gather_step(gathers[h], "row", n, bit)
-
-    weight_ec = out_weight.reshape(C, C, p_size).transpose(1, 0, 2).reshape(C * C, p_size)
 
     grad_m, *part_t = pl.pallas_call(
         functools.partial(project_kernel, n_seq=n_seq, orders=orders),

time: 75.2 us -> 75.2 us (level)
  transfers between devices with their start and end apart: 16 -> 16, of which waited for: 7 -> 7; matrix products, arithmetic and copies ran while one was open for 19% -> 17% of each run, Pallas kernels for 20% -> 20%
where the time goes in v17:
time: 75.2 us; the launch traced here: 74.8 us
  waiting for transfers between devices  22.5 us (30%)
  starting transfers between devices  17.8 us (24%)
  Pallas kernels  15.2 us (20%)
  other arithmetic  10.1 us (13%)
  local copies, waits for them, and re-layouts  8.14 us (11%)
  between operations  0.93 us (1%)
    ppermute x8, waiting for transfers between devices, scatter_step(): return keep + lax.ppermute(send, axis, xor_pairs(n, bit))  13 us
    ppermute x8, starting transfers between devices, gather_step(): other = lax.ppermute(buf, axis, xor_pairs(n, bit))  9.82 us
    ppermute x8, waiting for transfers between devices, gather_step(): other = lax.ppermute(buf, axis, xor_pairs(n, bit))  9.57 us
    pallas_call x1, Pallas kernels, per_device(): pl.pallas_call(functools.partial(project_kernel, n_seq=n_seq, orders=orde...  8.18 us
    ppermute x8, starting transfers between devices, scatter_step(): return keep + lax.ppermute(send, axis, xor_pairs(n, bit))  8.02 us
    pallas_call x1, Pallas kernels, per_device(): pl.pallas_call(left_kernel, grid=(steps,), in_specs=[pl.BlockSpec((C, own...  7 us
    unnamed x9, local copies, waits for them, and re-layouts  3.04 us
    add x6, other arithmetic, scatter_step(): return keep + lax.ppermute(send, axis, xor_pairs(n, bit))  2.94 us
  transfers between devices with their start and end apart: 16, of which 7 were waited for; matrix products, arithmetic and copies ran while one was open for 17% of the time, Pallas kernels for 20%

profile of v17, /device:TPU:0, one launch (start us, length us, event | category | flops | bytes accessed | tf_op | source)
XLA Modules:
  0.0 74.8 jit_solution(18247341990663556294)
XLA Ops:
  0.6 1.0 %copy.8 = bf16[64,512]{0,1:T(8,128)(2,1)S(1)} copy(bf16[64,512]{1,0:T(8,128)(2,1)} %param.5) | data formatting | bytes 131072 | tf_op args[1]
  1.6 1.8 %copy.9 = bf16[32,32,128]{2,0,1:T(8,128)(2,1)} copy(bf16[32,32,128]{2,1,0:T(8,128)(2,1)} %bitcast.43) | data formatting | bytes 524288 | tf_op jit(solution)/shard_map/reshape | solution.py:154
  3.4 4.1 %collective-permute-start.4 = (bf16[1,16,16,64]{3,1,2,0:T(8,128)(2,1)S(1)}, bf16[1,16,16,64]{3,1,2,0:T(8,128)(2,1)S(1)}, u32[]{:S(2)}, u32[]{:S(2)}) collective-permute-start(bf16[1,16,16,64]{3,1,2,0:T(8,128)(2,1)S(1)} %get-tuple-element.42), channel_id=1, source_target_pairs={{0,8},{1,9},{2,10},{3,11},{4,12},{5,13},{6,14},{7,15},{8,0},{9,1},... | collective-permute-start | bytes 98312 | tf_op jit(solution)/shard_map/ppermute | solution.py:55
  7.5 0.1 collective-permute-start.2
  7.6 8.2 %shard_map.59 = (bf16[32,512,256]{2,1,0:T(8,128)(2,1)}, f32[16,16,16,64]{3,2,1,0:T(8,128)}, f32[16,16,16,64]{3,2,1,0:T(8,128)}) custom-call(bf16[16,256,128]{2,1,0:T(8,128)(2,1)} %p_ref.1, bf16[1024,128]{1,0:T(8,128)(2,1)} %bitcast.44, bf16[64,512]{1,0:T(8,128)(2,1)} %l_ref.1), custom_call_target="tpu_custom_call" | custom-call | flops 1610612736 | bytes 11534336 | tf_op jit(solution)/shard_map/pallas_call | solution.py:161
  15.7 1.5 %constant_dynamic-slice_fusion.7 = f32[8,16,16,64]{3,2,1,0:T(8,128)S(1)} fusion(f32[16,16,16,64]{3,2,1,0:T(8,128)} %get-tuple-element.13, s32[]{:T(128)S(6)} %select_n.127), kind=kLoop, calls=%fused_computation.46 | loop fusion | bytes 1048580 | tf_op jit(solution)/shard_map/dynamic_slice | solution.py:76
  17.2 0.1 collective-permute-start
  17.3 0.0 collective-permute-done.4
  17.3 0.0 copy-start.2
  17.3 0.6 copy-done.2
  17.9 0.0 collective-permute-done.2
  17.9 0.9 %broadcast_select_fusion.13 = (bf16[1,16,16,64]{3,1,2,0:T(8,128)(2,1)S(1)}, bf16[1,16,16,64]{3,1,2,0:T(8,128)(2,1)S(1)}, bf16[1,16,16,64]{3,1,2,0:T(8,128)(2,1)S(1)}, bf16[1,16,16,64]{3,1,2,0:T(8,128)(2,1)S(1)}) fusion(bf16[1,16,16,64]{3,1,2,0:T(8,128)(2,1)} %copy-done.2, pred[]{:T(512)S(6)} %eq.11, bf16[32,16,64]{2,0,1:T(8,128)(2,1)S(1)} %bitcast.41, ...), kind=kLoop, calls=%fused_computation.36 | loop fusion | flops 65536 | bytes 262145 | tf_op jit(solution)/shard_map/jit(_where)/select_n | solution.py:57
  18.8 0.7 pad_maximum_fusion.8
  19.5 1.8 %collective-permute-start.5 = (bf16[2,16,16,64]{3,1,2,0:T(8,128)(2,1)}, bf16[2,16,16,64]{3,1,2,0:T(8,128)(2,1)S(1)}, u32[]{:S(2)}, u32[]{:S(2)}) collective-permute-start(bf16[2,16,16,64]{3,1,2,0:T(8,128)(2,1)} %pad_maximum_fusion.8), channel_id=1, source_target_pairs={{0,2},{1,3},{2,0},{3,1},{4,6},{5,7},{6,4},{7,5},{8,10},{9,11},{10,... | collective-permute-start | bytes 196616 | tf_op jit(solution)/shard_map/ppermute | solution.py:55
  21.3 0.7 pad_maximum_fusion.7
  22.0 1.6 %collective-permute-start.3 = (bf16[2,16,16,64]{3,1,2,0:T(8,128)(2,1)}, bf16[2,16,16,64]{3,1,2,0:T(8,128)(2,1)}, u32[]{:S(2)}, u32[]{:S(2)}) collective-permute-start(bf16[2,16,16,64]{3,1,2,0:T(8,128)(2,1)} %pad_maximum_fusion.7), channel_id=1, source_target_pairs={{0,4},{1,5},{2,6},{3,7},{4,0},{5,1},{6,2},{7,3},{8,12},{9,13},{10,... | collective-permute-start | bytes 196616 | tf_op jit(solution)/shard_map/ppermute | solution.py:55
  23.6 0.0 copy-done
  23.6 1.1 %constant_dynamic-slice_fusion.6 = f32[8,16,16,64]{3,2,1,0:T(8,128)} fusion(f32[16,16,16,64]{3,2,1,0:T(8,128)S(1)} %copy-done, s32[]{:T(128)S(6)} %select_n.127), kind=kLoop, calls=%fused_computation.45 | loop fusion | bytes 1048580 | tf_op jit(solution)/shard_map/dynamic_slice | solution.py:76
  24.7 0.0 collective-permute-start.1
  24.7 1.0 %collective-permute-done.5 = bf16[2,16,16,64]{3,1,2,0:T(8,128)(2,1)S(1)} collective-permute-done((bf16[2,16,16,64]{3,1,2,0:T(8,128)(2,1)}, bf16[2,16,16,64]{3,1,2,0:T(8,128)(2,1)S(1)}, u32[]{:S(2)}, u32[]{:S(2)}) %collective-permute-start.5) | collective-permute-done | bytes 65568 | tf_op jit(solution)/shard_map/ppermute | solution.py:55
  25.7 2.3 %collective-permute-done.3 = bf16[2,16,16,64]{3,1,2,0:T(8,128)(2,1)} collective-permute-done((bf16[2,16,16,64]{3,1,2,0:T(8,128)(2,1)}, bf16[2,16,16,64]{3,1,2,0:T(8,128)(2,1)}, u32[]{:S(2)}, u32[]{:S(2)}) %collective-permute-start.3) | collective-permute-done | bytes 65568 | tf_op jit(solution)/shard_map/ppermute | solution.py:55
  27.9 1.0 %broadcast_select_fusion.9 = (bf16[2,16,16,64]{3,1,2,0:T(8,128)(2,1)S(1)}, bf16[2,16,16,64]{3,1,2,0:T(8,128)(2,1)S(1)}, bf16[2,16,16,64]{3,1,2,0:T(8,128)(2,1)S(1)}, bf16[2,16,16,64]{3,1,2,0:T(8,128)(2,1)S(1)}) fusion(bf16[2,16,16,64]{3,1,2,0:T(8,128)(2,1)S(1)} %collective-permute-done.5, pred[]{:T(512)S(6)} %eq.9, ...), kind=kLoop, calls=%fused_computation.28 | loop fusion | flops 196608 | bytes 524290 | tf_op jit(solution)/shard_map/jit(_where)/select_n | solution.py:57
  28.9 0.1 pad_maximum_fusion.5
  29.0 0.1 pad_maximum_fusion.6
  29.0 0.0 collective-permute-done
  29.0 0.0 copy-done.1
  29.0 1.4 %dynamic-slice_add_fusion.1 = f32[8,16,16,64]{3,2,1,0:T(8,128)S(1)} fusion(f32[8,16,16,64]{3,2,1,0:T(8,128)} %collective-permute-done, f32[16,16,16,64]{3,2,1,0:T(8,128)S(1)} %copy-done.1, s32[]{:T(128)S(6)} %select_n.126), kind=kLoop, calls=%fused_computation.4 | loop fusion | flops 131072 | bytes 1572868 | tf_op jit(solution)/shard_map/add | solution.py:77
  30.4 0.0 collective-permute-done.1
  30.4 1.4 %dynamic-slice_add_fusion = f32[8,16,16,64]{3,2,1,0:T(8,128)S(1)} fusion(f32[8,16,16,64]{3,2,1,0:T(8,128)} %collective-permute-done.1, f32[16,16,16,64]{3,2,1,0:T(8,128)S(1)} %copy-done, s32[]{:T(128)S(6)} %select_n.126), kind=kLoop, calls=%fused_computation.3 | loop fusion | flops 131072 | bytes 1572868 | tf_op jit(solution)/shard_map/add | solution.py:77
  31.8 1.6 %collective-permute-start.8 = (bf16[4,16,16,64]{3,1,2,0:T(8,128)(2,1)S(1)}, bf16[4,16,16,64]{3,1,2,0:T(8,128)(2,1)S(1)}, u32[]{:S(2)}, u32[]{:S(2)}) collective-permute-start(bf16[4,16,16,64]{3,1,2,0:T(8,128)(2,1)S(1)} %pad_maximum_fusion.6), channel_id=1, source_target_pairs={{0,4},{1,5},{2,6},{3,7},{4,0},{5,1},{6,2},{7,3},{8,12},{9,13},{10,... | collective-permute-start | bytes 393224 | tf_op jit(solution)/shard_map/ppermute | solution.py:55
  33.4 0.5 collective-permute-start.6
  34.0 0.3 collective-permute-start.13
  34.4 1.8 %collective-permute-start.10 = (f32[4,16,16,64]{3,2,1,0:T(8,128)S(1)}, f32[4,16,16,64]{3,2,1,0:T(8,128)S(1)}, u32[]{:S(2)}, u32[]{:S(2)}) collective-permute-start(f32[4,16,16,64]{3,2,1,0:T(8,128)S(1)} %constant_dynamic-slice_fusion.5), channel_id=1, source_target_pairs={{0,2},{1,3},{2,0},{3,1},{4,6},{5,7},{6,4},{7,5},{8,10},{9,11},{10,... | collective-permute-start | bytes 786440 | tf_op jit(solution)/shard_map/ppermute | solution.py:77
  36.1 5.0 %collective-permute-done.8 = bf16[4,16,16,64]{3,1,2,0:T(8,128)(2,1)S(1)} collective-permute-done((bf16[4,16,16,64]{3,1,2,0:T(8,128)(2,1)S(1)}, bf16[4,16,16,64]{3,1,2,0:T(8,128)(2,1)S(1)}, u32[]{:S(2)}, u32[]{:S(2)}) %collective-permute-start.8) | collective-permute-done | bytes 131104 | tf_op jit(solution)/shard_map/ppermute | solution.py:55
  41.2 0.1 pad_maximum_fusion.4
  41.3 0.1 collective-permute-start.9
  41.3 1.3 %collective-permute-done.6 = bf16[4,16,16,64]{3,1,2,0:T(8,128)(2,1)S(1)} collective-permute-done((bf16[4,16,16,64]{3,1,2,0:T(8,128)(2,1)S(1)}, bf16[4,16,16,64]{3,1,2,0:T(8,128)(2,1)S(1)}, u32[]{:S(2)}, u32[]{:S(2)}) %collective-permute-start.6) | collective-permute-done | bytes 131104 | tf_op jit(solution)/shard_map/ppermute | solution.py:55
  42.7 0.1 pad_maximum_fusion.3
  42.8 0.1 collective-permute-start.7
  42.9 7.8 %collective-permute-done.13 = f32[4,16,16,64]{3,2,1,0:T(8,128)S(1)} collective-permute-done((f32[4,16,16,64]{3,2,1,0:T(8,128)S(1)}, f32[4,16,16,64]{3,2,1,0:T(8,128)S(1)}, u32[]{:S(2)}, u32[]{:S(2)}) %collective-permute-start.13) | collective-permute-done | bytes 262176 | tf_op jit(solution)/shard_map/ppermute | solution.py:77
  50.7 0.1 dynamic-slice_add_fusion.2
  50.8 0.5 collective-permute-start.14
  51.3 0.7 collective-permute-done.10
  52.0 0.1 dynamic-slice_add_fusion.3
  52.1 1.0 %collective-permute-start.11 = (f32[2,16,16,64]{3,2,1,0:T(8,128)S(1)}, f32[2,16,16,64]{3,2,1,0:T(8,128)S(1)}, u32[]{:S(2)}, u32[]{:S(2)}) collective-permute-start(f32[2,16,16,64]{3,2,1,0:T(8,128)S(1)} %constant_dynamic-slice_fusion.4), channel_id=1, source_target_pairs={{0,4},{1,5},{2,6},{3,7},{4,0},{5,1},{6,2},{7,3},{8,12},{9,13},{10,... | collective-permute-start | bytes 393224 | tf_op jit(solution)/shard_map/ppermute | solution.py:77
  53.1 4.5 %collective-permute-done.14 = f32[2,16,16,64]{3,2,1,0:T(8,128)S(1)} collective-permute-done((f32[2,16,16,64]{3,2,1,0:T(8,128)S(1)}, f32[2,16,16,64]{3,2,1,0:T(8,128)S(1)}, u32[]{:S(2)}, u32[]{:S(2)}) %collective-permute-start.14) | collective-permute-done | bytes 131104 | tf_op jit(solution)/shard_map/ppermute | solution.py:77
  57.7 2.7 %collective-permute-start.15 = (f32[1,16,16,64]{3,2,1,0:T(8,128)S(1)}, f32[1,16,16,64]{3,2,1,0:T(8,128)S(1)}, u32[]{:S(2)}, u32[]{:S(2)}) collective-permute-start(f32[1,16,16,64]{3,2,1,0:T(8,128)S(1)} %constant_dynamic-slice_fusion), channel_id=1, source_target_pairs={{0,8},{1,9},{2,10},{3,11},{4,12},{5,13},{6,14},{7,15},{8,0},{9,1},... | collective-permute-start | bytes 196616 | tf_op jit(solution)/shard_map/ppermute | solution.py:77
  60.3 0.0 collective-permute-done.11
  60.4 1.7 %collective-permute-start.12 = (f32[1,16,16,64]{3,2,1,0:T(8,128)S(1)}, f32[1,16,16,64]{3,2,1,0:T(8,128)S(1)}, u32[]{:S(2)}, u32[]{:S(2)}) collective-permute-start(f32[1,16,16,64]{3,2,1,0:T(8,128)S(1)} %constant_dynamic-slice_fusion.3), channel_id=1, source_target_pairs={{0,8},{1,9},{2,10},{3,11},{4,12},{5,13},{6,14},{7,15},{8,0},{9,1},... | collective-permute-start | bytes 196616 | tf_op jit(solution)/shard_map/ppermute | solution.py:77
  62.1 0.0 collective-permute-done.9
  62.1 0.1 broadcast_select_fusion.1
  62.2 0.2 pad_maximum_fusion.2
  62.4 0.3 copy.13
  62.7 0.0 collective-permute-done.7
  62.7 0.1 broadcast_select_fusion.3
  62.9 0.2 pad_maximum_fusion.1
  63.1 0.3 copy.11
  63.4 1.8 %pad_maximum_fusion.rt_ref = bf16[16,32,16,64]{3,2,1,0:T(8,128)(2,1)} fusion(bf16[16,16,16,64]{3,2,1,0:T(8,128)(2,1)S(1)} %bitcast.38, bf16[16,16,16,64]{3,2,1,0:T(8,128)(2,1)S(1)} %bitcast.39), kind=kLoop, calls=%fused_computation | loop fusion | flops 524288 | bytes 2097152 | tf_op jit(solution)/shard_map/concatenate | solution.py:192
  65.2 7.0 %shard_map.60 = f32[512,64]{1,0:T(8,128)} custom-call(bf16[32,512,256]{2,1,0:T(8,128)(2,1)} %get-tuple-element.12.gm_ref, bf16[16,32,16,64]{3,2,1,0:T(8,128)(2,1)} %pad_maximum_fusion.rt_ref), custom_call_target="tpu_custom_call" | custom-call | flops 536870912 | bytes 9437184 | tf_op jit(solution)/shard_map/pallas_call | solution.py:201
  72.2 1.0 %convert_bitcast_fusion = bf16[64,512]{0,1:T(8,128)(2,1)S(1)} fusion(f32[512,64]{1,0:T(8,128)} %shard_map.60), kind=kLoop, calls=%fused_computation.26 | loop fusion | flops 32768 | bytes 196608 | tf_op jit(solution)/shard_map/convert_element_type | solution.py:217
  73.2 0.7 copy.15
  73.9 0.0 collective-permute-done.15
  73.9 0.0 collective-permute-done.12
  74.0 0.7 copy.16
  (17 shorter events, 0.4 us)
Async XLA Ops:
  3.4 13.9 %collective-permute-start.4 = (bf16[1,16,16,64]{3,1,2,0:T(8,128)(2,1)S(1)}, bf16[1,16,16,64]{3,1,2,0:T(8,128)(2,1)S(1)}, u32[]{:S(2)}, u32[]{:S(2)}) collective-permute-start(bf16[1,16,16,64]{3,1,2,0:T(8,128)(2,1)S(1)} %get-tuple-element.42), channel_id=1, source_target_pairs={{0,8},{1,9},{2,10},{3,11},{4,12},{5,13},{6,14},{7,15},{8,0},{9,1},... | collective-permute-start | bytes 98312 | tf_op jit(solution)/shard_map/ppermute | solution.py:55
  7.5 10.5 %collective-permute-start.2 = (bf16[1,16,16,64]{3,1,2,0:T(8,128)(2,1)S(1)}, bf16[1,16,16,64]{3,1,2,0:T(8,128)(2,1)}, u32[]{:S(2)}, u32[]{:S(2)}) collective-permute-start(bf16[1,16,16,64]{3,1,2,0:T(8,128)(2,1)S(1)} %get-tuple-element.43), channel_id=1, source_target_pairs={{0,8},{1,9},{2,10},{3,11},{4,12},{5,13},{6,14},{7,15},{8,0},{9,1},... | collective-permute-start | bytes 98312 | tf_op jit(solution)/shard_map/ppermute | solution.py:55
  15.7 7.8 %copy-start = (f32[16,16,16,64]{3,2,1,0:T(8,128)S(1)}, f32[16,16,16,64]{3,2,1,0:T(8,128)}, u32[]{:S(2)}) copy-start(f32[16,16,16,64]{3,2,1,0:T(8,128)} %get-tuple-element.14) | copy-start | bytes 3145732
  17.2 11.8 %collective-permute-start = (f32[8,16,16,64]{3,2,1,0:T(8,128)S(1)}, f32[8,16,16,64]{3,2,1,0:T(8,128)}, u32[]{:S(2)}, u32[]{:S(2)}) collective-permute-start(f32[8,16,16,64]{3,2,1,0:T(8,128)S(1)} %constant_dynamic-slice_fusion.7), channel_id=1, source_target_pairs={{0,1},{1,0},{2,3},{3,2},{4,5},{5,4},{6,7},{7,6},{8,9},{9,8},{10,11... | collective-permute-start | bytes 1572872 | tf_op jit(solution)/shard_map/ppermute | solution.py:77
  17.3 0.6 copy-start.2
  19.5 6.1 %collective-permute-start.5 = (bf16[2,16,16,64]{3,1,2,0:T(8,128)(2,1)}, bf16[2,16,16,64]{3,1,2,0:T(8,128)(2,1)S(1)}, u32[]{:S(2)}, u32[]{:S(2)}) collective-permute-start(bf16[2,16,16,64]{3,1,2,0:T(8,128)(2,1)} %pad_maximum_fusion.8), channel_id=1, source_target_pairs={{0,2},{1,3},{2,0},{3,1},{4,6},{5,7},{6,4},{7,5},{8,10},{9,11},{10,... | collective-permute-start | bytes 196616 | tf_op jit(solution)/shard_map/ppermute | solution.py:55
  22.0 5.9 %collective-permute-start.3 = (bf16[2,16,16,64]{3,1,2,0:T(8,128)(2,1)}, bf16[2,16,16,64]{3,1,2,0:T(8,128)(2,1)}, u32[]{:S(2)}, u32[]{:S(2)}) collective-permute-start(bf16[2,16,16,64]{3,1,2,0:T(8,128)(2,1)} %pad_maximum_fusion.7), channel_id=1, source_target_pairs={{0,4},{1,5},{2,6},{3,7},{4,0},{5,1},{6,2},{7,3},{8,12},{9,13},{10,... | collective-permute-start | bytes 196616 | tf_op jit(solution)/shard_map/ppermute | solution.py:55
  24.7 5.7 %collective-permute-start.1 = (f32[8,16,16,64]{3,2,1,0:T(8,128)}, f32[8,16,16,64]{3,2,1,0:T(8,128)}, u32[]{:S(2)}, u32[]{:S(2)}) collective-permute-start(f32[8,16,16,64]{3,2,1,0:T(8,128)} %constant_dynamic-slice_fusion.6), channel_id=1, source_target_pairs={{0,1},{1,0},{2,3},{3,2},{4,5},{5,4},{6,7},{7,6},{8,9},{9,8},{10,11... | collective-permute-start | bytes 1572872 | tf_op jit(solution)/shard_map/ppermute | solution.py:77
  24.7 4.4 %copy-start.1 = (f32[16,16,16,64]{3,2,1,0:T(8,128)S(1)}, f32[16,16,16,64]{3,2,1,0:T(8,128)}, u32[]{:S(2)}) copy-start(f32[16,16,16,64]{3,2,1,0:T(8,128)} %get-tuple-element.13) | copy-start | bytes 3145732
  31.8 9.3 %collective-permute-start.8 = (bf16[4,16,16,64]{3,1,2,0:T(8,128)(2,1)S(1)}, bf16[4,16,16,64]{3,1,2,0:T(8,128)(2,1)S(1)}, u32[]{:S(2)}, u32[]{:S(2)}) collective-permute-start(bf16[4,16,16,64]{3,1,2,0:T(8,128)(2,1)S(1)} %pad_maximum_fusion.6), channel_id=1, source_target_pairs={{0,4},{1,5},{2,6},{3,7},{4,0},{5,1},{6,2},{7,3},{8,12},{9,13},{10,... | collective-permute-start | bytes 393224 | tf_op jit(solution)/shard_map/ppermute | solution.py:55
  33.4 9.2 %collective-permute-start.6 = (bf16[4,16,16,64]{3,1,2,0:T(8,128)(2,1)S(1)}, bf16[4,16,16,64]{3,1,2,0:T(8,128)(2,1)S(1)}, u32[]{:S(2)}, u32[]{:S(2)}) collective-permute-start(bf16[4,16,16,64]{3,1,2,0:T(8,128)(2,1)S(1)} %pad_maximum_fusion.5), channel_id=1, source_target_pairs={{0,2},{1,3},{2,0},{3,1},{4,6},{5,7},{6,4},{7,5},{8,10},{9,11},{10,... | collective-permute-start | bytes 393224 | tf_op jit(solution)/shard_map/ppermute | solution.py:55
  34.0 16.7 %collective-permute-start.13 = (f32[4,16,16,64]{3,2,1,0:T(8,128)S(1)}, f32[4,16,16,64]{3,2,1,0:T(8,128)S(1)}, u32[]{:S(2)}, u32[]{:S(2)}) collective-permute-start(f32[4,16,16,64]{3,2,1,0:T(8,128)S(1)} %constant_dynamic-slice_fusion.2), channel_id=1, source_target_pairs={{0,4},{1,5},{2,6},{3,7},{4,0},{5,1},{6,2},{7,3},{8,12},{9,13},{10,... | collective-permute-start | bytes 786440 | tf_op jit(solution)/shard_map/ppermute | solution.py:77
  34.4 17.6 %collective-permute-start.10 = (f32[4,16,16,64]{3,2,1,0:T(8,128)S(1)}, f32[4,16,16,64]{3,2,1,0:T(8,128)S(1)}, u32[]{:S(2)}, u32[]{:S(2)}) collective-permute-start(f32[4,16,16,64]{3,2,1,0:T(8,128)S(1)} %constant_dynamic-slice_fusion.5), channel_id=1, source_target_pairs={{0,2},{1,3},{2,0},{3,1},{4,6},{5,7},{6,4},{7,5},{8,10},{9,11},{10,... | collective-permute-start | bytes 786440 | tf_op jit(solution)/shard_map/ppermute | solution.py:77
  41.3 20.8 %collective-permute-start.9 = (bf16[8,16,16,64]{3,1,2,0:T(8,128)(2,1)S(1)}, bf16[8,16,16,64]{3,1,2,0:T(8,128)(2,1)S(1)}, u32[]{:S(2)}, u32[]{:S(2)}) collective-permute-start(bf16[8,16,16,64]{3,1,2,0:T(8,128)(2,1)S(1)} %pad_maximum_fusion.4), channel_id=1, source_target_pairs={{0,1},{1,0},{2,3},{3,2},{4,5},{5,4},{6,7},{7,6},{8,9},{9,8},{10,11... | collective-permute-start | bytes 786440 | tf_op jit(solution)/shard_map/ppermute | solution.py:55
  42.8 19.9 %collective-permute-start.7 = (bf16[8,16,16,64]{3,1,2,0:T(8,128)(2,1)S(1)}, bf16[8,16,16,64]{3,1,2,0:T(8,128)(2,1)S(1)}, u32[]{:S(2)}, u32[]{:S(2)}) collective-permute-start(bf16[8,16,16,64]{3,1,2,0:T(8,128)(2,1)S(1)} %pad_maximum_fusion.3), channel_id=1, source_target_pairs={{0,1},{1,0},{2,3},{3,2},{4,5},{5,4},{6,7},{7,6},{8,9},{9,8},{10,11... | collective-permute-start | bytes 786440 | tf_op jit(solution)/shard_map/ppermute | solution.py:55
  50.8 6.8 %collective-permute-start.14 = (f32[2,16,16,64]{3,2,1,0:T(8,128)S(1)}, f32[2,16,16,64]{3,2,1,0:T(8,128)S(1)}, u32[]{:S(2)}, u32[]{:S(2)}) collective-permute-start(f32[2,16,16,64]{3,2,1,0:T(8,128)S(1)} %constant_dynamic-slice_fusion.1), channel_id=1, source_target_pairs={{0,2},{1,3},{2,0},{3,1},{4,6},{5,7},{6,4},{7,5},{8,10},{9,11},{10,... | collective-permute-start | bytes 393224 | tf_op jit(solution)/shard_map/ppermute | solution.py:77
  52.1 8.2 %collective-permute-start.11 = (f32[2,16,16,64]{3,2,1,0:T(8,128)S(1)}, f32[2,16,16,64]{3,2,1,0:T(8,128)S(1)}, u32[]{:S(2)}, u32[]{:S(2)}) collective-permute-start(f32[2,16,16,64]{3,2,1,0:T(8,128)S(1)} %constant_dynamic-slice_fusion.4), channel_id=1, source_target_pairs={{0,4},{1,5},{2,6},{3,7},{4,0},{5,1},{6,2},{7,3},{8,12},{9,13},{10,... | collective-permute-start | bytes 393224 | tf_op jit(solution)/shard_map/ppermute | solution.py:77
  57.7 16.2 %collective-permute-start.15 = (f32[1,16,16,64]{3,2,1,0:T(8,128)S(1)}, f32[1,16,16,64]{3,2,1,0:T(8,128)S(1)}, u32[]{:S(2)}, u32[]{:S(2)}) collective-permute-start(f32[1,16,16,64]{3,2,1,0:T(8,128)S(1)} %constant_dynamic-slice_fusion), channel_id=1, source_target_pairs={{0,8},{1,9},{2,10},{3,11},{4,12},{5,13},{6,14},{7,15},{8,0},{9,1},... | collective-permute-start | bytes 196616 | tf_op jit(solution)/shard_map/ppermute | solution.py:77
  60.4 13.5 %collective-permute-start.12 = (f32[1,16,16,64]{3,2,1,0:T(8,128)S(1)}, f32[1,16,16,64]{3,2,1,0:T(8,128)S(1)}, u32[]{:S(2)}, u32[]{:S(2)}) collective-permute-start(f32[1,16,16,64]{3,2,1,0:T(8,128)S(1)} %constant_dynamic-slice_fusion.3), channel_id=1, source_target_pairs={{0,8},{1,9},{2,10},{3,11},{4,12},{5,13},{6,14},{7,15},{8,0},{9,1},... | collective-permute-start | bytes 196616 | tf_op jit(solution)/shard_map/ppermute | solution.py:77

commit v18 on v14

--- a/solution.py
+++ b/solution.py
@@ -147,7 +147,7 @@
     per_dev = right_proj.shape[1] // C
 
     right_t = right_proj.reshape(n_seq, per_dev, C).transpose(2, 1, 0)
-    swapped = bits[:1] + bits[1:3][::-1] + bits[3:]
+    swapped = bits[:1] + bits[2:] + bits[1:2]
     orders = (tuple(bits), tuple(swapped))
     half = C // len(orders)
     early = 2

time: 75.2 us -> 82.2 us (1.093)
  waiting for transfers between devices: 22.5 us -> 29.6 us
    ppermute x8, waiting for transfers between devices: 13 us -> 18.5 us  [scatter_step(): return keep + lax.ppermute(send, axis, xor_pairs(n, bit))]
    ppermute x8, waiting for transfers between devices: 9.57 us -> 11.1 us  [gather_step(): other = lax.ppermute(buf, axis, xor_pairs(n, bit))]
    ppermute x8, starting transfers between devices: 9.82 us -> 8.8 us  [gather_step(): other = lax.ppermute(buf, axis, xor_pairs(n, bit))]
  transfers between devices with their start and end apart: 16 -> 16, of which waited for: 7 -> 4; matrix products, arithmetic and copies ran while one was open for 19% -> 18% of each run, Pallas kernels for 20% -> 19%
where the time goes in v18:
time: 82.2 us; the launch traced here: 81.6 us
  waiting for transfers between devices  29.6 us (36%)
  starting transfers between devices  17.6 us (21%)
  Pallas kernels  15.2 us (18%)
  other arithmetic  10.1 us (12%)
  local copies, waits for them, and re-layouts  8.13 us (10%)
  between operations  0.95 us (1%)
    ppermute x8, waiting for transfers between devices, scatter_step(): return keep + lax.ppermute(send, axis, xor_pairs(n, bit))  18.5 us
    ppermute x8, waiting for transfers between devices, gather_step(): other = lax.ppermute(buf, axis, xor_pairs(n, bit))  11.1 us
    ppermute x8, starting transfers between devices, gather_step(): other = lax.ppermute(buf, axis, xor_pairs(n, bit))  8.8 us
    ppermute x8, starting transfers between devices, scatter_step(): return keep + lax.ppermute(send, axis, xor_pairs(n, bit))  8.78 us
    pallas_call x1, Pallas kernels, per_device(): pl.pallas_call(functools.partial(project_kernel, n_seq=n_seq, orders=orde...  8.17 us
    pallas_call x1, Pallas kernels, per_device(): pl.pallas_call(left_kernel, grid=(steps,), in_specs=[pl.BlockSpec((C, own...  7 us
    unnamed x9, local copies, waits for them, and re-layouts  3.04 us
    add x6, other arithmetic, scatter_step(): return keep + lax.ppermute(send, axis, xor_pairs(n, bit))  2.94 us
  transfers between devices with their start and end apart: 16, of which 4 were waited for; matrix products, arithmetic and copies ran while one was open for 18% of the time, Pallas kernels for 19%

profile of v18, /device:TPU:0, one launch (start us, length us, event | category | flops | bytes accessed | tf_op | source)
XLA Modules:
  0.0 81.6 jit_solution(2642483543808218210)
XLA Ops:
  0.6 1.0 %copy.9 = bf16[64,512]{0,1:T(8,128)(2,1)S(1)} copy(bf16[64,512]{1,0:T(8,128)(2,1)} %param.5) | data formatting | bytes 131072 | tf_op args[1]
  1.6 3.0 %collective-permute-start.4 = (bf16[1,16,16,64]{3,1,2,0:T(8,128)(2,1)S(1)}, bf16[1,16,16,64]{3,1,2,0:T(8,128)(2,1)S(1)}, u32[]{:S(2)}, u32[]{:S(2)}) collective-permute-start(bf16[1,16,16,64]{3,1,2,0:T(8,128)(2,1)S(1)} %get-tuple-element.38), channel_id=1, source_target_pairs={{0,2},{1,3},{2,0},{3,1},{4,6},{5,7},{6,4},{7,5},{8,10},{9,11},{10,... | collective-permute-start | bytes 98312 | tf_op jit(solution)/shard_map/ppermute | solution.py:55
  4.6 2.6 %collective-permute-start.2 = (bf16[1,16,16,64]{3,1,2,0:T(8,128)(2,1)S(1)}, bf16[1,16,16,64]{3,1,2,0:T(8,128)(2,1)}, u32[]{:S(2)}, u32[]{:S(2)}) collective-permute-start(bf16[1,16,16,64]{3,1,2,0:T(8,128)(2,1)S(1)} %get-tuple-element.39), channel_id=1, source_target_pairs={{0,8},{1,9},{2,10},{3,11},{4,12},{5,13},{6,14},{7,15},{8,0},{9,1},... | collective-permute-start | bytes 98312 | tf_op jit(solution)/shard_map/ppermute | solution.py:55
  7.2 1.8 %copy.8 = bf16[32,32,128]{2,0,1:T(8,128)(2,1)} copy(bf16[32,32,128]{2,1,0:T(8,128)(2,1)} %bitcast.43) | data formatting | bytes 524288 | tf_op jit(solution)/shard_map/reshape | solution.py:159
  9.0 8.2 %shard_map.59 = (bf16[32,512,256]{2,1,0:T(8,128)(2,1)}, f32[16,16,16,64]{3,2,1,0:T(8,128)}, f32[16,16,16,64]{3,2,1,0:T(8,128)}) custom-call(bf16[16,256,128]{2,1,0:T(8,128)(2,1)} %p_ref.1, bf16[1024,128]{1,0:T(8,128)(2,1)} %bitcast.44, bf16[64,512]{1,0:T(8,128)(2,1)} %l_ref.1), custom_call_target="tpu_custom_call" | custom-call | flops 1610612736 | bytes 11534336 | tf_op jit(solution)/shard_map/pallas_call | solution.py:161
  17.2 1.5 %constant_dynamic-slice_fusion.7 = f32[8,16,16,64]{3,2,1,0:T(8,128)S(1)} fusion(f32[16,16,16,64]{3,2,1,0:T(8,128)} %get-tuple-element.10, s32[]{:T(128)S(6)} %select_n.133), kind=kLoop, calls=%fused_computation.46 | loop fusion | bytes 1048580 | tf_op jit(solution)/shard_map/dynamic_slice | solution.py:76
  18.7 0.1 collective-permute-start
  18.7 0.0 collective-permute-done.4
  18.8 0.0 copy-start.2
  18.8 0.6 copy-done.2
  19.4 0.0 collective-permute-done.2
  19.4 0.9 %broadcast_select_fusion.13 = (bf16[1,16,16,64]{3,1,2,0:T(8,128)(2,1)S(1)}, bf16[1,16,16,64]{3,1,2,0:T(8,128)(2,1)S(1)}, bf16[1,16,16,64]{3,1,2,0:T(8,128)(2,1)S(1)}, bf16[1,16,16,64]{3,1,2,0:T(8,128)(2,1)S(1)}) fusion(bf16[1,16,16,64]{3,1,2,0:T(8,128)(2,1)} %copy-done.2, pred[]{:T(512)S(6)} %eq.9, bf16[32,16,64]{2,0,1:T(8,128)(2,1)S(1)} %bitcast.41, ...), kind=kLoop, calls=%fused_computation.36 | loop fusion | flops 65536 | bytes 262146 | tf_op jit(solution)/shard_map/jit(_where)/select_n | solution.py:57
  20.3 0.7 pad_maximum_fusion.8
  21.0 0.3 collective-permute-start.5
  21.3 0.7 pad_maximum_fusion.7
  22.0 1.6 %collective-permute-start.3 = (bf16[2,16,16,64]{3,1,2,0:T(8,128)(2,1)}, bf16[2,16,16,64]{3,1,2,0:T(8,128)(2,1)}, u32[]{:S(2)}, u32[]{:S(2)}) collective-permute-start(bf16[2,16,16,64]{3,1,2,0:T(8,128)(2,1)} %pad_maximum_fusion.7), channel_id=1, source_target_pairs={{0,4},{1,5},{2,6},{3,7},{4,0},{5,1},{6,2},{7,3},{8,12},{9,13},{10,... | collective-permute-start | bytes 196616 | tf_op jit(solution)/shard_map/ppermute | solution.py:55
  23.6 0.0 copy-done
  23.6 1.1 %constant_dynamic-slice_fusion.6 = f32[8,16,16,64]{3,2,1,0:T(8,128)} fusion(f32[16,16,16,64]{3,2,1,0:T(8,128)S(1)} %copy-done, s32[]{:T(128)S(6)} %select_n.133), kind=kLoop, calls=%fused_computation.45 | loop fusion | bytes 1048580 | tf_op jit(solution)/shard_map/dynamic_slice | solution.py:76
  24.7 0.0 collective-permute-start.1
  24.7 6.1 %collective-permute-done.5 = bf16[2,16,16,64]{3,1,2,0:T(8,128)(2,1)S(1)} collective-permute-done((bf16[2,16,16,64]{3,1,2,0:T(8,128)(2,1)}, bf16[2,16,16,64]{3,1,2,0:T(8,128)(2,1)S(1)}, u32[]{:S(2)}, u32[]{:S(2)}) %collective-permute-start.5) | collective-permute-done | bytes 65568 | tf_op jit(solution)/shard_map/ppermute | solution.py:55
  30.8 0.0 collective-permute-done.3
  30.8 1.0 %broadcast_select_fusion.9 = (bf16[2,16,16,64]{3,1,2,0:T(8,128)(2,1)S(1)}, bf16[2,16,16,64]{3,1,2,0:T(8,128)(2,1)S(1)}, bf16[2,16,16,64]{3,1,2,0:T(8,128)(2,1)S(1)}, bf16[2,16,16,64]{3,1,2,0:T(8,128)(2,1)S(1)}) fusion(bf16[2,16,16,64]{3,1,2,0:T(8,128)(2,1)S(1)} %collective-permute-done.5, pred[]{:T(512)S(6)} %eq.11, ...), kind=kLoop, calls=%fused_computation.28 | loop fusion | flops 196608 | bytes 524290 | tf_op jit(solution)/shard_map/jit(_where)/select_n | solution.py:57
  31.8 0.1 pad_maximum_fusion.5
  31.9 0.1 pad_maximum_fusion.6
  31.9 0.0 collective-permute-done
  31.9 0.0 copy-done.1
  31.9 1.4 %dynamic-slice_add_fusion.1 = f32[8,16,16,64]{3,2,1,0:T(8,128)S(1)} fusion(f32[8,16,16,64]{3,2,1,0:T(8,128)} %collective-permute-done, f32[16,16,16,64]{3,2,1,0:T(8,128)S(1)} %copy-done.1, s32[]{:T(128)S(6)} %select_n.132), kind=kLoop, calls=%fused_computation.4 | loop fusion | flops 131072 | bytes 1572868 | tf_op jit(solution)/shard_map/add | solution.py:77
  33.3 0.0 collective-permute-done.1
  33.3 1.4 %dynamic-slice_add_fusion = f32[8,16,16,64]{3,2,1,0:T(8,128)S(1)} fusion(f32[8,16,16,64]{3,2,1,0:T(8,128)} %collective-permute-done.1, f32[16,16,16,64]{3,2,1,0:T(8,128)S(1)} %copy-done, s32[]{:T(128)S(6)} %select_n.132), kind=kLoop, calls=%fused_computation.3 | loop fusion | flops 131072 | bytes 1572868 | tf_op jit(solution)/shard_map/add | solution.py:77
  34.7 0.1 collective-permute-start.8
  34.8 0.6 collective-permute-start.6
  35.4 2.0 %collective-permute-start.13 = (f32[4,16,16,64]{3,2,1,0:T(8,128)S(1)}, f32[4,16,16,64]{3,2,1,0:T(8,128)S(1)}, u32[]{:S(2)}, u32[]{:S(2)}) collective-permute-start(f32[4,16,16,64]{3,2,1,0:T(8,128)S(1)} %constant_dynamic-slice_fusion.2), channel_id=1, source_target_pairs={{0,4},{1,5},{2,6},{3,7},{4,0},{5,1},{6,2},{7,3},{8,12},{9,13},{10,... | collective-permute-start | bytes 786440 | tf_op jit(solution)/shard_map/ppermute | solution.py:77
  37.4 1.6 %collective-permute-start.10 = (f32[4,16,16,64]{3,2,1,0:T(8,128)S(1)}, f32[4,16,16,64]{3,2,1,0:T(8,128)S(1)}, u32[]{:S(2)}, u32[]{:S(2)}) collective-permute-start(f32[4,16,16,64]{3,2,1,0:T(8,128)S(1)} %constant_dynamic-slice_fusion.5), channel_id=1, source_target_pairs={{0,2},{1,3},{2,0},{3,1},{4,6},{5,7},{6,4},{7,5},{8,10},{9,11},{10,... | collective-permute-start | bytes 786440 | tf_op jit(solution)/shard_map/ppermute | solution.py:77
  39.0 5.0 %collective-permute-done.8 = bf16[4,16,16,64]{3,1,2,0:T(8,128)(2,1)S(1)} collective-permute-done((bf16[4,16,16,64]{3,1,2,0:T(8,128)(2,1)S(1)}, bf16[4,16,16,64]{3,1,2,0:T(8,128)(2,1)S(1)}, u32[]{:S(2)}, u32[]{:S(2)}) %collective-permute-start.8) | collective-permute-done | bytes 131104 | tf_op jit(solution)/shard_map/ppermute | solution.py:55
  44.0 0.1 pad_maximum_fusion.4
  44.1 0.1 collective-permute-start.9
  44.2 0.0 collective-permute-done.6
  44.3 0.1 pad_maximum_fusion.3
  44.4 0.5 collective-permute-start.7
  44.9 9.0 %collective-permute-done.13 = f32[4,16,16,64]{3,2,1,0:T(8,128)S(1)} collective-permute-done((f32[4,16,16,64]{3,2,1,0:T(8,128)S(1)}, f32[4,16,16,64]{3,2,1,0:T(8,128)S(1)}, u32[]{:S(2)}, u32[]{:S(2)}) %collective-permute-start.13) | collective-permute-done | bytes 262176 | tf_op jit(solution)/shard_map/ppermute | solution.py:77
  53.9 0.1 dynamic-slice_add_fusion.2
  54.0 2.2 %collective-permute-start.14 = (f32[2,16,16,64]{3,2,1,0:T(8,128)S(1)}, f32[2,16,16,64]{3,2,1,0:T(8,128)S(1)}, u32[]{:S(2)}, u32[]{:S(2)}) collective-permute-start(f32[2,16,16,64]{3,2,1,0:T(8,128)S(1)} %constant_dynamic-slice_fusion.1), channel_id=1, source_target_pairs={{0,8},{1,9},{2,10},{3,11},{4,12},{5,13},{6,14},{7,15},{8,0},{9,1},... | collective-permute-start | bytes 393224 | tf_op jit(solution)/shard_map/ppermute | solution.py:77
  56.2 0.0 collective-permute-done.10
  56.2 0.1 dynamic-slice_add_fusion.3
  56.3 1.8 %collective-permute-start.11 = (f32[2,16,16,64]{3,2,1,0:T(8,128)S(1)}, f32[2,16,16,64]{3,2,1,0:T(8,128)S(1)}, u32[]{:S(2)}, u32[]{:S(2)}) collective-permute-start(f32[2,16,16,64]{3,2,1,0:T(8,128)S(1)} %constant_dynamic-slice_fusion.4), channel_id=1, source_target_pairs={{0,4},{1,5},{2,6},{3,7},{4,0},{5,1},{6,2},{7,3},{8,12},{9,13},{10,... | collective-permute-start | bytes 393224 | tf_op jit(solution)/shard_map/ppermute | solution.py:77
  58.1 9.6 %collective-permute-done.14 = f32[2,16,16,64]{3,2,1,0:T(8,128)S(1)} collective-permute-done((f32[2,16,16,64]{3,2,1,0:T(8,128)S(1)}, f32[2,16,16,64]{3,2,1,0:T(8,128)S(1)}, u32[]{:S(2)}, u32[]{:S(2)}) %collective-permute-start.14) | collective-permute-done | bytes 131104 | tf_op jit(solution)/shard_map/ppermute | solution.py:77
  67.8 0.6 collective-permute-start.15
  68.3 0.0 collective-permute-done.11
  68.4 0.5 collective-permute-start.12
  68.9 0.0 collective-permute-done.9
  68.9 0.1 broadcast_select_fusion.1
  69.1 0.2 pad_maximum_fusion.2
  69.3 0.3 copy.13
  69.6 0.0 collective-permute-done.7
  69.6 0.1 broadcast_select_fusion.3
  69.7 0.2 pad_maximum_fusion.1
  69.9 0.3 copy.11
  70.2 1.8 %pad_maximum_fusion.rt_ref = bf16[16,32,16,64]{3,2,1,0:T(8,128)(2,1)} fusion(bf16[16,16,16,64]{3,2,1,0:T(8,128)(2,1)S(1)} %bitcast.38, bf16[16,16,16,64]{3,2,1,0:T(8,128)(2,1)S(1)} %bitcast.39), kind=kLoop, calls=%fused_computation | loop fusion | flops 524288 | bytes 2097152 | tf_op jit(solution)/shard_map/concatenate | solution.py:192
  72.0 7.0 %shard_map.60 = f32[512,64]{1,0:T(8,128)} custom-call(bf16[32,512,256]{2,1,0:T(8,128)(2,1)} %get-tuple-element.9.gm_ref, bf16[16,32,16,64]{3,2,1,0:T(8,128)(2,1)} %pad_maximum_fusion.rt_ref), custom_call_target="tpu_custom_call" | custom-call | flops 536870912 | bytes 9437184 | tf_op jit(solution)/shard_map/pallas_call | solution.py:201
  79.0 1.0 %convert_bitcast_fusion = bf16[64,512]{0,1:T(8,128)(2,1)S(1)} fusion(f32[512,64]{1,0:T(8,128)} %shard_map.60), kind=kLoop, calls=%fused_computation.26 | loop fusion | flops 32768 | bytes 196608 | tf_op jit(solution)/shard_map/convert_element_type | solution.py:217
  80.0 0.7 copy.15
  80.7 0.0 collective-permute-done.15
  80.8 0.0 collective-permute-done.12
  80.9 0.7 copy.16
  (17 shorter events, 0.4 us)
Async XLA Ops:
  1.6 17.1 %collective-permute-start.4 = (bf16[1,16,16,64]{3,1,2,0:T(8,128)(2,1)S(1)}, bf16[1,16,16,64]{3,1,2,0:T(8,128)(2,1)S(1)}, u32[]{:S(2)}, u32[]{:S(2)}) collective-permute-start(bf16[1,16,16,64]{3,1,2,0:T(8,128)(2,1)S(1)} %get-tuple-element.38), channel_id=1, source_target_pairs={{0,2},{1,3},{2,0},{3,1},{4,6},{5,7},{6,4},{7,5},{8,10},{9,11},{10,... | collective-permute-start | bytes 98312 | tf_op jit(solution)/shard_map/ppermute | solution.py:55
  4.6 14.7 %collective-permute-start.2 = (bf16[1,16,16,64]{3,1,2,0:T(8,128)(2,1)S(1)}, bf16[1,16,16,64]{3,1,2,0:T(8,128)(2,1)}, u32[]{:S(2)}, u32[]{:S(2)}) collective-permute-start(bf16[1,16,16,64]{3,1,2,0:T(8,128)(2,1)S(1)} %get-tuple-element.39), channel_id=1, source_target_pairs={{0,8},{1,9},{2,10},{3,11},{4,12},{5,13},{6,14},{7,15},{8,0},{9,1},... | collective-permute-start | bytes 98312 | tf_op jit(solution)/shard_map/ppermute | solution.py:55
  17.2 6.4 %copy-start = (f32[16,16,16,64]{3,2,1,0:T(8,128)S(1)}, f32[16,16,16,64]{3,2,1,0:T(8,128)}, u32[]{:S(2)}) copy-start(f32[16,16,16,64]{3,2,1,0:T(8,128)} %get-tuple-element.11) | copy-start | bytes 3145732
  18.7 13.3 %collective-permute-start = (f32[8,16,16,64]{3,2,1,0:T(8,128)S(1)}, f32[8,16,16,64]{3,2,1,0:T(8,128)}, u32[]{:S(2)}, u32[]{:S(2)}) collective-permute-start(f32[8,16,16,64]{3,2,1,0:T(8,128)S(1)} %constant_dynamic-slice_fusion.7), channel_id=1, source_target_pairs={{0,1},{1,0},{2,3},{3,2},{4,5},{5,4},{6,7},{7,6},{8,9},{9,8},{10,11... | collective-permute-start | bytes 1572872 | tf_op jit(solution)/shard_map/ppermute | solution.py:77
  18.8 0.6 copy-start.2
  21.0 9.8 %collective-permute-start.5 = (bf16[2,16,16,64]{3,1,2,0:T(8,128)(2,1)}, bf16[2,16,16,64]{3,1,2,0:T(8,128)(2,1)S(1)}, u32[]{:S(2)}, u32[]{:S(2)}) collective-permute-start(bf16[2,16,16,64]{3,1,2,0:T(8,128)(2,1)} %pad_maximum_fusion.8), channel_id=1, source_target_pairs={{0,8},{1,9},{2,10},{3,11},{4,12},{5,13},{6,14},{7,15},{8,0},{9,1},... | collective-permute-start | bytes 196616 | tf_op jit(solution)/shard_map/ppermute | solution.py:55
  22.0 8.8 %collective-permute-start.3 = (bf16[2,16,16,64]{3,1,2,0:T(8,128)(2,1)}, bf16[2,16,16,64]{3,1,2,0:T(8,128)(2,1)}, u32[]{:S(2)}, u32[]{:S(2)}) collective-permute-start(bf16[2,16,16,64]{3,1,2,0:T(8,128)(2,1)} %pad_maximum_fusion.7), channel_id=1, source_target_pairs={{0,4},{1,5},{2,6},{3,7},{4,0},{5,1},{6,2},{7,3},{8,12},{9,13},{10,... | collective-permute-start | bytes 196616 | tf_op jit(solution)/shard_map/ppermute | solution.py:55
  24.7 8.6 %collective-permute-start.1 = (f32[8,16,16,64]{3,2,1,0:T(8,128)}, f32[8,16,16,64]{3,2,1,0:T(8,128)}, u32[]{:S(2)}, u32[]{:S(2)}) collective-permute-start(f32[8,16,16,64]{3,2,1,0:T(8,128)} %constant_dynamic-slice_fusion.6), channel_id=1, source_target_pairs={{0,1},{1,0},{2,3},{3,2},{4,5},{5,4},{6,7},{7,6},{8,9},{9,8},{10,11... | collective-permute-start | bytes 1572872 | tf_op jit(solution)/shard_map/ppermute | solution.py:77
  24.7 7.3 %copy-start.1 = (f32[16,16,16,64]{3,2,1,0:T(8,128)S(1)}, f32[16,16,16,64]{3,2,1,0:T(8,128)}, u32[]{:S(2)}) copy-start(f32[16,16,16,64]{3,2,1,0:T(8,128)} %get-tuple-element.10) | copy-start | bytes 3145732
  34.7 9.3 %collective-permute-start.8 = (bf16[4,16,16,64]{3,1,2,0:T(8,128)(2,1)S(1)}, bf16[4,16,16,64]{3,1,2,0:T(8,128)(2,1)S(1)}, u32[]{:S(2)}, u32[]{:S(2)}) collective-permute-start(bf16[4,16,16,64]{3,1,2,0:T(8,128)(2,1)S(1)} %pad_maximum_fusion.6), channel_id=1, source_target_pairs={{0,4},{1,5},{2,6},{3,7},{4,0},{5,1},{6,2},{7,3},{8,12},{9,13},{10,... | collective-permute-start | bytes 393224 | tf_op jit(solution)/shard_map/ppermute | solution.py:55
  34.8 9.4 %collective-permute-start.6 = (bf16[4,16,16,64]{3,1,2,0:T(8,128)(2,1)S(1)}, bf16[4,16,16,64]{3,1,2,0:T(8,128)(2,1)S(1)}, u32[]{:S(2)}, u32[]{:S(2)}) collective-permute-start(bf16[4,16,16,64]{3,1,2,0:T(8,128)(2,1)S(1)} %pad_maximum_fusion.5), channel_id=1, source_target_pairs={{0,2},{1,3},{2,0},{3,1},{4,6},{5,7},{6,4},{7,5},{8,10},{9,11},{10,... | collective-permute-start | bytes 393224 | tf_op jit(solution)/shard_map/ppermute | solution.py:55
  35.4 18.5 %collective-permute-start.13 = (f32[4,16,16,64]{3,2,1,0:T(8,128)S(1)}, f32[4,16,16,64]{3,2,1,0:T(8,128)S(1)}, u32[]{:S(2)}, u32[]{:S(2)}) collective-permute-start(f32[4,16,16,64]{3,2,1,0:T(8,128)S(1)} %constant_dynamic-slice_fusion.2), channel_id=1, source_target_pairs={{0,4},{1,5},{2,6},{3,7},{4,0},{5,1},{6,2},{7,3},{8,12},{9,13},{10,... | collective-permute-start | bytes 786440 | tf_op jit(solution)/shard_map/ppermute | solution.py:77
  37.4 18.8 %collective-permute-start.10 = (f32[4,16,16,64]{3,2,1,0:T(8,128)S(1)}, f32[4,16,16,64]{3,2,1,0:T(8,128)S(1)}, u32[]{:S(2)}, u32[]{:S(2)}) collective-permute-start(f32[4,16,16,64]{3,2,1,0:T(8,128)S(1)} %constant_dynamic-slice_fusion.5), channel_id=1, source_target_pairs={{0,2},{1,3},{2,0},{3,1},{4,6},{5,7},{6,4},{7,5},{8,10},{9,11},{10,... | collective-permute-start | bytes 786440 | tf_op jit(solution)/shard_map/ppermute | solution.py:77
  44.1 24.8 %collective-permute-start.9 = (bf16[8,16,16,64]{3,1,2,0:T(8,128)(2,1)S(1)}, bf16[8,16,16,64]{3,1,2,0:T(8,128)(2,1)S(1)}, u32[]{:S(2)}, u32[]{:S(2)}) collective-permute-start(bf16[8,16,16,64]{3,1,2,0:T(8,128)(2,1)S(1)} %pad_maximum_fusion.4), channel_id=1, source_target_pairs={{0,1},{1,0},{2,3},{3,2},{4,5},{5,4},{6,7},{7,6},{8,9},{9,8},{10,11... | collective-permute-start | bytes 786440 | tf_op jit(solution)/shard_map/ppermute | solution.py:55
  44.4 25.2 %collective-permute-start.7 = (bf16[8,16,16,64]{3,1,2,0:T(8,128)(2,1)S(1)}, bf16[8,16,16,64]{3,1,2,0:T(8,128)(2,1)S(1)}, u32[]{:S(2)}, u32[]{:S(2)}) collective-permute-start(bf16[8,16,16,64]{3,1,2,0:T(8,128)(2,1)S(1)} %pad_maximum_fusion.3), channel_id=1, source_target_pairs={{0,1},{1,0},{2,3},{3,2},{4,5},{5,4},{6,7},{7,6},{8,9},{9,8},{10,11... | collective-permute-start | bytes 786440 | tf_op jit(solution)/shard_map/ppermute | solution.py:55
  54.0 13.7 %collective-permute-start.14 = (f32[2,16,16,64]{3,2,1,0:T(8,128)S(1)}, f32[2,16,16,64]{3,2,1,0:T(8,128)S(1)}, u32[]{:S(2)}, u32[]{:S(2)}) collective-permute-start(f32[2,16,16,64]{3,2,1,0:T(8,128)S(1)} %constant_dynamic-slice_fusion.1), channel_id=1, source_target_pairs={{0,8},{1,9},{2,10},{3,11},{4,12},{5,13},{6,14},{7,15},{8,0},{9,1},... | collective-permute-start | bytes 393224 | tf_op jit(solution)/shard_map/ppermute | solution.py:77
  56.3 12.0 %collective-permute-start.11 = (f32[2,16,16,64]{3,2,1,0:T(8,128)S(1)}, f32[2,16,16,64]{3,2,1,0:T(8,128)S(1)}, u32[]{:S(2)}, u32[]{:S(2)}) collective-permute-start(f32[2,16,16,64]{3,2,1,0:T(8,128)S(1)} %constant_dynamic-slice_fusion.4), channel_id=1, source_target_pairs={{0,4},{1,5},{2,6},{3,7},{4,0},{5,1},{6,2},{7,3},{8,12},{9,13},{10,... | collective-permute-start | bytes 393224 | tf_op jit(solution)/shard_map/ppermute | solution.py:77
  67.8 13.0 %collective-permute-start.15 = (f32[1,16,16,64]{3,2,1,0:T(8,128)S(1)}, f32[1,16,16,64]{3,2,1,0:T(8,128)S(1)}, u32[]{:S(2)}, u32[]{:S(2)}) collective-permute-start(f32[1,16,16,64]{3,2,1,0:T(8,128)S(1)} %constant_dynamic-slice_fusion), channel_id=1, source_target_pairs={{0,2},{1,3},{2,0},{3,1},{4,6},{5,7},{6,4},{7,5},{8,10},{9,11},{10,... | collective-permute-start | bytes 196616 | tf_op jit(solution)/shard_map/ppermute | solution.py:77
  68.4 12.4 %collective-permute-start.12 = (f32[1,16,16,64]{3,2,1,0:T(8,128)S(1)}, f32[1,16,16,64]{3,2,1,0:T(8,128)S(1)}, u32[]{:S(2)}, u32[]{:S(2)}) collective-permute-start(f32[1,16,16,64]{3,2,1,0:T(8,128)S(1)} %constant_dynamic-slice_fusion.3), channel_id=1, source_target_pairs={{0,8},{1,9},{2,10},{3,11},{4,12},{5,13},{6,14},{7,15},{8,0},{9,1},... | collective-permute-start | bytes 196616 | tf_op jit(solution)/shard_map/ppermute | solution.py:77
